TPU v7x, 32 devices: a whole 2x2x4 slice. The times are simulated.
32 devices in a mesh: seq: 8 (over z, y), head: 4 (over x, core).
Axes of the slice: x: 2, y: 2, z: 4, core: 2. Of those that a mesh axis runs over, the one named last changes fastest.
Arguments:
- projected: bfloat16 [1024, 3, 4096], P('seq', None, 'head'), may hold values from -8 to 8
- destination: int32 [1024], P('seq'), may hold values from 0 to 1023, as said below
- doc_lengths: int32 [4], replicated, may hold values from 1 to 512, 1024 in all
- random_blocks: int32 [8, 3], replicated, may hold values from 0 to 7, as said below
- global_owner: int32 [8], replicated, may hold values from 0 to 7, as said below
- out_weight: bfloat16 [4096, 4096], P('head'), may hold values from -0.09375 to 0.09375
Outputs:
- attended: bfloat16 [1024, 4096], P(('seq', 'head'))
Inputs may be any that keep to these rules, and one draw needn't show every extreme that they name: Each packed position appears exactly once. Of the rows of one device (one index of seq, 128 rows), at most 32 have destinations owned by one owner (destination // 128), and in every draw some device sends exactly 32 rows to some owner. The owner (index) of random_blocks[b, r] lies at most 2 owners away from the owner of block b, counted cyclically over the owners. `global_owner`: each owner appears exactly once.
All inputs are finite; a program needn't handle non-finite values.
Results may differ from a plain program's by a relative error of at most 0.015.
Values may be sent and summed in bfloat16 or wider, within the bound.
No kernel may reach another device: no remote copies, remote signals or barrier semaphores. Data moves between devices by JAX's collectives and lax.ppermute only.
A program may use at most 128 MiB of HBM per device.

v0:
```python
import math

import jax
import jax.numpy as jnp
from jax import lax
from jax.sharding import PartitionSpec as P

HD = 128
BLK = 128
R = 3
RDEV = 2


big_negative = -1e30


def from_behind(block, axis, distance):
    devices = range(lax.axis_size(axis))
    route = [((i - distance) % len(devices), i) for i in devices]
    return lax.ppermute(block, axis, route)


def from_root(x, axis, root):
    mine = lax.axis_index(axis) == root
    return lax.psum(jnp.where(mine, x, jnp.zeros_like(x)), axis)


def combined_all(x, axis, combine):
    everything = jax.tree.map(lambda part: lax.all_gather(part, axis), x)
    first = jax.tree.map(lambda part: part[0], everything)

    def step(k, so_far):
        return combine(so_far, jax.tree.map(lambda part: part[k], everything))

    return lax.fori_loop(1, lax.axis_size(axis), step, first)


def segment_of(positions, bounds):
    return jnp.sum((bounds[None, :] <= positions[:, None]).astype(jnp.int32), axis=1)


def combine_parts(left_part, right_part):
    top_left, total_left, accum_left = left_part
    top_right, total_right, accum_right = right_part
    row_peak = jnp.maximum(top_left, top_right)
    factor_left = jnp.exp(top_left - row_peak)
    factor_right = jnp.exp(top_right - row_peak)
    return (
        row_peak,
        total_left * factor_left + total_right * factor_right,
        accum_left * factor_left[:, :, None] + accum_right * factor_right[:, :, None],
    )


def shards(projected, destination, doc_lengths, random_blocks, global_owner, out_weight):
    owners = lax.axis_size("seq")
    own_index = lax.axis_index("seq")
    tok_dev = projected.shape[0]
    columns = projected.shape[2]
    heads_here = columns // HD
    per_dev = tok_dev // BLK
    blocks_all = owners * per_dev
    capacity = 2 * (tok_dev // owners)
    score_scale = 1.0 / math.sqrt(HD)
    target_owner = destination // tok_dev
    onehot = (target_owner[:, None] == jnp.arange(owners, dtype=jnp.int32)[None, :]).astype(
        jnp.int32
    )
    before = jnp.cumsum(onehot, axis=0) - onehot
    slot_rank = jnp.sum(before * onehot, axis=1)
    outgoing = (
        jnp.zeros((owners, capacity, 3, columns), projected.dtype)
        .at[target_owner, slot_rank]
        .set(projected)
    )
    slots = (
        jnp.full((owners, capacity), -1, jnp.int32)
        .at[target_owner, slot_rank]
        .set(destination % tok_dev)
    )
    incoming, landing = (
        lax.all_to_all(outgoing, "seq", split_axis=0, concat_axis=0, tiled=True),
        lax.all_to_all(slots, "seq", split_axis=0, concat_axis=0, tiled=True),
    )
    landing = landing.reshape(-1)
    landing = jnp.where(landing >= 0, landing, tok_dev)
    routed = (
        jnp.zeros((tok_dev, 3, columns), projected.dtype)
        .at[landing]
        .set(incoming.reshape(owners * capacity, 3, columns), mode="drop")
    )
    keyval = routed[:, 1:, :]
    fetched = {0: keyval}
    offsets = list(range(-RDEV, 0)) + list(range(1, RDEV + 1))
    for offset in offsets:
        fetched[offset] = from_behind(keyval, "seq", -offset)
    band_blocks = jnp.stack([fetched[offset] for offset in range(-RDEV, RDEV + 1)])
    block_ids = own_index * per_dev + jnp.arange(per_dev, dtype=jnp.int32)
    local_pick = jnp.arange(per_dev, dtype=jnp.int32) + RDEV * per_dev
    window_pick = local_pick[:, None] + jnp.arange(-1, 2, dtype=jnp.int32)[None, :]
    chosen_rand = lax.dynamic_slice_in_dim(random_blocks, own_index * per_dev, per_dev, 0)
    away_dev = (chosen_rand // per_dev - own_index) % owners
    away_dev = jnp.where(away_dev > owners // 2, away_dev - owners, away_dev)
    rand_pick = (away_dev + RDEV) * per_dev + chosen_rand % per_dev
    block_picks = jnp.concatenate([window_pick, rand_pick], axis=1)
    gathered = jnp.take(band_blocks, block_picks, axis=0)
    near_keys = gathered[:, :, :, 0, :].reshape(per_dev, (3 + R) * BLK, heads_here, HD)
    near_values = gathered[:, :, :, 1, :].reshape(per_dev, (3 + R) * BLK, heads_here, HD)
    owner_dev = global_owner[0]
    global_rows = from_root(routed, "seq", owner_dev)
    glob_keys = global_rows[:, 1, :].reshape(tok_dev, heads_here, HD)
    glob_values = global_rows[:, 2, :].reshape(tok_dev, heads_here, HD)
    queries = routed[:, 0, :].reshape(per_dev, BLK, heads_here, HD)
    near_scores = (
        jnp.einsum("bqhd,bkhd->bhqk", queries, near_keys, preferred_element_type=jnp.float32)
        * score_scale
    )
    far_scores = (
        jnp.einsum("bqhd,khd->bhqk", queries, glob_keys, preferred_element_type=jnp.float32)
        * score_scale
    )
    bounds = jnp.cumsum(doc_lengths)
    query_pos = own_index * tok_dev + jnp.arange(tok_dev, dtype=jnp.int32)
    query_doc = segment_of(query_pos, bounds).reshape(per_dev, BLK)
    window_blocks = (block_ids[:, None] + jnp.arange(-1, 2, dtype=jnp.int32)[None, :]) % blocks_all
    key_pos = (
        window_blocks[:, :, None] * BLK + jnp.arange(BLK, dtype=jnp.int32)[None, None, :]
    ).reshape(-1)
    key_doc = segment_of(key_pos, bounds).reshape(per_dev, 3 * BLK)
    same_doc = query_doc[:, :, None] == key_doc[:, None, :]
    allowed = jnp.concatenate(
        [same_doc, jnp.ones((per_dev, BLK, R * BLK), dtype=jnp.bool_)], axis=2
    )
    near_scores = jnp.where(allowed[:, None], near_scores, big_negative)
    row_peak = jnp.maximum(jnp.max(near_scores, axis=3), jnp.max(far_scores, axis=3))
    near_exp = jnp.exp(near_scores - row_peak[..., None])
    far_exp = jnp.exp(far_scores - row_peak[..., None])
    denominator = jnp.sum(near_exp, axis=3) + jnp.sum(far_exp, axis=3)
    mixed_sum = jnp.einsum(
        "bhqk,bkhd->bqhd",
        near_exp.astype(jnp.bfloat16),
        near_values,
        preferred_element_type=jnp.float32,
    )
    mixed_sum = mixed_sum + jnp.einsum(
        "bhqk,khd->bqhd",
        far_exp.astype(jnp.bfloat16),
        glob_values,
        preferred_element_type=jnp.float32,
    )
    sparse = (mixed_sum / jnp.transpose(denominator, (0, 2, 1))[..., None]).reshape(
        tok_dev, columns
    )
    sparse = sparse.astype(jnp.bfloat16)
    glob_queries = global_rows[:, 0, :].reshape(tok_dev, heads_here, HD)
    local_keys = routed[:, 1, :].reshape(tok_dev, heads_here, HD)
    local_values = routed[:, 2, :].reshape(tok_dev, heads_here, HD).astype(jnp.float32)
    all_scores = (
        jnp.einsum("qhd,khd->hqk", glob_queries, local_keys, preferred_element_type=jnp.float32)
        * score_scale
    )
    local_peak = jnp.max(all_scores, axis=2)
    weights = jnp.exp(all_scores - local_peak[..., None])
    part_total = jnp.sum(weights, axis=2)
    part_accum = jnp.einsum("hqk,khd->hqd", weights, local_values, precision=lax.Precision.HIGHEST)
    peak_all, total_all, accum_all = combined_all(
        (local_peak, part_total, part_accum), "seq", combine_parts
    )
    glob_out = jnp.transpose(accum_all / total_all[..., None], (1, 0, 2)).reshape(tok_dev, columns)
    glob_out = glob_out.astype(jnp.bfloat16)
    attn_rows = jnp.where(own_index == owner_dev, glob_out, sparse)
    return lax.psum_scatter(
        jnp.dot(attn_rows, out_weight, preferred_element_type=jnp.float32).astype(jnp.bfloat16),
        "head",
        scatter_dimension=0,
        tiled=True,
    )


def solution(mesh):
    in_specs = (P("seq", None, "head"), P("seq"), P(), P(), P(), P("head", None))
    out_specs = P(("seq", "head"), None)
    return jax.shard_map(shards, mesh=mesh, in_specs=in_specs, out_specs=out_specs, check_vma=False)
```

profile of v0, /device:TPU:0, one launch (start us, length us, event | category | flops | bytes accessed | tf_op | source)
XLA Modules:
  0.0 372.2 jit_solution(12199506883128773803)
XLA Ops:
  8.3 19.9 %scatter_fusion = s32[8,32]{1,0:T(8,128)} fusion(s32[8,32]{1,0:T(8,128)} %broadcast_in_dim.38, s32[128]{0:T(128)S(1)} %fusion.41, s32[128]{0:T(128)S(1)} %get-tuple-element.210), kind=kCustom, calls=%fused_computation.1 | custom fusion | bytes 2560 | tf_op jit(solution)/shard_map/scatter | solution.py:79
  28.1 7.3 %all-to-all-start = ((s32[8,1,32]{2,1,0:T(1,128)}), s32[8,1,32]{2,1,0:T(1,128)S(1)}, u32[]{:S(2)}, u32[]{:S(2)}) async-start(s32[8,1,32]{2,1,0:T(1,128)} %bitcast.8), calls=%async_computation | async-start | bytes 8192 | tf_op jit(solution)/shard_map/all_to_all | solution.py:83
  35.4 1.8 copy.54
  37.9 5.7 %scatter_fusion.1 = bf16[8,32,3,1024]{3,2,1,0:T(4,128)(2,1)S(1)} fusion(bf16[8,32,3,1024]{3,2,1,0:T(4,128)(2,1)S(1)} %broadcast_in_dim.66, s32[128]{0:T(128)S(1)} %fusion.41, bf16[128,3,1024]{2,1,0:T(4,128)(2,1)S(1)} %copy.54), kind=kCustom, calls=%fused_computation.2 | custom fusion | bytes 2360320 | tf_op jit(solution)/shard_map/scatter | solution.py:74
  43.6 1.8 copy.55
  45.4 6.0 %all-to-all-start.1 = ((bf16[8,32,3,1024]{3,1,2,0:T(8,128)(2,1)}), bf16[8,32,3,1024]{3,1,2,0:T(8,128)(2,1)S(1)}, u32[]{:S(2)}, u32[]{:S(2)}) async-start(bf16[8,32,3,1024]{3,1,2,0:T(8,128)(2,1)} %copy.55), calls=%async_computation.1 | async-start | bytes 3145728 | tf_op jit(solution)/shard_map/all_to_all | solution.py:82
  52.8 35.1 %all-to-all-done.1 = bf16[8,32,3,1024]{3,1,2,0:T(8,128)(2,1)S(1)} async-done(((bf16[8,32,3,1024]{3,1,2,0:T(8,128)(2,1)}), bf16[8,32,3,1024]{3,1,2,0:T(8,128)(2,1)S(1)}, u32[]{:S(2)}, u32[]{:S(2)}) %all-to-all-start.1) | async-done | bytes 1572896 | tf_op jit(solution)/shard_map/all_to_all | solution.py:82
  89.7 7.3 %scatter_fusion.2 = bf16[128,3,1024]{2,1,0:T(4,128)(2,1)S(1)} fusion(bf16[128,3,1024]{2,1,0:T(4,128)(2,1)S(1)} %broadcast.347, s32[256]{0:T(256)S(1)} %bitcast.139, bf16[256,3,1024]{2,1,0:T(4,128)(2,1)S(1)} %copy.57), kind=kCustom, calls=%fused_computation.3 | custom fusion | bytes 4719616 | tf_op jit(solution)/shard_map/scatter | solution.py:90
  100.6 75.2 %all-reduce.3.cloned.1.call-done = bf16[128,3,1024]{2,1,0:T(4,128)(2,1)} async-done(((bf16[128,3,1024]{2,1,0:T(4,128)(2,1)}), bf16[128,3,1024]{2,1,0:T(4,128)(2,1)}) %all-reduce.3.cloned.1.call-update) | async-done | bytes 786448 | tf_op jit(solution)/shard_map/psum | solution.py:25
  175.7 4.5 %fusion.47 = (bf16[128,1,1024]{2,1,0:T(2,128)(2,1)}, bf16[128,1,1024]{2,1,0:T(2,128)(2,1)}, bf16[128,1,1024]{2,1,0:T(2,128)(2,1)S(1)}) fusion(bf16[128,3,1024]{2,1,0:T(4,128)(2,1)} %all-reduce.3.cloned.1.call-done), kind=kLoop, calls=%fused_computation.100 | loop fusion | bytes 1572864 | tf_op jit(solution)/shard_map/slice | solution.py:112
  185.8 1.8 collective-permute-start.1
  187.7 3.2 collective-permute-start.2
  192.5 14.4 %collective-permute-done = bf16[128,2,1024]{2,1,0:T(2,128)(2,1)S(1)} collective-permute-done((bf16[128,2,1024]{2,1,0:T(2,128)(2,1)S(1)}, bf16[128,2,1024]{2,1,0:T(2,128)(2,1)S(1)}, u32[]{:S(2)}, u32[]{:S(2)}) %collective-permute-start) | collective-permute-done | bytes 524320 | tf_op jit(solution)/shard_map/ppermute | solution.py:20
  207.2 22.6 %collective-permute-done.1 = bf16[128,2,1024]{2,1,0:T(2,128)(2,1)S(1)} collective-permute-done((bf16[128,2,1024]{2,1,0:T(2,128)(2,1)S(1)}, bf16[128,2,1024]{2,1,0:T(2,128)(2,1)S(1)}, u32[]{:S(2)}, u32[]{:S(2)}) %collective-permute-start.1) | collective-permute-done | bytes 524320 | tf_op jit(solution)/shard_map/ppermute | solution.py:20
  232.2 6.8 %collective-permute-done.3 = bf16[128,2,1024]{2,1,0:T(2,128)(2,1)} collective-permute-done((bf16[128,2,1024]{2,1,0:T(2,128)(2,1)S(1)}, bf16[128,2,1024]{2,1,0:T(2,128)(2,1)}, u32[]{:S(2)}, u32[]{:S(2)}) %collective-permute-start.3) | collective-permute-done | bytes 524320 | tf_op jit(solution)/shard_map/ppermute | solution.py:20
  241.2 2.5 gather_fusion
  243.8 2.3 bitcast_select_fusion
  246.9 1.6 copy.84
  249.5 30.7 %all-gather = f32[64,128]{1,0:T(8,128)S(1)} all-gather(f32[8,128]{1,0:T(8,128)S(1)} %get-tuple-element.212), channel_id=2, replica_groups=mesh['seq'=8,'head'=4] {'seq'}, dimensions={0}, use_global_device_ids=true | all-gather | bytes 36864 | tf_op jit(solution)/shard_map/all_gather | solution.py:29
  280.3 30.4 %all-gather.1 = f32[64,128]{1,0:T(8,128)S(1)} all-gather(f32[8,128]{1,0:T(8,128)S(1)} %fusion.25), channel_id=3, replica_groups=mesh['seq'=8,'head'=4] {'seq'}, dimensions={0}, use_global_device_ids=true | all-gather | bytes 36864 | tf_op jit(solution)/shard_map/all_gather | solution.py:29
  311.4 1.9 copy.70
  313.2 1.9 copy.75
  320.6 15.6 %while.19 = (s32[]{:T(128)}, f32[8,128]{1,0:T(8,128)S(1)}, f32[8,128]{1,0:T(8,128)S(1)}, f32[8,128,128]{2,1,0:T(8,128)S(1)}, f32[8,8,128]{2,1,0:T(8,128)S(1)}, /...) while((s32[]{:T(128)}, f32[8,128]{1,0:T(8,128)S(1)}, ...), condition=%wide.region_9.10_spmd, body=%wide.region_8.9_spmd.sunk | while | flops 399365 | bytes 1613975 | solution.py:35
  321.3 1.5 fusion.63
  323.5 1.5 fusion.63
  325.8 1.5 fusion.63
  328.0 1.5 fusion.63
  330.2 1.5 fusion.63
  332.5 1.5 fusion.63
  334.7 1.5 fusion.63
  336.6 5.7 %convolution_convert_fusion = bf16[128,4096]{1,0:T(8,128)(2,1)} fusion(bf16[128,1024]{0,1:T(8,128)(2,1)S(1)} %bitcast_select_fusion.1, bf16[1024,4096]{1,0:T(8,128)(2,1)} %param.13), kind=kOutput, calls=%fused_computation.12 | convolution fusion | flops 1074266112 | bytes 9699328 | tf_op jit(solution)/shard_map/dot_general | solution.py:173
  342.3 23.4 %reduce-scatter.2.cloned.1.call-done = bf16[32,4096]{1,0:T(8,128)(2,1)} async-done(((bf16[128,4096]{1,0:T(8,128)(2,1)}), bf16[32,4096]{1,0:T(8,128)(2,1)}) %reduce-scatter.2.cloned.1.call-update) | async-done | bytes 262160 | tf_op jit(solution)/shard_map/reduce_scatter | solution.py:172
  (95 shorter events, 34.2 us)
Async XLA Ops:
  28.1 17.3 %all-to-all-start = ((s32[8,1,32]{2,1,0:T(1,128)}), s32[8,1,32]{2,1,0:T(1,128)S(1)}, u32[]{:S(2)}, u32[]{:S(2)}) async-start(s32[8,1,32]{2,1,0:T(1,128)} %bitcast.8), calls=%async_computation | async-start | bytes 8192 | tf_op jit(solution)/shard_map/all_to_all | solution.py:83
  43.6 7.8 %copy-start.6 = (s32[8]{0:T(128)S(1)}, s32[8]{0:T(128)}, u32[]{:S(2)}) copy-start(s32[8]{0:T(128)} %param.12) | copy-start | bytes 100
  45.4 42.4 %all-to-all-start.1 = ((bf16[8,32,3,1024]{3,1,2,0:T(8,128)(2,1)}), bf16[8,32,3,1024]{3,1,2,0:T(8,128)(2,1)S(1)}, u32[]{:S(2)}, u32[]{:S(2)}) async-start(bf16[8,32,3,1024]{3,1,2,0:T(8,128)(2,1)} %copy.55), calls=%async_computation.1 | async-start | bytes 3145728 | tf_op jit(solution)/shard_map/all_to_all | solution.py:82
  51.4 124.3 %all-reduce.3.cloned.1.call-start = ((), (), s32[]{:S(2)}) async-start(), calls=%async_computation.3 | async-start | bytes 2097152 | tf_op jit(solution)/shard_map/psum | solution.py:25
  98.5 221.0 %all-gather.5.cloned.1.call-start = ((), (), s32[]{:S(2)}) async-start(), calls=%async_computation.5 | async-start | bytes 4718592 | tf_op jit(solution)/shard_map/all_gather | solution.py:29
  180.3 3.1 copy-start.7
  180.3 3.3 copy-start.5
  181.0 0.9 copy-start
  183.3 182.4 %reduce-scatter.2.cloned.1.call-start = ((), (), s32[]{:S(2)}) async-start(), calls=%async_computation.4 | async-start | bytes 1310720 | tf_op jit(solution)/shard_map/reduce_scatter | solution.py:172
  184.7 22.1 %collective-permute-start = (bf16[128,2,1024]{2,1,0:T(2,128)(2,1)S(1)}, bf16[128,2,1024]{2,1,0:T(2,128)(2,1)S(1)}, u32[]{:S(2)}, u32[]{:S(2)}) collective-permute-start(bf16[128,2,1024]{2,1,0:T(2,128)(2,1)S(1)} %slice.67), channel_id=1, source_target_pairs={{24,0},{28,4},{0,8},{4,12},{8,16},{12,20},{16,24},{20,28},{25,1},{... | collective-permute-start | bytes 1572872 | tf_op jit(solution)/shard_map/ppermute | solution.py:20
  185.8 44.0 %collective-permute-start.1 = (bf16[128,2,1024]{2,1,0:T(2,128)(2,1)S(1)}, bf16[128,2,1024]{2,1,0:T(2,128)(2,1)S(1)}, u32[]{:S(2)}, u32[]{:S(2)}) collective-permute-start(bf16[128,2,1024]{2,1,0:T(2,128)(2,1)S(1)} %slice.67), channel_id=1, source_target_pairs={{28,0},{0,4},{4,8},{8,12},{12,16},{16,20},{20,24},{24,28},{29,1},{... | collective-permute-start | bytes 1572872 | tf_op jit(solution)/shard_map/ppermute | solution.py:20
  187.7 43.1 %collective-permute-start.2 = (bf16[128,2,1024]{2,1,0:T(2,128)(2,1)S(1)}, bf16[128,2,1024]{2,1,0:T(2,128)(2,1)}, u32[]{:S(2)}, u32[]{:S(2)}) collective-permute-start(bf16[128,2,1024]{2,1,0:T(2,128)(2,1)S(1)} %slice.67), channel_id=1, source_target_pairs={{4,0},{8,4},{12,8},{16,12},{20,16},{24,20},{28,24},{0,28},{5,1},{9... | collective-permute-start | bytes 1572872 | tf_op jit(solution)/shard_map/ppermute | solution.py:20
  190.9 48.1 %collective-permute-start.3 = (bf16[128,2,1024]{2,1,0:T(2,128)(2,1)S(1)}, bf16[128,2,1024]{2,1,0:T(2,128)(2,1)}, u32[]{:S(2)}, u32[]{:S(2)}) collective-permute-start(bf16[128,2,1024]{2,1,0:T(2,128)(2,1)S(1)} %slice.67), channel_id=1, source_target_pairs={{8,0},{12,4},{16,8},{20,12},{24,16},{28,20},{0,24},{4,28},{9,1},{1... | collective-permute-start | bytes 1572872 | tf_op jit(solution)/shard_map/ppermute | solution.py:20
  248.5 31.7 %copy-start.1 = (f32[8,128,128]{1,2,0:T(8,128)S(1)}, f32[8,128,128]{1,2,0:T(8,128)}, u32[]{:S(2)}) copy-start(f32[8,128,128]{1,2,0:T(8,128)} %copy-done) | copy-start | bytes 1572868
  310.8 0.6 copy-start.4
  315.1 2.7 copy-start.2
  317.9 1.2 copy-start.3
Sparse Core Ops, SparseCore 0:
  98.6 77.0 all-reduce.2
  183.4 97.0 all-gather.4
  342.4 23.2 reduce-scatter.1
where the time goes:
time: 374 us; the launch traced here: 372 us
  waiting for transfers between devices  177 us (47%)
  local copies, waits for them, and re-layouts  64.8 us (17%)
  blocking collectives  61.2 us (16%)
  other arithmetic  23.2 us (6%)
  starting transfers between devices  20.5 us (5%)
  between operations  13.5 us (4%)
  matrix products  11.4 us (3%)
    psum x1, waiting for transfers between devices, from_root(): return lax.psum(jnp.where(mine, x, jnp.zeros_like(x)), axis)  75.2 us
    all_gather x2, blocking collectives, combined_all(): everything = jax.tree.map(lambda part: lax.all_gather(part, axis), x)  61.2 us
    ppermute x4, waiting for transfers between devices, from_behind(): return lax.ppermute(block, axis, route)  43.7 us
    all_to_all x1, waiting for transfers between devices, shards(): lax.all_to_all(outgoing, 'seq', split_axis=0, concat_axis=0, tiled=True)  35.1 us
    reduce_scatter x1, waiting for transfers between devices, shards(): lax.psum_scatter(jnp.dot(attn_rows, out_weight, preferred_element_type=jn...  23.4 us
    scatter x1, local copies, waits for them, and re-layouts, shards(): slots = jnp.full((owners, capacity), -1, jnp.int32).at[target_owner, slot...  19.9 us
    add x7, other arithmetic, combine_parts(): accum_left * factor_left[:, :, None]  10.6 us
    unnamed x23, local copies, waits for them, and re-layouts  8.14 us
  transfers between devices with their start and end apart: 9, of which 6 were waited for; matrix products, arithmetic and copies ran while one was open for 10% of the time, Pallas kernels for 0%

commit v1 on v0

--- a/solution.py
+++ b/solution.py
@@ -52,7 +52,7 @@
     )
 
 
-def shards(projected, destination, doc_lengths, random_blocks, global_owner, out_weight):
+def shards_ring(projected, destination, doc_lengths, random_blocks, global_owner, out_weight):
     owners = lax.axis_size("seq")
     own_index = lax.axis_index("seq")
     tok_dev = projected.shape[0]
@@ -177,6 +177,89 @@
     )
 
 
+def gathered_plan(projected, destination, doc_lengths, random_blocks, global_owner, out_weight):
+    owners = lax.axis_size("seq")
+    own_index = lax.axis_index("seq")
+    tok_dev = projected.shape[0]
+    columns = projected.shape[2]
+    heads_here = columns // HD
+    tokens = owners * tok_dev
+    blocks_all = tokens // BLK
+    score_scale = 1.0 / math.sqrt(HD)
+    everything = lax.all_gather(projected, "seq", tiled=True)
+    arrival_dest = lax.all_gather(destination, "seq", tiled=True)
+    my_pos = own_index * tok_dev + jnp.arange(tok_dev, dtype=jnp.int32)
+    pick = (arrival_dest[None, :] == my_pos[:, None]).astype(projected.dtype)
+    queries = jnp.dot(pick, everything[:, 0, :], preferred_element_type=jnp.float32)
+    queries = queries.astype(projected.dtype).reshape(tok_dev, heads_here, HD)
+    keys = everything[:, 1, :].reshape(tokens, heads_here, HD)
+    values = everything[:, 2, :].reshape(tokens, heads_here, HD)
+    scores = (
+        jnp.einsum("qhd,khd->hqk", queries, keys, preferred_element_type=jnp.float32)
+        * score_scale
+    )
+    bounds = jnp.cumsum(doc_lengths)
+    key_block = arrival_dest // BLK
+    key_doc = segment_of(arrival_dest, bounds)
+    query_block = my_pos // BLK
+    query_doc = segment_of(my_pos, bounds)
+    same_doc = query_doc[:, None] == key_doc[None, :]
+    window = jnp.zeros((tok_dev, tokens), jnp.int32)
+    for step in (-1, 0, 1):
+        near = (query_block + step) % blocks_all
+        window = window + (key_block[None, :] == near[:, None]).astype(jnp.int32)
+    window = jnp.where(same_doc, window, 0)
+    chosen = random_blocks[query_block]
+    drawn = jnp.zeros((tok_dev, tokens), jnp.int32)
+    for r in range(chosen.shape[1]):
+        drawn = drawn + (key_block[None, :] == chosen[:, r][:, None]).astype(jnp.int32)
+    glob_start = global_owner[0] * tok_dev
+    in_glob = (arrival_dest >= glob_start) & (arrival_dest < glob_start + tok_dev)
+    count = window + drawn + in_glob[None, :].astype(jnp.int32)
+    live = count > 0
+    near_scores = jnp.where(live[None], scores, big_negative)
+    row_peak = jnp.max(near_scores, axis=2)
+    near_exp = jnp.exp(near_scores - row_peak[..., None])
+    count_f = count.astype(jnp.float32)[None]
+    denominator = jnp.sum(near_exp * count_f, axis=2)
+    weighted = near_exp.astype(jnp.bfloat16).astype(jnp.float32) * count_f
+    weight_hi = weighted.astype(jnp.bfloat16)
+    weight_lo = (weighted - weight_hi.astype(jnp.float32)).astype(jnp.bfloat16)
+    mixed_sum = jnp.einsum("hqk,khd->qhd", weight_hi, values, preferred_element_type=jnp.float32)
+    mixed_sum = mixed_sum + jnp.einsum(
+        "hqk,khd->qhd", weight_lo, values, preferred_element_type=jnp.float32
+    )
+    sparse = (mixed_sum / jnp.transpose(denominator)[..., None]).reshape(tok_dev, columns)
+    sparse = sparse.astype(jnp.bfloat16)
+    glob_peak = jnp.max(scores, axis=2)
+    glob_exp = jnp.exp(scores - glob_peak[..., None])
+    glob_total = jnp.sum(glob_exp, axis=2)
+    glob_accum = jnp.einsum(
+        "hqk,khd->qhd", glob_exp, values.astype(jnp.float32), precision=lax.Precision.HIGHEST
+    )
+    glob_out = (glob_accum / jnp.transpose(glob_total)[..., None]).reshape(tok_dev, columns)
+    glob_out = glob_out.astype(jnp.bfloat16)
+    attn_rows = jnp.where(own_index == global_owner[0], glob_out, sparse)
+    return lax.psum_scatter(
+        jnp.dot(attn_rows, out_weight, preferred_element_type=jnp.float32).astype(jnp.bfloat16),
+        "head",
+        scatter_dimension=0,
+        tiled=True,
+    )
+
+
+GATHER_LIMIT = 16 * 2**20
+
+
+def shards(projected, destination, doc_lengths, random_blocks, global_owner, out_weight):
+    gathered_bytes = lax.axis_size("seq") * projected.size * projected.dtype.itemsize
+    if gathered_bytes <= GATHER_LIMIT:
+        return gathered_plan(
+            projected, destination, doc_lengths, random_blocks, global_owner, out_weight
+        )
+    return shards_ring(projected, destination, doc_lengths, random_blocks, global_owner, out_weight)
+
+
 def solution(mesh):
     in_specs = (P("seq", None, "head"), P("seq"), P(), P(), P(), P("head", None))
     out_specs = P(("seq", "head"), None)

time: 374 us -> 159 us (0.43)
  waiting for transfers between devices: 177 us -> 98.9 us
  local copies, waits for them, and re-layouts: 64.8 us -> 6.94 us
  blocking collectives: 61.2 us -> 22.5 us
  starting transfers between devices: 20.5 us -> 0.04 us
  other arithmetic: 23.2 us -> 5.17 us
    all_gather x1, waiting for transfers between devices: 0.02 us -> 75.7 us  [gathered_plan(): everything = lax.all_gather(projected, 'seq', tiled=True)]
    psum x1 -> x0, waiting for transfers between devices: 75.2 us -> none  [from_root(): return lax.psum(jnp.where(mine, x, jnp.zeros_like(x)), axis)]
    ppermute x4 -> x0, waiting for transfers between devices: 43.7 us -> none  [from_behind(): return lax.ppermute(block, axis, route)]
    all_gather x2 -> x1, blocking collectives: 61.2 us -> 22.5 us  [gathered_plan(): arrival_dest = lax.all_gather(destination, 'seq', tiled=True)]
    all_to_all x2 -> x0, waiting for transfers between devices: 35.1 us -> none  [the longest x1 35.1 us: shards(): lax.all_to_all(outgoing, 'seq', split_axis=0, concat_axis=0, tiled=True)]
    scatter x4 -> x0, local copies, waits for them, and re-layouts: 34.7 us -> none  [the longest x1 19.9 us: shards(): slots = jnp.full((owners, capacity), -1, jnp.int32).at[target_owner, slot...]
    add x18 -> x0, other arithmetic: 15.7 us -> none  [the longest x7 10.6 us: combine_parts(): accum_left * factor_left[:, :, None]]
    all_to_all x2 -> x0, starting transfers between devices: 13.3 us -> none  [the longest x1 7.28 us: shards(): lax.all_to_all(slots, 'seq', split_axis=0, concat_axis=0, tiled=True)]
  transfers between devices with their start and end apart: 9 -> 2, of which waited for: 6 -> 2; matrix products, arithmetic and copies ran while one was open for 10% -> 2% of each run, Pallas kernels for 0% -> 0%
where the time goes in v1:
time: 159 us
  waiting for transfers between devices  98.9 us (62%)
  blocking collectives  22.5 us (14%)
  between operations  14.8 us (9%)
  matrix products  10.2 us (6%)
  local copies, waits for them, and re-layouts  6.94 us (4%)
  other arithmetic  5.17 us (3%)
    all_gather x1, waiting for transfers between devices, gathered_plan(): everything = lax.all_gather(projected, 'seq', tiled=True)  75.7 us
    reduce_scatter x1, waiting for transfers between devices, gathered_plan(): lax.psum_scatter(jnp.dot(attn_rows, out_weight, preferred_element_type=jn...  23.2 us
    all_gather x1, blocking collectives, gathered_plan(): arrival_dest = lax.all_gather(destination, 'seq', tiled=True)  22.5 us
    unnamed x6, local copies, waits for them, and re-layouts  3.44 us
  transfers between devices with their start and end apart: 2, of which 2 were waited for; matrix products, arithmetic and copies ran while one was open for 2% of the time, Pallas kernels for 0%

profile of v1, /device:TPU:0, one launch (start us, length us, event | category | flops | bytes accessed | tf_op | source)
XLA Modules:
  0.0 158.5 jit_solution(2768139149473016350)
XLA Ops:
  6.5 0.0 all-gather.3.cloned.1.call-start
  6.5 2.3 %copy.18 = bf16[128,3,1024]{0,2,1:T(8,128)(2,1)} copy(bf16[128,3,1024]{2,0,1:T(8,128)(2,1)} %param.6) | data formatting | bytes 1572864 | tf_op args[0]
  8.8 0.0 all-gather.3.cloned.1.call-update
  8.9 0.0 reduce-scatter.2.cloned.1.call-start
  10.2 0.8 copy.21
  11.0 0.8 reduce-window.8
  11.8 0.6 gather_fusion
  12.5 22.5 %all-gather = s32[8,1,128]{2,1,0:T(1,128)S(1)} all-gather(s32[1,1,128]{2,1,0:T(1,128)} %bitcast.59), channel_id=1, replica_groups=mesh['seq'=8,'head'=4] {'seq'}, dimensions={0}, use_global_device_ids=true | all-gather | bytes 4608 | tf_op jit(solution)/shard_map/all_gather | solution.py:190
  35.0 0.1 convert_reduce_fusion.1
  35.1 0.1 convert_reduce_fusion
  35.2 0.2 slice_reduce_fusion.2
  35.4 0.5 fusion.34
  35.9 0.5 fusion.33
  36.4 75.7 %all-gather.3.cloned.1.call-done = bf16[1024,3,1024]{0,2,1:T(8,128)(2,1)} async-done(((bf16[128,3,1024]{0,2,1:T(8,128)(2,1)}), bf16[1024,3,1024]{0,2,1:T(8,128)(2,1)}) %all-gather.3.cloned.1.call-update) | async-done | bytes 6291472 | tf_op jit(solution)/shard_map/all_gather | solution.py:189
  112.1 2.7 %fusion.49 = (bf16[1024,1,1024]{0,2,1:T(8,128)(2,1)S(1)}, bf16[1024,1,1024]{0,2,1:T(8,128)(2,1)S(1)}) fusion(bf16[1024,3,1024]{0,2,1:T(8,128)(2,1)} %all-gather.3.cloned.1.call-done), kind=kLoop, calls=%fused_computation.88 | loop fusion | bytes 8388608 | tf_op jit(solution)/shard_map/slice | solution.py:195
  114.8 2.4 %fusion.24 = bf16[16,8,8,128]{3,2,1,0:T(8,128)(2,1)S(1)} fusion(bf16[1024,3,1024]{0,2,1:T(8,128)(2,1)} %all-gather.3.cloned.1.call-done, s32[1024]{0:T(1024)S(1)} %bitcast.57, s32[128]{0:T(128)S(1)} %get-tuple-element.17), kind=kOutput, calls=%fused_computation.31 | convolution fusion | flops 268697600 | bytes 2363904 | tf_op jit(solution)/shard_map/dot_general | solution.py:193
  117.2 0.8 multiply_reduce_fusion.1
  118.0 0.9 fusion.2
  118.9 2.9 %fusion.31 = bf16[128,8,128]{0,2,1:T(8,128)(2,1)S(1)} fusion(bf16[1024,8,128]{0,2,1:T(8,128)(2,1)S(1)} %bitcast.49, f32[8,128,1024]{2,1,0:T(8,128)S(1)} %get-tuple-element.11, f32[8,128]{1,0:T(8,128)S(1)} %get-tuple-element.10, f32[128,8]{0,1:T(8,128)S(1)} %bitcast.58), kind=kOutput, calls=%fused_computation.38 | convolution fusion | flops 1612972032 | bytes 6561792 | tf_op jit(solution)/shard_map/hqk,khd->qhd/dot_general | solution.py:237
  121.8 0.0 slice-start
  121.8 2.2 %multiply_reduce_fusion = (f32[8,128]{1,0:T(8,128)S(1)}, bf16[8,128,1024]{2,1,0:T(8,128)(2,1)S(1)}) fusion(f32[128,1024]{1,0:T(8,128)S(1)} %fusion.33, f32[8,128,1024]{2,1,0:T(8,128)S(1)} %get-tuple-element.11, pred[128,1024]{1,0:T(8,128)(4,1)S(1)} %fusion.34), kind=kOutput, calls=%fused_computation.3 | output fusion | flops 8389631 | bytes 6950912 | tf_op jit(solution)/shard_map/sub | solution.py:222
  124.0 0.0 slice-start.1
  124.0 0.8 fusion.9
  124.8 1.0 fusion.29
  125.8 0.0 slice-done
  125.8 0.4 slice-done.1
  126.2 2.3 %convolution_convert_fusion = bf16[128,4096]{1,0:T(8,128)(2,1)} fusion(bf16[128,1024]{0,1:T(8,128)(2,1)S(1)} %bitcast.53, bf16[1024,4096]{1,0:T(8,128)(2,1)S(1)} %bitcast.48), kind=kOutput, calls=%fused_computation.2 | convolution fusion | flops 1074266112 | bytes 9699328 | tf_op jit(solution)/shard_map/dot_general | solution.py:244
  128.5 0.0 reduce-scatter.2.cloned.1.call-update
  128.5 23.2 %reduce-scatter.2.cloned.1.call-done = bf16[32,4096]{1,0:T(8,128)(2,1)} async-done(((bf16[128,4096]{1,0:T(8,128)(2,1)}), bf16[32,4096]{1,0:T(8,128)(2,1)}) %reduce-scatter.2.cloned.1.call-update) | async-done | bytes 262160 | tf_op jit(solution)/shard_map/reduce_scatter | solution.py:243
  (7 shorter events, 0.1 us)
Async XLA Ops:
  6.5 105.6 %all-gather.3.cloned.1.call-start = ((), (), s32[]{:S(2)}) async-start(), calls=%async_computation.1 | async-start | bytes 7077888 | tf_op jit(solution)/shard_map/all_gather | solution.py:189
  8.9 142.9 %reduce-scatter.2.cloned.1.call-start = ((), (), s32[]{:S(2)}) async-start(), calls=%async_computation.2 | async-start | bytes 1310720 | tf_op jit(solution)/shard_map/reduce_scatter | solution.py:243
  121.8 4.0 %slice-start = ((s8[8388608]{0:T(1024)(128)(4,1)}), s8[4194304]{0:T(1024)(128)(4,1)S(1)}, s32[]{:S(2)}) async-start(s8[8388608]{0:T(1024)(128)(4,1)} %bitcast.47), calls=%async_computation.3 | async-start | bytes 8388608
  124.0 2.2 %slice-start.1 = ((s8[8388608]{0:T(1024)(128)(4,1)}), s8[4194304]{0:T(1024)(128)(4,1)S(1)}, s32[]{:S(2)}) async-start(s8[8388608]{0:T(1024)(128)(4,1)} %bitcast.47), calls=%async_computation.4 | async-start | bytes 8388608
Sparse Core Ops, SparseCore 0:
  9.4 102.6 all-gather.2
  128.6 23.0 reduce-scatter.1

commit v2 on v1

--- a/solution.py
+++ b/solution.py
@@ -186,14 +186,36 @@
     tokens = owners * tok_dev
     blocks_all = tokens // BLK
     score_scale = 1.0 / math.sqrt(HD)
-    everything = lax.all_gather(projected, "seq", tiled=True)
+    capacity = 2 * (tok_dev // owners)
     arrival_dest = lax.all_gather(destination, "seq", tiled=True)
+    keyval = lax.all_gather(projected[:, 1:, :], "seq", tiled=True)
+    target_all = arrival_dest.reshape(owners, tok_dev) // tok_dev
+    onehot = (target_all[:, :, None] == jnp.arange(owners, dtype=jnp.int32)).astype(jnp.int32)
+    slot_all = jnp.sum((jnp.cumsum(onehot, axis=1) - onehot) * onehot, axis=2)
+    target = destination // tok_dev
+    mine = (target[:, None] == jnp.arange(owners, dtype=jnp.int32)[None, :]).astype(jnp.int32)
+    slot = jnp.sum((jnp.cumsum(mine, axis=0) - mine) * mine, axis=1)
+    send_col = target * capacity + slot
+    send_pick = (
+        jnp.arange(owners * capacity, dtype=jnp.int32)[:, None] == send_col[None, :]
+    ).astype(projected.dtype)
+    outgoing = jnp.dot(send_pick, projected[:, 0, :], preferred_element_type=jnp.float32)
+    outgoing = outgoing.astype(projected.dtype).reshape(owners, capacity, columns)
+    incoming = lax.all_to_all(outgoing, "seq", split_axis=0, concat_axis=0, tiled=True)
     my_pos = own_index * tok_dev + jnp.arange(tok_dev, dtype=jnp.int32)
-    pick = (arrival_dest[None, :] == my_pos[:, None]).astype(projected.dtype)
-    queries = jnp.dot(pick, everything[:, 0, :], preferred_element_type=jnp.float32)
+    source = jnp.arange(tokens, dtype=jnp.int32) // tok_dev
+    land_col = (source * capacity + slot_all.reshape(-1))[None, :]
+    hit = arrival_dest[None, :] == my_pos[:, None]
+    col_of_pos = jnp.sum(jnp.where(hit, land_col, 0), axis=1)
+    land_pick = (
+        col_of_pos[:, None] == jnp.arange(owners * capacity, dtype=jnp.int32)[None, :]
+    ).astype(projected.dtype)
+    queries = jnp.dot(
+        land_pick, incoming.reshape(owners * capacity, columns), preferred_element_type=jnp.float32
+    )
     queries = queries.astype(projected.dtype).reshape(tok_dev, heads_here, HD)
-    keys = everything[:, 1, :].reshape(tokens, heads_here, HD)
-    values = everything[:, 2, :].reshape(tokens, heads_here, HD)
+    keys = keyval[:, 0, :].reshape(tokens, heads_here, HD)
+    values = keyval[:, 1, :].reshape(tokens, heads_here, HD)
     scores = (
         jnp.einsum("qhd,khd->hqk", queries, keys, preferred_element_type=jnp.float32)
         * score_scale

time: 159 us -> 142 us (0.89)
  waiting for transfers between devices: 98.9 us -> 64.2 us
  blocking collectives: 22.5 us -> 30.8 us
  starting transfers between devices: 0.04 us -> 7.35 us
  other arithmetic: 5.17 us -> 9.05 us
    all_gather x1, waiting for transfers between devices: 75.7 us -> 41 us  [gathered_plan(): keyval = lax.all_gather(projected[:, 1:, :], 'seq', tiled=True)]
    all_gather x1, blocking collectives: 22.5 us -> 30.8 us  [gathered_plan(): arrival_dest = lax.all_gather(destination, 'seq', tiled=True)]
    all_to_all x0 -> x1, starting transfers between devices: none -> 7.28 us  [gathered_plan(): lax.all_to_all(outgoing, 'seq', split_axis=0, concat_axis=0, tiled=True)]
    another operation x1 -> x3, other arithmetic: 0.83 us -> 2.87 us  [the longest x1 2.52 us: gathered_plan(): slot_all = jnp.sum((jnp.cumsum(onehot, axis=1) - onehot) * onehot, axis=2)]
    unnamed x6 -> x14, local copies, waits for them, and re-layouts: 3.44 us -> 1.48 us
    slice x1 -> x2, local copies, waits for them, and re-layouts: 2.66 us -> 3.76 us  [the longest x1 2.66 us: gathered_plan(): keys = keyval[:, 0, :].reshape(tokens, heads_here, HD)]
  transfers between devices with their start and end apart: 2 -> 3, of which waited for: 2 -> 2; matrix products, arithmetic and copies ran while one was open for 2% -> 7% of each run, Pallas kernels for 0% -> 0%
where the time goes in v2:
time: 142 us; the launch traced here: 141 us
  waiting for transfers between devices  64.2 us (45%)
  blocking collectives  30.8 us (22%)
  between operations  13.7 us (10%)
  matrix products  10.1 us (7%)
  other arithmetic  9.05 us (6%)
  starting transfers between devices  7.35 us (5%)
  local copies, waits for them, and re-layouts  6.24 us (4%)
    all_gather x1, waiting for transfers between devices, gathered_plan(): keyval = lax.all_gather(projected[:, 1:, :], 'seq', tiled=True)  41 us
    all_gather x1, blocking collectives, gathered_plan(): arrival_dest = lax.all_gather(destination, 'seq', tiled=True)  30.8 us
    reduce_scatter x1, waiting for transfers between devices, gathered_plan(): lax.psum_scatter(jnp.dot(attn_rows, out_weight, preferred_element_type=jn...  23.2 us
    all_to_all x1, starting transfers between devices, gathered_plan(): lax.all_to_all(outgoing, 'seq', split_axis=0, concat_axis=0, tiled=True)  7.28 us
    dot_general x1, matrix products, gathered_plan(): jnp.einsum('hqk,khd->qhd', glob_exp, values.astype(jnp.float32), precisio...  2.9 us
  transfers between devices with their start and end apart: 3, of which 2 were waited for; matrix products, arithmetic and copies ran while one was open for 7% of the time, Pallas kernels for 0%

profile of v2, /device:TPU:0, one launch (start us, length us, event | category | flops | bytes accessed | tf_op | source)
XLA Modules:
  0.0 141.4 jit_solution(5249411871004553347)
XLA Ops:
  6.6 1.1 slice.27
  7.7 1.0 copy.34
  8.7 0.7 and_select_fusion.5
  9.4 0.1 fusion.43
  9.5 0.2 reduce_window_sum.30
  9.6 0.2 select_reduce_fusion.3
  9.8 0.7 multiply_add_fusion
  10.5 2.1 %convolution_convert_fusion.1 = bf16[256,1024]{1,0:T(8,128)(2,1)} fusion(bf16[128,3,1024]{2,0,1:T(8,128)(2,1)} %param.6, s32[128]{0:T(128)S(1)} %multiply_add_fusion), kind=kOutput, calls=%fused_computation.25 | convolution fusion | flops 67403776 | bytes 786944 | tf_op jit(solution)/shard_map/dot_general | solution.py:202
  12.5 7.3 %all-to-all-start = ((bf16[8,32,1024]{2,1,0:T(8,128)(2,1)}), bf16[8,32,1024]{2,1,0:T(8,128)(2,1)S(1)}, u32[]{:S(2)}, u32[]{:S(2)}) async-start(bf16[8,32,1024]{2,1,0:T(8,128)(2,1)} %bitcast.6), calls=%async_computation | async-start | bytes 1048576 | tf_op jit(solution)/shard_map/all_to_all | solution.py:204
  19.9 0.2 reduce-window.8
  20.2 30.8 %all-gather = s32[8,1,128]{2,1,0:T(1,128)S(1)} all-gather(s32[1,1,128]{2,1,0:T(1,128)S(1)} %bitcast.63), channel_id=1, replica_groups=mesh['seq'=8,'head'=4] {'seq'}, dimensions={0}, use_global_device_ids=true | all-gather | bytes 4608 | tf_op jit(solution)/shard_map/all_gather | solution.py:190
  51.0 0.1 copy.27
  51.1 2.5 %select_reduce_fusion.2 = s32[8,128]{0,1:T(8,128)S(1)} fusion(s32[8,128]{0,1:T(8,128)S(1)} %copy.27), kind=kOutput, calls=%fused_computation.43 | output fusion | flops 1096704 | bytes 8192 | tf_op jit(solution)/shard_map/jit(cumsum)/reduce_window_sum | solution.py:194
  53.7 0.6 gather_fusion
  54.4 0.1 convert_reduce_fusion.1
  54.4 0.1 convert_reduce_fusion
  54.5 0.2 slice_reduce_fusion.2
  54.7 0.2 select_reduce_fusion.1
  55.1 0.5 fusion.35
  55.6 0.5 fusion.34
  56.1 0.3 fusion.22
  56.4 41.0 %all-gather.3.cloned.1.call-done = bf16[1024,2,1024]{0,2,1:T(8,128)(2,1)} async-done(((bf16[128,2,1024]{0,2,1:T(8,128)(2,1)}), bf16[1024,2,1024]{0,2,1:T(8,128)(2,1)}) %all-gather.3.cloned.1.call-update) | async-done | bytes 4194320 | tf_op jit(solution)/shard_map/all_gather | solution.py:191
  97.4 2.7 %fusion.61 = (bf16[1024,1,1024]{0,2,1:T(8,128)(2,1)S(1)}, bf16[1024,1,1024]{0,2,1:T(8,128)(2,1)S(1)}) fusion(bf16[1024,2,1024]{0,2,1:T(8,128)(2,1)} %all-gather.3.cloned.1.call-done), kind=kLoop, calls=%fused_computation.121 | loop fusion | bytes 8388608 | tf_op jit(solution)/shard_map/slice | solution.py:217
  100.0 0.8 multiply_reduce_fusion.1
  100.8 0.9 fusion.2
  101.7 2.9 %fusion.29 = bf16[128,8,128]{0,2,1:T(8,128)(2,1)S(1)} fusion(bf16[1024,8,128]{0,2,1:T(8,128)(2,1)S(1)} %bitcast.51, f32[8,128,1024]{2,1,0:T(8,128)S(1)} %get-tuple-element.11, f32[8,128]{1,0:T(8,128)S(1)} %get-tuple-element.10, f32[128,8]{0,1:T(8,128)S(1)} %bitcast.62), kind=kOutput, calls=%fused_computation.37 | convolution fusion | flops 1612972032 | bytes 6561792 | tf_op jit(solution)/shard_map/hqk,khd->qhd/dot_general | solution.py:259
  104.7 2.2 %multiply_reduce_fusion = (f32[8,128]{1,0:T(8,128)S(1)}, bf16[8,128,1024]{2,1,0:T(8,128)(2,1)S(1)}) fusion(f32[128,1024]{1,0:T(8,128)S(1)} %fusion.34, f32[8,128,1024]{2,1,0:T(8,128)S(1)} %get-tuple-element.11, pred[128,1024]{1,0:T(8,128)(4,1)S(1)} %fusion.35), kind=kOutput, calls=%fused_computation.3 | output fusion | flops 8389631 | bytes 6950912 | tf_op jit(solution)/shard_map/sub | solution.py:244
  106.8 0.8 fusion.9
  107.6 1.0 fusion.27
  108.6 0.4 slice-done.1
  109.0 2.3 %convolution_convert_fusion = bf16[128,4096]{1,0:T(8,128)(2,1)} fusion(bf16[128,1024]{0,1:T(8,128)(2,1)S(1)} %bitcast.56, bf16[1024,4096]{1,0:T(8,128)(2,1)S(1)} %bitcast.50), kind=kOutput, calls=%fused_computation.2 | convolution fusion | flops 1074266112 | bytes 9699328 | tf_op jit(solution)/shard_map/dot_general | solution.py:266
  111.3 23.2 %reduce-scatter.2.cloned.1.call-done = bf16[32,4096]{1,0:T(8,128)(2,1)} async-done(((bf16[128,4096]{1,0:T(8,128)(2,1)}), bf16[32,4096]{1,0:T(8,128)(2,1)}) %reduce-scatter.2.cloned.1.call-update) | async-done | bytes 262160 | tf_op jit(solution)/shard_map/reduce_scatter | solution.py:265
  (28 shorter events, 0.4 us)
Async XLA Ops:
  6.5 13.6 %copy-start.1 = (s32[128]{0:T(128)S(1)}, s32[128]{0:T(128)}, u32[]{:S(2)}) copy-start(s32[128]{0:T(128)} %param.7) | copy-start | bytes 1540
  6.5 13.3 %copy-start.2 = (s32[4]{0:T(128)S(1)}, s32[4]{0:T(128)}, u32[]{:S(2)}) copy-start(s32[4]{0:T(128)} %param.8) | copy-start | bytes 52
  6.5 13.5 %copy-start = (s32[8,3]{0,1:T(4,128)S(1)}, s32[8,3]{0,1:T(4,128)}, u32[]{:S(2)}) copy-start(s32[8,3]{0,1:T(4,128)} %param.9) | copy-start | bytes 292
  6.5 48.4 %copy-start.3 = (s32[8]{0:T(128)S(1)}, s32[8]{0:T(128)}, u32[]{:S(2)}) copy-start(s32[8]{0:T(128)} %param.10) | copy-start | bytes 100
  6.5 90.8 %all-gather.3.cloned.1.call-start = ((), (), s32[]{:S(2)}) async-start(), calls=%async_computation.2 | async-start | bytes 4718592 | tf_op jit(solution)/shard_map/all_gather | solution.py:191
  12.5 43.6 %all-to-all-start = ((bf16[8,32,1024]{2,1,0:T(8,128)(2,1)}), bf16[8,32,1024]{2,1,0:T(8,128)(2,1)S(1)}, u32[]{:S(2)}, u32[]{:S(2)}) async-start(bf16[8,32,1024]{2,1,0:T(8,128)(2,1)} %bitcast.6), calls=%async_computation | async-start | bytes 1048576 | tf_op jit(solution)/shard_map/all_to_all | solution.py:204
  19.8 114.7 %reduce-scatter.2.cloned.1.call-start = ((), (), s32[]{:S(2)}) async-start(), calls=%async_computation.3 | async-start | bytes 1310720 | tf_op jit(solution)/shard_map/reduce_scatter | solution.py:265
  104.6 4.0 %slice-start = ((s8[8388608]{0:T(1024)(128)(4,1)}), s8[4194304]{0:T(1024)(128)(4,1)S(1)}, s32[]{:S(2)}) async-start(s8[8388608]{0:T(1024)(128)(4,1)} %bitcast.49), calls=%async_computation.4 | async-start | bytes 8388608
  106.8 2.2 %slice-start.1 = ((s8[8388608]{0:T(1024)(128)(4,1)}), s8[4194304]{0:T(1024)(128)(4,1)S(1)}, s32[]{:S(2)}) async-start(s8[8388608]{0:T(1024)(128)(4,1)} %bitcast.49), calls=%async_computation.5 | async-start | bytes 8388608
Sparse Core Ops, SparseCore 0:
  9.4 87.8 all-gather.2
  111.4 23.0 reduce-scatter.1

commit v3 on v2

--- a/solution.py
+++ b/solution.py
@@ -262,12 +262,26 @@
     glob_out = (glob_accum / jnp.transpose(glob_total)[..., None]).reshape(tok_dev, columns)
     glob_out = glob_out.astype(jnp.bfloat16)
     attn_rows = jnp.where(own_index == global_owner[0], glob_out, sparse)
-    return lax.psum_scatter(
-        jnp.dot(attn_rows, out_weight, preferred_element_type=jnp.float32).astype(jnp.bfloat16),
-        "head",
-        scatter_dimension=0,
-        tiled=True,
-    )
+    return head_sum(jnp.dot(attn_rows, out_weight, preferred_element_type=jnp.float32))
+
+
+def head_sum(partial):
+    members = lax.axis_size("head")
+    if members & (members - 1):
+        return lax.psum_scatter(
+            partial.astype(jnp.bfloat16), "head", scatter_dimension=0, tiled=True
+        )
+    me = lax.axis_index("head")
+    bit = members // 2
+    while bit >= 1:
+        half = partial.shape[0] // 2
+        upper = (me & bit) != 0
+        keep = jnp.where(upper, partial[half:], partial[:half])
+        send = jnp.where(upper, partial[:half], partial[half:]).astype(jnp.bfloat16)
+        got = lax.ppermute(send, "head", [(i, i ^ bit) for i in range(members)])
+        partial = keep + got.astype(jnp.float32)
+        bit //= 2
+    return partial.astype(jnp.bfloat16)
 
 
 GATHER_LIMIT = 16 * 2**20

time: 142 us -> 133 us (0.937)
  waiting for transfers between devices: 64.2 us -> 54.1 us
  starting transfers between devices: 7.35 us -> 8.92 us
    reduce_scatter x1 -> x0, waiting for transfers between devices: 23.2 us -> none  [gathered_plan(): lax.psum_scatter(jnp.dot(attn_rows, out_weight, preferred_element_type=jn...]
    ppermute x0 -> x2, waiting for transfers between devices: none -> 13.3 us  [head_sum(): got = lax.ppermute(send, 'head', [(i, i ^ bit) for i in range(members)])]
    ppermute x0 -> x2, starting transfers between devices: none -> 1.61 us  [head_sum(): got = lax.ppermute(send, 'head', [(i, i ^ bit) for i in range(members)])]
  transfers between devices with their start and end apart: 3 -> 4, of which waited for: 2 -> 3; matrix products, arithmetic and copies ran while one was open for 7% -> 7% of each run, Pallas kernels for 0% -> 0%
where the time goes in v3:
time: 133 us
  waiting for transfers between devices  54.1 us (41%)
  blocking collectives  31.1 us (23%)
  between operations  13.7 us (10%)
  other arithmetic  10.1 us (8%)
  matrix products  9.08 us (7%)
  starting transfers between devices  8.92 us (7%)
  local copies, waits for them, and re-layouts  6.23 us (5%)
    all_gather x1, waiting for transfers between devices, gathered_plan(): keyval = lax.all_gather(projected[:, 1:, :], 'seq', tiled=True)  40.8 us
    all_gather x1, blocking collectives, gathered_plan(): arrival_dest = lax.all_gather(destination, 'seq', tiled=True)  31.1 us
    ppermute x2, waiting for transfers between devices, head_sum(): got = lax.ppermute(send, 'head', [(i, i ^ bit) for i in range(members)])  13.3 us
    all_to_all x1, starting transfers between devices, gathered_plan(): lax.all_to_all(outgoing, 'seq', split_axis=0, concat_axis=0, tiled=True)  7.28 us
    dot_general x1, matrix products, gathered_plan(): jnp.einsum('hqk,khd->qhd', glob_exp, values.astype(jnp.float32), precisio...  2.9 us
    slice x1, local copies, waits for them, and re-layouts, gathered_plan(): keys = keyval[:, 0, :].reshape(tokens, heads_here, HD)  2.66 us
  transfers between devices with their start and end apart: 4, of which 3 were waited for; matrix products, arithmetic and copies ran while one was open for 7% of the time, Pallas kernels for 0%

profile of v3, /device:TPU:0, one launch (start us, length us, event | category | flops | bytes accessed | tf_op | source)
XLA Modules:
  0.0 133.2 jit_solution(3839195240739852634)
XLA Ops:
  6.6 1.1 slice.43
  7.7 1.0 copy.34
  8.7 0.7 and_select_fusion.5
  9.5 0.2 reduce_window_sum.30
  9.6 0.2 select_reduce_fusion.3
  9.8 0.7 multiply_add_fusion
  10.5 2.1 %convolution_convert_fusion = bf16[256,1024]{1,0:T(8,128)(2,1)} fusion(bf16[128,3,1024]{2,0,1:T(8,128)(2,1)} %param.6, s32[128]{0:T(128)S(1)} %multiply_add_fusion), kind=kOutput, calls=%fused_computation.24 | convolution fusion | flops 67403776 | bytes 786944 | tf_op jit(solution)/shard_map/dot_general | solution.py:202
  12.5 7.3 %all-to-all-start = ((bf16[8,32,1024]{2,1,0:T(8,128)(2,1)}), bf16[8,32,1024]{2,1,0:T(8,128)(2,1)S(1)}, u32[]{:S(2)}, u32[]{:S(2)}) async-start(bf16[8,32,1024]{2,1,0:T(8,128)(2,1)} %bitcast.6), calls=%async_computation | async-start | bytes 1048576 | tf_op jit(solution)/shard_map/all_to_all | solution.py:204
  19.8 31.1 %all-gather = s32[8,1,128]{2,1,0:T(1,128)S(1)} all-gather(s32[1,1,128]{2,1,0:T(1,128)S(1)} %bitcast.63), channel_id=1, replica_groups=mesh['seq'=8,'head'=4] {'seq'}, dimensions={0}, use_global_device_ids=true | all-gather | bytes 4608 | tf_op jit(solution)/shard_map/all_gather | solution.py:190
  51.0 2.5 %select_reduce_fusion.2 = s32[8,128]{0,1:T(8,128)S(1)} fusion(s32[8,128]{0,1:T(8,128)S(1)} %copy.27), kind=kOutput, calls=%fused_computation.46 | output fusion | flops 1096704 | bytes 8192 | tf_op jit(solution)/shard_map/jit(cumsum)/reduce_window_sum | solution.py:194
  53.6 0.2 reduce-window.8
  53.9 0.6 gather_fusion
  54.7 0.2 slice_reduce_fusion.2
  54.9 0.2 select_reduce_fusion.1
  55.3 0.5 fusion.35
  55.8 0.5 fusion.34
  56.3 0.3 fusion.22
  56.6 40.8 %all-gather.3.cloned.1.call-done = bf16[1024,2,1024]{0,2,1:T(8,128)(2,1)} async-done(((bf16[128,2,1024]{0,2,1:T(8,128)(2,1)}), bf16[1024,2,1024]{0,2,1:T(8,128)(2,1)}) %all-gather.3.cloned.1.call-update) | async-done | bytes 4194320 | tf_op jit(solution)/shard_map/all_gather | solution.py:191
  97.4 2.7 %fusion.61 = (bf16[1024,1,1024]{0,2,1:T(8,128)(2,1)S(1)}, bf16[1024,1,1024]{0,2,1:T(8,128)(2,1)S(1)}) fusion(bf16[1024,2,1024]{0,2,1:T(8,128)(2,1)} %all-gather.3.cloned.1.call-done), kind=kLoop, calls=%fused_computation.124 | loop fusion | bytes 8388608 | tf_op jit(solution)/shard_map/slice | solution.py:217
  100.0 0.8 multiply_reduce_fusion.1
  100.8 0.9 fusion.2
  101.8 2.9 %fusion.29 = bf16[128,8,128]{0,2,1:T(8,128)(2,1)S(1)} fusion(bf16[1024,8,128]{0,2,1:T(8,128)(2,1)S(1)} %bitcast.51, f32[8,128,1024]{2,1,0:T(8,128)S(1)} %get-tuple-element.11, f32[8,128]{1,0:T(8,128)S(1)} %get-tuple-element.10, f32[128,8]{0,1:T(8,128)S(1)} %bitcast.62), kind=kOutput, calls=%fused_computation.38 | convolution fusion | flops 1612972032 | bytes 6561792 | tf_op jit(solution)/shard_map/hqk,khd->qhd/dot_general | solution.py:259
  104.7 2.2 %multiply_reduce_fusion = (f32[8,128]{1,0:T(8,128)S(1)}, bf16[8,128,1024]{2,1,0:T(8,128)(2,1)S(1)}) fusion(f32[128,1024]{1,0:T(8,128)S(1)} %fusion.34, f32[8,128,1024]{2,1,0:T(8,128)S(1)} %get-tuple-element.11, pred[128,1024]{1,0:T(8,128)(4,1)S(1)} %fusion.35), kind=kOutput, calls=%fused_computation.2 | output fusion | flops 8389631 | bytes 6950912 | tf_op jit(solution)/shard_map/sub | solution.py:244
  106.8 0.8 fusion.9
  107.6 1.0 fusion.27
  108.7 0.4 slice-done.1
  109.0 1.3 fusion.62
  110.4 1.5 %collective-permute-start = (bf16[64,4096]{1,0:T(8,128)(2,1)S(1)}, bf16[64,4096]{1,0:T(8,128)(2,1)S(1)}, u32[]{:S(2)}, u32[]{:S(2)}) collective-permute-start(bf16[64,4096]{1,0:T(8,128)(2,1)S(1)} %select_convert_fusion), channel_id=1, source_target_pairs={{0,2},{1,3},{2,0},{3,1},{4,6},{5,7},{6,4},{7,5},{8,10},{9,11},{10,... | collective-permute-start | bytes 1572872 | tf_op jit(solution)/shard_map/ppermute | solution.py:281
  112.0 11.8 %collective-permute-done = bf16[64,4096]{1,0:T(8,128)(2,1)S(1)} collective-permute-done((bf16[64,4096]{1,0:T(8,128)(2,1)S(1)}, bf16[64,4096]{1,0:T(8,128)(2,1)S(1)}, u32[]{:S(2)}, u32[]{:S(2)}) %collective-permute-start) | collective-permute-done | bytes 524320 | tf_op jit(solution)/shard_map/ppermute | solution.py:281
  123.7 0.1 convert_add_fusion
  124.0 1.5 %collective-permute-done.1 = bf16[32,4096]{1,0:T(8,128)(2,1)S(1)} collective-permute-done((bf16[32,4096]{1,0:T(8,128)(2,1)S(1)}, bf16[32,4096]{1,0:T(8,128)(2,1)S(1)}, u32[]{:S(2)}, u32[]{:S(2)}) %collective-permute-start.1) | collective-permute-done | bytes 262176 | tf_op jit(solution)/shard_map/ppermute | solution.py:281
  125.5 0.8 add_convert_fusion
  (33 shorter events, 0.9 us)
Async XLA Ops:
  6.5 13.3 %copy-start.1 = (s32[128]{0:T(128)S(1)}, s32[128]{0:T(128)}, u32[]{:S(2)}) copy-start(s32[128]{0:T(128)} %param.7) | copy-start | bytes 1540
  6.5 47.0 %copy-start.2 = (s32[4]{0:T(128)S(1)}, s32[4]{0:T(128)}, u32[]{:S(2)}) copy-start(s32[4]{0:T(128)} %param.8) | copy-start | bytes 52
  6.5 47.2 %copy-start = (s32[8,3]{0,1:T(4,128)S(1)}, s32[8,3]{0,1:T(4,128)}, u32[]{:S(2)}) copy-start(s32[8,3]{0,1:T(4,128)} %param.9) | copy-start | bytes 292
  6.5 48.6 %copy-start.3 = (s32[8]{0:T(128)S(1)}, s32[8]{0:T(128)}, u32[]{:S(2)}) copy-start(s32[8]{0:T(128)} %param.10) | copy-start | bytes 100
  6.5 90.8 %all-gather.3.cloned.1.call-start = ((), (), s32[]{:S(2)}) async-start(), calls=%async_computation.1 | async-start | bytes 4718592 | tf_op jit(solution)/shard_map/all_gather | solution.py:191
  12.5 43.8 %all-to-all-start = ((bf16[8,32,1024]{2,1,0:T(8,128)(2,1)}), bf16[8,32,1024]{2,1,0:T(8,128)(2,1)S(1)}, u32[]{:S(2)}, u32[]{:S(2)}) async-start(bf16[8,32,1024]{2,1,0:T(8,128)(2,1)} %bitcast.6), calls=%async_computation | async-start | bytes 1048576 | tf_op jit(solution)/shard_map/all_to_all | solution.py:204
  104.7 4.0 %slice-start = ((s8[8388608]{0:T(1024)(128)(4,1)}), s8[4194304]{0:T(1024)(128)(4,1)S(1)}, s32[]{:S(2)}) async-start(s8[8388608]{0:T(1024)(128)(4,1)} %bitcast.49), calls=%async_computation.2 | async-start | bytes 8388608
  106.8 2.2 %slice-start.1 = ((s8[8388608]{0:T(1024)(128)(4,1)}), s8[4194304]{0:T(1024)(128)(4,1)S(1)}, s32[]{:S(2)}) async-start(s8[8388608]{0:T(1024)(128)(4,1)} %bitcast.49), calls=%async_computation.3 | async-start | bytes 8388608
  110.4 13.3 %collective-permute-start = (bf16[64,4096]{1,0:T(8,128)(2,1)S(1)}, bf16[64,4096]{1,0:T(8,128)(2,1)S(1)}, u32[]{:S(2)}, u32[]{:S(2)}) collective-permute-start(bf16[64,4096]{1,0:T(8,128)(2,1)S(1)} %select_convert_fusion), channel_id=1, source_target_pairs={{0,2},{1,3},{2,0},{3,1},{4,6},{5,7},{6,4},{7,5},{8,10},{9,11},{10,... | collective-permute-start | bytes 1572872 | tf_op jit(solution)/shard_map/ppermute | solution.py:281
  123.9 1.6 %collective-permute-start.1 = (bf16[32,4096]{1,0:T(8,128)(2,1)S(1)}, bf16[32,4096]{1,0:T(8,128)(2,1)S(1)}, u32[]{:S(2)}, u32[]{:S(2)}) collective-permute-start(bf16[32,4096]{1,0:T(8,128)(2,1)S(1)} %select_convert_fusion.1), channel_id=1, source_target_pairs={{0,1},{1,0},{2,3},{3,2},{4,5},{5,4},{6,7},{7,6},{8,9},{9,8},{10,11... | collective-permute-start | bytes 786440 | tf_op jit(solution)/shard_map/ppermute | solution.py:281
Sparse Core Ops, SparseCore 0:
  9.4 87.9 all-gather.2

commit v4 on v3

--- a/solution.py
+++ b/solution.py
@@ -237,31 +237,25 @@
         drawn = drawn + (key_block[None, :] == chosen[:, r][:, None]).astype(jnp.int32)
     glob_start = global_owner[0] * tok_dev
     in_glob = (arrival_dest >= glob_start) & (arrival_dest < glob_start + tok_dev)
+    holds_glob = own_index == global_owner[0]
     count = window + drawn + in_glob[None, :].astype(jnp.int32)
+    count = jnp.where(holds_glob, 1, count)
     live = count > 0
     near_scores = jnp.where(live[None], scores, big_negative)
     row_peak = jnp.max(near_scores, axis=2)
     near_exp = jnp.exp(near_scores - row_peak[..., None])
     count_f = count.astype(jnp.float32)[None]
     denominator = jnp.sum(near_exp * count_f, axis=2)
-    weighted = near_exp.astype(jnp.bfloat16).astype(jnp.float32) * count_f
+    rounded = jnp.where(holds_glob, near_exp, near_exp.astype(jnp.bfloat16).astype(jnp.float32))
+    weighted = rounded * count_f
     weight_hi = weighted.astype(jnp.bfloat16)
     weight_lo = (weighted - weight_hi.astype(jnp.float32)).astype(jnp.bfloat16)
     mixed_sum = jnp.einsum("hqk,khd->qhd", weight_hi, values, preferred_element_type=jnp.float32)
     mixed_sum = mixed_sum + jnp.einsum(
         "hqk,khd->qhd", weight_lo, values, preferred_element_type=jnp.float32
     )
-    sparse = (mixed_sum / jnp.transpose(denominator)[..., None]).reshape(tok_dev, columns)
-    sparse = sparse.astype(jnp.bfloat16)
-    glob_peak = jnp.max(scores, axis=2)
-    glob_exp = jnp.exp(scores - glob_peak[..., None])
-    glob_total = jnp.sum(glob_exp, axis=2)
-    glob_accum = jnp.einsum(
-        "hqk,khd->qhd", glob_exp, values.astype(jnp.float32), precision=lax.Precision.HIGHEST
-    )
-    glob_out = (glob_accum / jnp.transpose(glob_total)[..., None]).reshape(tok_dev, columns)
-    glob_out = glob_out.astype(jnp.bfloat16)
-    attn_rows = jnp.where(own_index == global_owner[0], glob_out, sparse)
+    attn_rows = (mixed_sum / jnp.transpose(denominator)[..., None]).reshape(tok_dev, columns)
+    attn_rows = attn_rows.astype(jnp.bfloat16)
     return head_sum(jnp.dot(attn_rows, out_weight, preferred_element_type=jnp.float32))
 
 

time: 133 us -> 131 us (0.985)
  matrix products: 9.08 us -> 6.25 us
    dot_general x1 -> x0, matrix products: 2.9 us -> none  [gathered_plan(): jnp.einsum('hqk,khd->qhd', glob_exp, values.astype(jnp.float32), precisio...]
where the time goes in v4:
time: 131 us
  waiting for transfers between devices  54.3 us (41%)
  blocking collectives  30.8 us (24%)
  between operations  13.7 us (10%)
  other arithmetic  9.26 us (7%)
  starting transfers between devices  8.92 us (7%)
  local copies, waits for them, and re-layouts  7.56 us (6%)
  matrix products  6.25 us (5%)
    all_gather x1, waiting for transfers between devices, gathered_plan(): keyval = lax.all_gather(projected[:, 1:, :], 'seq', tiled=True)  40.9 us
    all_gather x1, blocking collectives, gathered_plan(): arrival_dest = lax.all_gather(destination, 'seq', tiled=True)  30.8 us
    ppermute x2, waiting for transfers between devices, head_sum(): got = lax.ppermute(send, 'head', [(i, i ^ bit) for i in range(members)])  13.3 us
    all_to_all x1, starting transfers between devices, gathered_plan(): lax.all_to_all(outgoing, 'seq', split_axis=0, concat_axis=0, tiled=True)  7.28 us
    unnamed x14, local copies, waits for them, and re-layouts  2.81 us
    slice x1, local copies, waits for them, and re-layouts, gathered_plan(): keys = keyval[:, 0, :].reshape(tokens, heads_here, HD)  2.66 us
  transfers between devices with their start and end apart: 4, of which 3 were waited for; matrix products, arithmetic and copies ran while one was open for 7% of the time, Pallas kernels for 0%

profile of v4, /device:TPU:0, one launch (start us, length us, event | category | flops | bytes accessed | tf_op | source)
XLA Modules:
  0.0 130.7 jit_solution(12408893289997481308)
XLA Ops:
  6.6 1.1 slice.46
  7.7 1.0 copy.34
  8.7 0.7 and_select_fusion
  9.5 0.2 reduce_window_sum.30
  9.6 0.2 select_reduce_fusion.2
  9.8 0.7 multiply_add_fusion
  10.5 2.1 %convolution_convert_fusion = bf16[256,1024]{1,0:T(8,128)(2,1)} fusion(bf16[128,3,1024]{2,0,1:T(8,128)(2,1)} %param.6, s32[128]{0:T(128)S(1)} %multiply_add_fusion), kind=kOutput, calls=%fused_computation.18 | convolution fusion | flops 67403776 | bytes 786944 | tf_op jit(solution)/shard_map/dot_general | solution.py:202
  12.5 7.3 %all-to-all-start = ((bf16[8,32,1024]{2,1,0:T(8,128)(2,1)}), bf16[8,32,1024]{2,1,0:T(8,128)(2,1)S(1)}, u32[]{:S(2)}, u32[]{:S(2)}) async-start(bf16[8,32,1024]{2,1,0:T(8,128)(2,1)} %bitcast.9), calls=%async_computation | async-start | bytes 1048576 | tf_op jit(solution)/shard_map/all_to_all | solution.py:204
  19.8 0.2 reduce-window.8
  20.1 30.8 %all-gather = s32[8,1,128]{2,1,0:T(1,128)S(1)} all-gather(s32[1,1,128]{2,1,0:T(1,128)S(1)} %bitcast.49), channel_id=1, replica_groups=mesh['seq'=8,'head'=4] {'seq'}, dimensions={0}, use_global_device_ids=true | all-gather | bytes 4608 | tf_op jit(solution)/shard_map/all_gather | solution.py:190
  51.0 0.1 copy.28
  51.1 2.5 %select_reduce_fusion.1 = s32[8,128]{0,1:T(8,128)S(1)} fusion(s32[8,128]{0,1:T(8,128)S(1)} %copy.28), kind=kOutput, calls=%fused_computation.33 | output fusion | flops 1096704 | bytes 8192 | tf_op jit(solution)/shard_map/jit(cumsum)/reduce_window_sum | solution.py:194
  53.7 0.6 gather_fusion
  54.5 0.2 slice_reduce_fusion.2
  54.7 0.2 select_reduce_fusion
  55.1 0.5 fusion.31
  55.6 0.5 fusion.30
  56.2 0.3 fusion.19
  56.4 40.9 %all-gather.3.cloned.1.call-done = bf16[1024,2,1024]{0,2,1:T(8,128)(2,1)} async-done(((bf16[128,2,1024]{0,2,1:T(8,128)(2,1)}), bf16[1024,2,1024]{0,2,1:T(8,128)(2,1)}) %all-gather.3.cloned.1.call-update) | async-done | bytes 4194320 | tf_op jit(solution)/shard_map/all_gather | solution.py:191
  97.4 2.7 %fusion.56 = (bf16[1024,1,1024]{0,2,1:T(8,128)(2,1)S(1)}, bf16[1024,1,1024]{0,2,1:T(8,128)(2,1)S(1)}) fusion(bf16[1024,2,1024]{0,2,1:T(8,128)(2,1)} %all-gather.3.cloned.1.call-done), kind=kLoop, calls=%fused_computation.111 | loop fusion | bytes 8388608 | tf_op jit(solution)/shard_map/slice | solution.py:217
  100.0 0.7 fusion.32
  100.7 2.2 %multiply_reduce_fusion = (f32[8,128]{1,0:T(8,128)S(1)}, f32[8,128,1024]{2,1,0:T(8,128)S(1)}) fusion(f32[128,1024]{1,0:T(8,128)S(1)} %fusion.30, f32[8,128,1024]{2,1,0:T(8,128)S(1)} %fusion.32, pred[128,1024]{1,0:T(8,128)(4,1)S(1)} %fusion.31), kind=kOutput, calls=%fused_computation.2 | output fusion | flops 7341055 | bytes 9048064 | tf_op jit(solution)/shard_map/sub | solution.py:246
  102.9 0.8 fusion.5
  103.7 1.1 fusion.23
  104.9 0.2 slice-done
  105.1 1.5 %slice-done.1 = s8[4194304]{0:T(1024)(128)(4,1)S(1)} async-done(((s8[8388608]{0:T(1024)(128)(4,1)}), s8[4194304]{0:T(1024)(128)(4,1)S(1)}, s32[]{:S(2)}) %slice-start.1) | async-done | bytes 4194328
  106.6 1.3 fusion.57
  108.0 1.5 %collective-permute-start = (bf16[64,4096]{1,0:T(8,128)(2,1)S(1)}, bf16[64,4096]{1,0:T(8,128)(2,1)S(1)}, u32[]{:S(2)}, u32[]{:S(2)}) collective-permute-start(bf16[64,4096]{1,0:T(8,128)(2,1)S(1)} %select_convert_fusion), channel_id=1, source_target_pairs={{0,2},{1,3},{2,0},{3,1},{4,6},{5,7},{6,4},{7,5},{8,10},{9,11},{10,... | collective-permute-start | bytes 1572872 | tf_op jit(solution)/shard_map/ppermute | solution.py:275
  109.5 11.8 %collective-permute-done = bf16[64,4096]{1,0:T(8,128)(2,1)S(1)} collective-permute-done((bf16[64,4096]{1,0:T(8,128)(2,1)S(1)}, bf16[64,4096]{1,0:T(8,128)(2,1)S(1)}, u32[]{:S(2)}, u32[]{:S(2)}) %collective-permute-start) | collective-permute-done | bytes 524320 | tf_op jit(solution)/shard_map/ppermute | solution.py:275
  121.3 0.1 convert_add_fusion
  121.6 1.5 %collective-permute-done.1 = bf16[32,4096]{1,0:T(8,128)(2,1)S(1)} collective-permute-done((bf16[32,4096]{1,0:T(8,128)(2,1)S(1)}, bf16[32,4096]{1,0:T(8,128)(2,1)S(1)}, u32[]{:S(2)}, u32[]{:S(2)}) %collective-permute-start.1) | collective-permute-done | bytes 262176 | tf_op jit(solution)/shard_map/ppermute | solution.py:275
  123.1 0.8 add_convert_fusion
  (30 shorter events, 0.8 us)
Async XLA Ops:
  6.5 13.6 %copy-start.1 = (s32[128]{0:T(128)S(1)}, s32[128]{0:T(128)}, u32[]{:S(2)}) copy-start(s32[128]{0:T(128)} %param.7) | copy-start | bytes 1540
  6.5 13.3 %copy-start.2 = (s32[4]{0:T(128)S(1)}, s32[4]{0:T(128)}, u32[]{:S(2)}) copy-start(s32[4]{0:T(128)} %param.8) | copy-start | bytes 52
  6.5 13.5 %copy-start = (s32[8,3]{0,1:T(4,128)S(1)}, s32[8,3]{0,1:T(4,128)}, u32[]{:S(2)}) copy-start(s32[8,3]{0,1:T(4,128)} %param.9) | copy-start | bytes 292
  6.5 48.4 %copy-start.3 = (s32[8]{0:T(128)S(1)}, s32[8]{0:T(128)}, u32[]{:S(2)}) copy-start(s32[8]{0:T(128)} %param.10) | copy-start | bytes 100
  6.5 90.8 %all-gather.3.cloned.1.call-start = ((), (), s32[]{:S(2)}) async-start(), calls=%async_computation.1 | async-start | bytes 4718592 | tf_op jit(solution)/shard_map/all_gather | solution.py:191
  12.5 43.6 %all-to-all-start = ((bf16[8,32,1024]{2,1,0:T(8,128)(2,1)}), bf16[8,32,1024]{2,1,0:T(8,128)(2,1)S(1)}, u32[]{:S(2)}, u32[]{:S(2)}) async-start(bf16[8,32,1024]{2,1,0:T(8,128)(2,1)} %bitcast.9), calls=%async_computation | async-start | bytes 1048576 | tf_op jit(solution)/shard_map/all_to_all | solution.py:204
  102.9 2.2 %slice-start = ((s8[8388608]{0:T(1024)(128)(4,1)}), s8[4194304]{0:T(1024)(128)(4,1)S(1)}, s32[]{:S(2)}) async-start(s8[8388608]{0:T(1024)(128)(4,1)} %bitcast.37), calls=%async_computation.2 | async-start | bytes 8388608
  103.7 2.9 %slice-start.1 = ((s8[8388608]{0:T(1024)(128)(4,1)}), s8[4194304]{0:T(1024)(128)(4,1)S(1)}, s32[]{:S(2)}) async-start(s8[8388608]{0:T(1024)(128)(4,1)} %bitcast.37), calls=%async_computation.3 | async-start | bytes 8388608
  108.0 13.3 %collective-permute-start = (bf16[64,4096]{1,0:T(8,128)(2,1)S(1)}, bf16[64,4096]{1,0:T(8,128)(2,1)S(1)}, u32[]{:S(2)}, u32[]{:S(2)}) collective-permute-start(bf16[64,4096]{1,0:T(8,128)(2,1)S(1)} %select_convert_fusion), channel_id=1, source_target_pairs={{0,2},{1,3},{2,0},{3,1},{4,6},{5,7},{6,4},{7,5},{8,10},{9,11},{10,... | collective-permute-start | bytes 1572872 | tf_op jit(solution)/shard_map/ppermute | solution.py:275
  121.5 1.6 %collective-permute-start.1 = (bf16[32,4096]{1,0:T(8,128)(2,1)S(1)}, bf16[32,4096]{1,0:T(8,128)(2,1)S(1)}, u32[]{:S(2)}, u32[]{:S(2)}) collective-permute-start(bf16[32,4096]{1,0:T(8,128)(2,1)S(1)} %select_convert_fusion.1), channel_id=1, source_target_pairs={{0,1},{1,0},{2,3},{3,2},{4,5},{5,4},{6,7},{7,6},{8,9},{9,8},{10,11... | collective-permute-start | bytes 786440 | tf_op jit(solution)/shard_map/ppermute | solution.py:275
Sparse Core Ops, SparseCore 0:
  9.4 87.8 all-gather.2

commit v5 on v4

--- a/solution.py
+++ b/solution.py
@@ -266,15 +266,18 @@
             partial.astype(jnp.bfloat16), "head", scatter_dimension=0, tiled=True
         )
     me = lax.axis_index("head")
-    bit = members // 2
-    while bit >= 1:
-        half = partial.shape[0] // 2
+    rows = partial.shape[0] // members
+    partial = partial.reshape(members, rows, partial.shape[1])
+    bit = 1
+    while bit < members:
+        pairs = partial.reshape(partial.shape[0] // 2, 2, rows, partial.shape[2])
         upper = (me & bit) != 0
-        keep = jnp.where(upper, partial[half:], partial[:half])
-        send = jnp.where(upper, partial[:half], partial[half:]).astype(jnp.bfloat16)
+        keep = jnp.where(upper, pairs[:, 1], pairs[:, 0])
+        send = jnp.where(upper, pairs[:, 0], pairs[:, 1]).astype(jnp.bfloat16)
         got = lax.ppermute(send, "head", [(i, i ^ bit) for i in range(members)])
         partial = keep + got.astype(jnp.float32)
-        bit //= 2
+        bit *= 2
+    partial = partial.reshape(rows, partial.shape[2])
     return partial.astype(jnp.bfloat16)
 
 

time: 131 us -> 128 us (0.977)
  waiting for transfers between devices: 54.3 us -> 49.7 us
  matrix products: 6.25 us -> 9.57 us
  local copies, waits for them, and re-layouts: 7.56 us -> 6.14 us
    ppermute x2, waiting for transfers between devices: 13.3 us -> 8.75 us  [head_sum(): got = lax.ppermute(send, 'head', [(i, i ^ bit) for i in range(members)])]
    dot_general x1, matrix products: 1.3 us -> 4.64 us  [gathered_plan(): jnp.dot(attn_rows, out_weight, preferred_element_type=jnp.float32)]
    unnamed x14 -> x10, local copies, waits for them, and re-layouts: 2.81 us -> 1.1 us
where the time goes in v5:
time: 128 us
  waiting for transfers between devices  49.7 us (39%)
  blocking collectives  30.8 us (24%)
  between operations  13.7 us (11%)
  matrix products  9.57 us (7%)
  other arithmetic  9.26 us (7%)
  starting transfers between devices  8.94 us (7%)
  local copies, waits for them, and re-layouts  6.14 us (5%)
    all_gather x1, waiting for transfers between devices, gathered_plan(): keyval = lax.all_gather(projected[:, 1:, :], 'seq', tiled=True)  40.9 us
    all_gather x1, blocking collectives, gathered_plan(): arrival_dest = lax.all_gather(destination, 'seq', tiled=True)  30.8 us
    ppermute x2, waiting for transfers between devices, head_sum(): got = lax.ppermute(send, 'head', [(i, i ^ bit) for i in range(members)])  8.75 us
    all_to_all x1, starting transfers between devices, gathered_plan(): lax.all_to_all(outgoing, 'seq', split_axis=0, concat_axis=0, tiled=True)  7.28 us
    dot_general x1, matrix products, gathered_plan(): jnp.dot(attn_rows, out_weight, preferred_element_type=jnp.float32)  4.64 us
    slice x1, local copies, waits for them, and re-layouts, gathered_plan(): keys = keyval[:, 0, :].reshape(tokens, heads_here, HD)  2.66 us
  transfers between devices with their start and end apart: 4, of which 3 were waited for; matrix products, arithmetic and copies ran while one was open for 7% of the time, Pallas kernels for 0%

profile of v5, /device:TPU:0, one launch (start us, length us, event | category | flops | bytes accessed | tf_op | source)
XLA Modules:
  0.0 128.1 jit_solution(13260214112426134094)
XLA Ops:
  6.6 1.1 slice.46
  7.7 1.0 copy.68
  8.7 0.7 and_select_fusion
  9.5 0.2 reduce_window_sum.30
  9.6 0.2 select_reduce_fusion.2
  9.8 0.7 multiply_add_fusion
  10.5 2.1 %convolution_convert_fusion = bf16[256,1024]{1,0:T(8,128)(2,1)} fusion(bf16[128,3,1024]{2,0,1:T(8,128)(2,1)} %param.6, s32[128]{0:T(128)S(1)} %multiply_add_fusion), kind=kOutput, calls=%fused_computation.20 | convolution fusion | flops 67403776 | bytes 786944 | tf_op jit(solution)/shard_map/dot_general | solution.py:202
  12.5 7.3 %all-to-all-start = ((bf16[8,32,1024]{2,1,0:T(8,128)(2,1)}), bf16[8,32,1024]{2,1,0:T(8,128)(2,1)S(1)}, u32[]{:S(2)}, u32[]{:S(2)}) async-start(bf16[8,32,1024]{2,1,0:T(8,128)(2,1)} %bitcast.9), calls=%async_computation | async-start | bytes 1048576 | tf_op jit(solution)/shard_map/all_to_all | solution.py:204
  19.8 0.2 reduce-window.8
  20.1 30.8 %all-gather = s32[8,1,128]{2,1,0:T(1,128)S(1)} all-gather(s32[1,1,128]{2,1,0:T(1,128)S(1)} %bitcast.85), channel_id=1, replica_groups=mesh['seq'=8,'head'=4] {'seq'}, dimensions={0}, use_global_device_ids=true | all-gather | bytes 4608 | tf_op jit(solution)/shard_map/all_gather | solution.py:190
  51.0 0.1 copy.52
  51.1 2.5 %select_reduce_fusion.1 = s32[8,128]{0,1:T(8,128)S(1)} fusion(s32[8,128]{0,1:T(8,128)S(1)} %copy.52), kind=kOutput, calls=%fused_computation.40 | output fusion | flops 1096704 | bytes 8192 | tf_op jit(solution)/shard_map/jit(cumsum)/reduce_window_sum | solution.py:194
  53.7 0.6 gather_fusion
  54.5 0.2 slice_reduce_fusion.2
  54.7 0.2 select_reduce_fusion
  55.1 0.5 fusion.38
  55.6 0.5 fusion.37
  56.2 0.3 fusion.21
  56.4 40.9 %all-gather.3.cloned.1.call-done = bf16[1024,2,1024]{0,2,1:T(8,128)(2,1)} async-done(((bf16[128,2,1024]{0,2,1:T(8,128)(2,1)}), bf16[1024,2,1024]{0,2,1:T(8,128)(2,1)}) %all-gather.3.cloned.1.call-update) | async-done | bytes 4194320 | tf_op jit(solution)/shard_map/all_gather | solution.py:191
  97.3 2.7 %fusion.65 = (bf16[1024,1,1024]{0,2,1:T(8,128)(2,1)S(1)}, bf16[1024,1,1024]{0,2,1:T(8,128)(2,1)S(1)}) fusion(bf16[1024,2,1024]{0,2,1:T(8,128)(2,1)} %all-gather.3.cloned.1.call-done), kind=kLoop, calls=%fused_computation.120 | loop fusion | bytes 8388608 | tf_op jit(solution)/shard_map/slice | solution.py:217
  100.0 0.7 fusion.41
  100.7 2.2 %multiply_reduce_fusion = (f32[8,128]{1,0:T(8,128)S(1)}, f32[8,128,1024]{2,1,0:T(8,128)S(1)}) fusion(f32[128,1024]{1,0:T(8,128)S(1)} %fusion.37, f32[8,128,1024]{2,1,0:T(8,128)S(1)} %fusion.41, pred[128,1024]{1,0:T(8,128)(4,1)S(1)} %fusion.38), kind=kOutput, calls=%fused_computation.4 | output fusion | flops 7341055 | bytes 9048064 | tf_op jit(solution)/shard_map/sub | solution.py:246
  102.9 0.8 fusion.7
  103.7 1.1 fusion.28
  104.8 0.2 copy.59
  105.0 0.1 convert_element_type.165
  105.1 4.6 %fusion.1 = f32[2,2,32,4096]{3,2,1,0:T(8,128)S(1)} fusion(bf16[2,2,32,1024]{3,2,1,0:T(8,128)(2,1)S(1)} %convert_element_type.165, bf16[1024,4096]{1,0:T(8,128)(2,1)} %param.11), kind=kOutput, calls=%fused_computation.2 | convolution fusion | flops 1073741824 | bytes 10747904 | tf_op jit(solution)/shard_map/dot_general | solution.py:259
  110.0 1.9 %collective-permute-done = bf16[2,32,4096]{2,1,0:T(8,128)(2,1)S(1)} collective-permute-done((bf16[2,32,4096]{2,1,0:T(8,128)(2,1)S(1)}, bf16[2,32,4096]{2,1,0:T(8,128)(2,1)S(1)}, u32[]{:S(2)}, u32[]{:S(2)}) %collective-permute-start) | collective-permute-done | bytes 524320 | tf_op jit(solution)/shard_map/ppermute | solution.py:277
  111.8 0.1 fusion.24
  112.0 1.6 %collective-permute-start.1 = (bf16[1,32,4096]{2,1,0:T(8,128)(2,1)S(1)}, bf16[1,32,4096]{2,1,0:T(8,128)(2,1)S(1)}, u32[]{:S(2)}, u32[]{:S(2)}) collective-permute-start(bf16[1,32,4096]{2,1,0:T(8,128)(2,1)S(1)} %fusion.39), channel_id=1, source_target_pairs={{0,2},{1,3},{2,0},{3,1},{4,6},{5,7},{6,4},{7,5},{8,10},{9,11},{10,... | collective-permute-start | bytes 786440 | tf_op jit(solution)/shard_map/ppermute | solution.py:277
  113.6 6.9 %collective-permute-done.1 = bf16[1,32,4096]{2,1,0:T(8,128)(2,1)S(1)} collective-permute-done((bf16[1,32,4096]{2,1,0:T(8,128)(2,1)S(1)}, bf16[1,32,4096]{2,1,0:T(8,128)(2,1)S(1)}, u32[]{:S(2)}, u32[]{:S(2)}) %collective-permute-start.1) | collective-permute-done | bytes 262176 | tf_op jit(solution)/shard_map/ppermute | solution.py:277
  120.5 0.8 fusion.40
  (27 shorter events, 0.8 us)
Async XLA Ops:
  6.5 13.6 %copy-start.1 = (s32[128]{0:T(128)S(1)}, s32[128]{0:T(128)}, u32[]{:S(2)}) copy-start(s32[128]{0:T(128)} %param.7) | copy-start | bytes 1540
  6.5 13.3 %copy-start.2 = (s32[4]{0:T(128)S(1)}, s32[4]{0:T(128)}, u32[]{:S(2)}) copy-start(s32[4]{0:T(128)} %param.8) | copy-start | bytes 52
  6.5 13.5 %copy-start = (s32[8,3]{0,1:T(4,128)S(1)}, s32[8,3]{0,1:T(4,128)}, u32[]{:S(2)}) copy-start(s32[8,3]{0,1:T(4,128)} %param.9) | copy-start | bytes 292
  6.5 48.4 %copy-start.3 = (s32[8]{0:T(128)S(1)}, s32[8]{0:T(128)}, u32[]{:S(2)}) copy-start(s32[8]{0:T(128)} %param.10) | copy-start | bytes 100
  6.5 90.8 %all-gather.3.cloned.1.call-start = ((), (), s32[]{:S(2)}) async-start(), calls=%async_computation.1 | async-start | bytes 4718592 | tf_op jit(solution)/shard_map/all_gather | solution.py:191
  12.5 43.6 %all-to-all-start = ((bf16[8,32,1024]{2,1,0:T(8,128)(2,1)}), bf16[8,32,1024]{2,1,0:T(8,128)(2,1)S(1)}, u32[]{:S(2)}, u32[]{:S(2)}) async-start(bf16[8,32,1024]{2,1,0:T(8,128)(2,1)} %bitcast.9), calls=%async_computation | async-start | bytes 1048576 | tf_op jit(solution)/shard_map/all_to_all | solution.py:204
  109.9 2.0 %collective-permute-start = (bf16[2,32,4096]{2,1,0:T(8,128)(2,1)S(1)}, bf16[2,32,4096]{2,1,0:T(8,128)(2,1)S(1)}, u32[]{:S(2)}, u32[]{:S(2)}) collective-permute-start(bf16[2,32,4096]{2,1,0:T(8,128)(2,1)S(1)} %fusion.35), channel_id=1, source_target_pairs={{0,1},{1,0},{2,3},{3,2},{4,5},{5,4},{6,7},{7,6},{8,9},{9,8},{10,11... | collective-permute-start | bytes 1572872 | tf_op jit(solution)/shard_map/ppermute | solution.py:277
  112.0 8.4 %collective-permute-start.1 = (bf16[1,32,4096]{2,1,0:T(8,128)(2,1)S(1)}, bf16[1,32,4096]{2,1,0:T(8,128)(2,1)S(1)}, u32[]{:S(2)}, u32[]{:S(2)}) collective-permute-start(bf16[1,32,4096]{2,1,0:T(8,128)(2,1)S(1)} %fusion.39), channel_id=1, source_target_pairs={{0,2},{1,3},{2,0},{3,1},{4,6},{5,7},{6,4},{7,5},{8,10},{9,11},{10,... | collective-permute-start | bytes 786440 | tf_op jit(solution)/shard_map/ppermute | solution.py:277
Sparse Core Ops, SparseCore 0:
  9.4 87.8 all-gather.2

commit v6 on v5

--- a/solution.py
+++ b/solution.py
@@ -256,7 +256,8 @@
     )
     attn_rows = (mixed_sum / jnp.transpose(denominator)[..., None]).reshape(tok_dev, columns)
     attn_rows = attn_rows.astype(jnp.bfloat16)
-    return head_sum(jnp.dot(attn_rows, out_weight, preferred_element_type=jnp.float32))
+    projected_rows = jnp.dot(attn_rows, out_weight, preferred_element_type=jnp.float32)
+    return head_sum(lax.optimization_barrier(projected_rows))
 
 
 def head_sum(partial):

time: 128 us -> 126 us (0.984)
  matrix products: 9.57 us -> 6.25 us
  local copies, waits for them, and re-layouts: 6.14 us -> 7.56 us
    dot_general x1, matrix products: 4.64 us -> 1.3 us  [gathered_plan(): jnp.dot(attn_rows, out_weight, preferred_element_type=jnp.float32)]
    unnamed x10 -> x14, local copies, waits for them, and re-layouts: 1.1 us -> 2.81 us
where the time goes in v6:
time: 126 us
  waiting for transfers between devices  49.7 us (39%)
  blocking collectives  30.8 us (24%)
  between operations  13.7 us (11%)
  other arithmetic  9.26 us (7%)
  starting transfers between devices  8.93 us (7%)
  local copies, waits for them, and re-layouts  7.56 us (6%)
  matrix products  6.25 us (5%)
    all_gather x1, waiting for transfers between devices, gathered_plan(): keyval = lax.all_gather(projected[:, 1:, :], 'seq', tiled=True)  40.9 us
    all_gather x1, blocking collectives, gathered_plan(): arrival_dest = lax.all_gather(destination, 'seq', tiled=True)  30.8 us
    ppermute x2, waiting for transfers between devices, head_sum(): got = lax.ppermute(send, 'head', [(i, i ^ bit) for i in range(members)])  8.76 us
    all_to_all x1, starting transfers between devices, gathered_plan(): lax.all_to_all(outgoing, 'seq', split_axis=0, concat_axis=0, tiled=True)  7.28 us
    unnamed x14, local copies, waits for them, and re-layouts  2.81 us
    slice x1, local copies, waits for them, and re-layouts, gathered_plan(): keys = keyval[:, 0, :].reshape(tokens, heads_here, HD)  2.66 us
    another operation x1, other arithmetic, gathered_plan(): slot_all = jnp.sum((jnp.cumsum(onehot, axis=1) - onehot) * onehot, axis=2)  2.52 us
  transfers between devices with their start and end apart: 4, of which 3 were waited for; matrix products, arithmetic and copies ran while one was open for 7% of the time, Pallas kernels for 0%

profile of v6, /device:TPU:0, one launch (start us, length us, event | category | flops | bytes accessed | tf_op | source)
XLA Modules:
  0.0 126.2 jit_solution(7470693322288038065)
XLA Ops:
  6.6 1.1 slice.46
  7.7 1.0 copy.44
  8.7 0.7 and_select_fusion
  9.5 0.2 reduce_window_sum.30
  9.6 0.2 select_reduce_fusion.2
  9.8 0.7 multiply_add_fusion
  10.5 2.1 %convolution_convert_fusion = bf16[256,1024]{1,0:T(8,128)(2,1)} fusion(bf16[128,3,1024]{2,0,1:T(8,128)(2,1)} %param.6, s32[128]{0:T(128)S(1)} %multiply_add_fusion), kind=kOutput, calls=%fused_computation.18 | convolution fusion | flops 67403776 | bytes 786944 | tf_op jit(solution)/shard_map/dot_general | solution.py:202
  12.5 7.3 %all-to-all-start = ((bf16[8,32,1024]{2,1,0:T(8,128)(2,1)}), bf16[8,32,1024]{2,1,0:T(8,128)(2,1)S(1)}, u32[]{:S(2)}, u32[]{:S(2)}) async-start(bf16[8,32,1024]{2,1,0:T(8,128)(2,1)} %bitcast.9), calls=%async_computation | async-start | bytes 1048576 | tf_op jit(solution)/shard_map/all_to_all | solution.py:204
  19.8 0.2 reduce-window.8
  20.1 30.8 %all-gather = s32[8,1,128]{2,1,0:T(1,128)S(1)} all-gather(s32[1,1,128]{2,1,0:T(1,128)S(1)} %bitcast.86), channel_id=1, replica_groups=mesh['seq'=8,'head'=4] {'seq'}, dimensions={0}, use_global_device_ids=true | all-gather | bytes 4608 | tf_op jit(solution)/shard_map/all_gather | solution.py:190
  51.0 0.1 copy.36
  51.1 2.5 %select_reduce_fusion.1 = s32[8,128]{0,1:T(8,128)S(1)} fusion(s32[8,128]{0,1:T(8,128)S(1)} %copy.36), kind=kOutput, calls=%fused_computation.38 | output fusion | flops 1096704 | bytes 8192 | tf_op jit(solution)/shard_map/jit(cumsum)/reduce_window_sum | solution.py:194
  53.7 0.6 gather_fusion
  54.5 0.2 slice_reduce_fusion.2
  54.7 0.2 select_reduce_fusion
  55.1 0.5 fusion.34
  55.6 0.5 fusion.33
  56.2 0.3 fusion.19
  56.4 40.9 %all-gather.3.cloned.1.call-done = bf16[1024,2,1024]{0,2,1:T(8,128)(2,1)} async-done(((bf16[128,2,1024]{0,2,1:T(8,128)(2,1)}), bf16[1024,2,1024]{0,2,1:T(8,128)(2,1)}) %all-gather.3.cloned.1.call-update) | async-done | bytes 4194320 | tf_op jit(solution)/shard_map/all_gather | solution.py:191
  97.3 2.7 %fusion.61 = (bf16[1024,1,1024]{0,2,1:T(8,128)(2,1)S(1)}, bf16[1024,1,1024]{0,2,1:T(8,128)(2,1)S(1)}) fusion(bf16[1024,2,1024]{0,2,1:T(8,128)(2,1)} %all-gather.3.cloned.1.call-done), kind=kLoop, calls=%fused_computation.118 | loop fusion | bytes 8388608 | tf_op jit(solution)/shard_map/slice | solution.py:217
  100.0 0.7 fusion.37
  100.7 2.2 %multiply_reduce_fusion = (f32[8,128]{1,0:T(8,128)S(1)}, f32[8,128,1024]{2,1,0:T(8,128)S(1)}) fusion(f32[128,1024]{1,0:T(8,128)S(1)} %fusion.33, f32[8,128,1024]{2,1,0:T(8,128)S(1)} %fusion.37, pred[128,1024]{1,0:T(8,128)(4,1)S(1)} %fusion.34), kind=kOutput, calls=%fused_computation.2 | output fusion | flops 7341055 | bytes 9048064 | tf_op jit(solution)/shard_map/sub | solution.py:246
  102.9 0.8 fusion.5
  103.7 1.1 fusion.24
  104.9 0.2 slice-done
  105.1 1.5 %slice-done.1 = s8[4194304]{0:T(1024)(128)(4,1)S(1)} async-done(((s8[8388608]{0:T(1024)(128)(4,1)}), s8[4194304]{0:T(1024)(128)(4,1)S(1)}, s32[]{:S(2)}) %slice-start.1) | async-done | bytes 4194328
  106.6 1.3 %fusion.62 = f32[128,4096]{1,0:T(8,128)S(1)} fusion(bf16[128,1024]{0,1:T(8,128)(2,1)S(1)} %bitcast.80, bf16[1024,4096]{1,0:T(8,128)(2,1)S(1)} %bitcast.73), kind=kOutput, calls=%fused_computation.119 | convolution fusion | flops 1073741824 | bytes 10747904 | tf_op jit(solution)/shard_map/dot_general | solution.py:259
  108.1 1.9 %collective-permute-done = bf16[2,32,4096]{2,1,0:T(8,128)(2,1)S(1)} collective-permute-done((bf16[2,32,4096]{2,1,0:T(8,128)(2,1)S(1)}, bf16[2,32,4096]{2,1,0:T(8,128)(2,1)S(1)}, u32[]{:S(2)}, u32[]{:S(2)}) %collective-permute-start) | collective-permute-done | bytes 524320 | tf_op jit(solution)/shard_map/ppermute | solution.py:278
  109.9 0.1 fusion.20
  110.1 1.5 %collective-permute-start.1 = (bf16[1,32,4096]{2,1,0:T(8,128)(2,1)S(1)}, bf16[1,32,4096]{2,1,0:T(8,128)(2,1)S(1)}, u32[]{:S(2)}, u32[]{:S(2)}) collective-permute-start(bf16[1,32,4096]{2,1,0:T(8,128)(2,1)S(1)} %fusion.35), channel_id=1, source_target_pairs={{0,2},{1,3},{2,0},{3,1},{4,6},{5,7},{6,4},{7,5},{8,10},{9,11},{10,... | collective-permute-start | bytes 786440 | tf_op jit(solution)/shard_map/ppermute | solution.py:278
  111.7 6.9 %collective-permute-done.1 = bf16[1,32,4096]{2,1,0:T(8,128)(2,1)S(1)} collective-permute-done((bf16[1,32,4096]{2,1,0:T(8,128)(2,1)S(1)}, bf16[1,32,4096]{2,1,0:T(8,128)(2,1)S(1)}, u32[]{:S(2)}, u32[]{:S(2)}) %collective-permute-start.1) | collective-permute-done | bytes 262176 | tf_op jit(solution)/shard_map/ppermute | solution.py:278
  118.6 0.8 fusion.36
  (30 shorter events, 0.8 us)
Async XLA Ops:
  6.5 13.6 %copy-start.1 = (s32[128]{0:T(128)S(1)}, s32[128]{0:T(128)}, u32[]{:S(2)}) copy-start(s32[128]{0:T(128)} %param.7) | copy-start | bytes 1540
  6.5 13.3 %copy-start.2 = (s32[4]{0:T(128)S(1)}, s32[4]{0:T(128)}, u32[]{:S(2)}) copy-start(s32[4]{0:T(128)} %param.8) | copy-start | bytes 52
  6.5 13.5 %copy-start = (s32[8,3]{0,1:T(4,128)S(1)}, s32[8,3]{0,1:T(4,128)}, u32[]{:S(2)}) copy-start(s32[8,3]{0,1:T(4,128)} %param.9) | copy-start | bytes 292
  6.5 48.4 %copy-start.3 = (s32[8]{0:T(128)S(1)}, s32[8]{0:T(128)}, u32[]{:S(2)}) copy-start(s32[8]{0:T(128)} %param.10) | copy-start | bytes 100
  6.5 90.8 %all-gather.3.cloned.1.call-start = ((), (), s32[]{:S(2)}) async-start(), calls=%async_computation.1 | async-start | bytes 4718592 | tf_op jit(solution)/shard_map/all_gather | solution.py:191
  12.5 43.6 %all-to-all-start = ((bf16[8,32,1024]{2,1,0:T(8,128)(2,1)}), bf16[8,32,1024]{2,1,0:T(8,128)(2,1)S(1)}, u32[]{:S(2)}, u32[]{:S(2)}) async-start(bf16[8,32,1024]{2,1,0:T(8,128)(2,1)} %bitcast.9), calls=%async_computation | async-start | bytes 1048576 | tf_op jit(solution)/shard_map/all_to_all | solution.py:204
  102.9 2.2 %slice-start = ((s8[8388608]{0:T(1024)(128)(4,1)}), s8[4194304]{0:T(1024)(128)(4,1)S(1)}, s32[]{:S(2)}) async-start(s8[8388608]{0:T(1024)(128)(4,1)} %bitcast.72), calls=%async_computation.2 | async-start | bytes 8388608
  103.7 2.9 %slice-start.1 = ((s8[8388608]{0:T(1024)(128)(4,1)}), s8[4194304]{0:T(1024)(128)(4,1)S(1)}, s32[]{:S(2)}) async-start(s8[8388608]{0:T(1024)(128)(4,1)} %bitcast.72), calls=%async_computation.3 | async-start | bytes 8388608
  108.0 2.0 %collective-permute-start = (bf16[2,32,4096]{2,1,0:T(8,128)(2,1)S(1)}, bf16[2,32,4096]{2,1,0:T(8,128)(2,1)S(1)}, u32[]{:S(2)}, u32[]{:S(2)}) collective-permute-start(bf16[2,32,4096]{2,1,0:T(8,128)(2,1)S(1)} %fusion.31), channel_id=1, source_target_pairs={{0,1},{1,0},{2,3},{3,2},{4,5},{5,4},{6,7},{7,6},{8,9},{9,8},{10,11... | collective-permute-start | bytes 1572872 | tf_op jit(solution)/shard_map/ppermute | solution.py:278
  110.1 8.4 %collective-permute-start.1 = (bf16[1,32,4096]{2,1,0:T(8,128)(2,1)S(1)}, bf16[1,32,4096]{2,1,0:T(8,128)(2,1)S(1)}, u32[]{:S(2)}, u32[]{:S(2)}) collective-permute-start(bf16[1,32,4096]{2,1,0:T(8,128)(2,1)S(1)} %fusion.35), channel_id=1, source_target_pairs={{0,2},{1,3},{2,0},{3,1},{4,6},{5,7},{6,4},{7,5},{8,10},{9,11},{10,... | collective-permute-start | bytes 786440 | tf_op jit(solution)/shard_map/ppermute | solution.py:278
Sparse Core Ops, SparseCore 0:
  9.4 87.8 all-gather.2

commit v7 on v5

--- a/solution.py
+++ b/solution.py
@@ -202,61 +202,96 @@
     outgoing = jnp.dot(send_pick, projected[:, 0, :], preferred_element_type=jnp.float32)
     outgoing = outgoing.astype(projected.dtype).reshape(owners, capacity, columns)
     incoming = lax.all_to_all(outgoing, "seq", split_axis=0, concat_axis=0, tiled=True)
-    my_pos = own_index * tok_dev + jnp.arange(tok_dev, dtype=jnp.int32)
     source = jnp.arange(tokens, dtype=jnp.int32) // tok_dev
-    land_col = (source * capacity + slot_all.reshape(-1))[None, :]
-    hit = arrival_dest[None, :] == my_pos[:, None]
-    col_of_pos = jnp.sum(jnp.where(hit, land_col, 0), axis=1)
-    land_pick = (
-        col_of_pos[:, None] == jnp.arange(owners * capacity, dtype=jnp.int32)[None, :]
-    ).astype(projected.dtype)
-    queries = jnp.dot(
-        land_pick, incoming.reshape(owners * capacity, columns), preferred_element_type=jnp.float32
-    )
-    queries = queries.astype(projected.dtype).reshape(tok_dev, heads_here, HD)
+    land_col = source * capacity + slot_all.reshape(-1)
+    flat_in = incoming.reshape(owners * capacity, columns)
     keys = keyval[:, 0, :].reshape(tokens, heads_here, HD)
     values = keyval[:, 1, :].reshape(tokens, heads_here, HD)
-    scores = (
-        jnp.einsum("qhd,khd->hqk", queries, keys, preferred_element_type=jnp.float32)
-        * score_scale
-    )
     bounds = jnp.cumsum(doc_lengths)
     key_block = arrival_dest // BLK
     key_doc = segment_of(arrival_dest, bounds)
-    query_block = my_pos // BLK
-    query_doc = segment_of(my_pos, bounds)
-    same_doc = query_doc[:, None] == key_doc[None, :]
-    window = jnp.zeros((tok_dev, tokens), jnp.int32)
-    for step in (-1, 0, 1):
-        near = (query_block + step) % blocks_all
-        window = window + (key_block[None, :] == near[:, None]).astype(jnp.int32)
-    window = jnp.where(same_doc, window, 0)
-    chosen = random_blocks[query_block]
-    drawn = jnp.zeros((tok_dev, tokens), jnp.int32)
-    for r in range(chosen.shape[1]):
-        drawn = drawn + (key_block[None, :] == chosen[:, r][:, None]).astype(jnp.int32)
     glob_start = global_owner[0] * tok_dev
     in_glob = (arrival_dest >= glob_start) & (arrival_dest < glob_start + tok_dev)
     holds_glob = own_index == global_owner[0]
-    count = window + drawn + in_glob[None, :].astype(jnp.int32)
-    count = jnp.where(holds_glob, 1, count)
-    live = count > 0
-    near_scores = jnp.where(live[None], scores, big_negative)
-    row_peak = jnp.max(near_scores, axis=2)
-    near_exp = jnp.exp(near_scores - row_peak[..., None])
-    count_f = count.astype(jnp.float32)[None]
-    denominator = jnp.sum(near_exp * count_f, axis=2)
-    rounded = jnp.where(holds_glob, near_exp, near_exp.astype(jnp.bfloat16).astype(jnp.float32))
-    weighted = rounded * count_f
-    weight_hi = weighted.astype(jnp.bfloat16)
-    weight_lo = (weighted - weight_hi.astype(jnp.float32)).astype(jnp.bfloat16)
-    mixed_sum = jnp.einsum("hqk,khd->qhd", weight_hi, values, preferred_element_type=jnp.float32)
-    mixed_sum = mixed_sum + jnp.einsum(
-        "hqk,khd->qhd", weight_lo, values, preferred_element_type=jnp.float32
-    )
-    attn_rows = (mixed_sum / jnp.transpose(denominator)[..., None]).reshape(tok_dev, columns)
-    attn_rows = attn_rows.astype(jnp.bfloat16)
-    return head_sum(jnp.dot(attn_rows, out_weight, preferred_element_type=jnp.float32))
+
+    def attend(local_rows):
+        rows = local_rows.shape[0]
+        my_pos = own_index * tok_dev + local_rows
+        hit = arrival_dest[None, :] == my_pos[:, None]
+        col_of_pos = jnp.sum(jnp.where(hit, land_col[None, :], 0), axis=1)
+        land_pick = (
+            col_of_pos[:, None] == jnp.arange(owners * capacity, dtype=jnp.int32)[None, :]
+        ).astype(projected.dtype)
+        queries = jnp.dot(land_pick, flat_in, preferred_element_type=jnp.float32)
+        queries = queries.astype(projected.dtype).reshape(rows, heads_here, HD)
+        scores = (
+            jnp.einsum("qhd,khd->hqk", queries, keys, preferred_element_type=jnp.float32)
+            * score_scale
+        )
+        query_block = my_pos // BLK
+        query_doc = segment_of(my_pos, bounds)
+        same_doc = query_doc[:, None] == key_doc[None, :]
+        window = jnp.zeros((rows, tokens), jnp.int32)
+        for step in (-1, 0, 1):
+            near = (query_block + step) % blocks_all
+            window = window + (key_block[None, :] == near[:, None]).astype(jnp.int32)
+        window = jnp.where(same_doc, window, 0)
+        chosen = random_blocks[query_block]
+        drawn = jnp.zeros((rows, tokens), jnp.int32)
+        for r in range(chosen.shape[1]):
+            drawn = drawn + (key_block[None, :] == chosen[:, r][:, None]).astype(jnp.int32)
+        count = window + drawn + in_glob[None, :].astype(jnp.int32)
+        count = jnp.where(holds_glob, 1, count)
+        live = count > 0
+        near_scores = jnp.where(live[None], scores, big_negative)
+        row_peak = jnp.max(near_scores, axis=2)
+        near_exp = jnp.exp(near_scores - row_peak[..., None])
+        count_f = count.astype(jnp.float32)[None]
+        denominator = jnp.sum(near_exp * count_f, axis=2)
+        rounded = jnp.where(
+            holds_glob, near_exp, near_exp.astype(jnp.bfloat16).astype(jnp.float32)
+        )
+        weighted = rounded * count_f
+        weight_hi = weighted.astype(jnp.bfloat16)
+        weight_lo = (weighted - weight_hi.astype(jnp.float32)).astype(jnp.bfloat16)
+        mixed_sum = jnp.einsum(
+            "hqk,khd->qhd", weight_hi, values, preferred_element_type=jnp.float32
+        )
+        mixed_sum = mixed_sum + jnp.einsum(
+            "hqk,khd->qhd", weight_lo, values, preferred_element_type=jnp.float32
+        )
+        attn_rows = (mixed_sum / jnp.transpose(denominator)[..., None]).reshape(rows, columns)
+        return attn_rows.astype(jnp.bfloat16)
+
+    def project(local_rows):
+        out = jnp.dot(attend(local_rows), out_weight, preferred_element_type=jnp.float32)
+        return lax.optimization_barrier(out)
+
+    members = lax.axis_size("head")
+    if members & (members - 1):
+        return head_sum(project(jnp.arange(tok_dev, dtype=jnp.int32)))
+    me = lax.axis_index("head")
+    rows_per = tok_dev // members
+    stages = members.bit_length() - 1
+    received = []
+    for stage in range(stages + 1):
+        if stage < stages:
+            ahead = jnp.arange(members >> (stage + 1), dtype=jnp.int32)
+            flip = ((me >> stage) & 1) ^ 1
+            blocks = (ahead << (stage + 1)) | (flip << stage) | (me & ((1 << stage) - 1))
+        else:
+            blocks = jnp.reshape(me, (1,)).astype(jnp.int32)
+        local_rows = (
+            blocks[:, None] * rows_per + jnp.arange(rows_per, dtype=jnp.int32)[None, :]
+        ).reshape(-1)
+        part = project(local_rows).reshape(blocks.shape[0], rows_per, -1)
+        for done, got in received:
+            part = part + jnp.take(got, blocks >> (done + 1), axis=0)
+        if stage == stages:
+            return part.reshape(rows_per, -1).astype(jnp.bfloat16)
+        pairs = [(i, i ^ (1 << stage)) for i in range(members)]
+        got = lax.ppermute(part.astype(jnp.bfloat16), "head", pairs)
+        received.append((stage, got.astype(jnp.float32)))
 
 
 def head_sum(partial):

time: 128 us -> 156 us (1.22)
  matrix products: 9.57 us -> 40.3 us
  waiting for transfers between devices: 49.7 us -> 43.5 us
  local copies, waits for them, and re-layouts: 6.14 us -> 10.8 us
  blocking collectives: 30.8 us -> 28 us
    dot_general x5 -> x15, matrix products: 7.52 us -> 38.2 us  [the longest x3 15.6 us: project(): jnp.dot(attend(local_rows), out_weight, preferred_element_type=jnp.float32)]
    ppermute x2, waiting for transfers between devices: 8.75 us -> 2.32 us  [gathered_plan(): got = lax.ppermute(part.astype(jnp.bfloat16), 'head', pairs)]
    all_gather x1, blocking collectives: 30.8 us -> 28 us  [gathered_plan(): arrival_dest = lax.all_gather(destination, 'seq', tiled=True)]
    unnamed x10 -> x18, local copies, waits for them, and re-layouts: 1.1 us -> 3.07 us
  transfers between devices with their start and end apart: 4 -> 4, of which waited for: 3 -> 2; matrix products, arithmetic and copies ran while one was open for 7% -> 15% of each run, Pallas kernels for 0% -> 0%
where the time goes in v7:
time: 156 us; the launch traced here: 155 us
  waiting for transfers between devices  43.5 us (28%)
  matrix products  40.3 us (26%)
  blocking collectives  28 us (18%)
  between operations  13.8 us (9%)
  local copies, waits for them, and re-layouts  10.8 us (7%)
  other arithmetic  9.85 us (6%)
  starting transfers between devices  8.83 us (6%)
    all_gather x1, waiting for transfers between devices, gathered_plan(): keyval = lax.all_gather(projected[:, 1:, :], 'seq', tiled=True)  41.2 us
    all_gather x1, blocking collectives, gathered_plan(): arrival_dest = lax.all_gather(destination, 'seq', tiled=True)  28 us
    dot_general x3, matrix products, project(): jnp.dot(attend(local_rows), out_weight, preferred_element_type=jnp.float32)  15.6 us
    dot_general x3, matrix products, attend(): jnp.einsum('hqk,khd->qhd', weight_hi, values, preferred_element_type=jnp....  9.68 us
    dot_general x3, matrix products, attend(): jnp.einsum('hqk,khd->qhd', weight_lo, values, preferred_element_type=jnp....  9.57 us
    all_to_all x1, starting transfers between devices, gathered_plan(): lax.all_to_all(outgoing, 'seq', split_axis=0, concat_axis=0, tiled=True)  7.28 us
    slice x1, local copies, waits for them, and re-layouts, gathered_plan(): keys = keyval[:, 0, :].reshape(tokens, heads_here, HD)  3.99 us
  transfers between devices with their start and end apart: 4, of which 2 were waited for; matrix products, arithmetic and copies ran while one was open for 15% of the time, Pallas kernels for 0%

profile of v7, /device:TPU:0, one launch (start us, length us, event | category | flops | bytes accessed | tf_op | source)
XLA Modules:
  0.0 155.1 jit_solution(4165521080941532681)
XLA Ops:
  6.5 1.1 slice.48
  7.7 1.0 copy.105
  9.2 2.1 %convolution_convert_fusion = bf16[256,1024]{1,0:T(8,128)(2,1)} fusion(bf16[128,3,1024]{2,0,1:T(8,128)(2,1)} %param.8, s32[128]{0:T(128)S(1)} %multiply_add_fusion), kind=kOutput, calls=%fused_computation.22 | convolution fusion | flops 67403776 | bytes 786944 | tf_op jit(solution)/shard_map/dot_general | solution.py:202
  11.2 7.3 %all-to-all-start = ((bf16[8,32,1024]{2,1,0:T(8,128)(2,1)}), bf16[8,32,1024]{2,1,0:T(8,128)(2,1)S(1)}, u32[]{:S(2)}, u32[]{:S(2)}) async-start(bf16[8,32,1024]{2,1,0:T(8,128)(2,1)} %bitcast.9), calls=%async_computation | async-start | bytes 1048576 | tf_op jit(solution)/shard_map/all_to_all | solution.py:204
  19.1 0.6 gather_fusion
  19.7 0.6 gather_fusion.2
  20.3 28.0 %all-gather = s32[8,1,128]{2,1,0:T(1,128)S(1)} all-gather(s32[1,1,128]{2,1,0:T(1,128)S(1)} %bitcast.144), channel_id=1, replica_groups=mesh['seq'=8,'head'=4] {'seq'}, dimensions={0}, use_global_device_ids=true | all-gather | bytes 4608 | tf_op jit(solution)/shard_map/all_gather | solution.py:190
  48.4 2.5 %select_reduce_fusion = s32[8,128]{0,1:T(8,128)S(1)} fusion(s32[8,128]{0,1:T(8,128)S(1)} %copy.76), kind=kOutput, calls=%fused_computation.74 | output fusion | flops 1096704 | bytes 8192 | tf_op jit(solution)/shard_map/jit(cumsum)/reduce_window_sum | solution.py:194
  51.0 0.6 gather_fusion.1
  53.1 0.9 fusion.73
  55.6 41.2 %all-gather.3.cloned.1.call-done = bf16[1024,2,1024]{0,2,1:T(8,128)(2,1)} async-done(((bf16[128,2,1024]{0,2,1:T(8,128)(2,1)}), bf16[1024,2,1024]{0,2,1:T(8,128)(2,1)}) %all-gather.3.cloned.1.call-update) | async-done | bytes 4194320 | tf_op jit(solution)/shard_map/all_gather | solution.py:191
  96.7 4.0 %fusion.136 = (bf16[1024,1,1024]{0,2,1:T(8,128)(2,1)S(1)}, bf16[1024,1,1024]{0,2,1:T(8,128)(2,1)}) fusion(bf16[1024,2,1024]{0,2,1:T(8,128)(2,1)} %all-gather.3.cloned.1.call-done), kind=kLoop, calls=%fused_computation.250 | loop fusion | bytes 8388608 | tf_op jit(solution)/shard_map/slice | solution.py:208
  100.7 0.4 fusion.8
  101.2 1.0 copy-done.1
  102.2 0.3 multiply_reduce_fusion.1
  102.5 3.1 %fusion.55 = f32[8,32,128]{2,1,0:T(8,128)S(1)} fusion(bf16[1024,8,128]{0,2,1:T(8,128)(2,1)} %bitcast.129, f32[32,1024]{1,0:T(8,128)S(1)} %get-tuple-element.43, pred[]{:T(512)S(6)} %eq.533, f32[8,32,1024]{2,1,0:T(8,128)} %copy-done.1), kind=kOutput, calls=%fused_computation.64 | convolution fusion | flops 68683008 | bytes 3407873 | tf_op jit(solution)/shard_map/hqk,khd->qhd/dot_general | solution.py:257
  105.6 1.8 %fusion.77 = f32[8,64,1024]{2,1,0:T(8,128)} fusion(bf16[1024,8,128]{0,2,1:T(8,128)(2,1)S(1)} %bitcast.124, bf16[8,8,8,128]{3,2,1,0:T(8,128)(2,1)S(1)} %fusion.25), kind=kOutput, calls=%fused_computation.91 | convolution fusion | flops 134217728 | bytes 4325376 | tf_op jit(solution)/shard_map/qhd,khd->hqk/dot_general | solution.py:228
  107.4 4.0 %fusion.39 = f32[8,64,128]{2,1,0:T(8,128)} fusion(bf16[1024,8,128]{0,2,1:T(8,128)(2,1)} %bitcast.130, f32[64,1024]{1,0:T(8,128)S(1)} %fusion.72, pred[]{:T(512)S(6)} %eq.533, f32[8,64,1024]{2,1,0:T(8,128)} %fusion.77, pred[64,1024]{1,0:T(8,128)(4,1)S(1)} %copy-done.3), kind=kOutput, calls=%fused_computation.44 | convolution fusion | flops 139986432 | bytes 4784129 | tf_op jit(solution)/shard_map/hqk,khd->qhd/dot_general | solution.py:260
  111.4 2.4 %multiply_reduce_fusion = f32[8,64]{1,0:T(8,128)S(1)} fusion(f32[64,1024]{1,0:T(8,128)S(1)} %fusion.72, f32[8,64,1024]{2,1,0:T(8,128)} %fusion.77, pred[64,1024]{1,0:T(8,128)(4,1)S(1)} %copy-done.3), kind=kOutput, calls=%fused_computation.6 | output fusion | flops 2622463 | bytes 2426880 | tf_op jit(solution)/shard_map/sub | solution.py:248
  113.8 3.1 %fusion.35 = bf16[8,4,8,128]{3,2,1,0:T(8,128)(2,1)S(1)} fusion(f32[8,32,128]{2,1,0:T(8,128)S(1)} %fusion.55, bf16[1024,8,128]{0,2,1:T(8,128)(2,1)} %bitcast.131, f32[32,1024]{1,0:T(8,128)S(1)} %get-tuple-element.43, pred[]{:T(512)S(6)} %eq.533, f32[8,32,1024]{2,1,0:T(8,128)} %copy-done.1, f32[32,8]{0,1:T(8,128)S(1)} %bitcast.149), kind=kOutput, calls=%fused_computation.40 | convolution fusion | flops 69567744 | bytes 3474433 | tf_op jit(solution)/shard_map/hqk,khd->qhd/dot_general | solution.py:260
  117.0 4.9 %fusion.84 = f32[32,4096]{1,0:T(8,128)S(1)} fusion(bf16[1024,4096]{1,0:T(8,128)(2,1)} %param.13, bf16[8,4,8,128]{3,2,1,0:T(8,128)(2,1)S(1)} %fusion.35), kind=kOutput, calls=%fused_computation.103 | convolution fusion | flops 268435456 | bytes 8978432 | tf_op jit(solution)/shard_map/dot_general | solution.py:267
  121.9 3.3 %fusion.30 = bf16[8,8,8,128]{3,2,1,0:T(8,128)(2,1)S(1)} fusion(f32[8,64,128]{2,1,0:T(8,128)} %fusion.39, bf16[1024,8,128]{0,2,1:T(8,128)(2,1)} %bitcast.132, f32[64,1024]{1,0:T(8,128)S(1)} %fusion.72, pred[]{:T(512)S(6)} %eq.533, f32[8,64,1024]{2,1,0:T(8,128)} %fusion.77, pred[64,1024]{1,0:T(8,128)(4,1)S(1)} %copy-done.3, f32[64,8]{0,1:T(8,128)S(1)} %bitcast.148), kind=kOutput, calls=%fused_computation.35 | convolution fusion | flops 138610176 | bytes 4917249 | tf_op jit(solution)/shard_map/hqk,khd->qhd/dot_general | solution.py:257
  125.2 5.8 %fusion.74 = bf16[64,4096]{1,0:T(8,128)(2,1)} fusion(bf16[1024,4096]{1,0:T(8,128)(2,1)} %param.13, bf16[8,8,8,128]{3,2,1,0:T(8,128)(2,1)S(1)} %fusion.30), kind=kOutput, calls=%fused_computation.88 | convolution fusion | flops 536870912 | bytes 9043968 | tf_op jit(solution)/shard_map/dot_general | solution.py:267
  131.0 0.4 fusion.9
  131.5 1.0 copy-done.2
  132.4 0.3 multiply_reduce_fusion.2
  132.8 3.3 %fusion.52 = f32[8,32,128]{2,1,0:T(8,128)S(1)} fusion(bf16[1024,8,128]{0,2,1:T(8,128)(2,1)} %bitcast.133, f32[32,1024]{1,0:T(8,128)S(1)} %get-tuple-element.42, pred[]{:T(512)S(6)} %eq.533, f32[8,32,1024]{2,1,0:T(8,128)} %copy-done.2), kind=kOutput, calls=%fused_computation.62 | convolution fusion | flops 68683008 | bytes 3407873 | tf_op jit(solution)/shard_map/hqk,khd->qhd/dot_general | solution.py:257
  136.1 2.4 %fusion.36 = bf16[8,4,8,128]{3,2,1,0:T(8,128)(2,1)S(1)} fusion(f32[8,32,128]{2,1,0:T(8,128)S(1)} %fusion.52, bf16[1024,8,128]{0,2,1:T(8,128)(2,1)S(1)} %bitcast.134, f32[32,1024]{1,0:T(8,128)S(1)} %get-tuple-element.42, pred[]{:T(512)S(6)} %eq.533, f32[8,32,1024]{2,1,0:T(8,128)} %copy-done.2, f32[32,8]{0,1:T(8,128)S(1)} %bitcast.150), kind=kOutput, calls=%fused_computation.41 | convolution fusion | flops 69567744 | bytes 3474433 | tf_op jit(solution)/shard_map/hqk,khd->qhd/dot_general | solution.py:260
  138.7 1.5 collective-permute-start.1
  140.2 4.9 %fusion.87 = f32[32,4096]{1,0:T(8,128)S(1)} fusion(bf16[1024,4096]{1,0:T(8,128)(2,1)} %param.13, bf16[8,4,8,128]{3,2,1,0:T(8,128)(2,1)S(1)} %fusion.36), kind=kOutput, calls=%fused_computation.106 | convolution fusion | flops 268435456 | bytes 8978432 | tf_op jit(solution)/shard_map/dot_general | solution.py:267
  145.1 2.3 %collective-permute-done.1 = bf16[1,32,4096]{2,1,0:T(8,128)(2,1)S(1)} collective-permute-done((bf16[1,32,4096]{2,1,0:T(8,128)(2,1)S(1)}, bf16[1,32,4096]{2,1,0:T(8,128)(2,1)S(1)}, u32[]{:S(2)}, u32[]{:S(2)}) %collective-permute-start.1) | collective-permute-done | bytes 262176 | tf_op jit(solution)/shard_map/ppermute | solution.py:293
  147.5 0.8 fusion.68
  (62 shorter events, 4.2 us)
Async XLA Ops:
  6.5 2.2 %copy-start.5 = (s32[128]{0:T(128)S(1)}, s32[128]{0:T(128)}, u32[]{:S(2)}) copy-start(s32[128]{0:T(128)} %param.9) | copy-start | bytes 1540
  6.5 90.2 %all-gather.3.cloned.1.call-start = ((), (), s32[]{:S(2)}) async-start(), calls=%async_computation.1 | async-start | bytes 4718592 | tf_op jit(solution)/shard_map/all_gather | solution.py:191
  7.6 11.1 %copy-start.7 = (s32[8]{0:T(128)S(1)}, s32[8]{0:T(128)}, u32[]{:S(2)}) copy-start(s32[8]{0:T(128)} %param.12) | copy-start | bytes 100
  7.6 11.2 %copy-start.6 = (s32[4]{0:T(128)S(1)}, s32[4]{0:T(128)}, u32[]{:S(2)}) copy-start(s32[4]{0:T(128)} %param.10) | copy-start | bytes 52
  7.7 11.3 %copy-start.4 = (s32[8,3]{0,1:T(4,128)S(1)}, s32[8,3]{0,1:T(4,128)}, u32[]{:S(2)}) copy-start(s32[8,3]{0,1:T(4,128)} %param.11) | copy-start | bytes 292
  11.2 43.6 %all-to-all-start = ((bf16[8,32,1024]{2,1,0:T(8,128)(2,1)}), bf16[8,32,1024]{2,1,0:T(8,128)(2,1)S(1)}, u32[]{:S(2)}, u32[]{:S(2)}) async-start(bf16[8,32,1024]{2,1,0:T(8,128)(2,1)} %bitcast.9), calls=%async_computation | async-start | bytes 1048576 | tf_op jit(solution)/shard_map/all_to_all | solution.py:204
  101.2 1.0 copy-start.1
  105.6 1.8 %copy-start.3 = (pred[64,1024]{1,0:T(8,128)(4,1)S(1)}, pred[64,1024]{1,0:T(8,128)(4,1)}, u32[]{:S(2)}) copy-start(pred[64,1024]{1,0:T(8,128)(4,1)} %fusion.73) | copy-start | bytes 196612
  131.0 7.5 %collective-permute-start = (bf16[2,32,4096]{2,1,0:T(8,128)(2,1)}, bf16[2,32,4096]{2,1,0:T(8,128)(2,1)S(1)}, u32[]{:S(2)}, u32[]{:S(2)}) collective-permute-start(bf16[2,32,4096]{2,1,0:T(8,128)(2,1)} %bitcast.21), channel_id=1, source_target_pairs={{0,1},{1,0},{2,3},{3,2},{4,5},{5,4},{6,7},{7,6},{8,9},{9,8},{10,11... | collective-permute-start | bytes 1572872 | tf_op jit(solution)/shard_map/ppermute | solution.py:293
  131.5 1.0 copy-start.2
  132.4 3.6 %copy-start = (bf16[1024,1,1024]{0,2,1:T(8,128)(2,1)S(1)}, bf16[1024,1,1024]{0,2,1:T(8,128)(2,1)}, u32[]{:S(2)}) copy-start(bf16[1024,1,1024]{0,2,1:T(8,128)(2,1)} %get-tuple-element.39) | copy-start | bytes 6291460
  138.7 8.8 %collective-permute-start.1 = (bf16[1,32,4096]{2,1,0:T(8,128)(2,1)S(1)}, bf16[1,32,4096]{2,1,0:T(8,128)(2,1)S(1)}, u32[]{:S(2)}, u32[]{:S(2)}) collective-permute-start(bf16[1,32,4096]{2,1,0:T(8,128)(2,1)S(1)} %fusion.57), channel_id=1, source_target_pairs={{0,2},{1,3},{2,0},{3,1},{4,6},{5,7},{6,4},{7,5},{8,10},{9,11},{10,... | collective-permute-start | bytes 786440 | tf_op jit(solution)/shard_map/ppermute | solution.py:293
Sparse Core Ops, SparseCore 0:
  9.4 87.2 all-gather.2

commit v8 on v6

--- a/solution.py
+++ b/solution.py
@@ -3,6 +3,7 @@
 import jax
 import jax.numpy as jnp
 from jax import lax
+from jax.experimental.layout import Layout, with_layout_constraint
 from jax.sharding import PartitionSpec as P
 
 HD = 128
@@ -189,6 +190,7 @@
     capacity = 2 * (tok_dev // owners)
     arrival_dest = lax.all_gather(destination, "seq", tiled=True)
     keyval = lax.all_gather(projected[:, 1:, :], "seq", tiled=True)
+    keyval = with_layout_constraint(keyval, Layout((1, 0, 2)))
     target_all = arrival_dest.reshape(owners, tok_dev) // tok_dev
     onehot = (target_all[:, :, None] == jnp.arange(owners, dtype=jnp.int32)).astype(jnp.int32)
     slot_all = jnp.sum((jnp.cumsum(onehot, axis=1) - onehot) * onehot, axis=2)

time: 126 us -> 132 us (1.048)
  local copies, waits for them, and re-layouts: 7.56 us -> 15.8 us
  waiting for transfers between devices: 49.7 us -> 48.1 us
    unnamed x14 -> x9, local copies, waits for them, and re-layouts: 2.81 us -> 10.1 us
    another operation x0 -> x1, local copies, waits for them, and re-layouts: none -> 2.85 us  [gathered_plan(): values = keyval[:, 1, :].reshape(tokens, heads_here, HD)]
    slice x1 -> x0, local copies, waits for them, and re-layouts: 2.66 us -> none  [gathered_plan(): keys = keyval[:, 0, :].reshape(tokens, heads_here, HD)]
    all_gather x1, waiting for transfers between devices: 40.9 us -> 39.3 us  [gathered_plan(): keyval = lax.all_gather(projected[:, 1:, :], 'seq', tiled=True)]
  transfers between devices with their start and end apart: 4 -> 4, of which waited for: 3 -> 3; matrix products, arithmetic and copies ran while one was open for 7% -> 8% of each run, Pallas kernels for 0% -> 0%
where the time goes in v8:
time: 132 us
  waiting for transfers between devices  48.1 us (36%)
  blocking collectives  29.6 us (22%)
  local copies, waits for them, and re-layouts  15.8 us (12%)
  between operations  13.7 us (10%)
  other arithmetic  9.85 us (7%)
  starting transfers between devices  8.84 us (7%)
  matrix products  5.95 us (5%)
    all_gather x1, waiting for transfers between devices, gathered_plan(): keyval = lax.all_gather(projected[:, 1:, :], 'seq', tiled=True)  39.3 us
    all_gather x1, blocking collectives, gathered_plan(): arrival_dest = lax.all_gather(destination, 'seq', tiled=True)  29.6 us
    unnamed x9, local copies, waits for them, and re-layouts  10.1 us
    ppermute x2, waiting for transfers between devices, head_sum(): got = lax.ppermute(send, 'head', [(i, i ^ bit) for i in range(members)])  8.81 us
    all_to_all x1, starting transfers between devices, gathered_plan(): lax.all_to_all(outgoing, 'seq', split_axis=0, concat_axis=0, tiled=True)  7.28 us
    another operation x1, local copies, waits for them, and re-layouts, gathered_plan(): values = keyval[:, 1, :].reshape(tokens, heads_here, HD)  2.85 us
  transfers between devices with their start and end apart: 4, of which 3 were waited for; matrix products, arithmetic and copies ran while one was open for 8% of the time, Pallas kernels for 0%

profile of v8, /device:TPU:0, one launch (start us, length us, event | category | flops | bytes accessed | tf_op | source)
XLA Modules:
  0.0 131.8 jit_solution(1160835930883300082)
XLA Ops:
  6.5 1.9 %slice.46 = bf16[128,2,1024]{2,0,1:T(8,128)(2,1)} slice(bf16[128,3,1024]{2,0,1:T(8,128)(2,1)} %param.6), slice={[0:128], [1:3], [0:1024]} | slice | bytes 1048576 | tf_op jit(solution)/shard_map/slice | solution.py:192
  8.4 0.7 and_select_fusion
  9.2 0.2 reduce_window_sum.30
  9.4 0.2 select_reduce_fusion.2
  9.5 0.7 multiply_add_fusion
  10.2 2.1 %convolution_convert_fusion = bf16[256,1024]{1,0:T(8,128)(2,1)} fusion(bf16[128,3,1024]{2,0,1:T(8,128)(2,1)} %param.6, s32[128]{0:T(128)S(1)} %multiply_add_fusion), kind=kOutput, calls=%fused_computation.21 | convolution fusion | flops 67403776 | bytes 786944 | tf_op jit(solution)/shard_map/dot_general | solution.py:204
  12.3 7.3 %all-to-all-start = ((bf16[8,32,1024]{2,1,0:T(8,128)(2,1)}), bf16[8,32,1024]{2,1,0:T(8,128)(2,1)S(1)}, u32[]{:S(2)}, u32[]{:S(2)}) async-start(bf16[8,32,1024]{2,1,0:T(8,128)(2,1)} %bitcast.9), calls=%async_computation | async-start | bytes 1048576 | tf_op jit(solution)/shard_map/all_to_all | solution.py:206
  19.6 0.8 reduce-window.8
  20.4 0.8 copy.40
  21.1 29.6 %all-gather = s32[8,1,128]{2,1,0:T(1,128)S(1)} all-gather(s32[1,1,128]{2,1,0:T(1,128)} %bitcast.89), channel_id=1, replica_groups=mesh['seq'=8,'head'=4] {'seq'}, dimensions={0}, use_global_device_ids=true | all-gather | bytes 4608 | tf_op jit(solution)/shard_map/all_gather | solution.py:191
  50.9 2.5 %select_reduce_fusion.1 = s32[8,128]{0,1:T(8,128)S(1)} fusion(s32[8,128]{0,1:T(8,128)S(1)} %copy.41), kind=kOutput, calls=%fused_computation.41 | output fusion | flops 1096704 | bytes 8192 | tf_op jit(solution)/shard_map/jit(cumsum)/reduce_window_sum | solution.py:196
  53.5 0.6 gather_fusion
  54.3 0.2 slice_reduce_fusion.2
  54.5 0.2 select_reduce_fusion
  54.9 0.5 fusion.36
  55.4 0.5 fusion.35
  56.0 0.3 fusion.21
  56.2 39.3 %all-gather.3.cloned.1.call-done = bf16[1024,2,1024]{2,0,1:T(8,128)(2,1)} async-done(((bf16[128,2,1024]{2,0,1:T(8,128)(2,1)}), bf16[1024,2,1024]{2,0,1:T(8,128)(2,1)}) %all-gather.3.cloned.1.call-update) | async-done | bytes 4194320 | tf_op jit(solution)/shard_map/all_gather | solution.py:192
  95.5 5.1 %slice_bitcast_fusion = (bf16[128,8,8,128]{3,1,2,0:T(8,128)(2,1)}, bf16[1024,1,1024]{2,0,1:T(8,128)(2,1)}) fusion(bf16[1024,2,1024]{2,0,1:T(8,128)(2,1)} %all-gather.3.cloned.1.call-done), kind=kLoop, calls=%fused_computation.11 | loop fusion | bytes 8388608
  100.6 2.9 %copy.49 = bf16[1024,1,1024]{0,2,1:T(8,128)(2,1)S(1)} copy(bf16[1024,1,1024]{2,0,1:T(8,128)(2,1)} %get-tuple-element.9) | data formatting | bytes 4194304 | tf_op jit(solution)/shard_map/reshape;squeeze | solution.py:220
  103.4 2.2 %copy.53 = bf16[128,8,8,128]{3,2,1,0:T(8,128)(2,1)S(1)} copy(bf16[128,8,8,128]{3,1,2,0:T(8,128)(2,1)} %get-tuple-element.8) | data formatting | bytes 4194304
  105.7 0.8 fusion.6
  106.4 2.1 %multiply_reduce_fusion = (f32[8,128]{1,0:T(8,128)S(1)}, f32[8,128,1024]{2,1,0:T(8,128)S(1)}) fusion(f32[128,1024]{1,0:T(8,128)S(1)} %fusion.35, f32[8,128,1024]{2,1,0:T(8,128)S(1)} %fusion.6, pred[128,1024]{1,0:T(8,128)(4,1)S(1)} %fusion.36), kind=kOutput, calls=%fused_computation.2 | output fusion | flops 7341055 | bytes 9048064 | tf_op jit(solution)/shard_map/sub | solution.py:248
  108.6 0.7 fusion.5
  109.3 0.8 fusion.26
  110.2 0.6 slice-done
  110.7 1.5 %slice-done.1 = s8[4194304]{0:T(1024)(128)(4,1)S(1)} async-done(((s8[8388608]{0:T(1024)(128)(4,1)}), s8[4194304]{0:T(1024)(128)(4,1)S(1)}, s32[]{:S(2)}) %slice-start.1) | async-done | bytes 4194328
  112.2 1.3 fusion.62
  113.7 1.9 %collective-permute-done = bf16[2,32,4096]{2,1,0:T(8,128)(2,1)S(1)} collective-permute-done((bf16[2,32,4096]{2,1,0:T(8,128)(2,1)S(1)}, bf16[2,32,4096]{2,1,0:T(8,128)(2,1)S(1)}, u32[]{:S(2)}, u32[]{:S(2)}) %collective-permute-start) | collective-permute-done | bytes 524320 | tf_op jit(solution)/shard_map/ppermute | solution.py:280
  115.8 1.5 %collective-permute-start.1 = (bf16[1,32,4096]{2,1,0:T(8,128)(2,1)S(1)}, bf16[1,32,4096]{2,1,0:T(8,128)(2,1)S(1)}, u32[]{:S(2)}, u32[]{:S(2)}) collective-permute-start(bf16[1,32,4096]{2,1,0:T(8,128)(2,1)S(1)} %fusion.37), channel_id=1, source_target_pairs={{0,2},{1,3},{2,0},{3,1},{4,6},{5,7},{6,4},{7,5},{8,10},{9,11},{10,... | collective-permute-start | bytes 786440 | tf_op jit(solution)/shard_map/ppermute | solution.py:280
  117.3 6.9 %collective-permute-done.1 = bf16[1,32,4096]{2,1,0:T(8,128)(2,1)S(1)} collective-permute-done((bf16[1,32,4096]{2,1,0:T(8,128)(2,1)S(1)}, bf16[1,32,4096]{2,1,0:T(8,128)(2,1)S(1)}, u32[]{:S(2)}, u32[]{:S(2)}) %collective-permute-start.1) | collective-permute-done | bytes 262176 | tf_op jit(solution)/shard_map/ppermute | solution.py:280
  124.2 0.8 fusion.38
  (25 shorter events, 0.9 us)
Async XLA Ops:
  6.5 48.2 %copy-start = (s32[8]{0:T(128)S(1)}, s32[8]{0:T(128)}, u32[]{:S(2)}) copy-start(s32[8]{0:T(128)} %param.10) | copy-start | bytes 100
  6.5 89.0 %all-gather.3.cloned.1.call-start = ((), (), s32[]{:S(2)}) async-start(), calls=%async_computation.1 | async-start | bytes 4718592 | tf_op jit(solution)/shard_map/all_gather | solution.py:192
  12.3 43.7 %all-to-all-start = ((bf16[8,32,1024]{2,1,0:T(8,128)(2,1)}), bf16[8,32,1024]{2,1,0:T(8,128)(2,1)S(1)}, u32[]{:S(2)}, u32[]{:S(2)}) async-start(bf16[8,32,1024]{2,1,0:T(8,128)(2,1)} %bitcast.9), calls=%async_computation | async-start | bytes 1048576 | tf_op jit(solution)/shard_map/all_to_all | solution.py:206
  108.6 2.2 %slice-start = ((s8[8388608]{0:T(1024)(128)(4,1)}), s8[4194304]{0:T(1024)(128)(4,1)S(1)}, s32[]{:S(2)}) async-start(s8[8388608]{0:T(1024)(128)(4,1)} %bitcast.75), calls=%async_computation.2 | async-start | bytes 8388608
  109.3 2.9 %slice-start.1 = ((s8[8388608]{0:T(1024)(128)(4,1)}), s8[4194304]{0:T(1024)(128)(4,1)S(1)}, s32[]{:S(2)}) async-start(s8[8388608]{0:T(1024)(128)(4,1)} %bitcast.75), calls=%async_computation.3 | async-start | bytes 8388608
  113.6 2.0 %collective-permute-start = (bf16[2,32,4096]{2,1,0:T(8,128)(2,1)S(1)}, bf16[2,32,4096]{2,1,0:T(8,128)(2,1)S(1)}, u32[]{:S(2)}, u32[]{:S(2)}) collective-permute-start(bf16[2,32,4096]{2,1,0:T(8,128)(2,1)S(1)} %fusion.33), channel_id=1, source_target_pairs={{0,1},{1,0},{2,3},{3,2},{4,5},{5,4},{6,7},{7,6},{8,9},{9,8},{10,11... | collective-permute-start | bytes 1572872 | tf_op jit(solution)/shard_map/ppermute | solution.py:280
  115.8 8.4 %collective-permute-start.1 = (bf16[1,32,4096]{2,1,0:T(8,128)(2,1)S(1)}, bf16[1,32,4096]{2,1,0:T(8,128)(2,1)S(1)}, u32[]{:S(2)}, u32[]{:S(2)}) collective-permute-start(bf16[1,32,4096]{2,1,0:T(8,128)(2,1)S(1)} %fusion.37), channel_id=1, source_target_pairs={{0,2},{1,3},{2,0},{3,1},{4,6},{5,7},{6,4},{7,5},{8,10},{9,11},{10,... | collective-permute-start | bytes 786440 | tf_op jit(solution)/shard_map/ppermute | solution.py:280
Sparse Core Ops, SparseCore 0:
  9.5 85.9 all-gather.2

commit v9 on v6

--- a/solution.py
+++ b/solution.py
@@ -3,6 +3,8 @@
 import jax
 import jax.numpy as jnp
 from jax import lax
+from jax.experimental import pallas as pl
+from jax.experimental.pallas import tpu as pltpu
 from jax.sharding import PartitionSpec as P
 
 HD = 128
@@ -175,6 +177,51 @@
         scatter_dimension=0,
         tiled=True,
     )
+
+
+def attend_body(q_ref, k_ref, v_ref, count_ref, flag_ref, out_ref):
+    scores = lax.dot_general(
+        q_ref[...], k_ref[...], (((1,), (1,)), ((), ())), preferred_element_type=jnp.float32
+    ) * (1.0 / math.sqrt(HD))
+    count = count_ref[...]
+    near_scores = jnp.where(count > 0, scores, big_negative)
+    row_peak = jnp.max(near_scores, axis=1, keepdims=True)
+    near_exp = jnp.exp(near_scores - row_peak)
+    denominator = jnp.sum(near_exp * count, axis=1, keepdims=True)
+    exact = flag_ref[0:1, 0:1] > 0
+    rounded = jnp.where(exact, near_exp, near_exp.astype(jnp.bfloat16).astype(jnp.float32))
+    weighted = rounded * count
+    weight_hi = weighted.astype(jnp.bfloat16)
+    weight_lo = (weighted - weight_hi.astype(jnp.float32)).astype(jnp.bfloat16)
+    values = v_ref[...]
+    mixed_sum = jnp.dot(weight_hi, values, preferred_element_type=jnp.float32)
+    mixed_sum = mixed_sum + jnp.dot(weight_lo, values, preferred_element_type=jnp.float32)
+    out_ref[...] = (mixed_sum / denominator).astype(out_ref.dtype)
+
+
+def attend_all(queries, keys, values, count, flag):
+    rows, columns = queries.shape
+    tokens = keys.shape[0]
+    heads = columns // HD
+    flops = heads * rows * tokens * HD * 2 * 3
+    return pl.pallas_call(
+        attend_body,
+        grid=(heads,),
+        in_specs=[
+            pl.BlockSpec((rows, HD), lambda h: (0, h)),
+            pl.BlockSpec((tokens, HD), lambda h: (0, h)),
+            pl.BlockSpec((tokens, HD), lambda h: (0, h)),
+            pl.BlockSpec((rows, tokens), lambda h: (0, 0)),
+            pl.BlockSpec((8, 128), lambda h: (0, 0)),
+        ],
+        out_specs=pl.BlockSpec((rows, HD), lambda h: (0, h)),
+        out_shape=jax.ShapeDtypeStruct((rows, columns), jnp.bfloat16),
+        cost_estimate=pl.CostEstimate(
+            flops=flops,
+            transcendentals=heads * rows * tokens,
+            bytes_accessed=2 * tokens * columns * 2 + rows * tokens * 4 + 2 * rows * columns * 2,
+        ),
+    )(queries, keys, values, count, flag)
 
 
 def gathered_plan(projected, destination, doc_lengths, random_blocks, global_owner, out_weight):
@@ -216,10 +263,6 @@
     queries = queries.astype(projected.dtype).reshape(tok_dev, heads_here, HD)
     keys = keyval[:, 0, :].reshape(tokens, heads_here, HD)
     values = keyval[:, 1, :].reshape(tokens, heads_here, HD)
-    scores = (
-        jnp.einsum("qhd,khd->hqk", queries, keys, preferred_element_type=jnp.float32)
-        * score_scale
-    )
     bounds = jnp.cumsum(doc_lengths)
     key_block = arrival_dest // BLK
     key_doc = segment_of(arrival_dest, bounds)
@@ -240,22 +283,13 @@
     holds_glob = own_index == global_owner[0]
     count = window + drawn + in_glob[None, :].astype(jnp.int32)
     count = jnp.where(holds_glob, 1, count)
-    live = count > 0
-    near_scores = jnp.where(live[None], scores, big_negative)
-    row_peak = jnp.max(near_scores, axis=2)
-    near_exp = jnp.exp(near_scores - row_peak[..., None])
-    count_f = count.astype(jnp.float32)[None]
-    denominator = jnp.sum(near_exp * count_f, axis=2)
-    rounded = jnp.where(holds_glob, near_exp, near_exp.astype(jnp.bfloat16).astype(jnp.float32))
-    weighted = rounded * count_f
-    weight_hi = weighted.astype(jnp.bfloat16)
-    weight_lo = (weighted - weight_hi.astype(jnp.float32)).astype(jnp.bfloat16)
-    mixed_sum = jnp.einsum("hqk,khd->qhd", weight_hi, values, preferred_element_type=jnp.float32)
-    mixed_sum = mixed_sum + jnp.einsum(
-        "hqk,khd->qhd", weight_lo, values, preferred_element_type=jnp.float32
-    )
-    attn_rows = (mixed_sum / jnp.transpose(denominator)[..., None]).reshape(tok_dev, columns)
-    attn_rows = attn_rows.astype(jnp.bfloat16)
+    attn_rows = attend_all(
+        queries.reshape(tok_dev, columns),
+        keyval[:, 0, :],
+        keyval[:, 1, :],
+        count.astype(jnp.float32),
+        jnp.full((8, 128), holds_glob.astype(jnp.float32)),
+    )
     projected_rows = jnp.dot(attn_rows, out_weight, preferred_element_type=jnp.float32)
     return head_sum(lax.optimization_barrier(projected_rows))
 

time: 126 us -> 133 us (1.056)
  Pallas kernels: 0 us -> 8.69 us
  waiting for transfers between devices: 49.7 us -> 46.7 us
  other arithmetic: 9.26 us -> 7.38 us
  matrix products: 6.25 us -> 7.76 us
    pallas_call x0 -> x1, Pallas kernels: none -> 8.69 us  [attend_all(): pl.pallas_call(attend_body, grid=(heads,), in_specs=[pl.BlockSpec((rows,...]
    squeeze x0 -> x1, local copies, waits for them, and re-layouts: none -> 4.63 us  [gathered_plan(): keyval[:, 1, :]]
    dot_general x1, matrix products: 1.3 us -> 4.74 us  [gathered_plan(): jnp.dot(attn_rows, out_weight, preferred_element_type=jnp.float32)]
    all_gather x1, waiting for transfers between devices: 40.9 us -> 37.9 us  [gathered_plan(): keyval = lax.all_gather(projected[:, 1:, :], 'seq', tiled=True)]
    unnamed x14 -> x9, local copies, waits for them, and re-layouts: 2.81 us -> 0.1 us
    slice x1 -> x0, local copies, waits for them, and re-layouts: 2.66 us -> none  [gathered_plan(): keys = keyval[:, 0, :].reshape(tokens, heads_here, HD)]
    dot_general x3 -> x0, matrix products: 2.63 us -> none  [the longest x1 1.14 us: gathered_plan(): jnp.einsum('hqk,khd->qhd', weight_hi, values, preferred_element_type=jnp....]
    sub x1 -> x0, other arithmetic: 2.18 us -> none  [gathered_plan(): near_exp = jnp.exp(near_scores - row_peak[..., None])]
  transfers between devices with their start and end apart: 4 -> 4, of which waited for: 3 -> 3; matrix products, arithmetic and copies ran while one was open for 7% -> 8% of each run, Pallas kernels for 0% -> 0%
where the time goes in v9:
time: 133 us; the launch traced here: 132 us
  waiting for transfers between devices  46.7 us (35%)
  blocking collectives  31.2 us (23%)
  between operations  13.6 us (10%)
  starting transfers between devices  8.95 us (7%)
  Pallas kernels  8.69 us (7%)
  local copies, waits for them, and re-layouts  8.19 us (6%)
  matrix products  7.76 us (6%)
  other arithmetic  7.38 us (6%)
    all_gather x1, waiting for transfers between devices, gathered_plan(): keyval = lax.all_gather(projected[:, 1:, :], 'seq', tiled=True)  37.9 us
    all_gather x1, blocking collectives, gathered_plan(): arrival_dest = lax.all_gather(destination, 'seq', tiled=True)  31.2 us
    ppermute x2, waiting for transfers between devices, head_sum(): got = lax.ppermute(send, 'head', [(i, i ^ bit) for i in range(members)])  8.74 us
    pallas_call x1, Pallas kernels, attend_all(): pl.pallas_call(attend_body, grid=(heads,), in_specs=[pl.BlockSpec((rows,...  8.69 us
    all_to_all x1, starting transfers between devices, gathered_plan(): lax.all_to_all(outgoing, 'seq', split_axis=0, concat_axis=0, tiled=True)  7.29 us
    dot_general x1, matrix products, gathered_plan(): jnp.dot(attn_rows, out_weight, preferred_element_type=jnp.float32)  4.74 us
    squeeze x1, local copies, waits for them, and re-layouts, gathered_plan(): keyval[:, 1, :]  4.63 us
  transfers between devices with their start and end apart: 4, of which 3 were waited for; matrix products, arithmetic and copies ran while one was open for 8% of the time, Pallas kernels for 0%

profile of v9, /device:TPU:0, one launch (start us, length us, event | category | flops | bytes accessed | tf_op | source)
XLA Modules:
  0.0 132.5 jit_solution(13735358294671646483)
XLA Ops:
  6.6 1.9 %slice.42 = bf16[128,2,1024]{2,0,1:T(8,128)(2,1)} slice(bf16[128,3,1024]{2,0,1:T(8,128)(2,1)} %param.6), slice={[0:128], [1:3], [0:1024]} | slice | bytes 1048576 | tf_op jit(solution)/shard_map/slice | solution.py:238
  8.5 0.7 and_select_fusion.5
  9.2 0.1 fusion.13
  9.2 0.2 reduce_window_sum.30
  9.4 0.2 select_reduce_fusion.2
  9.6 0.7 multiply_add_fusion
  10.3 2.1 %convolution_convert_fusion = bf16[256,1024]{1,0:T(8,128)(2,1)} fusion(bf16[128,3,1024]{2,0,1:T(8,128)(2,1)} %param.6, s32[128]{0:T(128)S(1)} %multiply_add_fusion), kind=kOutput, calls=%fused_computation.3 | convolution fusion | flops 67403776 | bytes 786944 | tf_op jit(solution)/shard_map/dot_general | solution.py:249
  12.3 7.3 %all-to-all-start = ((bf16[8,32,1024]{2,1,0:T(8,128)(2,1)}), bf16[8,32,1024]{2,1,0:T(8,128)(2,1)S(1)}, u32[]{:S(2)}, u32[]{:S(2)}) async-start(bf16[8,32,1024]{2,1,0:T(8,128)(2,1)} %bitcast.5), calls=%async_computation | async-start | bytes 1048576 | tf_op jit(solution)/shard_map/all_to_all | solution.py:251
  19.7 31.2 %all-gather = s32[8,1,128]{2,1,0:T(1,128)S(1)} all-gather(s32[1,1,128]{2,1,0:T(1,128)S(1)} %bitcast.66), channel_id=1, replica_groups=mesh['seq'=8,'head'=4] {'seq'}, dimensions={0}, use_global_device_ids=true | all-gather | bytes 4608 | tf_op jit(solution)/shard_map/all_gather | solution.py:237
  51.0 0.1 copy.24
  51.1 2.5 %select_reduce_fusion.1 = s32[8,128]{0,1:T(8,128)S(1)} fusion(s32[8,128]{0,1:T(8,128)S(1)} %copy.24), kind=kOutput, calls=%fused_computation.19 | output fusion | flops 1096704 | bytes 8192 | tf_op jit(solution)/shard_map/jit(cumsum)/reduce_window_sum | solution.py:241
  53.6 0.2 reduce-window.8
  53.8 0.1 copy.26
  53.9 0.6 gather_fusion
  54.6 0.1 convert_reduce_fusion.1
  54.7 0.1 convert_reduce_fusion
  54.8 0.2 slice_reduce_fusion.2
  55.0 0.2 select_reduce_fusion
  55.2 1.4 %select_convert_fusion.2.count_ref = f32[128,1024]{1,0:T(8,128)} fusion(s32[1024]{0:T(1024)S(1)} %and_convert_fusion, s32[1024]{0:T(1024)S(1)} %add_select_fusion, s32[1024]{0:T(1024)S(1)} %convert_reduce_fusion, s32[128]{0:T(128)S(1)} %get-tuple-element.7, s32[128]{0:T(128)S(1)} %get-tuple-element.6, s32[128]{0:T(128)S(1)} %get-tuple-element.5, ...), kind=kLoop, calls=%fused_computation.17 | loop fusion | flops 2883584 | bytes 540161 | tf_op jit(solution)/shard_map/convert_element_type | solution.py:290
  56.6 1.0 convolution_convert_fusion.1.q_ref
  57.6 37.9 %all-gather.3.cloned.1.call-done = bf16[1024,2,1024]{2,0,1:T(8,128)(2,1)} async-done(((bf16[128,2,1024]{2,0,1:T(8,128)(2,1)}), bf16[1024,2,1024]{2,0,1:T(8,128)(2,1)}) %all-gather.3.cloned.1.call-update) | async-done | bytes 4194320 | tf_op jit(solution)/shard_map/all_gather | solution.py:238
  95.5 4.6 %slice_bitcast_fusion = (bf16[1024,1024]{1,0:T(8,128)(2,1)}, bf16[1024,1024]{1,0:T(8,128)(2,1)}) fusion(bf16[1024,2,1024]{2,0,1:T(8,128)(2,1)} %all-gather.3.cloned.1.call-done), kind=kLoop, calls=%fused_computation.1 | loop fusion | bytes 8388608 | tf_op jit(solution)/shard_map/squeeze | solution.py:289
  100.2 0.6 broadcast_in_dim.21.flag_ref
  100.7 8.7 %shard_map.64 = bf16[128,1024]{1,0:T(8,128)(2,1)} custom-call(bf16[128,1024]{1,0:T(8,128)(2,1)} %convolution_convert_fusion.1.q_ref, bf16[1024,1024]{1,0:T(8,128)(2,1)} %get-tuple-element.9.k_ref, bf16[1024,1024]{1,0:T(8,128)(2,1)} %get-tuple-element.8.v_ref, f32[128,1024]{1,0:T(8,128)} %select_convert_fusion.2.count_ref, f32[8,128]{1,0:T(8,128)} %broadcast_in_dim.21.flag_ref), custom_call_target="tpu_custom_call" | custom-call | flops 805306368 | bytes 5242880 | tf_op jit(solution)/shard_map/pallas_call | solution.py:207
  109.4 4.7 %fusion.28 = f32[128,4096]{1,0:T(8,128)S(1)} fusion(bf16[128,1024]{1,0:T(8,128)(2,1)} %shard_map.64, bf16[1024,4096]{1,0:T(8,128)(2,1)} %param.11), kind=kOutput, calls=%fused_computation.91 | convolution fusion | flops 1073741824 | bytes 10747904 | tf_op jit(solution)/shard_map/dot_general | solution.py:293
  114.2 0.1 fusion.5
  114.3 0.1 collective-permute-start
  114.4 1.9 %collective-permute-done = bf16[2,32,4096]{2,1,0:T(8,128)(2,1)S(1)} collective-permute-done((bf16[2,32,4096]{2,1,0:T(8,128)(2,1)S(1)}, bf16[2,32,4096]{2,1,0:T(8,128)(2,1)S(1)}, u32[]{:S(2)}, u32[]{:S(2)}) %collective-permute-start) | collective-permute-done | bytes 524320 | tf_op jit(solution)/shard_map/ppermute | solution.py:312
  116.3 0.1 fusion
  116.5 1.6 %collective-permute-start.1 = (bf16[1,32,4096]{2,1,0:T(8,128)(2,1)S(1)}, bf16[1,32,4096]{2,1,0:T(8,128)(2,1)S(1)}, u32[]{:S(2)}, u32[]{:S(2)}) collective-permute-start(bf16[1,32,4096]{2,1,0:T(8,128)(2,1)S(1)} %fusion.7), channel_id=1, source_target_pairs={{0,2},{1,3},{2,0},{3,1},{4,6},{5,7},{6,4},{7,5},{8,10},{9,11},{10,... | collective-permute-start | bytes 786440 | tf_op jit(solution)/shard_map/ppermute | solution.py:312
  118.0 6.8 %collective-permute-done.1 = bf16[1,32,4096]{2,1,0:T(8,128)(2,1)S(1)} collective-permute-done((bf16[1,32,4096]{2,1,0:T(8,128)(2,1)S(1)}, bf16[1,32,4096]{2,1,0:T(8,128)(2,1)S(1)}, u32[]{:S(2)}, u32[]{:S(2)}) %collective-permute-start.1) | collective-permute-done | bytes 262176 | tf_op jit(solution)/shard_map/ppermute | solution.py:312
  124.9 0.8 fusion.8
  (22 shorter events, 0.3 us)
Async XLA Ops:
  6.5 13.2 %copy-start.1 = (s32[128]{0:T(128)S(1)}, s32[128]{0:T(128)}, u32[]{:S(2)}) copy-start(s32[128]{0:T(128)} %param.7) | copy-start | bytes 1540
  6.5 13.1 %copy-start.2 = (s32[8]{0:T(128)S(1)}, s32[8]{0:T(128)}, u32[]{:S(2)}) copy-start(s32[8]{0:T(128)} %param.10) | copy-start | bytes 100
  6.5 47.1 %copy-start.3 = (s32[4]{0:T(128)S(1)}, s32[4]{0:T(128)}, u32[]{:S(2)}) copy-start(s32[4]{0:T(128)} %param.8) | copy-start | bytes 52
  6.5 47.3 %copy-start = (s32[8,3]{0,1:T(4,128)S(1)}, s32[8,3]{0,1:T(4,128)}, u32[]{:S(2)}) copy-start(s32[8,3]{0,1:T(4,128)} %param.9) | copy-start | bytes 292
  6.5 89.0 %all-gather.3.cloned.1.call-start = ((), (), s32[]{:S(2)}) async-start(), calls=%async_computation.1 | async-start | bytes 4718592 | tf_op jit(solution)/shard_map/all_gather | solution.py:238
  12.3 44.3 %all-to-all-start = ((bf16[8,32,1024]{2,1,0:T(8,128)(2,1)}), bf16[8,32,1024]{2,1,0:T(8,128)(2,1)S(1)}, u32[]{:S(2)}, u32[]{:S(2)}) async-start(bf16[8,32,1024]{2,1,0:T(8,128)(2,1)} %bitcast.5), calls=%async_computation | async-start | bytes 1048576 | tf_op jit(solution)/shard_map/all_to_all | solution.py:251
  114.3 2.0 %collective-permute-start = (bf16[2,32,4096]{2,1,0:T(8,128)(2,1)S(1)}, bf16[2,32,4096]{2,1,0:T(8,128)(2,1)S(1)}, u32[]{:S(2)}, u32[]{:S(2)}) collective-permute-start(bf16[2,32,4096]{2,1,0:T(8,128)(2,1)S(1)} %fusion.5), channel_id=1, source_target_pairs={{0,1},{1,0},{2,3},{3,2},{4,5},{5,4},{6,7},{7,6},{8,9},{9,8},{10,11... | collective-permute-start | bytes 1572872 | tf_op jit(solution)/shard_map/ppermute | solution.py:312
  116.5 8.4 %collective-permute-start.1 = (bf16[1,32,4096]{2,1,0:T(8,128)(2,1)S(1)}, bf16[1,32,4096]{2,1,0:T(8,128)(2,1)S(1)}, u32[]{:S(2)}, u32[]{:S(2)}) collective-permute-start(bf16[1,32,4096]{2,1,0:T(8,128)(2,1)S(1)} %fusion.7), channel_id=1, source_target_pairs={{0,2},{1,3},{2,0},{3,1},{4,6},{5,7},{6,4},{7,5},{8,10},{9,11},{10,... | collective-permute-start | bytes 786440 | tf_op jit(solution)/shard_map/ppermute | solution.py:312
Sparse Core Ops, SparseCore 0:
  9.6 85.9 all-gather.2

commit v10 on v6

--- a/solution.py
+++ b/solution.py
@@ -177,6 +177,33 @@
     )
 
 
+def ring_gather(block, own_index, owners):
+    if owners % 2:
+        ring = list(range(owners))
+    else:
+        half = owners // 2
+        ring = [2 * i for i in range(half)] + [2 * i + 1 for i in reversed(range(half))]
+    place = [0] * owners
+    for i, s in enumerate(ring):
+        place[s] = i
+    right = [(ring[i], ring[(i + 1) % owners]) for i in range(owners)]
+    left = [(ring[i], ring[(i - 1) % owners]) for i in range(owners)]
+    pieces = {0: block}
+    moving_right = block
+    moving_left = block
+    for step in range(1, owners // 2 + 1):
+        moving_right = lax.ppermute(moving_right, "seq", right)
+        pieces[-step] = moving_right
+        if step <= (owners - 1) // 2:
+            moving_left = lax.ppermute(moving_left, "seq", left)
+            pieces[step] = moving_left
+    offsets = sorted(pieces)
+    stacked = jnp.concatenate([pieces[k] for k in offsets], axis=0)
+    where = jnp.asarray(place, jnp.int32)[own_index]
+    order = jnp.asarray(ring, jnp.int32)[(where + jnp.asarray(offsets, jnp.int32)) % owners]
+    return stacked, order
+
+
 def gathered_plan(projected, destination, doc_lengths, random_blocks, global_owner, out_weight):
     owners = lax.axis_size("seq")
     own_index = lax.axis_index("seq")
@@ -188,7 +215,8 @@
     score_scale = 1.0 / math.sqrt(HD)
     capacity = 2 * (tok_dev // owners)
     arrival_dest = lax.all_gather(destination, "seq", tiled=True)
-    keyval = lax.all_gather(projected[:, 1:, :], "seq", tiled=True)
+    keyval, key_order = ring_gather(projected[:, 1:, :], own_index, owners)
+    key_dest = arrival_dest.reshape(owners, tok_dev)[key_order].reshape(-1)
     target_all = arrival_dest.reshape(owners, tok_dev) // tok_dev
     onehot = (target_all[:, :, None] == jnp.arange(owners, dtype=jnp.int32)).astype(jnp.int32)
     slot_all = jnp.sum((jnp.cumsum(onehot, axis=1) - onehot) * onehot, axis=2)
@@ -221,8 +249,8 @@
         * score_scale
     )
     bounds = jnp.cumsum(doc_lengths)
-    key_block = arrival_dest // BLK
-    key_doc = segment_of(arrival_dest, bounds)
+    key_block = key_dest // BLK
+    key_doc = segment_of(key_dest, bounds)
     query_block = my_pos // BLK
     query_doc = segment_of(my_pos, bounds)
     same_doc = query_doc[:, None] == key_doc[None, :]
@@ -236,7 +264,7 @@
     for r in range(chosen.shape[1]):
         drawn = drawn + (key_block[None, :] == chosen[:, r][:, None]).astype(jnp.int32)
     glob_start = global_owner[0] * tok_dev
-    in_glob = (arrival_dest >= glob_start) & (arrival_dest < glob_start + tok_dev)
+    in_glob = (key_dest >= glob_start) & (key_dest < glob_start + tok_dev)
     holds_glob = own_index == global_owner[0]
     count = window + drawn + in_glob[None, :].astype(jnp.int32)
     count = jnp.where(holds_glob, 1, count)

time: 126 us -> 104 us (0.83)
  waiting for transfers between devices: 49.7 us -> 35.3 us
  between operations: 13.7 us -> 0.42 us
  starting transfers between devices: 8.93 us -> 16.4 us
  blocking collectives: 30.8 us -> 23.9 us
  local copies, waits for them, and re-layouts: 7.56 us -> 11 us
    all_gather x1 -> x0, waiting for transfers between devices: 40.9 us -> none  [gathered_plan(): keyval = lax.all_gather(projected[:, 1:, :], 'seq', tiled=True)]
    ppermute x0 -> x7, waiting for transfers between devices: none -> 26.5 us  [the longest x4 26.5 us: ring_gather(): moving_right = lax.ppermute(moving_right, 'seq', right)]
    ppermute x0 -> x7, starting transfers between devices: none -> 8.54 us  [the longest x4 6.66 us: ring_gather(): moving_right = lax.ppermute(moving_right, 'seq', right)]
    all_gather x1, blocking collectives: 30.8 us -> 23.9 us  [gathered_plan(): arrival_dest = lax.all_gather(destination, 'seq', tiled=True)]
    unnamed x14 -> x27, local copies, waits for them, and re-layouts: 2.81 us -> 6.47 us
    slice x1, local copies, waits for them, and re-layouts: 2.66 us -> 0.44 us  [gathered_plan(): keys = keyval[:, 0, :].reshape(tokens, heads_here, HD)]
  transfers between devices with their start and end apart: 4 -> 10, of which waited for: 3 -> 5; matrix products, arithmetic and copies ran while one was open for 7% -> 16% of each run, Pallas kernels for 0% -> 0%
where the time goes in v10:
time: 104 us; the launch traced here: 103 us
  waiting for transfers between devices  35.3 us (34%)
  blocking collectives  23.9 us (23%)
  starting transfers between devices  16.4 us (16%)
  local copies, waits for them, and re-layouts  11 us (11%)
  other arithmetic  9.89 us (10%)
  matrix products  6.22 us (6%)
    ppermute x4, waiting for transfers between devices, ring_gather(): moving_right = lax.ppermute(moving_right, 'seq', right)  26.5 us
    all_gather x1, blocking collectives, gathered_plan(): arrival_dest = lax.all_gather(destination, 'seq', tiled=True)  23.9 us
    ppermute x2, waiting for transfers between devices, head_sum(): got = lax.ppermute(send, 'head', [(i, i ^ bit) for i in range(members)])  8.74 us
    ppermute x4, starting transfers between devices, ring_gather(): moving_right = lax.ppermute(moving_right, 'seq', right)  6.66 us
    unnamed x27, local copies, waits for them, and re-layouts  6.47 us
    all_to_all x1, starting transfers between devices, gathered_plan(): lax.all_to_all(outgoing, 'seq', split_axis=0, concat_axis=0, tiled=True)  6.28 us
    another operation x1, other arithmetic, gathered_plan(): slot_all = jnp.sum((jnp.cumsum(onehot, axis=1) - onehot) * onehot, axis=2)  2.52 us
    sub x1, other arithmetic, gathered_plan(): near_exp = jnp.exp(near_scores - row_peak[..., None])  2.18 us
  transfers between devices with their start and end apart: 10, of which 5 were waited for; matrix products, arithmetic and copies ran while one was open for 16% of the time, Pallas kernels for 0%

profile of v10, /device:TPU:0, one launch (start us, length us, event | category | flops | bytes accessed | tf_op | source)
XLA Modules:
  0.0 103.2 jit_solution(3569183544681013545)
XLA Ops:
  0.0 1.1 %slice.41 = bf16[128,2,1024]{2,0,1:T(8,128)(2,1)S(1)} slice(bf16[128,3,1024]{2,0,1:T(8,128)(2,1)} %param.9), slice={[0:128], [1:3], [0:1024]} | slice | bytes 1048576 | tf_op jit(solution)/shard_map/slice | solution.py:218
  1.5 3.1 %collective-permute-start = (bf16[128,2,1024]{0,2,1:T(8,128)(2,1)S(1)}, bf16[128,2,1024]{0,2,1:T(8,128)(2,1)S(1)}, u32[]{:S(2)}, u32[]{:S(2)}) collective-permute-start(bf16[128,2,1024]{0,2,1:T(8,128)(2,1)S(1)} %copy.49), channel_id=1, source_target_pairs={{0,8},{8,16},{16,24},{24,28},{28,20},{20,12},{12,4},{4,0},{1,9},{9... | collective-permute-start | bytes 1572872 | tf_op jit(solution)/shard_map/ppermute | solution.py:195
  4.6 0.7 and_select_fusion
  5.7 0.7 multiply_add_fusion
  6.3 2.1 %convolution_convert_fusion = bf16[256,1024]{1,0:T(8,128)(2,1)} fusion(bf16[128,3,1024]{2,0,1:T(8,128)(2,1)} %param.9, s32[128]{0:T(128)S(1)} %multiply_add_fusion), kind=kOutput, calls=%fused_computation.20 | convolution fusion | flops 67403776 | bytes 786944 | tf_op jit(solution)/shard_map/dot_general | solution.py:230
  8.4 6.3 %all-to-all-start = ((bf16[8,32,1024]{2,1,0:T(8,128)(2,1)}), bf16[8,32,1024]{2,1,0:T(8,128)(2,1)S(1)}, u32[]{:S(2)}, u32[]{:S(2)}) async-start(bf16[8,32,1024]{2,1,0:T(8,128)(2,1)} %bitcast.14), calls=%async_computation | async-start | bytes 1048576 | tf_op jit(solution)/shard_map/all_to_all | solution.py:232
  14.7 23.9 %all-gather = s32[8,1,128]{2,1,0:T(1,128)S(1)} all-gather(s32[1,1,128]{2,1,0:T(1,128)S(1)} %bitcast.93), channel_id=1, replica_groups=mesh['seq'=8,'head'=4] {'seq'}, dimensions={0}, use_global_device_ids=true | all-gather | bytes 4608 | tf_op jit(solution)/shard_map/all_gather | solution.py:217
  39.2 0.7 compare_select_fusion.2
  39.9 0.6 gather_fusion
  41.6 2.5 %select_reduce_fusion.1 = s32[8,128]{0,1:T(8,128)S(1)} fusion(s32[8,128]{0,1:T(8,128)S(1)} %copy.42), kind=kOutput, calls=%fused_computation.40 | output fusion | flops 1096704 | bytes 8192 | tf_op jit(solution)/shard_map/jit(cumsum)/reduce_window_sum | solution.py:222
  44.2 0.7 gather_fusion.2
  44.9 1.1 %collective-permute-start.1 = (bf16[128,2,1024]{0,2,1:T(8,128)(2,1)S(1)}, bf16[128,2,1024]{0,2,1:T(8,128)(2,1)S(1)}, u32[]{:S(2)}, u32[]{:S(2)}) collective-permute-start(bf16[128,2,1024]{0,2,1:T(8,128)(2,1)S(1)} %collective-permute-done), channel_id=1, source_target_pairs={{0,8},{8,16},{16,24},{24,28},{28,20},{20,12},{12,4},{4,0},{1,9},{9... | collective-permute-start | bytes 1572872 | tf_op jit(solution)/shard_map/ppermute | solution.py:195
  46.4 10.7 %collective-permute-done.1 = bf16[128,2,1024]{0,2,1:T(8,128)(2,1)S(1)} collective-permute-done((bf16[128,2,1024]{0,2,1:T(8,128)(2,1)S(1)}, bf16[128,2,1024]{0,2,1:T(8,128)(2,1)S(1)}, u32[]{:S(2)}, u32[]{:S(2)}) %collective-permute-start.1) | collective-permute-done | bytes 524320 | tf_op jit(solution)/shard_map/ppermute | solution.py:195
  57.1 1.1 %collective-permute-start.2 = (bf16[128,2,1024]{0,2,1:T(8,128)(2,1)S(1)}, bf16[128,2,1024]{0,2,1:T(8,128)(2,1)}, u32[]{:S(2)}, u32[]{:S(2)}) collective-permute-start(bf16[128,2,1024]{0,2,1:T(8,128)(2,1)S(1)} %collective-permute-done.1), channel_id=1, source_target_pairs={{0,8},{8,16},{16,24},{24,28},{28,20},{20,12},{12,4},{4,0},{1,9},{9... | collective-permute-start | bytes 1572872 | tf_op jit(solution)/shard_map/ppermute | solution.py:195
  58.7 1.0 collective-permute-start.5
  59.7 9.6 %collective-permute-done.2 = bf16[128,2,1024]{0,2,1:T(8,128)(2,1)} collective-permute-done((bf16[128,2,1024]{0,2,1:T(8,128)(2,1)S(1)}, bf16[128,2,1024]{0,2,1:T(8,128)(2,1)}, u32[]{:S(2)}, u32[]{:S(2)}) %collective-permute-start.2) | collective-permute-done | bytes 524320 | tf_op jit(solution)/shard_map/ppermute | solution.py:195
  69.3 1.4 %collective-permute-start.3 = (bf16[128,2,1024]{0,2,1:T(8,128)(2,1)}, bf16[128,2,1024]{0,2,1:T(8,128)(2,1)}, u32[]{:S(2)}, u32[]{:S(2)}) collective-permute-start(bf16[128,2,1024]{0,2,1:T(8,128)(2,1)} %collective-permute-done.2), channel_id=1, source_target_pairs={{0,8},{8,16},{16,24},{24,28},{28,20},{20,12},{12,4},{4,0},{1,9},{9... | collective-permute-start | bytes 1572872 | tf_op jit(solution)/shard_map/ppermute | solution.py:195
  71.8 0.9 collective-permute-start.6
  72.6 6.2 %collective-permute-done.3 = bf16[128,2,1024]{0,2,1:T(8,128)(2,1)} collective-permute-done((bf16[128,2,1024]{0,2,1:T(8,128)(2,1)}, bf16[128,2,1024]{0,2,1:T(8,128)(2,1)}, u32[]{:S(2)}, u32[]{:S(2)}) %collective-permute-start.3) | collective-permute-done | bytes 524320 | tf_op jit(solution)/shard_map/ppermute | solution.py:195
  78.8 1.2 %constant_dynamic-update-slice_fusion.7 = bf16[1024,2,1024]{0,2,1:T(8,128)(2,1)S(1)} fusion(bf16[128,2,1024]{0,2,1:T(8,128)(2,1)} %collective-permute-done.3), kind=kLoop, calls=%fused_computation.70 | loop fusion | bytes 1048576
  80.0 1.2 %constant_dynamic-update-slice_fusion.6 = bf16[1024,2,1024]{0,2,1:T(8,128)(2,1)S(1)} fusion(bf16[1024,2,1024]{0,2,1:T(8,128)(2,1)S(1)} %constant_dynamic-update-slice_fusion.7, bf16[128,2,1024]{0,2,1:T(8,128)(2,1)} %collective-permute-done.2), kind=kLoop, calls=%fused_computation.69 | loop fusion | bytes 1048576
  82.0 1.2 %constant_dynamic-update-slice_fusion.1 = bf16[1024,2,1024]{0,2,1:T(8,128)(2,1)S(1)} fusion(bf16[1024,2,1024]{0,2,1:T(8,128)(2,1)S(1)} %constant_dynamic-update-slice_fusion.2, bf16[128,2,1024]{0,2,1:T(8,128)(2,1)} %collective-permute-done.5), kind=kLoop, calls=%fused_computation.64 | loop fusion | bytes 1048576
  83.9 0.7 fusion.37
  84.6 2.2 %multiply_reduce_fusion = (f32[8,128]{1,0:T(8,128)S(1)}, f32[8,128,1024]{2,1,0:T(8,128)S(1)}) fusion(f32[128,1024]{1,0:T(8,128)S(1)} %fusion.33, f32[8,128,1024]{2,1,0:T(8,128)S(1)} %fusion.37, pred[128,1024]{1,0:T(8,128)(4,1)S(1)} %fusion.34), kind=kOutput, calls=%fused_computation.4 | output fusion | flops 7341055 | bytes 9048064 | tf_op jit(solution)/shard_map/sub | solution.py:274
  86.8 0.8 fusion.5
  87.6 1.1 %fusion.24 = bf16[128,8,128]{0,2,1:T(8,128)(2,1)S(1)} fusion(f32[8,128,128]{2,1,0:T(8,128)S(1)} %fusion.5, bf16[1024,8,128]{0,2,1:T(8,128)(2,1)S(1)} %bitcast.86, f32[8,128,1024]{2,1,0:T(8,128)S(1)} %get-tuple-element.11, f32[128,1024]{1,0:T(8,128)S(1)} %fusion.33, pred[]{:T(512)S(6)} %eq.210, f32[128,8]{0,1:T(8,128)S(1)} %bitcast.99), kind=kOutput, calls=%fused_computation.31 | convolution fusion | flops 274071552 | bytes 7606273 | tf_op jit(solution)/shard_map/hqk,khd->qhd/dot_general | solution.py:281
  88.9 1.5 %slice-done.1 = s8[4194304]{0:T(1024)(128)(4,1)S(1)} async-done(((s8[8388608]{0:T(1024)(128)(4,1)}), s8[4194304]{0:T(1024)(128)(4,1)S(1)}, s32[]{:S(2)}) %slice-start.1) | async-done | bytes 4194328
  90.4 1.3 %fusion.64 = f32[128,4096]{1,0:T(8,128)S(1)} fusion(bf16[128,1024]{0,1:T(8,128)(2,1)S(1)} %bitcast.88, bf16[1024,4096]{1,0:T(8,128)(2,1)S(1)} %bitcast.81), kind=kOutput, calls=%fused_computation.138 | convolution fusion | flops 1073741824 | bytes 10747904 | tf_op jit(solution)/shard_map/dot_general | solution.py:287
  91.9 1.9 %collective-permute-done.7 = bf16[2,32,4096]{2,1,0:T(8,128)(2,1)S(1)} collective-permute-done((bf16[2,32,4096]{2,1,0:T(8,128)(2,1)S(1)}, bf16[2,32,4096]{2,1,0:T(8,128)(2,1)S(1)}, u32[]{:S(2)}, u32[]{:S(2)}) %collective-permute-start.7) | collective-permute-done | bytes 524320 | tf_op jit(solution)/shard_map/ppermute | solution.py:306
  94.0 1.6 %collective-permute-start.8 = (bf16[1,32,4096]{2,1,0:T(8,128)(2,1)S(1)}, bf16[1,32,4096]{2,1,0:T(8,128)(2,1)S(1)}, u32[]{:S(2)}, u32[]{:S(2)}) collective-permute-start(bf16[1,32,4096]{2,1,0:T(8,128)(2,1)S(1)} %fusion.35), channel_id=1, source_target_pairs={{0,2},{1,3},{2,0},{3,1},{4,6},{5,7},{6,4},{7,5},{8,10},{9,11},{10,... | collective-permute-start | bytes 786440 | tf_op jit(solution)/shard_map/ppermute | solution.py:306
  95.5 6.9 %collective-permute-done.8 = bf16[1,32,4096]{2,1,0:T(8,128)(2,1)S(1)} collective-permute-done((bf16[1,32,4096]{2,1,0:T(8,128)(2,1)S(1)}, bf16[1,32,4096]{2,1,0:T(8,128)(2,1)S(1)}, u32[]{:S(2)}, u32[]{:S(2)}) %collective-permute-start.8) | collective-permute-done | bytes 262176 | tf_op jit(solution)/shard_map/ppermute | solution.py:306
  102.4 0.8 fusion.36
  (62 shorter events, 6.2 us)
Async XLA Ops:
  0.0 38.6 %copy-start.6 = (s32[8]{0:T(128)S(1)}, s32[8]{0:T(128)}, u32[]{:S(2)}) copy-start(s32[8]{0:T(128)} %constant.130.clone) | copy-start | bytes 100
  0.0 39.2 %copy-start.5 = (s32[8]{0:T(128)S(1)}, s32[8]{0:T(128)}, u32[]{:S(2)}) copy-start(s32[8]{0:T(128)} %constant.132.clone) | copy-start | bytes 100
  0.0 39.9 %copy-start = (s32[8]{0:T(128)S(1)}, s32[8]{0:T(128)}, u32[]{:S(2)}) copy-start(s32[8]{0:T(128)} %constant.131.clone) | copy-start | bytes 100
  0.0 14.7 %copy-start.2 = (s32[128]{0:T(128)S(1)}, s32[128]{0:T(128)}, u32[]{:S(2)}) copy-start(s32[128]{0:T(128)} %param.10) | copy-start | bytes 1540
  0.0 40.6 %copy-start.3 = (s32[8]{0:T(128)S(1)}, s32[8]{0:T(128)}, u32[]{:S(2)}) copy-start(s32[8]{0:T(128)} %param.13) | copy-start | bytes 100
  0.0 41.2 %copy-start.4 = (s32[4]{0:T(128)S(1)}, s32[4]{0:T(128)}, u32[]{:S(2)}) copy-start(s32[4]{0:T(128)} %param.11) | copy-start | bytes 52
  0.0 41.4 %copy-start.1 = (s32[8,3]{0,1:T(4,128)S(1)}, s32[8,3]{0,1:T(4,128)}, u32[]{:S(2)}) copy-start(s32[8,3]{0,1:T(4,128)} %param.12) | copy-start | bytes 292
  1.5 43.5 %collective-permute-start = (bf16[128,2,1024]{0,2,1:T(8,128)(2,1)S(1)}, bf16[128,2,1024]{0,2,1:T(8,128)(2,1)S(1)}, u32[]{:S(2)}, u32[]{:S(2)}) collective-permute-start(bf16[128,2,1024]{0,2,1:T(8,128)(2,1)S(1)} %copy.49), channel_id=1, source_target_pairs={{0,8},{8,16},{16,24},{24,28},{28,20},{20,12},{12,4},{4,0},{1,9},{9... | collective-permute-start | bytes 1572872 | tf_op jit(solution)/shard_map/ppermute | solution.py:195
  4.6 54.2 %collective-permute-start.4 = (bf16[128,2,1024]{0,2,1:T(8,128)(2,1)S(1)}, bf16[128,2,1024]{0,2,1:T(8,128)(2,1)S(1)}, u32[]{:S(2)}, u32[]{:S(2)}) collective-permute-start(bf16[128,2,1024]{0,2,1:T(8,128)(2,1)S(1)} %copy.49), channel_id=1, source_target_pairs={{0,4},{8,0},{16,8},{24,16},{28,24},{20,28},{12,20},{4,12},{1,5},{9... | collective-permute-start | bytes 1572872 | tf_op jit(solution)/shard_map/ppermute | solution.py:198
  8.4 63.1 %all-to-all-start = ((bf16[8,32,1024]{2,1,0:T(8,128)(2,1)}), bf16[8,32,1024]{2,1,0:T(8,128)(2,1)S(1)}, u32[]{:S(2)}, u32[]{:S(2)}) async-start(bf16[8,32,1024]{2,1,0:T(8,128)(2,1)} %bitcast.14), calls=%async_computation | async-start | bytes 1048576 | tf_op jit(solution)/shard_map/all_to_all | solution.py:232
  44.9 12.1 %collective-permute-start.1 = (bf16[128,2,1024]{0,2,1:T(8,128)(2,1)S(1)}, bf16[128,2,1024]{0,2,1:T(8,128)(2,1)S(1)}, u32[]{:S(2)}, u32[]{:S(2)}) collective-permute-start(bf16[128,2,1024]{0,2,1:T(8,128)(2,1)S(1)} %collective-permute-done), channel_id=1, source_target_pairs={{0,8},{8,16},{16,24},{24,28},{28,20},{20,12},{12,4},{4,0},{1,9},{9... | collective-permute-start | bytes 1572872 | tf_op jit(solution)/shard_map/ppermute | solution.py:195
  57.1 12.3 %collective-permute-start.2 = (bf16[128,2,1024]{0,2,1:T(8,128)(2,1)S(1)}, bf16[128,2,1024]{0,2,1:T(8,128)(2,1)}, u32[]{:S(2)}, u32[]{:S(2)}) collective-permute-start(bf16[128,2,1024]{0,2,1:T(8,128)(2,1)S(1)} %collective-permute-done.1), channel_id=1, source_target_pairs={{0,8},{8,16},{16,24},{24,28},{28,20},{20,12},{12,4},{4,0},{1,9},{9... | collective-permute-start | bytes 1572872 | tf_op jit(solution)/shard_map/ppermute | solution.py:195
  58.7 13.0 %collective-permute-start.5 = (bf16[128,2,1024]{0,2,1:T(8,128)(2,1)S(1)}, bf16[128,2,1024]{0,2,1:T(8,128)(2,1)}, u32[]{:S(2)}, u32[]{:S(2)}) collective-permute-start(bf16[128,2,1024]{0,2,1:T(8,128)(2,1)S(1)} %collective-permute-done.4), channel_id=1, source_target_pairs={{0,4},{8,0},{16,8},{24,16},{28,24},{20,28},{12,20},{4,12},{1,5},{9... | collective-permute-start | bytes 1572872 | tf_op jit(solution)/shard_map/ppermute | solution.py:198
  69.3 9.5 %collective-permute-start.3 = (bf16[128,2,1024]{0,2,1:T(8,128)(2,1)}, bf16[128,2,1024]{0,2,1:T(8,128)(2,1)}, u32[]{:S(2)}, u32[]{:S(2)}) collective-permute-start(bf16[128,2,1024]{0,2,1:T(8,128)(2,1)} %collective-permute-done.2), channel_id=1, source_target_pairs={{0,8},{8,16},{16,24},{24,28},{28,20},{20,12},{12,4},{4,0},{1,9},{9... | collective-permute-start | bytes 1572872 | tf_op jit(solution)/shard_map/ppermute | solution.py:195
  71.8 11.5 %collective-permute-start.6 = (bf16[128,2,1024]{0,2,1:T(8,128)(2,1)}, bf16[128,2,1024]{0,2,1:T(8,128)(2,1)S(1)}, u32[]{:S(2)}, u32[]{:S(2)}) collective-permute-start(bf16[128,2,1024]{0,2,1:T(8,128)(2,1)} %collective-permute-done.5), channel_id=1, source_target_pairs={{0,4},{8,0},{16,8},{24,16},{28,24},{20,28},{12,20},{4,12},{1,5},{9... | collective-permute-start | bytes 1572872 | tf_op jit(solution)/shard_map/ppermute | solution.py:198
  86.7 2.2 %slice-start = ((s8[8388608]{0:T(1024)(128)(4,1)}), s8[4194304]{0:T(1024)(128)(4,1)S(1)}, s32[]{:S(2)}) async-start(s8[8388608]{0:T(1024)(128)(4,1)} %bitcast.80), calls=%async_computation.1 | async-start | bytes 8388608
  87.6 2.9 %slice-start.1 = ((s8[8388608]{0:T(1024)(128)(4,1)}), s8[4194304]{0:T(1024)(128)(4,1)S(1)}, s32[]{:S(2)}) async-start(s8[8388608]{0:T(1024)(128)(4,1)} %bitcast.80), calls=%async_computation.2 | async-start | bytes 8388608
  91.8 2.0 %collective-permute-start.7 = (bf16[2,32,4096]{2,1,0:T(8,128)(2,1)S(1)}, bf16[2,32,4096]{2,1,0:T(8,128)(2,1)S(1)}, u32[]{:S(2)}, u32[]{:S(2)}) collective-permute-start(bf16[2,32,4096]{2,1,0:T(8,128)(2,1)S(1)} %fusion.31), channel_id=1, source_target_pairs={{0,1},{1,0},{2,3},{3,2},{4,5},{5,4},{6,7},{7,6},{8,9},{9,8},{10,11... | collective-permute-start | bytes 1572872 | tf_op jit(solution)/shard_map/ppermute | solution.py:306
  94.0 8.4 %collective-permute-start.8 = (bf16[1,32,4096]{2,1,0:T(8,128)(2,1)S(1)}, bf16[1,32,4096]{2,1,0:T(8,128)(2,1)S(1)}, u32[]{:S(2)}, u32[]{:S(2)}) collective-permute-start(bf16[1,32,4096]{2,1,0:T(8,128)(2,1)S(1)} %fusion.35), channel_id=1, source_target_pairs={{0,2},{1,3},{2,0},{3,1},{4,6},{5,7},{6,4},{7,5},{8,10},{9,11},{10,... | collective-permute-start | bytes 786440 | tf_op jit(solution)/shard_map/ppermute | solution.py:306

commit v11 on v10

--- a/solution.py
+++ b/solution.py
@@ -192,13 +192,15 @@
     moving_right = block
     moving_left = block
     for step in range(1, owners // 2 + 1):
-        moving_right = lax.ppermute(moving_right, "seq", right)
+        moving_right = jax.tree.map(lambda x: lax.ppermute(x, "seq", right), moving_right)
         pieces[-step] = moving_right
         if step <= (owners - 1) // 2:
-            moving_left = lax.ppermute(moving_left, "seq", left)
+            moving_left = jax.tree.map(lambda x: lax.ppermute(x, "seq", left), moving_left)
             pieces[step] = moving_left
     offsets = sorted(pieces)
-    stacked = jnp.concatenate([pieces[k] for k in offsets], axis=0)
+    stacked = jax.tree.map(
+        lambda *parts: jnp.concatenate(parts, axis=0), *[pieces[k] for k in offsets]
+    )
     where = jnp.asarray(place, jnp.int32)[own_index]
     order = jnp.asarray(ring, jnp.int32)[(where + jnp.asarray(offsets, jnp.int32)) % owners]
     return stacked, order
@@ -214,9 +216,10 @@
     blocks_all = tokens // BLK
     score_scale = 1.0 / math.sqrt(HD)
     capacity = 2 * (tok_dev // owners)
-    arrival_dest = lax.all_gather(destination, "seq", tiled=True)
-    keyval, key_order = ring_gather(projected[:, 1:, :], own_index, owners)
-    key_dest = arrival_dest.reshape(owners, tok_dev)[key_order].reshape(-1)
+    (keyval, key_dest), key_order = ring_gather(
+        (projected[:, 1:, :], destination), own_index, owners
+    )
+    arrival_dest = key_dest
     target_all = arrival_dest.reshape(owners, tok_dev) // tok_dev
     onehot = (target_all[:, :, None] == jnp.arange(owners, dtype=jnp.int32)).astype(jnp.int32)
     slot_all = jnp.sum((jnp.cumsum(onehot, axis=1) - onehot) * onehot, axis=2)
@@ -231,7 +234,7 @@
     outgoing = outgoing.astype(projected.dtype).reshape(owners, capacity, columns)
     incoming = lax.all_to_all(outgoing, "seq", split_axis=0, concat_axis=0, tiled=True)
     my_pos = own_index * tok_dev + jnp.arange(tok_dev, dtype=jnp.int32)
-    source = jnp.arange(tokens, dtype=jnp.int32) // tok_dev
+    source = jnp.repeat(key_order, tok_dev)
     land_col = (source * capacity + slot_all.reshape(-1))[None, :]
     hit = arrival_dest[None, :] == my_pos[:, None]
     col_of_pos = jnp.sum(jnp.where(hit, land_col, 0), axis=1)

time: 104 us -> 103 us (level)
  blocking collectives: 23.9 us -> 0 us
  starting transfers between devices: 16.4 us -> 29 us
  waiting for transfers between devices: 35.3 us -> 41.9 us
  local copies, waits for them, and re-layouts: 11 us -> 12.4 us
  between operations: 0.42 us -> 1.64 us
    all_gather x1 -> x0, blocking collectives: 23.9 us -> none  [gathered_plan(): arrival_dest = lax.all_gather(destination, 'seq', tiled=True)]
    ppermute x7 -> x14, starting transfers between devices: 8.54 us -> 21.3 us  [the longest x8 19.2 us: ring_gather(): lax.ppermute(x, 'seq', right)]
    ppermute x7 -> x14, waiting for transfers between devices: 26.5 us -> 33.1 us  [the longest x8 33 us: ring_gather(): lax.ppermute(x, 'seq', right)]
    unnamed x27 -> x21, local copies, waits for them, and re-layouts: 6.47 us -> 7.15 us
  transfers between devices with their start and end apart: 10 -> 17, of which waited for: 5 -> 10; matrix products, arithmetic and copies ran while one was open for 16% -> 18% of each run, Pallas kernels for 0% -> 0%
where the time goes in v11:
time: 103 us; the launch traced here: 102 us
  waiting for transfers between devices  41.9 us (41%)
  starting transfers between devices  29 us (28%)
  local copies, waits for them, and re-layouts  12.4 us (12%)
  other arithmetic  10.6 us (10%)
  matrix products  6.23 us (6%)
  between operations  1.64 us (2%)
    ppermute x8, waiting for transfers between devices, ring_gather(): lax.ppermute(x, 'seq', right)  33 us
    ppermute x8, starting transfers between devices, ring_gather(): lax.ppermute(x, 'seq', right)  19.2 us
    ppermute x2, waiting for transfers between devices, head_sum(): got = lax.ppermute(send, 'head', [(i, i ^ bit) for i in range(members)])  8.75 us
    unnamed x21, local copies, waits for them, and re-layouts  7.15 us
    all_to_all x1, starting transfers between devices, gathered_plan(): lax.all_to_all(outgoing, 'seq', split_axis=0, concat_axis=0, tiled=True)  6.05 us
    another operation x1, other arithmetic, gathered_plan(): slot_all = jnp.sum((jnp.cumsum(onehot, axis=1) - onehot) * onehot, axis=2)  2.52 us
    sub x1, other arithmetic, gathered_plan(): near_exp = jnp.exp(near_scores - row_peak[..., None])  2.18 us
    ppermute x6, starting transfers between devices, ring_gather(): lax.ppermute(x, 'seq', left)  2.11 us
  transfers between devices with their start and end apart: 17, of which 10 were waited for; matrix products, arithmetic and copies ran while one was open for 18% of the time, Pallas kernels for 0%

profile of v11, /device:TPU:0, one launch (start us, length us, event | category | flops | bytes accessed | tf_op | source)
XLA Modules:
  0.0 101.8 jit_solution(9472194437471615863)
XLA Ops:
  0.0 1.1 %slice.41 = bf16[128,2,1024]{2,0,1:T(8,128)(2,1)S(1)} slice(bf16[128,3,1024]{2,0,1:T(8,128)(2,1)} %param.9), slice={[0:128], [1:3], [0:1024]} | slice | bytes 1048576 | tf_op jit(solution)/shard_map/slice | solution.py:220
  1.4 3.1 %collective-permute-start = (bf16[128,2,1024]{0,2,1:T(8,128)(2,1)S(1)}, bf16[128,2,1024]{0,2,1:T(8,128)(2,1)S(1)}, u32[]{:S(2)}, u32[]{:S(2)}) collective-permute-start(bf16[128,2,1024]{0,2,1:T(8,128)(2,1)S(1)} %copy.55), channel_id=1, source_target_pairs={{0,8},{8,16},{16,24},{24,28},{28,20},{20,12},{12,4},{4,0},{1,9},{9... | collective-permute-start | bytes 1572872 | tf_op jit(solution)/shard_map/ppermute | solution.py:195
  4.5 2.0 %collective-permute-start.7 = (s32[128]{0:T(128)}, s32[128]{0:T(128)S(1)}, u32[]{:S(2)}, u32[]{:S(2)}) collective-permute-start(s32[128]{0:T(128)} %param.10), channel_id=1, source_target_pairs={{0,8},{8,16},{16,24},{24,28},{28,20},{20,12},{12,4},{4,0},{1,9},{9... | collective-permute-start | bytes 1544 | tf_op jit(solution)/shard_map/ppermute | solution.py:195
  6.5 0.8 reduce-window.8
  8.1 1.2 %dynamic_slice.3 = s32[1]{0:T(128)} dynamic-slice(s32[8]{0:T(128)} %constant.121.clone, s32[]{:T(128)S(6)} %select_n.196), dynamic_slice_sizes={1} | dynamic-slice | bytes 12 | tf_op jit(solution)/shard_map/dynamic_slice | solution.py:204
  9.3 1.3 %compare_select_fusion = s32[8]{0:T(128)S(1)} fusion(s32[8]{0:T(128)} %constant.123.clone, s32[]{:T(128)} %bitcast.5), kind=kLoop, calls=%fused_computation.97 | loop fusion | flops 120 | bytes 68 | tf_op jit(solution)/shard_map/select_n | solution.py:205
  11.5 1.3 %gather_fusion.1 = s32[8]{0:T(128)S(1)} fusion(s32[8]{0:T(128)} %constant.122.clone, s32[1024]{0:T(1024)S(1)} %get-tuple-element.16), kind=kCustom, calls=%fused_computation.1 | custom fusion | bytes 96 | tf_op jit(solution)/shard_map/gather | solution.py:205
  12.9 3.5 %collective-permute-done.7 = s32[128]{0:T(128)S(1)} collective-permute-done((s32[128]{0:T(128)}, s32[128]{0:T(128)S(1)}, u32[]{:S(2)}, u32[]{:S(2)}) %collective-permute-start.7) | collective-permute-done | bytes 544 | tf_op jit(solution)/shard_map/ppermute | solution.py:195
  16.4 1.8 %collective-permute-start.8 = (s32[128]{0:T(128)S(1)}, s32[128]{0:T(128)S(1)}, u32[]{:S(2)}, u32[]{:S(2)}) collective-permute-start(s32[128]{0:T(128)S(1)} %collective-permute-done.7), channel_id=1, source_target_pairs={{0,8},{8,16},{16,24},{24,28},{28,20},{20,12},{12,4},{4,0},{1,9},{9... | collective-permute-start | bytes 1544 | tf_op jit(solution)/shard_map/ppermute | solution.py:195
  18.2 1.7 %collective-permute-done.8 = s32[128]{0:T(128)S(1)} collective-permute-done((s32[128]{0:T(128)S(1)}, s32[128]{0:T(128)S(1)}, u32[]{:S(2)}, u32[]{:S(2)}) %collective-permute-start.8) | collective-permute-done | bytes 544 | tf_op jit(solution)/shard_map/ppermute | solution.py:195
  19.9 1.8 %collective-permute-start.9 = (s32[128]{0:T(128)S(1)}, s32[128]{0:T(128)S(1)}, u32[]{:S(2)}, u32[]{:S(2)}) collective-permute-start(s32[128]{0:T(128)S(1)} %collective-permute-done.8), channel_id=1, source_target_pairs={{0,8},{8,16},{16,24},{24,28},{28,20},{20,12},{12,4},{4,0},{1,9},{9... | collective-permute-start | bytes 1544 | tf_op jit(solution)/shard_map/ppermute | solution.py:195
  23.5 1.8 %collective-permute-start.10 = (s32[128]{0:T(128)S(1)}, s32[128]{0:T(128)S(1)}, u32[]{:S(2)}, u32[]{:S(2)}) collective-permute-start(s32[128]{0:T(128)S(1)} %collective-permute-done.9), channel_id=1, source_target_pairs={{0,8},{8,16},{16,24},{24,28},{28,20},{20,12},{12,4},{4,0},{1,9},{9... | collective-permute-start | bytes 1544 | tf_op jit(solution)/shard_map/ppermute | solution.py:195
  28.2 2.1 %convolution_convert_fusion = bf16[256,1024]{1,0:T(8,128)(2,1)} fusion(bf16[128,3,1024]{2,0,1:T(8,128)(2,1)} %param.9, s32[128]{0:T(128)S(1)} %multiply_add_fusion), kind=kOutput, calls=%fused_computation.19 | convolution fusion | flops 67403776 | bytes 786944 | tf_op jit(solution)/shard_map/dot_general | solution.py:233
  30.2 6.1 %all-to-all-start = ((bf16[8,32,1024]{2,1,0:T(8,128)(2,1)}), bf16[8,32,1024]{2,1,0:T(8,128)(2,1)S(1)}, u32[]{:S(2)}, u32[]{:S(2)}) async-start(bf16[8,32,1024]{2,1,0:T(8,128)(2,1)} %bitcast.16), calls=%async_computation | async-start | bytes 1048576 | tf_op jit(solution)/shard_map/all_to_all | solution.py:235
  36.5 2.5 %select_reduce_fusion.1 = s32[8,128]{0,1:T(8,128)S(1)} fusion(s32[8,128]{0,1:T(8,128)S(1)} %copy.48), kind=kOutput, calls=%fused_computation.39 | output fusion | flops 1096704 | bytes 8192 | tf_op jit(solution)/shard_map/jit(cumsum)/reduce_window_sum | solution.py:225
  39.0 2.0 %collective-permute-start.1 = (bf16[128,2,1024]{0,2,1:T(8,128)(2,1)S(1)}, bf16[128,2,1024]{0,2,1:T(8,128)(2,1)S(1)}, u32[]{:S(2)}, u32[]{:S(2)}) collective-permute-start(bf16[128,2,1024]{0,2,1:T(8,128)(2,1)S(1)} %collective-permute-done), channel_id=1, source_target_pairs={{0,8},{8,16},{16,24},{24,28},{28,20},{20,12},{12,4},{4,0},{1,9},{9... | collective-permute-start | bytes 1572872 | tf_op jit(solution)/shard_map/ppermute | solution.py:195
  41.1 10.9 %collective-permute-done.1 = bf16[128,2,1024]{0,2,1:T(8,128)(2,1)S(1)} collective-permute-done((bf16[128,2,1024]{0,2,1:T(8,128)(2,1)S(1)}, bf16[128,2,1024]{0,2,1:T(8,128)(2,1)S(1)}, u32[]{:S(2)}, u32[]{:S(2)}) %collective-permute-start.1) | collective-permute-done | bytes 524320 | tf_op jit(solution)/shard_map/ppermute | solution.py:195
  52.0 4.3 %collective-permute-start.2 = (bf16[128,2,1024]{0,2,1:T(8,128)(2,1)S(1)}, bf16[128,2,1024]{0,2,1:T(8,128)(2,1)}, u32[]{:S(2)}, u32[]{:S(2)}) collective-permute-start(bf16[128,2,1024]{0,2,1:T(8,128)(2,1)S(1)} %collective-permute-done.1), channel_id=1, source_target_pairs={{0,8},{8,16},{16,24},{24,28},{28,20},{20,12},{12,4},{4,0},{1,9},{9... | collective-permute-start | bytes 1572872 | tf_op jit(solution)/shard_map/ppermute | solution.py:195
  57.0 8.7 %collective-permute-done.2 = bf16[128,2,1024]{0,2,1:T(8,128)(2,1)} collective-permute-done((bf16[128,2,1024]{0,2,1:T(8,128)(2,1)S(1)}, bf16[128,2,1024]{0,2,1:T(8,128)(2,1)}, u32[]{:S(2)}, u32[]{:S(2)}) %collective-permute-start.2) | collective-permute-done | bytes 524320 | tf_op jit(solution)/shard_map/ppermute | solution.py:195
  65.7 2.4 %collective-permute-start.3 = (bf16[128,2,1024]{0,2,1:T(8,128)(2,1)}, bf16[128,2,1024]{0,2,1:T(8,128)(2,1)}, u32[]{:S(2)}, u32[]{:S(2)}) collective-permute-start(bf16[128,2,1024]{0,2,1:T(8,128)(2,1)} %collective-permute-done.2), channel_id=1, source_target_pairs={{0,8},{8,16},{16,24},{24,28},{28,20},{20,12},{12,4},{4,0},{1,9},{9... | collective-permute-start | bytes 1572872 | tf_op jit(solution)/shard_map/ppermute | solution.py:195
  69.2 1.5 %collective-permute-start.6 = (bf16[128,2,1024]{0,2,1:T(8,128)(2,1)}, bf16[128,2,1024]{0,2,1:T(8,128)(2,1)S(1)}, u32[]{:S(2)}, u32[]{:S(2)}) collective-permute-start(bf16[128,2,1024]{0,2,1:T(8,128)(2,1)} %collective-permute-done.5), channel_id=1, source_target_pairs={{0,4},{8,0},{16,8},{24,16},{28,24},{20,28},{12,20},{4,12},{1,5},{9... | collective-permute-start | bytes 1572872 | tf_op jit(solution)/shard_map/ppermute | solution.py:198
  70.7 6.7 %collective-permute-done.3 = bf16[128,2,1024]{0,2,1:T(8,128)(2,1)} collective-permute-done((bf16[128,2,1024]{0,2,1:T(8,128)(2,1)}, bf16[128,2,1024]{0,2,1:T(8,128)(2,1)}, u32[]{:S(2)}, u32[]{:S(2)}) %collective-permute-start.3) | collective-permute-done | bytes 524320 | tf_op jit(solution)/shard_map/ppermute | solution.py:195
  77.4 1.2 %constant_dynamic-update-slice_fusion.7 = bf16[1024,2,1024]{0,2,1:T(8,128)(2,1)S(1)} fusion(bf16[128,2,1024]{0,2,1:T(8,128)(2,1)} %collective-permute-done.3), kind=kLoop, calls=%fused_computation.69 | loop fusion | bytes 1048576
  78.6 1.2 %constant_dynamic-update-slice_fusion.6 = bf16[1024,2,1024]{0,2,1:T(8,128)(2,1)S(1)} fusion(bf16[1024,2,1024]{0,2,1:T(8,128)(2,1)S(1)} %constant_dynamic-update-slice_fusion.7, bf16[128,2,1024]{0,2,1:T(8,128)(2,1)} %collective-permute-done.2), kind=kLoop, calls=%fused_computation.68 | loop fusion | bytes 1048576
  80.6 1.2 %constant_dynamic-update-slice_fusion.1 = bf16[1024,2,1024]{0,2,1:T(8,128)(2,1)S(1)} fusion(bf16[1024,2,1024]{0,2,1:T(8,128)(2,1)S(1)} %constant_dynamic-update-slice_fusion.2, bf16[128,2,1024]{0,2,1:T(8,128)(2,1)} %collective-permute-done.5), kind=kLoop, calls=%fused_computation.63 | loop fusion | bytes 1048576
  83.2 2.2 %multiply_reduce_fusion = (f32[8,128]{1,0:T(8,128)S(1)}, f32[8,128,1024]{2,1,0:T(8,128)S(1)}) fusion(f32[128,1024]{1,0:T(8,128)S(1)} %fusion.33, f32[8,128,1024]{2,1,0:T(8,128)S(1)} %fusion.37, pred[128,1024]{1,0:T(8,128)(4,1)S(1)} %fusion.34), kind=kOutput, calls=%fused_computation.3 | output fusion | flops 7341055 | bytes 9048064 | tf_op jit(solution)/shard_map/sub | solution.py:277
  86.2 1.1 %fusion.24 = bf16[128,8,128]{0,2,1:T(8,128)(2,1)S(1)} fusion(f32[8,128,128]{2,1,0:T(8,128)S(1)} %fusion.5, bf16[1024,8,128]{0,2,1:T(8,128)(2,1)S(1)} %bitcast.84, f32[8,128,1024]{2,1,0:T(8,128)S(1)} %get-tuple-element.13, f32[128,1024]{1,0:T(8,128)S(1)} %fusion.33, pred[]{:T(512)S(6)} %eq.210, f32[128,8]{0,1:T(8,128)S(1)} %bitcast.100), kind=kOutput, calls=%fused_computation.30 | convolution fusion | flops 274071552 | bytes 7606273 | tf_op jit(solution)/shard_map/hqk,khd->qhd/dot_general | solution.py:284
  87.5 1.5 %slice-done.1 = s8[4194304]{0:T(1024)(128)(4,1)S(1)} async-done(((s8[8388608]{0:T(1024)(128)(4,1)}), s8[4194304]{0:T(1024)(128)(4,1)S(1)}, s32[]{:S(2)}) %slice-start.1) | async-done | bytes 4194328
  89.0 1.3 %fusion.58 = f32[128,4096]{1,0:T(8,128)S(1)} fusion(bf16[128,1024]{0,1:T(8,128)(2,1)S(1)} %bitcast.86, bf16[1024,4096]{1,0:T(8,128)(2,1)S(1)} %bitcast.79), kind=kOutput, calls=%fused_computation.135 | convolution fusion | flops 1073741824 | bytes 10747904 | tf_op jit(solution)/shard_map/dot_general | solution.py:290
  90.5 1.9 %collective-permute-done.14 = bf16[2,32,4096]{2,1,0:T(8,128)(2,1)S(1)} collective-permute-done((bf16[2,32,4096]{2,1,0:T(8,128)(2,1)S(1)}, bf16[2,32,4096]{2,1,0:T(8,128)(2,1)S(1)}, u32[]{:S(2)}, u32[]{:S(2)}) %collective-permute-start.14) | collective-permute-done | bytes 524320 | tf_op jit(solution)/shard_map/ppermute | solution.py:309
  92.6 1.6 %collective-permute-start.15 = (bf16[1,32,4096]{2,1,0:T(8,128)(2,1)S(1)}, bf16[1,32,4096]{2,1,0:T(8,128)(2,1)S(1)}, u32[]{:S(2)}, u32[]{:S(2)}) collective-permute-start(bf16[1,32,4096]{2,1,0:T(8,128)(2,1)S(1)} %fusion.35), channel_id=1, source_target_pairs={{0,2},{1,3},{2,0},{3,1},{4,6},{5,7},{6,4},{7,5},{8,10},{9,11},{10,... | collective-permute-start | bytes 786440 | tf_op jit(solution)/shard_map/ppermute | solution.py:309
  94.2 6.9 %collective-permute-done.15 = bf16[1,32,4096]{2,1,0:T(8,128)(2,1)S(1)} collective-permute-done((bf16[1,32,4096]{2,1,0:T(8,128)(2,1)S(1)}, bf16[1,32,4096]{2,1,0:T(8,128)(2,1)S(1)}, u32[]{:S(2)}, u32[]{:S(2)}) %collective-permute-start.15) | collective-permute-done | bytes 262176 | tf_op jit(solution)/shard_map/ppermute | solution.py:309
  (70 shorter events, 11.5 us)
Async XLA Ops:
  0.0 36.3 %copy-start = (s32[128]{0:T(128)S(1)}, s32[128]{0:T(128)}, u32[]{:S(2)}) copy-start(s32[128]{0:T(128)} %param.10) | copy-start | bytes 1540
  1.4 37.6 %collective-permute-start = (bf16[128,2,1024]{0,2,1:T(8,128)(2,1)S(1)}, bf16[128,2,1024]{0,2,1:T(8,128)(2,1)S(1)}, u32[]{:S(2)}, u32[]{:S(2)}) collective-permute-start(bf16[128,2,1024]{0,2,1:T(8,128)(2,1)S(1)} %copy.55), channel_id=1, source_target_pairs={{0,8},{8,16},{16,24},{24,28},{28,20},{20,12},{12,4},{4,0},{1,9},{9... | collective-permute-start | bytes 1572872 | tf_op jit(solution)/shard_map/ppermute | solution.py:195
  4.5 52.5 %collective-permute-start.4 = (bf16[128,2,1024]{0,2,1:T(8,128)(2,1)S(1)}, bf16[128,2,1024]{0,2,1:T(8,128)(2,1)S(1)}, u32[]{:S(2)}, u32[]{:S(2)}) collective-permute-start(bf16[128,2,1024]{0,2,1:T(8,128)(2,1)S(1)} %copy.55), channel_id=1, source_target_pairs={{0,4},{8,0},{16,8},{24,16},{28,24},{20,28},{12,20},{4,12},{1,5},{9... | collective-permute-start | bytes 1572872 | tf_op jit(solution)/shard_map/ppermute | solution.py:198
  4.5 11.9 %collective-permute-start.7 = (s32[128]{0:T(128)}, s32[128]{0:T(128)S(1)}, u32[]{:S(2)}, u32[]{:S(2)}) collective-permute-start(s32[128]{0:T(128)} %param.10), channel_id=1, source_target_pairs={{0,8},{8,16},{16,24},{24,28},{28,20},{20,12},{12,4},{4,0},{1,9},{9... | collective-permute-start | bytes 1544 | tf_op jit(solution)/shard_map/ppermute | solution.py:195
  6.5 15.9 %collective-permute-start.11 = (s32[128]{0:T(128)}, s32[128]{0:T(128)S(1)}, u32[]{:S(2)}, u32[]{:S(2)}) collective-permute-start(s32[128]{0:T(128)} %param.10), channel_id=1, source_target_pairs={{0,4},{8,0},{16,8},{24,16},{28,24},{20,28},{12,20},{4,12},{1,5},{9... | collective-permute-start | bytes 1544 | tf_op jit(solution)/shard_map/ppermute | solution.py:198
  16.4 3.5 %collective-permute-start.8 = (s32[128]{0:T(128)S(1)}, s32[128]{0:T(128)S(1)}, u32[]{:S(2)}, u32[]{:S(2)}) collective-permute-start(s32[128]{0:T(128)S(1)} %collective-permute-done.7), channel_id=1, source_target_pairs={{0,8},{8,16},{16,24},{24,28},{28,20},{20,12},{12,4},{4,0},{1,9},{9... | collective-permute-start | bytes 1544 | tf_op jit(solution)/shard_map/ppermute | solution.py:195
  19.9 3.5 %collective-permute-start.9 = (s32[128]{0:T(128)S(1)}, s32[128]{0:T(128)S(1)}, u32[]{:S(2)}, u32[]{:S(2)}) collective-permute-start(s32[128]{0:T(128)S(1)} %collective-permute-done.8), channel_id=1, source_target_pairs={{0,8},{8,16},{16,24},{24,28},{28,20},{20,12},{12,4},{4,0},{1,9},{9... | collective-permute-start | bytes 1544 | tf_op jit(solution)/shard_map/ppermute | solution.py:195
  22.4 3.6 %collective-permute-start.12 = (s32[128]{0:T(128)S(1)}, s32[128]{0:T(128)S(1)}, u32[]{:S(2)}, u32[]{:S(2)}) collective-permute-start(s32[128]{0:T(128)S(1)} %collective-permute-done.11), channel_id=1, source_target_pairs={{0,4},{8,0},{16,8},{24,16},{28,24},{20,28},{12,20},{4,12},{1,5},{9... | collective-permute-start | bytes 1544 | tf_op jit(solution)/shard_map/ppermute | solution.py:198
  23.5 3.5 %collective-permute-start.10 = (s32[128]{0:T(128)S(1)}, s32[128]{0:T(128)S(1)}, u32[]{:S(2)}, u32[]{:S(2)}) collective-permute-start(s32[128]{0:T(128)S(1)} %collective-permute-done.9), channel_id=1, source_target_pairs={{0,8},{8,16},{16,24},{24,28},{28,20},{20,12},{12,4},{4,0},{1,9},{9... | collective-permute-start | bytes 1544 | tf_op jit(solution)/shard_map/ppermute | solution.py:195
  26.0 10.3 %collective-permute-start.13 = (s32[128]{0:T(128)S(1)}, s32[128]{0:T(128)S(1)}, u32[]{:S(2)}, u32[]{:S(2)}) collective-permute-start(s32[128]{0:T(128)S(1)} %collective-permute-done.12), channel_id=1, source_target_pairs={{0,4},{8,0},{16,8},{24,16},{28,24},{20,28},{12,20},{4,12},{1,5},{9... | collective-permute-start | bytes 1544 | tf_op jit(solution)/shard_map/ppermute | solution.py:198
  30.2 38.7 %all-to-all-start = ((bf16[8,32,1024]{2,1,0:T(8,128)(2,1)}), bf16[8,32,1024]{2,1,0:T(8,128)(2,1)S(1)}, u32[]{:S(2)}, u32[]{:S(2)}) async-start(bf16[8,32,1024]{2,1,0:T(8,128)(2,1)} %bitcast.16), calls=%async_computation | async-start | bytes 1048576 | tf_op jit(solution)/shard_map/all_to_all | solution.py:235
  39.0 13.0 %collective-permute-start.1 = (bf16[128,2,1024]{0,2,1:T(8,128)(2,1)S(1)}, bf16[128,2,1024]{0,2,1:T(8,128)(2,1)S(1)}, u32[]{:S(2)}, u32[]{:S(2)}) collective-permute-start(bf16[128,2,1024]{0,2,1:T(8,128)(2,1)S(1)} %collective-permute-done), channel_id=1, source_target_pairs={{0,8},{8,16},{16,24},{24,28},{28,20},{20,12},{12,4},{4,0},{1,9},{9... | collective-permute-start | bytes 1572872 | tf_op jit(solution)/shard_map/ppermute | solution.py:195
  52.0 13.7 %collective-permute-start.2 = (bf16[128,2,1024]{0,2,1:T(8,128)(2,1)S(1)}, bf16[128,2,1024]{0,2,1:T(8,128)(2,1)}, u32[]{:S(2)}, u32[]{:S(2)}) collective-permute-start(bf16[128,2,1024]{0,2,1:T(8,128)(2,1)S(1)} %collective-permute-done.1), channel_id=1, source_target_pairs={{0,8},{8,16},{16,24},{24,28},{28,20},{20,12},{12,4},{4,0},{1,9},{9... | collective-permute-start | bytes 1572872 | tf_op jit(solution)/shard_map/ppermute | solution.py:195
  57.0 12.2 %collective-permute-start.5 = (bf16[128,2,1024]{0,2,1:T(8,128)(2,1)S(1)}, bf16[128,2,1024]{0,2,1:T(8,128)(2,1)}, u32[]{:S(2)}, u32[]{:S(2)}) collective-permute-start(bf16[128,2,1024]{0,2,1:T(8,128)(2,1)S(1)} %collective-permute-done.4), channel_id=1, source_target_pairs={{0,4},{8,0},{16,8},{24,16},{28,24},{20,28},{12,20},{4,12},{1,5},{9... | collective-permute-start | bytes 1572872 | tf_op jit(solution)/shard_map/ppermute | solution.py:198
  65.7 11.7 %collective-permute-start.3 = (bf16[128,2,1024]{0,2,1:T(8,128)(2,1)}, bf16[128,2,1024]{0,2,1:T(8,128)(2,1)}, u32[]{:S(2)}, u32[]{:S(2)}) collective-permute-start(bf16[128,2,1024]{0,2,1:T(8,128)(2,1)} %collective-permute-done.2), channel_id=1, source_target_pairs={{0,8},{8,16},{16,24},{24,28},{28,20},{20,12},{12,4},{4,0},{1,9},{9... | collective-permute-start | bytes 1572872 | tf_op jit(solution)/shard_map/ppermute | solution.py:195
  69.2 12.6 %collective-permute-start.6 = (bf16[128,2,1024]{0,2,1:T(8,128)(2,1)}, bf16[128,2,1024]{0,2,1:T(8,128)(2,1)S(1)}, u32[]{:S(2)}, u32[]{:S(2)}) collective-permute-start(bf16[128,2,1024]{0,2,1:T(8,128)(2,1)} %collective-permute-done.5), channel_id=1, source_target_pairs={{0,4},{8,0},{16,8},{24,16},{28,24},{20,28},{12,20},{4,12},{1,5},{9... | collective-permute-start | bytes 1572872 | tf_op jit(solution)/shard_map/ppermute | solution.py:198
  85.4 2.2 %slice-start = ((s8[8388608]{0:T(1024)(128)(4,1)}), s8[4194304]{0:T(1024)(128)(4,1)S(1)}, s32[]{:S(2)}) async-start(s8[8388608]{0:T(1024)(128)(4,1)} %bitcast.78), calls=%async_computation.1 | async-start | bytes 8388608
  86.2 2.9 %slice-start.1 = ((s8[8388608]{0:T(1024)(128)(4,1)}), s8[4194304]{0:T(1024)(128)(4,1)S(1)}, s32[]{:S(2)}) async-start(s8[8388608]{0:T(1024)(128)(4,1)} %bitcast.78), calls=%async_computation.2 | async-start | bytes 8388608
  90.4 2.0 %collective-permute-start.14 = (bf16[2,32,4096]{2,1,0:T(8,128)(2,1)S(1)}, bf16[2,32,4096]{2,1,0:T(8,128)(2,1)S(1)}, u32[]{:S(2)}, u32[]{:S(2)}) collective-permute-start(bf16[2,32,4096]{2,1,0:T(8,128)(2,1)S(1)} %fusion.31), channel_id=1, source_target_pairs={{0,1},{1,0},{2,3},{3,2},{4,5},{5,4},{6,7},{7,6},{8,9},{9,8},{10,11... | collective-permute-start | bytes 1572872 | tf_op jit(solution)/shard_map/ppermute | solution.py:309
  92.6 8.4 %collective-permute-start.15 = (bf16[1,32,4096]{2,1,0:T(8,128)(2,1)S(1)}, bf16[1,32,4096]{2,1,0:T(8,128)(2,1)S(1)}, u32[]{:S(2)}, u32[]{:S(2)}) collective-permute-start(bf16[1,32,4096]{2,1,0:T(8,128)(2,1)S(1)} %fusion.35), channel_id=1, source_target_pairs={{0,2},{1,3},{2,0},{3,1},{4,6},{5,7},{6,4},{7,5},{8,10},{9,11},{10,... | collective-permute-start | bytes 786440 | tf_op jit(solution)/shard_map/ppermute | solution.py:309

commit v12 on v11

--- a/solution.py
+++ b/solution.py
@@ -216,9 +216,16 @@
     blocks_all = tokens // BLK
     score_scale = 1.0 / math.sqrt(HD)
     capacity = 2 * (tok_dev // owners)
-    (keyval, key_dest), key_order = ring_gather(
-        (projected[:, 1:, :], destination), own_index, owners
-    )
+    lanes = jnp.arange(128, dtype=jnp.int32)[None, :]
+    dest_hi = jnp.where(lanes == 0, (destination // 32)[:, None], 0)
+    dest_lo = jnp.where(lanes == 0, (destination % 32)[:, None], 0)
+    tag = jnp.stack([dest_hi, dest_lo], axis=1).astype(projected.dtype)
+    message = jnp.concatenate([projected[:, 1:, :], tag], axis=2)
+    stacked, key_order = ring_gather(message, own_index, owners)
+    key_dest = stacked[:, 0, columns].astype(jnp.int32) * 32 + stacked[:, 1, columns].astype(
+        jnp.int32
+    )
+    keyval = stacked[:, :, :columns]
     arrival_dest = key_dest
     target_all = arrival_dest.reshape(owners, tok_dev) // tok_dev
     onehot = (target_all[:, :, None] == jnp.arange(owners, dtype=jnp.int32)).astype(jnp.int32)

time: 103 us -> 110 us (1.068)
  waiting for transfers between devices: 41.9 us -> 58 us
  starting transfers between devices: 29 us -> 18.5 us
  local copies, waits for them, and re-layouts: 12.4 us -> 16.1 us
  between operations: 1.64 us -> 0.43 us
    ppermute x6 -> x3, waiting for transfers between devices: 0.09 us -> 14.6 us  [ring_gather(): lax.ppermute(x, 'seq', left)]
    ppermute x8 -> x4, starting transfers between devices: 19.2 us -> 9.79 us  [ring_gather(): lax.ppermute(x, 'seq', right)]
    slice x1, local copies, waits for them, and re-layouts: 0.44 us -> 4.04 us  [gathered_plan(): keys = keyval[:, 0, :].reshape(tokens, heads_here, HD)]
    ppermute x8 -> x4, waiting for transfers between devices: 33 us -> 34.6 us  [ring_gather(): lax.ppermute(x, 'seq', right)]
    unnamed x21 -> x28, local copies, waits for them, and re-layouts: 7.15 us -> 8.55 us
    all_to_all x1, starting transfers between devices: 6.05 us -> 4.82 us  [gathered_plan(): lax.all_to_all(outgoing, 'seq', split_axis=0, concat_axis=0, tiled=True)]
    ppermute x6 -> x3, starting transfers between devices: 2.11 us -> 2.3 us  [ring_gather(): lax.ppermute(x, 'seq', left)]
  transfers between devices with their start and end apart: 17 -> 10, of which waited for: 10 -> 8; matrix products, arithmetic and copies ran while one was open for 18% -> 17% of each run, Pallas kernels for 0% -> 0%
where the time goes in v12:
time: 110 us
  waiting for transfers between devices  58 us (53%)
  starting transfers between devices  18.5 us (17%)
  local copies, waits for them, and re-layouts  16.1 us (15%)
  other arithmetic  10.5 us (10%)
  matrix products  6.28 us (6%)
    ppermute x4, waiting for transfers between devices, ring_gather(): lax.ppermute(x, 'seq', right)  34.6 us
    ppermute x3, waiting for transfers between devices, ring_gather(): lax.ppermute(x, 'seq', left)  14.6 us
    ppermute x4, starting transfers between devices, ring_gather(): lax.ppermute(x, 'seq', right)  9.79 us
    ppermute x2, waiting for transfers between devices, head_sum(): got = lax.ppermute(send, 'head', [(i, i ^ bit) for i in range(members)])  8.76 us
    unnamed x28, local copies, waits for them, and re-layouts  8.55 us
    all_to_all x1, starting transfers between devices, gathered_plan(): lax.all_to_all(outgoing, 'seq', split_axis=0, concat_axis=0, tiled=True)  4.82 us
    slice x1, local copies, waits for them, and re-layouts, gathered_plan(): keys = keyval[:, 0, :].reshape(tokens, heads_here, HD)  4.04 us
    another operation x1, other arithmetic, gathered_plan(): slot_all = jnp.sum((jnp.cumsum(onehot, axis=1) - onehot) * onehot, axis=2)  2.52 us
  transfers between devices with their start and end apart: 10, of which 8 were waited for; matrix products, arithmetic and copies ran while one was open for 17% of the time, Pallas kernels for 0%

profile of v12, /device:TPU:0, one launch (start us, length us, event | category | flops | bytes accessed | tf_op | source)
XLA Modules:
  0.0 109.8 jit_solution(4289463250426048031)
XLA Ops:
  0.0 0.7 and_select_fusion
  0.8 1.1 slice.50
  2.2 0.8 maximum_maximum_fusion
  3.1 3.0 %collective-permute-start = (bf16[128,2,1152]{0,2,1:T(8,128)(2,1)}, bf16[128,2,1152]{0,2,1:T(8,128)(2,1)S(1)}, u32[]{:S(2)}, u32[]{:S(2)}) collective-permute-start(bf16[128,2,1152]{0,2,1:T(8,128)(2,1)} %maximum_maximum_fusion), channel_id=1, source_target_pairs={{0,8},{8,16},{16,24},{24,28},{28,20},{20,12},{12,4},{4,0},{1,9},{9... | collective-permute-start | bytes 1769480 | tf_op jit(solution)/shard_map/ppermute | solution.py:195
  6.1 13.5 %collective-permute-done = bf16[128,2,1152]{0,2,1:T(8,128)(2,1)S(1)} collective-permute-done((bf16[128,2,1152]{0,2,1:T(8,128)(2,1)}, bf16[128,2,1152]{0,2,1:T(8,128)(2,1)S(1)}, u32[]{:S(2)}, u32[]{:S(2)}) %collective-permute-start) | collective-permute-done | bytes 589856 | tf_op jit(solution)/shard_map/ppermute | solution.py:195
  19.6 1.8 %collective-permute-start.1 = (bf16[128,2,1152]{0,2,1:T(8,128)(2,1)S(1)}, bf16[128,2,1152]{0,2,1:T(8,128)(2,1)S(1)}, u32[]{:S(2)}, u32[]{:S(2)}) collective-permute-start(bf16[128,2,1152]{0,2,1:T(8,128)(2,1)S(1)} %collective-permute-done), channel_id=1, source_target_pairs={{0,8},{8,16},{16,24},{24,28},{28,20},{20,12},{12,4},{4,0},{1,9},{9... | collective-permute-start | bytes 1769480 | tf_op jit(solution)/shard_map/ppermute | solution.py:195
  22.0 12.0 %collective-permute-done.1 = bf16[128,2,1152]{0,2,1:T(8,128)(2,1)S(1)} collective-permute-done((bf16[128,2,1152]{0,2,1:T(8,128)(2,1)S(1)}, bf16[128,2,1152]{0,2,1:T(8,128)(2,1)S(1)}, u32[]{:S(2)}, u32[]{:S(2)}) %collective-permute-start.1) | collective-permute-done | bytes 589856 | tf_op jit(solution)/shard_map/ppermute | solution.py:195
  34.1 1.5 %collective-permute-start.2 = (bf16[128,2,1152]{0,2,1:T(8,128)(2,1)S(1)}, bf16[128,2,1152]{0,2,1:T(8,128)(2,1)}, u32[]{:S(2)}, u32[]{:S(2)}) collective-permute-start(bf16[128,2,1152]{0,2,1:T(8,128)(2,1)S(1)} %collective-permute-done.1), channel_id=1, source_target_pairs={{0,8},{8,16},{16,24},{24,28},{28,20},{20,12},{12,4},{4,0},{1,9},{9... | collective-permute-start | bytes 1769480 | tf_op jit(solution)/shard_map/ppermute | solution.py:195
  35.6 2.1 %convolution_convert_fusion = bf16[256,1024]{1,0:T(8,128)(2,1)} fusion(bf16[128,3,1024]{2,0,1:T(8,128)(2,1)} %param.9, s32[128]{0:T(128)S(1)} %multiply_add_fusion), kind=kOutput, calls=%fused_computation.19 | convolution fusion | flops 67403776 | bytes 786944 | tf_op jit(solution)/shard_map/dot_general | solution.py:240
  37.6 4.8 %all-to-all-start = ((bf16[8,32,1024]{2,1,0:T(8,128)(2,1)}), bf16[8,32,1024]{2,1,0:T(8,128)(2,1)S(1)}, u32[]{:S(2)}, u32[]{:S(2)}) async-start(bf16[8,32,1024]{2,1,0:T(8,128)(2,1)} %bitcast.10), calls=%async_computation | async-start | bytes 1048576 | tf_op jit(solution)/shard_map/all_to_all | solution.py:242
  43.8 2.1 %collective-permute-start.5 = (bf16[128,2,1152]{0,2,1:T(8,128)(2,1)S(1)}, bf16[128,2,1152]{0,2,1:T(8,128)(2,1)}, u32[]{:S(2)}, u32[]{:S(2)}) collective-permute-start(bf16[128,2,1152]{0,2,1:T(8,128)(2,1)S(1)} %collective-permute-done.4), channel_id=1, source_target_pairs={{0,4},{8,0},{16,8},{24,16},{28,24},{20,28},{12,20},{4,12},{1,5},{9... | collective-permute-start | bytes 1769480 | tf_op jit(solution)/shard_map/ppermute | solution.py:198
  45.8 5.4 %collective-permute-done.2 = bf16[128,2,1152]{0,2,1:T(8,128)(2,1)} collective-permute-done((bf16[128,2,1152]{0,2,1:T(8,128)(2,1)S(1)}, bf16[128,2,1152]{0,2,1:T(8,128)(2,1)}, u32[]{:S(2)}, u32[]{:S(2)}) %collective-permute-start.2) | collective-permute-done | bytes 589856 | tf_op jit(solution)/shard_map/ppermute | solution.py:195
  51.2 3.5 %collective-permute-start.3 = (bf16[128,2,1152]{0,2,1:T(8,128)(2,1)}, bf16[128,2,1152]{0,2,1:T(8,128)(2,1)}, u32[]{:S(2)}, u32[]{:S(2)}) collective-permute-start(bf16[128,2,1152]{0,2,1:T(8,128)(2,1)} %collective-permute-done.2), channel_id=1, source_target_pairs={{0,8},{8,16},{16,24},{24,28},{28,20},{20,12},{12,4},{4,0},{1,9},{9... | collective-permute-start | bytes 1769480 | tf_op jit(solution)/shard_map/ppermute | solution.py:195
  56.7 7.2 %collective-permute-done.5 = bf16[128,2,1152]{0,2,1:T(8,128)(2,1)} collective-permute-done((bf16[128,2,1152]{0,2,1:T(8,128)(2,1)S(1)}, bf16[128,2,1152]{0,2,1:T(8,128)(2,1)}, u32[]{:S(2)}, u32[]{:S(2)}) %collective-permute-start.5) | collective-permute-done | bytes 589856 | tf_op jit(solution)/shard_map/ppermute | solution.py:198
  63.9 3.7 %collective-permute-done.3 = bf16[128,2,1152]{0,2,1:T(8,128)(2,1)} collective-permute-done((bf16[128,2,1152]{0,2,1:T(8,128)(2,1)}, bf16[128,2,1152]{0,2,1:T(8,128)(2,1)}, u32[]{:S(2)}, u32[]{:S(2)}) %collective-permute-start.3) | collective-permute-done | bytes 589856 | tf_op jit(solution)/shard_map/ppermute | solution.py:195
  67.6 1.2 %constant_dynamic-update-slice_fusion.7 = bf16[1024,2,1152]{0,2,1:T(8,128)(2,1)S(1)} fusion(bf16[128,2,1152]{0,2,1:T(8,128)(2,1)} %collective-permute-done.3), kind=kLoop, calls=%fused_computation.72 | loop fusion | bytes 1179648
  68.8 1.3 %constant_dynamic-update-slice_fusion.6 = bf16[1024,2,1152]{0,2,1:T(8,128)(2,1)S(1)} fusion(bf16[1024,2,1152]{0,2,1:T(8,128)(2,1)S(1)} %constant_dynamic-update-slice_fusion.7, bf16[128,2,1152]{0,2,1:T(8,128)(2,1)} %collective-permute-done.2), kind=kLoop, calls=%fused_computation.71 | loop fusion | bytes 1179648
  70.9 1.3 %constant_dynamic-update-slice_fusion.1 = bf16[1024,2,1152]{0,2,1:T(8,128)(2,1)S(1)} fusion(bf16[1024,2,1152]{0,2,1:T(8,128)(2,1)S(1)} %constant_dynamic-update-slice_fusion.2, bf16[128,2,1152]{0,2,1:T(8,128)(2,1)} %collective-permute-done.5), kind=kLoop, calls=%fused_computation.66 | loop fusion | bytes 1179648
  72.2 7.4 %collective-permute-done.6 = bf16[128,2,1152]{0,2,1:T(8,128)(2,1)S(1)} collective-permute-done((bf16[128,2,1152]{0,2,1:T(8,128)(2,1)}, bf16[128,2,1152]{0,2,1:T(8,128)(2,1)S(1)}, u32[]{:S(2)}, u32[]{:S(2)}) %collective-permute-start.6) | collective-permute-done | bytes 589856 | tf_op jit(solution)/shard_map/ppermute | solution.py:198
  79.8 2.1 %copy-done.2 = bf16[1024,2,1152]{0,2,1:T(8,128)(2,1)} copy-done((bf16[1024,2,1152]{0,2,1:T(8,128)(2,1)}, bf16[1024,2,1152]{0,2,1:T(8,128)(2,1)S(1)}, u32[]{:S(2)}) %copy-start.2) | copy-done | bytes 4718616
  82.1 2.5 %select_reduce_fusion.1 = s32[8,128]{0,1:T(8,128)S(1)} fusion(s32[8,128]{0,1:T(8,128)S(1)} %copy.51), kind=kOutput, calls=%fused_computation.40 | output fusion | flops 1096704 | bytes 8192 | tf_op jit(solution)/shard_map/jit(cumsum)/reduce_window_sum | solution.py:232
  86.2 4.0 %fusion.59 = (bf16[1024,1,1024]{0,2,1:T(8,128)(2,1)S(1)}, bf16[1024,1,1024]{0,2,1:T(8,128)(2,1)}) fusion(bf16[1024,2,1152]{0,2,1:T(8,128)(2,1)} %copy-done.2), kind=kLoop, calls=%fused_computation.139 | loop fusion | bytes 8388608 | tf_op jit(solution)/shard_map/slice | solution.py:255
  90.5 0.7 fusion.37
  91.2 2.2 %multiply_reduce_fusion = (f32[8,128]{1,0:T(8,128)S(1)}, f32[8,128,1024]{2,1,0:T(8,128)S(1)}) fusion(f32[128,1024]{1,0:T(8,128)S(1)} %fusion.33, f32[8,128,1024]{2,1,0:T(8,128)S(1)} %fusion.37, pred[128,1024]{1,0:T(8,128)(4,1)S(1)} %fusion.34), kind=kOutput, calls=%fused_computation.3 | output fusion | flops 7341055 | bytes 9048064 | tf_op jit(solution)/shard_map/sub | solution.py:284
  93.4 0.8 fusion.5
  94.2 1.1 %fusion.24 = bf16[128,8,128]{0,2,1:T(8,128)(2,1)S(1)} fusion(f32[8,128,128]{2,1,0:T(8,128)S(1)} %fusion.5, bf16[1024,8,128]{0,2,1:T(8,128)(2,1)S(1)} %bitcast.78, f32[8,128,1024]{2,1,0:T(8,128)S(1)} %get-tuple-element.16, f32[128,1024]{1,0:T(8,128)S(1)} %fusion.33, pred[]{:T(512)S(6)} %eq.223, f32[128,8]{0,1:T(8,128)S(1)} %bitcast.91), kind=kOutput, calls=%fused_computation.30 | convolution fusion | flops 274071552 | bytes 7606273 | tf_op jit(solution)/shard_map/hqk,khd->qhd/dot_general | solution.py:291
  95.6 1.5 %slice-done.1 = s8[4194304]{0:T(1024)(128)(4,1)S(1)} async-done(((s8[8388608]{0:T(1024)(128)(4,1)}), s8[4194304]{0:T(1024)(128)(4,1)S(1)}, s32[]{:S(2)}) %slice-start.1) | async-done | bytes 4194328
  97.0 1.3 %fusion.60 = f32[128,4096]{1,0:T(8,128)S(1)} fusion(bf16[128,1024]{0,1:T(8,128)(2,1)S(1)} %bitcast.80, bf16[1024,4096]{1,0:T(8,128)(2,1)S(1)} %bitcast.73), kind=kOutput, calls=%fused_computation.140 | convolution fusion | flops 1073741824 | bytes 10747904 | tf_op jit(solution)/shard_map/dot_general | solution.py:297
  98.5 1.9 %collective-permute-done.7 = bf16[2,32,4096]{2,1,0:T(8,128)(2,1)S(1)} collective-permute-done((bf16[2,32,4096]{2,1,0:T(8,128)(2,1)S(1)}, bf16[2,32,4096]{2,1,0:T(8,128)(2,1)S(1)}, u32[]{:S(2)}, u32[]{:S(2)}) %collective-permute-start.7) | collective-permute-done | bytes 524320 | tf_op jit(solution)/shard_map/ppermute | solution.py:316
  100.6 1.5 %collective-permute-start.8 = (bf16[1,32,4096]{2,1,0:T(8,128)(2,1)S(1)}, bf16[1,32,4096]{2,1,0:T(8,128)(2,1)S(1)}, u32[]{:S(2)}, u32[]{:S(2)}) collective-permute-start(bf16[1,32,4096]{2,1,0:T(8,128)(2,1)S(1)} %fusion.35), channel_id=1, source_target_pairs={{0,2},{1,3},{2,0},{3,1},{4,6},{5,7},{6,4},{7,5},{8,10},{9,11},{10,... | collective-permute-start | bytes 786440 | tf_op jit(solution)/shard_map/ppermute | solution.py:316
  102.2 6.9 %collective-permute-done.8 = bf16[1,32,4096]{2,1,0:T(8,128)(2,1)S(1)} collective-permute-done((bf16[1,32,4096]{2,1,0:T(8,128)(2,1)S(1)}, bf16[1,32,4096]{2,1,0:T(8,128)(2,1)S(1)}, u32[]{:S(2)}, u32[]{:S(2)}) %collective-permute-start.8) | collective-permute-done | bytes 262176 | tf_op jit(solution)/shard_map/ppermute | solution.py:316
  109.0 0.8 fusion.36
  (64 shorter events, 7.6 us)
Async XLA Ops:
  0.0 42.5 %copy-start.7 = (s32[8]{0:T(128)S(1)}, s32[8]{0:T(128)}, u32[]{:S(2)}) copy-start(s32[8]{0:T(128)} %constant.141.clone) | copy-start | bytes 100
  0.0 43.1 %copy-start.6 = (s32[8]{0:T(128)S(1)}, s32[8]{0:T(128)}, u32[]{:S(2)}) copy-start(s32[8]{0:T(128)} %constant.143.clone) | copy-start | bytes 100
  0.0 55.7 %copy-start = (s32[8]{0:T(128)S(1)}, s32[8]{0:T(128)}, u32[]{:S(2)}) copy-start(s32[8]{0:T(128)} %constant.142.clone) | copy-start | bytes 100
  0.0 54.7 %copy-start.4 = (s32[8]{0:T(128)S(1)}, s32[8]{0:T(128)}, u32[]{:S(2)}) copy-start(s32[8]{0:T(128)} %param.13) | copy-start | bytes 100
  0.0 54.8 %copy-start.5 = (s32[4]{0:T(128)S(1)}, s32[4]{0:T(128)}, u32[]{:S(2)}) copy-start(s32[4]{0:T(128)} %param.11) | copy-start | bytes 52
  0.0 55.0 %copy-start.3 = (s32[8,3]{0,1:T(4,128)S(1)}, s32[8,3]{0,1:T(4,128)}, u32[]{:S(2)}) copy-start(s32[8,3]{0,1:T(4,128)} %param.12) | copy-start | bytes 292
  3.1 16.5 %collective-permute-start = (bf16[128,2,1152]{0,2,1:T(8,128)(2,1)}, bf16[128,2,1152]{0,2,1:T(8,128)(2,1)S(1)}, u32[]{:S(2)}, u32[]{:S(2)}) collective-permute-start(bf16[128,2,1152]{0,2,1:T(8,128)(2,1)} %maximum_maximum_fusion), channel_id=1, source_target_pairs={{0,8},{8,16},{16,24},{24,28},{28,20},{20,12},{12,4},{4,0},{1,9},{9... | collective-permute-start | bytes 1769480 | tf_op jit(solution)/shard_map/ppermute | solution.py:195
  19.6 14.5 %collective-permute-start.1 = (bf16[128,2,1152]{0,2,1:T(8,128)(2,1)S(1)}, bf16[128,2,1152]{0,2,1:T(8,128)(2,1)S(1)}, u32[]{:S(2)}, u32[]{:S(2)}) collective-permute-start(bf16[128,2,1152]{0,2,1:T(8,128)(2,1)S(1)} %collective-permute-done), channel_id=1, source_target_pairs={{0,8},{8,16},{16,24},{24,28},{28,20},{20,12},{12,4},{4,0},{1,9},{9... | collective-permute-start | bytes 1769480 | tf_op jit(solution)/shard_map/ppermute | solution.py:195
  21.4 22.4 %collective-permute-start.4 = (bf16[128,2,1152]{0,2,1:T(8,128)(2,1)}, bf16[128,2,1152]{0,2,1:T(8,128)(2,1)S(1)}, u32[]{:S(2)}, u32[]{:S(2)}) collective-permute-start(bf16[128,2,1152]{0,2,1:T(8,128)(2,1)} %maximum_maximum_fusion), channel_id=1, source_target_pairs={{0,4},{8,0},{16,8},{24,16},{28,24},{20,28},{12,20},{4,12},{1,5},{9... | collective-permute-start | bytes 1769480 | tf_op jit(solution)/shard_map/ppermute | solution.py:198
  34.1 17.1 %collective-permute-start.2 = (bf16[128,2,1152]{0,2,1:T(8,128)(2,1)S(1)}, bf16[128,2,1152]{0,2,1:T(8,128)(2,1)}, u32[]{:S(2)}, u32[]{:S(2)}) collective-permute-start(bf16[128,2,1152]{0,2,1:T(8,128)(2,1)S(1)} %collective-permute-done.1), channel_id=1, source_target_pairs={{0,8},{8,16},{16,24},{24,28},{28,20},{20,12},{12,4},{4,0},{1,9},{9... | collective-permute-start | bytes 1769480 | tf_op jit(solution)/shard_map/ppermute | solution.py:195
  37.6 52.6 %all-to-all-start = ((bf16[8,32,1024]{2,1,0:T(8,128)(2,1)}), bf16[8,32,1024]{2,1,0:T(8,128)(2,1)S(1)}, u32[]{:S(2)}, u32[]{:S(2)}) async-start(bf16[8,32,1024]{2,1,0:T(8,128)(2,1)} %bitcast.10), calls=%async_computation | async-start | bytes 1048576 | tf_op jit(solution)/shard_map/all_to_all | solution.py:242
  43.8 20.1 %collective-permute-start.5 = (bf16[128,2,1152]{0,2,1:T(8,128)(2,1)S(1)}, bf16[128,2,1152]{0,2,1:T(8,128)(2,1)}, u32[]{:S(2)}, u32[]{:S(2)}) collective-permute-start(bf16[128,2,1152]{0,2,1:T(8,128)(2,1)S(1)} %collective-permute-done.4), channel_id=1, source_target_pairs={{0,4},{8,0},{16,8},{24,16},{28,24},{20,28},{12,20},{4,12},{1,5},{9... | collective-permute-start | bytes 1769480 | tf_op jit(solution)/shard_map/ppermute | solution.py:198
  51.2 16.4 %collective-permute-start.3 = (bf16[128,2,1152]{0,2,1:T(8,128)(2,1)}, bf16[128,2,1152]{0,2,1:T(8,128)(2,1)}, u32[]{:S(2)}, u32[]{:S(2)}) collective-permute-start(bf16[128,2,1152]{0,2,1:T(8,128)(2,1)} %collective-permute-done.2), channel_id=1, source_target_pairs={{0,8},{8,16},{16,24},{24,28},{28,20},{20,12},{12,4},{4,0},{1,9},{9... | collective-permute-start | bytes 1769480 | tf_op jit(solution)/shard_map/ppermute | solution.py:195
  63.9 15.7 %collective-permute-start.6 = (bf16[128,2,1152]{0,2,1:T(8,128)(2,1)}, bf16[128,2,1152]{0,2,1:T(8,128)(2,1)S(1)}, u32[]{:S(2)}, u32[]{:S(2)}) collective-permute-start(bf16[128,2,1152]{0,2,1:T(8,128)(2,1)} %collective-permute-done.5), channel_id=1, source_target_pairs={{0,4},{8,0},{16,8},{24,16},{28,24},{20,28},{12,20},{4,12},{1,5},{9... | collective-permute-start | bytes 1769480 | tf_op jit(solution)/shard_map/ppermute | solution.py:198
  79.8 2.1 %copy-start.2 = (bf16[1024,2,1152]{0,2,1:T(8,128)(2,1)}, bf16[1024,2,1152]{0,2,1:T(8,128)(2,1)S(1)}, u32[]{:S(2)}) copy-start(bf16[1024,2,1152]{0,2,1:T(8,128)(2,1)S(1)} %constant_dynamic-update-slice_fusion) | copy-start | bytes 14155780
  91.2 2.2 %copy-start.1 = (bf16[1024,1,1024]{0,2,1:T(8,128)(2,1)S(1)}, bf16[1024,1,1024]{0,2,1:T(8,128)(2,1)}, u32[]{:S(2)}) copy-start(bf16[1024,1,1024]{0,2,1:T(8,128)(2,1)} %get-tuple-element.9) | copy-start | bytes 6291460
  93.4 2.2 %slice-start = ((s8[8388608]{0:T(1024)(128)(4,1)}), s8[4194304]{0:T(1024)(128)(4,1)S(1)}, s32[]{:S(2)}) async-start(s8[8388608]{0:T(1024)(128)(4,1)} %bitcast.72), calls=%async_computation.1 | async-start | bytes 8388608
  94.2 2.8 %slice-start.1 = ((s8[8388608]{0:T(1024)(128)(4,1)}), s8[4194304]{0:T(1024)(128)(4,1)S(1)}, s32[]{:S(2)}) async-start(s8[8388608]{0:T(1024)(128)(4,1)} %bitcast.72), calls=%async_computation.2 | async-start | bytes 8388608
  98.5 2.0 %collective-permute-start.7 = (bf16[2,32,4096]{2,1,0:T(8,128)(2,1)S(1)}, bf16[2,32,4096]{2,1,0:T(8,128)(2,1)S(1)}, u32[]{:S(2)}, u32[]{:S(2)}) collective-permute-start(bf16[2,32,4096]{2,1,0:T(8,128)(2,1)S(1)} %fusion.31), channel_id=1, source_target_pairs={{0,1},{1,0},{2,3},{3,2},{4,5},{5,4},{6,7},{7,6},{8,9},{9,8},{10,11... | collective-permute-start | bytes 1572872 | tf_op jit(solution)/shard_map/ppermute | solution.py:316
  100.6 8.4 %collective-permute-start.8 = (bf16[1,32,4096]{2,1,0:T(8,128)(2,1)S(1)}, bf16[1,32,4096]{2,1,0:T(8,128)(2,1)S(1)}, u32[]{:S(2)}, u32[]{:S(2)}) collective-permute-start(bf16[1,32,4096]{2,1,0:T(8,128)(2,1)S(1)} %fusion.35), channel_id=1, source_target_pairs={{0,2},{1,3},{2,0},{3,1},{4,6},{5,7},{6,4},{7,5},{8,10},{9,11},{10,... | collective-permute-start | bytes 786440 | tf_op jit(solution)/shard_map/ppermute | solution.py:316

commit v13 on v11

--- a/solution.py
+++ b/solution.py
@@ -196,7 +196,9 @@
         pieces[-step] = moving_right
         if step <= (owners - 1) // 2:
             moving_left = jax.tree.map(lambda x: lax.ppermute(x, "seq", left), moving_left)
+            moving_right, moving_left = lax.optimization_barrier((moving_right, moving_left))
             pieces[step] = moving_left
+        pieces[-step] = moving_right
     offsets = sorted(pieces)
     stacked = jax.tree.map(
         lambda *parts: jnp.concatenate(parts, axis=0), *[pieces[k] for k in offsets]

time: 103 us -> 86.5 us (0.84)
  waiting for transfers between devices: 41.9 us -> 31.9 us
  starting transfers between devices: 29 us -> 21.2 us
  local copies, waits for them, and re-layouts: 12.4 us -> 13.8 us
    ppermute x8, waiting for transfers between devices: 33 us -> 19.1 us  [ring_gather(): lax.ppermute(x, 'seq', right)]
    ppermute x8, starting transfers between devices: 19.2 us -> 14 us  [ring_gather(): lax.ppermute(x, 'seq', right)]
    ppermute x6, waiting for transfers between devices: 0.09 us -> 4.07 us  [ring_gather(): lax.ppermute(x, 'seq', left)]
    all_to_all x1, starting transfers between devices: 6.05 us -> 3.67 us  [gathered_plan(): lax.all_to_all(outgoing, 'seq', split_axis=0, concat_axis=0, tiled=True)]
    slice x1, local copies, waits for them, and re-layouts: 0.44 us -> 1.8 us  [gathered_plan(): keys = keyval[:, 0, :].reshape(tokens, heads_here, HD)]
    unnamed x21 -> x32, local copies, waits for them, and re-layouts: 7.15 us -> 7.14 us
  transfers between devices with their start and end apart: 17 -> 17, of which waited for: 10 -> 10; matrix products, arithmetic and copies ran while one was open for 18% -> 24% of each run, Pallas kernels for 0% -> 0%
where the time goes in v13:
time: 86.5 us; the launch traced here: 85.4 us
  waiting for transfers between devices  31.9 us (37%)
  starting transfers between devices  21.2 us (25%)
  local copies, waits for them, and re-layouts  13.8 us (16%)
  other arithmetic  10.6 us (12%)
  matrix products  6.25 us (7%)
  between operations  1.68 us (2%)
    ppermute x8, waiting for transfers between devices, ring_gather(): lax.ppermute(x, 'seq', right)  19.1 us
    ppermute x8, starting transfers between devices, ring_gather(): lax.ppermute(x, 'seq', right)  14 us
    ppermute x2, waiting for transfers between devices, head_sum(): got = lax.ppermute(send, 'head', [(i, i ^ bit) for i in range(members)])  8.75 us
    unnamed x32, local copies, waits for them, and re-layouts  7.14 us
    ppermute x6, waiting for transfers between devices, ring_gather(): lax.ppermute(x, 'seq', left)  4.07 us
    all_to_all x1, starting transfers between devices, gathered_plan(): lax.all_to_all(outgoing, 'seq', split_axis=0, concat_axis=0, tiled=True)  3.67 us
    another operation x1, other arithmetic, gathered_plan(): slot_all = jnp.sum((jnp.cumsum(onehot, axis=1) - onehot) * onehot, axis=2)  2.52 us
    sub x1, other arithmetic, gathered_plan(): near_exp = jnp.exp(near_scores - row_peak[..., None])  2.15 us
  transfers between devices with their start and end apart: 17, of which 10 were waited for; matrix products, arithmetic and copies ran while one was open for 24% of the time, Pallas kernels for 0%

profile of v13, /device:TPU:0, one launch (start us, length us, event | category | flops | bytes accessed | tf_op | source)
XLA Modules:
  0.0 85.4 jit_solution(2092470448996579981)
XLA Ops:
  0.0 1.1 %slice.41 = bf16[128,2,1024]{2,0,1:T(8,128)(2,1)S(1)} slice(bf16[128,3,1024]{2,0,1:T(8,128)(2,1)} %param.9), slice={[0:128], [1:3], [0:1024]} | slice | bytes 1048576 | tf_op jit(solution)/shard_map/slice | solution.py:222
  1.4 3.1 %collective-permute-start = (bf16[128,2,1024]{0,2,1:T(8,128)(2,1)S(1)}, bf16[128,2,1024]{0,2,1:T(8,128)(2,1)S(1)}, u32[]{:S(2)}, u32[]{:S(2)}) collective-permute-start(bf16[128,2,1024]{0,2,1:T(8,128)(2,1)S(1)} %copy.55), channel_id=1, source_target_pairs={{0,8},{8,16},{16,24},{24,28},{28,20},{20,12},{12,4},{4,0},{1,9},{9... | collective-permute-start | bytes 1572872 | tf_op jit(solution)/shard_map/ppermute | solution.py:195
  4.5 2.0 %collective-permute-start.1 = (s32[128]{0:T(128)}, s32[128]{0:T(128)S(1)}, u32[]{:S(2)}, u32[]{:S(2)}) collective-permute-start(s32[128]{0:T(128)} %param.10), channel_id=1, source_target_pairs={{0,8},{8,16},{16,24},{24,28},{28,20},{20,12},{12,4},{4,0},{1,9},{9... | collective-permute-start | bytes 1544 | tf_op jit(solution)/shard_map/ppermute | solution.py:195
  6.5 1.2 %dynamic_slice.3 = s32[1]{0:T(128)} dynamic-slice(s32[8]{0:T(128)} %constant.121.clone, s32[]{:T(128)S(6)} %select_n.196), dynamic_slice_sizes={1} | dynamic-slice | bytes 12 | tf_op jit(solution)/shard_map/dynamic_slice | solution.py:206
  7.7 8.7 %collective-permute-done.1 = s32[128]{0:T(128)S(1)} collective-permute-done((s32[128]{0:T(128)}, s32[128]{0:T(128)S(1)}, u32[]{:S(2)}, u32[]{:S(2)}) %collective-permute-start.1) | collective-permute-done | bytes 544 | tf_op jit(solution)/shard_map/ppermute | solution.py:195
  16.4 1.5 %collective-permute-done.3 = s32[128]{0:T(128)S(1)} collective-permute-done((s32[128]{0:T(128)}, s32[128]{0:T(128)S(1)}, u32[]{:S(2)}, u32[]{:S(2)}) %collective-permute-start.3) | collective-permute-done | bytes 544 | tf_op jit(solution)/shard_map/ppermute | solution.py:198
  17.9 1.6 %collective-permute-start.4 = (bf16[128,2,1024]{0,2,1:T(8,128)(2,1)S(1)}, bf16[128,2,1024]{0,2,1:T(8,128)(2,1)S(1)}, u32[]{:S(2)}, u32[]{:S(2)}) collective-permute-start(bf16[128,2,1024]{0,2,1:T(8,128)(2,1)S(1)} %collective-permute-done), channel_id=1, source_target_pairs={{0,8},{8,16},{16,24},{24,28},{28,20},{20,12},{12,4},{4,0},{1,9},{9... | collective-permute-start | bytes 1572872 | tf_op jit(solution)/shard_map/ppermute | solution.py:195
  20.0 1.3 %compare_select_fusion = s32[8]{0:T(128)S(1)} fusion(s32[8]{0:T(128)} %constant.123.clone, s32[]{:T(128)} %bitcast.5), kind=kLoop, calls=%fused_computation.97 | loop fusion | flops 120 | bytes 68 | tf_op jit(solution)/shard_map/select_n | solution.py:207
  21.3 1.6 %collective-permute-start.5 = (s32[128]{0:T(128)S(1)}, s32[128]{0:T(128)S(1)}, u32[]{:S(2)}, u32[]{:S(2)}) collective-permute-start(s32[128]{0:T(128)S(1)} %collective-permute-done.1), channel_id=1, source_target_pairs={{0,8},{8,16},{16,24},{24,28},{28,20},{20,12},{12,4},{4,0},{1,9},{9... | collective-permute-start | bytes 1544 | tf_op jit(solution)/shard_map/ppermute | solution.py:195
  25.6 1.3 %gather_fusion.1 = s32[8]{0:T(128)S(1)} fusion(s32[8]{0:T(128)} %constant.122.clone, s32[1024]{0:T(1024)S(1)} %get-tuple-element.44), kind=kCustom, calls=%fused_computation.1 | custom fusion | bytes 96 | tf_op jit(solution)/shard_map/gather | solution.py:207
  26.9 3.5 %collective-permute-done.5 = s32[128]{0:T(128)S(1)} collective-permute-done((s32[128]{0:T(128)S(1)}, s32[128]{0:T(128)S(1)}, u32[]{:S(2)}, u32[]{:S(2)}) %collective-permute-start.5) | collective-permute-done | bytes 544 | tf_op jit(solution)/shard_map/ppermute | solution.py:195
  30.4 1.3 %collective-permute-done.7 = s32[128]{0:T(128)S(1)} collective-permute-done((s32[128]{0:T(128)S(1)}, s32[128]{0:T(128)S(1)}, u32[]{:S(2)}, u32[]{:S(2)}) %collective-permute-start.7) | collective-permute-done | bytes 544 | tf_op jit(solution)/shard_map/ppermute | solution.py:198
  31.7 1.6 %collective-permute-start.8 = (bf16[128,2,1024]{0,2,1:T(8,128)(2,1)S(1)}, bf16[128,2,1024]{0,2,1:T(8,128)(2,1)}, u32[]{:S(2)}, u32[]{:S(2)}) collective-permute-start(bf16[128,2,1024]{0,2,1:T(8,128)(2,1)S(1)} %collective-permute-done.4), channel_id=1, source_target_pairs={{0,8},{8,16},{16,24},{24,28},{28,20},{20,12},{12,4},{4,0},{1,9},{9... | collective-permute-start | bytes 1572872 | tf_op jit(solution)/shard_map/ppermute | solution.py:195
  34.1 1.6 %collective-permute-start.9 = (s32[128]{0:T(128)S(1)}, s32[128]{0:T(128)S(1)}, u32[]{:S(2)}, u32[]{:S(2)}) collective-permute-start(s32[128]{0:T(128)S(1)} %collective-permute-done.5), channel_id=1, source_target_pairs={{0,8},{8,16},{16,24},{24,28},{28,20},{20,12},{12,4},{4,0},{1,9},{9... | collective-permute-start | bytes 1544 | tf_op jit(solution)/shard_map/ppermute | solution.py:195
  36.8 6.2 %collective-permute-done.9 = s32[128]{0:T(128)S(1)} collective-permute-done((s32[128]{0:T(128)S(1)}, s32[128]{0:T(128)S(1)}, u32[]{:S(2)}, u32[]{:S(2)}) %collective-permute-start.9) | collective-permute-done | bytes 544 | tf_op jit(solution)/shard_map/ppermute | solution.py:195
  43.0 1.3 %collective-permute-done.11 = s32[128]{0:T(128)S(1)} collective-permute-done((s32[128]{0:T(128)S(1)}, s32[128]{0:T(128)S(1)}, u32[]{:S(2)}, u32[]{:S(2)}) %collective-permute-start.11) | collective-permute-done | bytes 544 | tf_op jit(solution)/shard_map/ppermute | solution.py:198
  44.3 1.6 %collective-permute-start.13 = (s32[128]{0:T(128)S(1)}, s32[128]{0:T(128)S(1)}, u32[]{:S(2)}, u32[]{:S(2)}) collective-permute-start(s32[128]{0:T(128)S(1)} %collective-permute-done.9), channel_id=1, source_target_pairs={{0,8},{8,16},{16,24},{24,28},{28,20},{20,12},{12,4},{4,0},{1,9},{9... | collective-permute-start | bytes 1544 | tf_op jit(solution)/shard_map/ppermute | solution.py:195
  46.5 0.9 %collective-permute-start.12 = (bf16[128,2,1024]{0,2,1:T(8,128)(2,1)}, bf16[128,2,1024]{0,2,1:T(8,128)(2,1)}, u32[]{:S(2)}, u32[]{:S(2)}) collective-permute-start(bf16[128,2,1024]{0,2,1:T(8,128)(2,1)} %collective-permute-done.8), channel_id=1, source_target_pairs={{0,8},{8,16},{16,24},{24,28},{28,20},{20,12},{12,4},{4,0},{1,9},{9... | collective-permute-start | bytes 1572872 | tf_op jit(solution)/shard_map/ppermute | solution.py:195
  49.2 2.0 %convolution_convert_fusion = bf16[256,1024]{1,0:T(8,128)(2,1)} fusion(bf16[128,3,1024]{2,0,1:T(8,128)(2,1)} %param.9, s32[128]{0:T(128)S(1)} %get-tuple-element.39), kind=kOutput, calls=%fused_computation.19 | convolution fusion | flops 67403776 | bytes 786944 | tf_op jit(solution)/shard_map/dot_general | solution.py:235
  51.2 3.7 %all-to-all-start = ((bf16[8,32,1024]{2,1,0:T(8,128)(2,1)}), bf16[8,32,1024]{2,1,0:T(8,128)(2,1)S(1)}, u32[]{:S(2)}, u32[]{:S(2)}) async-start(bf16[8,32,1024]{2,1,0:T(8,128)(2,1)} %bitcast.16), calls=%async_computation | async-start | bytes 1048576 | tf_op jit(solution)/shard_map/all_to_all | solution.py:237
  55.0 2.5 %select_reduce_fusion.1 = s32[8,128]{0,1:T(8,128)S(1)} fusion(s32[8,128]{0,1:T(8,128)S(1)} %copy.48), kind=kOutput, calls=%fused_computation.39 | output fusion | flops 1096704 | bytes 8192 | tf_op jit(solution)/shard_map/jit(cumsum)/reduce_window_sum | solution.py:227
  59.4 1.2 %constant_dynamic-update-slice_fusion.7 = bf16[1024,2,1024]{0,2,1:T(8,128)(2,1)S(1)} fusion(bf16[128,2,1024]{0,2,1:T(8,128)(2,1)} %collective-permute-done.12), kind=kLoop, calls=%fused_computation.69 | loop fusion | bytes 1048576
  60.6 1.2 %constant_dynamic-update-slice_fusion.6 = bf16[1024,2,1024]{0,2,1:T(8,128)(2,1)S(1)} fusion(bf16[1024,2,1024]{0,2,1:T(8,128)(2,1)S(1)} %constant_dynamic-update-slice_fusion.7, bf16[128,2,1024]{0,2,1:T(8,128)(2,1)} %collective-permute-done.8), kind=kLoop, calls=%fused_computation.68 | loop fusion | bytes 1048576
  61.8 1.2 %constant_dynamic-update-slice_fusion.5 = bf16[1024,2,1024]{0,2,1:T(8,128)(2,1)S(1)} fusion(bf16[1024,2,1024]{0,2,1:T(8,128)(2,1)S(1)} %constant_dynamic-update-slice_fusion.6, bf16[128,2,1024]{0,2,1:T(8,128)(2,1)} %copy-done.3), kind=kLoop, calls=%fused_computation.67 | loop fusion | bytes 1048576
  64.0 1.8 %fusion.57 = (bf16[1024,1,1024]{0,2,1:T(8,128)(2,1)S(1)}, bf16[1024,1,1024]{0,2,1:T(8,128)(2,1)}) fusion(bf16[1024,2,1024]{0,2,1:T(8,128)(2,1)S(1)} %constant_dynamic-update-slice_fusion), kind=kLoop, calls=%fused_computation.134 | loop fusion | bytes 8388608 | tf_op jit(solution)/shard_map/slice | solution.py:250
  66.8 2.2 %multiply_reduce_fusion = (f32[8,128]{1,0:T(8,128)S(1)}, f32[8,128,1024]{2,1,0:T(8,128)S(1)}) fusion(f32[128,1024]{1,0:T(8,128)S(1)} %fusion.33, f32[8,128,1024]{2,1,0:T(8,128)S(1)} %fusion.37, pred[128,1024]{1,0:T(8,128)(4,1)S(1)} %fusion.34), kind=kOutput, calls=%fused_computation.3 | output fusion | flops 7341055 | bytes 9048064 | tf_op jit(solution)/shard_map/sub | solution.py:279
  69.8 1.1 %fusion.24 = bf16[128,8,128]{0,2,1:T(8,128)(2,1)S(1)} fusion(f32[8,128,128]{2,1,0:T(8,128)S(1)} %fusion.5, bf16[1024,8,128]{0,2,1:T(8,128)(2,1)S(1)} %bitcast.84, f32[8,128,1024]{2,1,0:T(8,128)S(1)} %get-tuple-element.37, f32[128,1024]{1,0:T(8,128)S(1)} %fusion.33, pred[]{:T(512)S(6)} %eq.210, f32[128,8]{0,1:T(8,128)S(1)} %bitcast.100), kind=kOutput, calls=%fused_computation.30 | convolution fusion | flops 274071552 | bytes 7606273 | tf_op jit(solution)/shard_map/hqk,khd->qhd/dot_general | solution.py:286
  71.1 1.5 %slice-done.1 = s8[4194304]{0:T(1024)(128)(4,1)S(1)} async-done(((s8[8388608]{0:T(1024)(128)(4,1)}), s8[4194304]{0:T(1024)(128)(4,1)S(1)}, s32[]{:S(2)}) %slice-start.1) | async-done | bytes 4194328
  72.6 1.3 %fusion.58 = f32[128,4096]{1,0:T(8,128)S(1)} fusion(bf16[128,1024]{0,1:T(8,128)(2,1)S(1)} %bitcast.86, bf16[1024,4096]{1,0:T(8,128)(2,1)S(1)} %bitcast.79), kind=kOutput, calls=%fused_computation.135 | convolution fusion | flops 1073741824 | bytes 10747904 | tf_op jit(solution)/shard_map/dot_general | solution.py:292
  74.1 1.9 %collective-permute-done.14 = bf16[2,32,4096]{2,1,0:T(8,128)(2,1)S(1)} collective-permute-done((bf16[2,32,4096]{2,1,0:T(8,128)(2,1)S(1)}, bf16[2,32,4096]{2,1,0:T(8,128)(2,1)S(1)}, u32[]{:S(2)}, u32[]{:S(2)}) %collective-permute-start.14) | collective-permute-done | bytes 524320 | tf_op jit(solution)/shard_map/ppermute | solution.py:311
  76.2 1.6 %collective-permute-start.15 = (bf16[1,32,4096]{2,1,0:T(8,128)(2,1)S(1)}, bf16[1,32,4096]{2,1,0:T(8,128)(2,1)S(1)}, u32[]{:S(2)}, u32[]{:S(2)}) collective-permute-start(bf16[1,32,4096]{2,1,0:T(8,128)(2,1)S(1)} %fusion.35), channel_id=1, source_target_pairs={{0,2},{1,3},{2,0},{3,1},{4,6},{5,7},{6,4},{7,5},{8,10},{9,11},{10,... | collective-permute-start | bytes 786440 | tf_op jit(solution)/shard_map/ppermute | solution.py:311
  77.7 6.9 %collective-permute-done.15 = bf16[1,32,4096]{2,1,0:T(8,128)(2,1)S(1)} collective-permute-done((bf16[1,32,4096]{2,1,0:T(8,128)(2,1)S(1)}, bf16[1,32,4096]{2,1,0:T(8,128)(2,1)S(1)}, u32[]{:S(2)}, u32[]{:S(2)}) %collective-permute-start.15) | collective-permute-done | bytes 262176 | tf_op jit(solution)/shard_map/ppermute | solution.py:311
  (80 shorter events, 12.3 us)
Async XLA Ops:
  0.0 54.9 %copy-start.6 = (s32[128]{0:T(128)S(1)}, s32[128]{0:T(128)}, u32[]{:S(2)}) copy-start(s32[128]{0:T(128)} %param.10) | copy-start | bytes 1540
  1.4 16.5 %collective-permute-start = (bf16[128,2,1024]{0,2,1:T(8,128)(2,1)S(1)}, bf16[128,2,1024]{0,2,1:T(8,128)(2,1)S(1)}, u32[]{:S(2)}, u32[]{:S(2)}) collective-permute-start(bf16[128,2,1024]{0,2,1:T(8,128)(2,1)S(1)} %copy.55), channel_id=1, source_target_pairs={{0,8},{8,16},{16,24},{24,28},{28,20},{20,12},{12,4},{4,0},{1,9},{9... | collective-permute-start | bytes 1572872 | tf_op jit(solution)/shard_map/ppermute | solution.py:195
  4.5 13.5 %collective-permute-start.2 = (bf16[128,2,1024]{0,2,1:T(8,128)(2,1)S(1)}, bf16[128,2,1024]{0,2,1:T(8,128)(2,1)S(1)}, u32[]{:S(2)}, u32[]{:S(2)}) collective-permute-start(bf16[128,2,1024]{0,2,1:T(8,128)(2,1)S(1)} %copy.55), channel_id=1, source_target_pairs={{0,4},{8,0},{16,8},{24,16},{28,24},{20,28},{12,20},{4,12},{1,5},{9... | collective-permute-start | bytes 1572872 | tf_op jit(solution)/shard_map/ppermute | solution.py:198
  4.5 11.9 %collective-permute-start.1 = (s32[128]{0:T(128)}, s32[128]{0:T(128)S(1)}, u32[]{:S(2)}, u32[]{:S(2)}) collective-permute-start(s32[128]{0:T(128)} %param.10), channel_id=1, source_target_pairs={{0,8},{8,16},{16,24},{24,28},{28,20},{20,12},{12,4},{4,0},{1,9},{9... | collective-permute-start | bytes 1544 | tf_op jit(solution)/shard_map/ppermute | solution.py:195
  6.5 11.4 %collective-permute-start.3 = (s32[128]{0:T(128)}, s32[128]{0:T(128)S(1)}, u32[]{:S(2)}, u32[]{:S(2)}) collective-permute-start(s32[128]{0:T(128)} %param.10), channel_id=1, source_target_pairs={{0,4},{8,0},{16,8},{24,16},{28,24},{20,28},{12,20},{4,12},{1,5},{9... | collective-permute-start | bytes 1544 | tf_op jit(solution)/shard_map/ppermute | solution.py:198
  17.9 13.8 %collective-permute-start.4 = (bf16[128,2,1024]{0,2,1:T(8,128)(2,1)S(1)}, bf16[128,2,1024]{0,2,1:T(8,128)(2,1)S(1)}, u32[]{:S(2)}, u32[]{:S(2)}) collective-permute-start(bf16[128,2,1024]{0,2,1:T(8,128)(2,1)S(1)} %collective-permute-done), channel_id=1, source_target_pairs={{0,8},{8,16},{16,24},{24,28},{28,20},{20,12},{12,4},{4,0},{1,9},{9... | collective-permute-start | bytes 1572872 | tf_op jit(solution)/shard_map/ppermute | solution.py:195
  19.5 12.2 %collective-permute-start.6 = (bf16[128,2,1024]{0,2,1:T(8,128)(2,1)S(1)}, bf16[128,2,1024]{0,2,1:T(8,128)(2,1)S(1)}, u32[]{:S(2)}, u32[]{:S(2)}) collective-permute-start(bf16[128,2,1024]{0,2,1:T(8,128)(2,1)S(1)} %collective-permute-done.2), channel_id=1, source_target_pairs={{0,4},{8,0},{16,8},{24,16},{28,24},{20,28},{12,20},{4,12},{1,5},{9... | collective-permute-start | bytes 1572872 | tf_op jit(solution)/shard_map/ppermute | solution.py:198
  21.3 9.1 %collective-permute-start.5 = (s32[128]{0:T(128)S(1)}, s32[128]{0:T(128)S(1)}, u32[]{:S(2)}, u32[]{:S(2)}) collective-permute-start(s32[128]{0:T(128)S(1)} %collective-permute-done.1), channel_id=1, source_target_pairs={{0,8},{8,16},{16,24},{24,28},{28,20},{20,12},{12,4},{4,0},{1,9},{9... | collective-permute-start | bytes 1544 | tf_op jit(solution)/shard_map/ppermute | solution.py:195
  22.9 8.8 %collective-permute-start.7 = (s32[128]{0:T(128)S(1)}, s32[128]{0:T(128)S(1)}, u32[]{:S(2)}, u32[]{:S(2)}) collective-permute-start(s32[128]{0:T(128)S(1)} %collective-permute-done.3), channel_id=1, source_target_pairs={{0,4},{8,0},{16,8},{24,16},{28,24},{20,28},{12,20},{4,12},{1,5},{9... | collective-permute-start | bytes 1544 | tf_op jit(solution)/shard_map/ppermute | solution.py:198
  31.7 19.5 %copy-start.3 = (bf16[128,2,1024]{0,2,1:T(8,128)(2,1)}, bf16[128,2,1024]{0,2,1:T(8,128)(2,1)S(1)}, u32[]{:S(2)}) copy-start(bf16[128,2,1024]{0,2,1:T(8,128)(2,1)S(1)} %collective-permute-done.4) | copy-start | bytes 1572868
  31.7 19.5 %copy-start.1 = (bf16[128,2,1024]{0,2,1:T(8,128)(2,1)}, bf16[128,2,1024]{0,2,1:T(8,128)(2,1)S(1)}, u32[]{:S(2)}) copy-start(bf16[128,2,1024]{0,2,1:T(8,128)(2,1)S(1)} %collective-permute-done.6) | copy-start | bytes 1572868
  31.7 12.6 %collective-permute-start.8 = (bf16[128,2,1024]{0,2,1:T(8,128)(2,1)S(1)}, bf16[128,2,1024]{0,2,1:T(8,128)(2,1)}, u32[]{:S(2)}, u32[]{:S(2)}) collective-permute-start(bf16[128,2,1024]{0,2,1:T(8,128)(2,1)S(1)} %collective-permute-done.4), channel_id=1, source_target_pairs={{0,8},{8,16},{16,24},{24,28},{28,20},{20,12},{12,4},{4,0},{1,9},{9... | collective-permute-start | bytes 1572872 | tf_op jit(solution)/shard_map/ppermute | solution.py:195
  33.3 10.9 %collective-permute-start.10 = (bf16[128,2,1024]{0,2,1:T(8,128)(2,1)S(1)}, bf16[128,2,1024]{0,2,1:T(8,128)(2,1)S(1)}, u32[]{:S(2)}, u32[]{:S(2)}) collective-permute-start(bf16[128,2,1024]{0,2,1:T(8,128)(2,1)S(1)} %collective-permute-done.6), channel_id=1, source_target_pairs={{0,4},{8,0},{16,8},{24,16},{28,24},{20,28},{12,20},{4,12},{1,5},{9... | collective-permute-start | bytes 1572872 | tf_op jit(solution)/shard_map/ppermute | solution.py:198
  34.1 8.9 %collective-permute-start.9 = (s32[128]{0:T(128)S(1)}, s32[128]{0:T(128)S(1)}, u32[]{:S(2)}, u32[]{:S(2)}) collective-permute-start(s32[128]{0:T(128)S(1)} %collective-permute-done.5), channel_id=1, source_target_pairs={{0,8},{8,16},{16,24},{24,28},{28,20},{20,12},{12,4},{4,0},{1,9},{9... | collective-permute-start | bytes 1544 | tf_op jit(solution)/shard_map/ppermute | solution.py:195
  35.7 8.6 %collective-permute-start.11 = (s32[128]{0:T(128)S(1)}, s32[128]{0:T(128)S(1)}, u32[]{:S(2)}, u32[]{:S(2)}) collective-permute-start(s32[128]{0:T(128)S(1)} %collective-permute-done.7), channel_id=1, source_target_pairs={{0,4},{8,0},{16,8},{24,16},{28,24},{20,28},{12,20},{4,12},{1,5},{9... | collective-permute-start | bytes 1544 | tf_op jit(solution)/shard_map/ppermute | solution.py:198
  44.3 13.7 %copy-start.4 = (bf16[128,2,1024]{0,2,1:T(8,128)(2,1)}, bf16[128,2,1024]{0,2,1:T(8,128)(2,1)S(1)}, u32[]{:S(2)}) copy-start(bf16[128,2,1024]{0,2,1:T(8,128)(2,1)S(1)} %collective-permute-done.10) | copy-start | bytes 1572868
  44.3 3.7 %collective-permute-start.13 = (s32[128]{0:T(128)S(1)}, s32[128]{0:T(128)S(1)}, u32[]{:S(2)}, u32[]{:S(2)}) collective-permute-start(s32[128]{0:T(128)S(1)} %collective-permute-done.9), channel_id=1, source_target_pairs={{0,8},{8,16},{16,24},{24,28},{28,20},{20,12},{12,4},{4,0},{1,9},{9... | collective-permute-start | bytes 1544 | tf_op jit(solution)/shard_map/ppermute | solution.py:195
  46.5 12.9 %collective-permute-start.12 = (bf16[128,2,1024]{0,2,1:T(8,128)(2,1)}, bf16[128,2,1024]{0,2,1:T(8,128)(2,1)}, u32[]{:S(2)}, u32[]{:S(2)}) collective-permute-start(bf16[128,2,1024]{0,2,1:T(8,128)(2,1)} %collective-permute-done.8), channel_id=1, source_target_pairs={{0,8},{8,16},{16,24},{24,28},{28,20},{20,12},{12,4},{4,0},{1,9},{9... | collective-permute-start | bytes 1572872 | tf_op jit(solution)/shard_map/ppermute | solution.py:195
  51.2 14.6 %all-to-all-start = ((bf16[8,32,1024]{2,1,0:T(8,128)(2,1)}), bf16[8,32,1024]{2,1,0:T(8,128)(2,1)S(1)}, u32[]{:S(2)}, u32[]{:S(2)}) async-start(bf16[8,32,1024]{2,1,0:T(8,128)(2,1)} %bitcast.16), calls=%async_computation | async-start | bytes 1048576 | tf_op jit(solution)/shard_map/all_to_all | solution.py:237
  57.6 6.0 %copy-start.2 = (bf16[128,2,1024]{0,2,1:T(8,128)(2,1)S(1)}, bf16[128,2,1024]{0,2,1:T(8,128)(2,1)}, u32[]{:S(2)}) copy-start(bf16[128,2,1024]{0,2,1:T(8,128)(2,1)} %copy-done.1) | copy-start | bytes 1572868
  58.6 5.2 %copy-start.5 = (bf16[128,2,1024]{0,2,1:T(8,128)(2,1)S(1)}, bf16[128,2,1024]{0,2,1:T(8,128)(2,1)}, u32[]{:S(2)}) copy-start(bf16[128,2,1024]{0,2,1:T(8,128)(2,1)} %copy-done.4) | copy-start | bytes 1572868
  66.7 2.2 %copy-start = (bf16[1024,1,1024]{0,2,1:T(8,128)(2,1)S(1)}, bf16[1024,1,1024]{0,2,1:T(8,128)(2,1)}, u32[]{:S(2)}) copy-start(bf16[1024,1,1024]{0,2,1:T(8,128)(2,1)} %get-tuple-element.33) | copy-start | bytes 6291460
  68.9 2.2 %slice-start = ((s8[8388608]{0:T(1024)(128)(4,1)}), s8[4194304]{0:T(1024)(128)(4,1)S(1)}, s32[]{:S(2)}) async-start(s8[8388608]{0:T(1024)(128)(4,1)} %bitcast.78), calls=%async_computation.1 | async-start | bytes 8388608
  69.8 2.8 %slice-start.1 = ((s8[8388608]{0:T(1024)(128)(4,1)}), s8[4194304]{0:T(1024)(128)(4,1)S(1)}, s32[]{:S(2)}) async-start(s8[8388608]{0:T(1024)(128)(4,1)} %bitcast.78), calls=%async_computation.2 | async-start | bytes 8388608
  74.0 2.0 %collective-permute-start.14 = (bf16[2,32,4096]{2,1,0:T(8,128)(2,1)S(1)}, bf16[2,32,4096]{2,1,0:T(8,128)(2,1)S(1)}, u32[]{:S(2)}, u32[]{:S(2)}) collective-permute-start(bf16[2,32,4096]{2,1,0:T(8,128)(2,1)S(1)} %fusion.31), channel_id=1, source_target_pairs={{0,1},{1,0},{2,3},{3,2},{4,5},{5,4},{6,7},{7,6},{8,9},{9,8},{10,11... | collective-permute-start | bytes 1572872 | tf_op jit(solution)/shard_map/ppermute | solution.py:311
  76.2 8.4 %collective-permute-start.15 = (bf16[1,32,4096]{2,1,0:T(8,128)(2,1)S(1)}, bf16[1,32,4096]{2,1,0:T(8,128)(2,1)S(1)}, u32[]{:S(2)}, u32[]{:S(2)}) collective-permute-start(bf16[1,32,4096]{2,1,0:T(8,128)(2,1)S(1)} %fusion.35), channel_id=1, source_target_pairs={{0,2},{1,3},{2,0},{3,1},{4,6},{5,7},{6,4},{7,5},{8,10},{9,11},{10,... | collective-permute-start | bytes 786440 | tf_op jit(solution)/shard_map/ppermute | solution.py:311

commit v14 on v11

--- a/solution.py
+++ b/solution.py
@@ -192,11 +192,20 @@
     moving_right = block
     moving_left = block
     for step in range(1, owners // 2 + 1):
+        if step == owners - step:
+            cut = jax.tree.leaves(block)[0].shape[0] // 2
+            head_half = jax.tree.map(lambda x: lax.ppermute(x[:cut], "seq", right), moving_right)
+            tail_half = jax.tree.map(lambda x: lax.ppermute(x[cut:], "seq", left), moving_left)
+            head_half, tail_half = lax.optimization_barrier((head_half, tail_half))
+            pieces[-step] = jax.tree.map(
+                lambda a, b: jnp.concatenate([a, b], axis=0), head_half, tail_half
+            )
+            break
         moving_right = jax.tree.map(lambda x: lax.ppermute(x, "seq", right), moving_right)
+        moving_left = jax.tree.map(lambda x: lax.ppermute(x, "seq", left), moving_left)
+        moving_right, moving_left = lax.optimization_barrier((moving_right, moving_left))
         pieces[-step] = moving_right
-        if step <= (owners - 1) // 2:
-            moving_left = jax.tree.map(lambda x: lax.ppermute(x, "seq", left), moving_left)
-            pieces[step] = moving_left
+        pieces[step] = moving_left
     offsets = sorted(pieces)
     stacked = jax.tree.map(
         lambda *parts: jnp.concatenate(parts, axis=0), *[pieces[k] for k in offsets]

time: 103 us -> 103 us (level)
  local copies, waits for them, and re-layouts: 12.4 us -> 17.8 us
  waiting for transfers between devices: 41.9 us -> 39.4 us
  between operations: 1.64 us -> 0.33 us
    ppermute x8 -> x6, waiting for transfers between devices: 33 us -> 19.6 us  [ring_gather(): lax.ppermute(x, 'seq', right)]
    concatenate x3 -> x2, local copies, waits for them, and re-layouts: 0.21 us -> 7.29 us  [ring_gather(): jnp.concatenate(parts, axis=0)]
    ppermute x0 -> x4, waiting for transfers between devices: none -> 5.9 us  [the longest x2 3.87 us: ring_gather(): lax.ppermute(x[:cut], 'seq', right)]
    ppermute x6, waiting for transfers between devices: 0.09 us -> 5.22 us  [ring_gather(): lax.ppermute(x, 'seq', left)]
    unnamed x21 -> x22, local copies, waits for them, and re-layouts: 7.15 us -> 2.07 us
    ppermute x0 -> x4, starting transfers between devices: none -> 4.11 us  [the longest x2 2.52 us: ring_gather(): lax.ppermute(x[cut:], 'seq', left)]
    slice x1, local copies, waits for them, and re-layouts: 0.44 us -> 3.99 us  [gathered_plan(): keys = keyval[:, 0, :].reshape(tokens, heads_here, HD)]
    ppermute x8 -> x6, starting transfers between devices: 19.2 us -> 17.2 us  [ring_gather(): lax.ppermute(x, 'seq', right)]
  transfers between devices with their start and end apart: 17 -> 19, of which waited for: 10 -> 9; matrix products, arithmetic and copies ran while one was open for 18% -> 23% of each run, Pallas kernels for 0% -> 0%
where the time goes in v14:
time: 103 us; the launch traced here: 102 us
  waiting for transfers between devices  39.4 us (38%)
  starting transfers between devices  28.3 us (27%)
  local copies, waits for them, and re-layouts  17.8 us (17%)
  other arithmetic  10 us (10%)
  matrix products  6.28 us (6%)
    ppermute x6, waiting for transfers between devices, ring_gather(): lax.ppermute(x, 'seq', right)  19.6 us
    ppermute x6, starting transfers between devices, ring_gather(): lax.ppermute(x, 'seq', right)  17.2 us
    ppermute x2, waiting for transfers between devices, head_sum(): got = lax.ppermute(send, 'head', [(i, i ^ bit) for i in range(members)])  8.75 us
    concatenate x2, local copies, waits for them, and re-layouts, ring_gather(): jnp.concatenate(parts, axis=0)  7.29 us
    ppermute x6, waiting for transfers between devices, ring_gather(): lax.ppermute(x, 'seq', left)  5.22 us
    all_to_all x1, starting transfers between devices, gathered_plan(): lax.all_to_all(outgoing, 'seq', split_axis=0, concat_axis=0, tiled=True)  4.82 us
    slice x1, local copies, waits for them, and re-layouts, gathered_plan(): keys = keyval[:, 0, :].reshape(tokens, heads_here, HD)  3.99 us
    ppermute x2, waiting for transfers between devices, ring_gather(): lax.ppermute(x[:cut], 'seq', right)  3.87 us
  transfers between devices with their start and end apart: 19, of which 9 were waited for; matrix products, arithmetic and copies ran while one was open for 23% of the time, Pallas kernels for 0%

profile of v14, /device:TPU:0, one launch (start us, length us, event | category | flops | bytes accessed | tf_op | source)
XLA Modules:
  0.0 102.2 jit_solution(6166060373941674682)
XLA Ops:
  0.0 1.2 %slice.53 = bf16[128,2,1024]{2,0,1:T(8,128)(2,1)S(1)} slice(bf16[128,3,1024]{2,0,1:T(8,128)(2,1)} %param.9), slice={[0:128], [1:3], [0:1024]} | slice | bytes 1048576 | tf_op jit(solution)/shard_map/slice | solution.py:229
  1.5 3.1 %collective-permute-start = (bf16[128,2,1024]{0,2,1:T(8,128)(2,1)S(1)}, bf16[128,2,1024]{0,2,1:T(8,128)(2,1)S(1)}, u32[]{:S(2)}, u32[]{:S(2)}) collective-permute-start(bf16[128,2,1024]{0,2,1:T(8,128)(2,1)S(1)} %copy.54), channel_id=1, source_target_pairs={{0,8},{8,16},{16,24},{24,28},{28,20},{20,12},{12,4},{4,0},{1,9},{9... | collective-permute-start | bytes 1572872 | tf_op jit(solution)/shard_map/ppermute | solution.py:204
  4.6 2.0 %collective-permute-start.1 = (s32[128]{0:T(128)}, s32[128]{0:T(128)S(1)}, u32[]{:S(2)}, u32[]{:S(2)}) collective-permute-start(s32[128]{0:T(128)} %param.10), channel_id=1, source_target_pairs={{0,8},{8,16},{16,24},{24,28},{28,20},{20,12},{12,4},{4,0},{1,9},{9... | collective-permute-start | bytes 1544 | tf_op jit(solution)/shard_map/ppermute | solution.py:204
  8.4 8.1 %collective-permute-done.1 = s32[128]{0:T(128)S(1)} collective-permute-done((s32[128]{0:T(128)}, s32[128]{0:T(128)S(1)}, u32[]{:S(2)}, u32[]{:S(2)}) %collective-permute-start.1) | collective-permute-done | bytes 544 | tf_op jit(solution)/shard_map/ppermute | solution.py:204
  16.5 1.5 %collective-permute-done.3 = s32[128]{0:T(128)S(1)} collective-permute-done((s32[128]{0:T(128)}, s32[128]{0:T(128)S(1)}, u32[]{:S(2)}, u32[]{:S(2)}) %collective-permute-start.3) | collective-permute-done | bytes 544 | tf_op jit(solution)/shard_map/ppermute | solution.py:205
  18.0 1.6 %collective-permute-start.4 = (bf16[128,2,1024]{0,2,1:T(8,128)(2,1)S(1)}, bf16[128,2,1024]{0,2,1:T(8,128)(2,1)}, u32[]{:S(2)}, u32[]{:S(2)}) collective-permute-start(bf16[128,2,1024]{0,2,1:T(8,128)(2,1)S(1)} %collective-permute-done), channel_id=1, source_target_pairs={{0,8},{8,16},{16,24},{24,28},{28,20},{20,12},{12,4},{4,0},{1,9},{9... | collective-permute-start | bytes 1572872 | tf_op jit(solution)/shard_map/ppermute | solution.py:204
  20.0 2.0 %convolution_convert_fusion = bf16[256,1024]{1,0:T(8,128)(2,1)} fusion(bf16[128,3,1024]{2,0,1:T(8,128)(2,1)} %param.9, s32[128]{0:T(128)S(1)} %multiply_add_fusion), kind=kOutput, calls=%fused_computation.19 | convolution fusion | flops 67403776 | bytes 786944 | tf_op jit(solution)/shard_map/dot_general | solution.py:242
  22.1 4.8 %all-to-all-start = ((bf16[8,32,1024]{2,1,0:T(8,128)(2,1)}), bf16[8,32,1024]{2,1,0:T(8,128)(2,1)S(1)}, u32[]{:S(2)}, u32[]{:S(2)}) async-start(bf16[8,32,1024]{2,1,0:T(8,128)(2,1)} %bitcast.9), calls=%async_computation | async-start | bytes 1048576 | tf_op jit(solution)/shard_map/all_to_all | solution.py:244
  27.0 2.1 %collective-permute-start.5 = (s32[128]{0:T(128)S(1)}, s32[128]{0:T(128)S(1)}, u32[]{:S(2)}, u32[]{:S(2)}) collective-permute-start(s32[128]{0:T(128)S(1)} %collective-permute-done.1), channel_id=1, source_target_pairs={{0,8},{8,16},{16,24},{24,28},{28,20},{20,12},{12,4},{4,0},{1,9},{9... | collective-permute-start | bytes 1544 | tf_op jit(solution)/shard_map/ppermute | solution.py:204
  30.6 7.5 %collective-permute-done.5 = s32[128]{0:T(128)S(1)} collective-permute-done((s32[128]{0:T(128)S(1)}, s32[128]{0:T(128)S(1)}, u32[]{:S(2)}, u32[]{:S(2)}) %collective-permute-start.5) | collective-permute-done | bytes 544 | tf_op jit(solution)/shard_map/ppermute | solution.py:204
  38.1 6.4 %collective-permute-start.8 = (bf16[128,2,1024]{0,2,1:T(8,128)(2,1)}, bf16[128,2,1024]{0,2,1:T(8,128)(2,1)}, u32[]{:S(2)}, u32[]{:S(2)}) collective-permute-start(bf16[128,2,1024]{0,2,1:T(8,128)(2,1)} %collective-permute-done.4), channel_id=1, source_target_pairs={{0,8},{8,16},{16,24},{24,28},{28,20},{20,12},{12,4},{4,0},{1,9},{9... | collective-permute-start | bytes 1572872 | tf_op jit(solution)/shard_map/ppermute | solution.py:204
  45.5 2.1 %collective-permute-start.9 = (s32[128]{0:T(128)S(1)}, s32[128]{0:T(128)S(1)}, u32[]{:S(2)}, u32[]{:S(2)}) collective-permute-start(s32[128]{0:T(128)S(1)} %collective-permute-done.5), channel_id=1, source_target_pairs={{0,8},{8,16},{16,24},{24,28},{28,20},{20,12},{12,4},{4,0},{1,9},{9... | collective-permute-start | bytes 1544 | tf_op jit(solution)/shard_map/ppermute | solution.py:204
  47.6 4.0 %collective-permute-done.9 = s32[128]{0:T(128)S(1)} collective-permute-done((s32[128]{0:T(128)S(1)}, s32[128]{0:T(128)S(1)}, u32[]{:S(2)}, u32[]{:S(2)}) %collective-permute-start.9) | collective-permute-done | bytes 544 | tf_op jit(solution)/shard_map/ppermute | solution.py:204
  51.6 3.7 %collective-permute-done.11 = s32[128]{0:T(128)S(1)} collective-permute-done((s32[128]{0:T(128)S(1)}, s32[128]{0:T(128)S(1)}, u32[]{:S(2)}, u32[]{:S(2)}) %collective-permute-start.11) | collective-permute-done | bytes 544 | tf_op jit(solution)/shard_map/ppermute | solution.py:205
  56.1 1.0 slice.56
  57.1 1.3 %collective-permute-start.14 = (bf16[64,2,1024]{0,2,1:T(8,128)(2,1)}, bf16[64,2,1024]{0,2,1:T(8,128)(2,1)}, u32[]{:S(2)}, u32[]{:S(2)}) collective-permute-start(bf16[64,2,1024]{0,2,1:T(8,128)(2,1)} %slice.56), channel_id=1, source_target_pairs={{0,4},{8,0},{16,8},{24,16},{28,24},{20,28},{12,20},{4,12},{1,5},{9... | collective-permute-start | bytes 786440 | tf_op jit(solution)/shard_map/ppermute | solution.py:198
  59.1 0.8 collective-permute-start.13
  60.0 1.3 %collective-permute-start.15 = (s32[64]{0:T(128)S(1)}, s32[64]{0:T(128)S(1)}, u32[]{:S(2)}, u32[]{:S(2)}) collective-permute-start(s32[64]{0:T(128)S(1)} %slice.57), channel_id=1, source_target_pairs={{0,4},{8,0},{16,8},{24,16},{28,24},{20,28},{12,20},{4,12},{1,5},{9... | collective-permute-start | bytes 776 | tf_op jit(solution)/shard_map/ppermute | solution.py:198
  61.2 3.9 %collective-permute-done.13 = s32[64]{0:T(128)S(1)} collective-permute-done((s32[64]{0:T(128)S(1)}, s32[64]{0:T(128)S(1)}, u32[]{:S(2)}, u32[]{:S(2)}) %collective-permute-start.13) | collective-permute-done | bytes 288 | tf_op jit(solution)/shard_map/ppermute | solution.py:197
  65.1 2.0 %collective-permute-done.15 = s32[64]{0:T(128)S(1)} collective-permute-done((s32[64]{0:T(128)S(1)}, s32[64]{0:T(128)S(1)}, u32[]{:S(2)}, u32[]{:S(2)}) %collective-permute-start.15) | collective-permute-done | bytes 288 | tf_op jit(solution)/shard_map/ppermute | solution.py:198
  67.3 2.5 %select_reduce_fusion.1 = s32[8,128]{0,1:T(8,128)S(1)} fusion(s32[8,128]{0,1:T(8,128)S(1)} %copy.47), kind=kOutput, calls=%fused_computation.39 | output fusion | flops 1096704 | bytes 8192 | tf_op jit(solution)/shard_map/jit(cumsum)/reduce_window_sum | solution.py:234
  70.2 7.2 %concatenate.26 = bf16[1024,2,1024]{0,2,1:T(8,128)(2,1)} concatenate(bf16[64,2,1024]{0,2,1:T(8,128)(2,1)} %collective-permute-done.12, bf16[64,2,1024]{0,2,1:T(8,128)(2,1)} %collective-permute-done.14, bf16[128,2,1024]{0,2,1:T(8,128)(2,1)} %collective-permute-done.8, bf16[128,2,1024]{0,2,1:T(8,128)(2,1)} %collective-permute-done.4, ...), dimensions={0} | concatenate | bytes 8388608 | tf_op jit(solution)/shard_map/concatenate | solution.py:211
  78.6 4.0 %fusion.58 = (bf16[1024,1,1024]{0,2,1:T(8,128)(2,1)S(1)}, bf16[1024,1,1024]{0,2,1:T(8,128)(2,1)}) fusion(bf16[1024,2,1024]{0,2,1:T(8,128)(2,1)} %concatenate.26), kind=kLoop, calls=%fused_computation.120 | loop fusion | bytes 8388608 | tf_op jit(solution)/shard_map/slice | solution.py:257
  83.6 2.2 %multiply_reduce_fusion = (f32[8,128]{1,0:T(8,128)S(1)}, f32[8,128,1024]{2,1,0:T(8,128)S(1)}) fusion(f32[128,1024]{1,0:T(8,128)S(1)} %fusion.33, f32[8,128,1024]{2,1,0:T(8,128)S(1)} %fusion.37, pred[128,1024]{1,0:T(8,128)(4,1)S(1)} %fusion.34), kind=kOutput, calls=%fused_computation.3 | output fusion | flops 7341055 | bytes 9048064 | tf_op jit(solution)/shard_map/sub | solution.py:286
  85.8 0.8 fusion.5
  86.6 1.1 %fusion.24 = bf16[128,8,128]{0,2,1:T(8,128)(2,1)S(1)} fusion(f32[8,128,128]{2,1,0:T(8,128)S(1)} %fusion.5, bf16[1024,8,128]{0,2,1:T(8,128)(2,1)S(1)} %bitcast.94, f32[8,128,1024]{2,1,0:T(8,128)S(1)} %get-tuple-element.43, f32[128,1024]{1,0:T(8,128)S(1)} %fusion.33, pred[]{:T(512)S(6)} %eq.210, f32[128,8]{0,1:T(8,128)S(1)} %bitcast.103), kind=kOutput, calls=%fused_computation.30 | convolution fusion | flops 274071552 | bytes 7606273 | tf_op jit(solution)/shard_map/hqk,khd->qhd/dot_general | solution.py:293
  88.0 1.5 %slice-done.1 = s8[4194304]{0:T(1024)(128)(4,1)S(1)} async-done(((s8[8388608]{0:T(1024)(128)(4,1)}), s8[4194304]{0:T(1024)(128)(4,1)S(1)}, s32[]{:S(2)}) %slice-start.1) | async-done | bytes 4194328
  89.5 1.3 %fusion.59 = f32[128,4096]{1,0:T(8,128)S(1)} fusion(bf16[128,1024]{0,1:T(8,128)(2,1)S(1)} %bitcast.96, bf16[1024,4096]{1,0:T(8,128)(2,1)S(1)} %bitcast.89), kind=kOutput, calls=%fused_computation.121 | convolution fusion | flops 1073741824 | bytes 10747904 | tf_op jit(solution)/shard_map/dot_general | solution.py:299
  90.9 1.9 %collective-permute-done.16 = bf16[2,32,4096]{2,1,0:T(8,128)(2,1)S(1)} collective-permute-done((bf16[2,32,4096]{2,1,0:T(8,128)(2,1)S(1)}, bf16[2,32,4096]{2,1,0:T(8,128)(2,1)S(1)}, u32[]{:S(2)}, u32[]{:S(2)}) %collective-permute-start.16) | collective-permute-done | bytes 524320 | tf_op jit(solution)/shard_map/ppermute | solution.py:318
  93.0 1.6 %collective-permute-start.17 = (bf16[1,32,4096]{2,1,0:T(8,128)(2,1)S(1)}, bf16[1,32,4096]{2,1,0:T(8,128)(2,1)S(1)}, u32[]{:S(2)}, u32[]{:S(2)}) collective-permute-start(bf16[1,32,4096]{2,1,0:T(8,128)(2,1)S(1)} %fusion.35), channel_id=1, source_target_pairs={{0,2},{1,3},{2,0},{3,1},{4,6},{5,7},{6,4},{7,5},{8,10},{9,11},{10,... | collective-permute-start | bytes 786440 | tf_op jit(solution)/shard_map/ppermute | solution.py:318
  94.6 6.9 %collective-permute-done.17 = bf16[1,32,4096]{2,1,0:T(8,128)(2,1)S(1)} collective-permute-done((bf16[1,32,4096]{2,1,0:T(8,128)(2,1)S(1)}, bf16[1,32,4096]{2,1,0:T(8,128)(2,1)S(1)}, u32[]{:S(2)}, u32[]{:S(2)}) %collective-permute-start.17) | collective-permute-done | bytes 262176 | tf_op jit(solution)/shard_map/ppermute | solution.py:318
  101.4 0.8 fusion.36
  (75 shorter events, 9.9 us)
Async XLA Ops:
  0.0 30.0 %copy-start.7 = (s32[8]{0:T(128)S(1)}, s32[8]{0:T(128)}, u32[]{:S(2)}) copy-start(s32[8]{0:T(128)} %constant.121.clone) | copy-start | bytes 100
  0.0 44.8 %copy-start.6 = (s32[8]{0:T(128)S(1)}, s32[8]{0:T(128)}, u32[]{:S(2)}) copy-start(s32[8]{0:T(128)} %constant.123.clone) | copy-start | bytes 100
  0.0 58.4 %copy-start = (s32[8]{0:T(128)S(1)}, s32[8]{0:T(128)}, u32[]{:S(2)}) copy-start(s32[8]{0:T(128)} %constant.122.clone) | copy-start | bytes 100
  0.0 67.1 %copy-start.3 = (s32[128]{0:T(128)S(1)}, s32[128]{0:T(128)}, u32[]{:S(2)}) copy-start(s32[128]{0:T(128)} %param.10) | copy-start | bytes 1540
  0.0 29.1 %copy-start.4 = (s32[4]{0:T(128)S(1)}, s32[4]{0:T(128)}, u32[]{:S(2)}) copy-start(s32[4]{0:T(128)} %param.11) | copy-start | bytes 52
  0.0 29.3 %copy-start.2 = (s32[8,3]{0,1:T(4,128)S(1)}, s32[8,3]{0,1:T(4,128)}, u32[]{:S(2)}) copy-start(s32[8,3]{0,1:T(4,128)} %param.12) | copy-start | bytes 292
  0.0 58.3 %copy-start.5 = (s32[8]{0:T(128)S(1)}, s32[8]{0:T(128)}, u32[]{:S(2)}) copy-start(s32[8]{0:T(128)} %param.13) | copy-start | bytes 100
  1.5 16.5 %collective-permute-start = (bf16[128,2,1024]{0,2,1:T(8,128)(2,1)S(1)}, bf16[128,2,1024]{0,2,1:T(8,128)(2,1)S(1)}, u32[]{:S(2)}, u32[]{:S(2)}) collective-permute-start(bf16[128,2,1024]{0,2,1:T(8,128)(2,1)S(1)} %copy.54), channel_id=1, source_target_pairs={{0,8},{8,16},{16,24},{24,28},{28,20},{20,12},{12,4},{4,0},{1,9},{9... | collective-permute-start | bytes 1572872 | tf_op jit(solution)/shard_map/ppermute | solution.py:204
  4.6 13.5 %collective-permute-start.2 = (bf16[128,2,1024]{0,2,1:T(8,128)(2,1)S(1)}, bf16[128,2,1024]{0,2,1:T(8,128)(2,1)S(1)}, u32[]{:S(2)}, u32[]{:S(2)}) collective-permute-start(bf16[128,2,1024]{0,2,1:T(8,128)(2,1)S(1)} %copy.54), channel_id=1, source_target_pairs={{0,4},{8,0},{16,8},{24,16},{28,24},{20,28},{12,20},{4,12},{1,5},{9... | collective-permute-start | bytes 1572872 | tf_op jit(solution)/shard_map/ppermute | solution.py:205
  4.6 11.9 %collective-permute-start.1 = (s32[128]{0:T(128)}, s32[128]{0:T(128)S(1)}, u32[]{:S(2)}, u32[]{:S(2)}) collective-permute-start(s32[128]{0:T(128)} %param.10), channel_id=1, source_target_pairs={{0,8},{8,16},{16,24},{24,28},{28,20},{20,12},{12,4},{4,0},{1,9},{9... | collective-permute-start | bytes 1544 | tf_op jit(solution)/shard_map/ppermute | solution.py:204
  6.6 11.4 %collective-permute-start.3 = (s32[128]{0:T(128)}, s32[128]{0:T(128)S(1)}, u32[]{:S(2)}, u32[]{:S(2)}) collective-permute-start(s32[128]{0:T(128)} %param.10), channel_id=1, source_target_pairs={{0,4},{8,0},{16,8},{24,16},{28,24},{20,28},{12,20},{4,12},{1,5},{9... | collective-permute-start | bytes 1544 | tf_op jit(solution)/shard_map/ppermute | solution.py:205
  18.0 20.1 %collective-permute-start.4 = (bf16[128,2,1024]{0,2,1:T(8,128)(2,1)S(1)}, bf16[128,2,1024]{0,2,1:T(8,128)(2,1)}, u32[]{:S(2)}, u32[]{:S(2)}) collective-permute-start(bf16[128,2,1024]{0,2,1:T(8,128)(2,1)S(1)} %collective-permute-done), channel_id=1, source_target_pairs={{0,8},{8,16},{16,24},{24,28},{28,20},{20,12},{12,4},{4,0},{1,9},{9... | collective-permute-start | bytes 1572872 | tf_op jit(solution)/shard_map/ppermute | solution.py:204
  19.6 18.5 %collective-permute-start.6 = (bf16[128,2,1024]{0,2,1:T(8,128)(2,1)S(1)}, bf16[128,2,1024]{0,2,1:T(8,128)(2,1)}, u32[]{:S(2)}, u32[]{:S(2)}) collective-permute-start(bf16[128,2,1024]{0,2,1:T(8,128)(2,1)S(1)} %collective-permute-done.2), channel_id=1, source_target_pairs={{0,4},{8,0},{16,8},{24,16},{28,24},{20,28},{12,20},{4,12},{1,5},{9... | collective-permute-start | bytes 1572872 | tf_op jit(solution)/shard_map/ppermute | solution.py:205
  22.1 60.5 %all-to-all-start = ((bf16[8,32,1024]{2,1,0:T(8,128)(2,1)}), bf16[8,32,1024]{2,1,0:T(8,128)(2,1)S(1)}, u32[]{:S(2)}, u32[]{:S(2)}) async-start(bf16[8,32,1024]{2,1,0:T(8,128)(2,1)} %bitcast.9), calls=%async_computation | async-start | bytes 1048576 | tf_op jit(solution)/shard_map/all_to_all | solution.py:244
  27.0 11.1 %collective-permute-start.5 = (s32[128]{0:T(128)S(1)}, s32[128]{0:T(128)S(1)}, u32[]{:S(2)}, u32[]{:S(2)}) collective-permute-start(s32[128]{0:T(128)S(1)} %collective-permute-done.1), channel_id=1, source_target_pairs={{0,8},{8,16},{16,24},{24,28},{28,20},{20,12},{12,4},{4,0},{1,9},{9... | collective-permute-start | bytes 1544 | tf_op jit(solution)/shard_map/ppermute | solution.py:204
  29.0 9.1 %collective-permute-start.7 = (s32[128]{0:T(128)S(1)}, s32[128]{0:T(128)S(1)}, u32[]{:S(2)}, u32[]{:S(2)}) collective-permute-start(s32[128]{0:T(128)S(1)} %collective-permute-done.3), channel_id=1, source_target_pairs={{0,4},{8,0},{16,8},{24,16},{28,24},{20,28},{12,20},{4,12},{1,5},{9... | collective-permute-start | bytes 1544 | tf_op jit(solution)/shard_map/ppermute | solution.py:205
  38.1 17.2 %collective-permute-start.8 = (bf16[128,2,1024]{0,2,1:T(8,128)(2,1)}, bf16[128,2,1024]{0,2,1:T(8,128)(2,1)}, u32[]{:S(2)}, u32[]{:S(2)}) collective-permute-start(bf16[128,2,1024]{0,2,1:T(8,128)(2,1)} %collective-permute-done.4), channel_id=1, source_target_pairs={{0,8},{8,16},{16,24},{24,28},{28,20},{20,12},{12,4},{4,0},{1,9},{9... | collective-permute-start | bytes 1572872 | tf_op jit(solution)/shard_map/ppermute | solution.py:204
  44.5 10.8 %collective-permute-start.10 = (bf16[128,2,1024]{0,2,1:T(8,128)(2,1)}, bf16[128,2,1024]{0,2,1:T(8,128)(2,1)S(1)}, u32[]{:S(2)}, u32[]{:S(2)}) collective-permute-start(bf16[128,2,1024]{0,2,1:T(8,128)(2,1)} %collective-permute-done.6), channel_id=1, source_target_pairs={{0,4},{8,0},{16,8},{24,16},{28,24},{20,28},{12,20},{4,12},{1,5},{9... | collective-permute-start | bytes 1572872 | tf_op jit(solution)/shard_map/ppermute | solution.py:205
  45.5 6.1 %collective-permute-start.9 = (s32[128]{0:T(128)S(1)}, s32[128]{0:T(128)S(1)}, u32[]{:S(2)}, u32[]{:S(2)}) collective-permute-start(s32[128]{0:T(128)S(1)} %collective-permute-done.5), channel_id=1, source_target_pairs={{0,8},{8,16},{16,24},{24,28},{28,20},{20,12},{12,4},{4,0},{1,9},{9... | collective-permute-start | bytes 1544 | tf_op jit(solution)/shard_map/ppermute | solution.py:204
  47.6 7.7 %collective-permute-start.11 = (s32[128]{0:T(128)S(1)}, s32[128]{0:T(128)S(1)}, u32[]{:S(2)}, u32[]{:S(2)}) collective-permute-start(s32[128]{0:T(128)S(1)} %collective-permute-done.7), channel_id=1, source_target_pairs={{0,4},{8,0},{16,8},{24,16},{28,24},{20,28},{12,20},{4,12},{1,5},{9... | collective-permute-start | bytes 1544 | tf_op jit(solution)/shard_map/ppermute | solution.py:205
  55.3 11.8 %collective-permute-start.12 = (bf16[64,2,1024]{0,2,1:T(8,128)(2,1)}, bf16[64,2,1024]{0,2,1:T(8,128)(2,1)}, u32[]{:S(2)}, u32[]{:S(2)}) collective-permute-start(bf16[64,2,1024]{0,2,1:T(8,128)(2,1)} %bitcast.85), channel_id=1, source_target_pairs={{0,8},{8,16},{16,24},{24,28},{28,20},{20,12},{12,4},{4,0},{1,9},{9... | collective-permute-start | bytes 786440 | tf_op jit(solution)/shard_map/ppermute | solution.py:197
  57.1 10.1 %collective-permute-start.14 = (bf16[64,2,1024]{0,2,1:T(8,128)(2,1)}, bf16[64,2,1024]{0,2,1:T(8,128)(2,1)}, u32[]{:S(2)}, u32[]{:S(2)}) collective-permute-start(bf16[64,2,1024]{0,2,1:T(8,128)(2,1)} %slice.56), channel_id=1, source_target_pairs={{0,4},{8,0},{16,8},{24,16},{28,24},{20,28},{12,20},{4,12},{1,5},{9... | collective-permute-start | bytes 786440 | tf_op jit(solution)/shard_map/ppermute | solution.py:198
  59.1 6.0 %collective-permute-start.13 = (s32[64]{0:T(128)S(1)}, s32[64]{0:T(128)S(1)}, u32[]{:S(2)}, u32[]{:S(2)}) collective-permute-start(s32[64]{0:T(128)S(1)} %bitcast.99), channel_id=1, source_target_pairs={{0,8},{8,16},{16,24},{24,28},{28,20},{20,12},{12,4},{4,0},{1,9},{9... | collective-permute-start | bytes 776 | tf_op jit(solution)/shard_map/ppermute | solution.py:197
  60.0 7.2 %collective-permute-start.15 = (s32[64]{0:T(128)S(1)}, s32[64]{0:T(128)S(1)}, u32[]{:S(2)}, u32[]{:S(2)}) collective-permute-start(s32[64]{0:T(128)S(1)} %slice.57), channel_id=1, source_target_pairs={{0,4},{8,0},{16,8},{24,16},{28,24},{20,28},{12,20},{4,12},{1,5},{9... | collective-permute-start | bytes 776 | tf_op jit(solution)/shard_map/ppermute | solution.py:198
  83.6 2.2 %copy-start.1 = (bf16[1024,1,1024]{0,2,1:T(8,128)(2,1)S(1)}, bf16[1024,1,1024]{0,2,1:T(8,128)(2,1)}, u32[]{:S(2)}) copy-start(bf16[1024,1,1024]{0,2,1:T(8,128)(2,1)} %get-tuple-element.41) | copy-start | bytes 6291460
  85.8 2.2 %slice-start = ((s8[8388608]{0:T(1024)(128)(4,1)}), s8[4194304]{0:T(1024)(128)(4,1)S(1)}, s32[]{:S(2)}) async-start(s8[8388608]{0:T(1024)(128)(4,1)} %bitcast.88), calls=%async_computation.1 | async-start | bytes 8388608
  86.6 2.8 %slice-start.1 = ((s8[8388608]{0:T(1024)(128)(4,1)}), s8[4194304]{0:T(1024)(128)(4,1)S(1)}, s32[]{:S(2)}) async-start(s8[8388608]{0:T(1024)(128)(4,1)} %bitcast.88), calls=%async_computation.2 | async-start | bytes 8388608
  90.8 2.0 %collective-permute-start.16 = (bf16[2,32,4096]{2,1,0:T(8,128)(2,1)S(1)}, bf16[2,32,4096]{2,1,0:T(8,128)(2,1)S(1)}, u32[]{:S(2)}, u32[]{:S(2)}) collective-permute-start(bf16[2,32,4096]{2,1,0:T(8,128)(2,1)S(1)} %fusion.31), channel_id=1, source_target_pairs={{0,1},{1,0},{2,3},{3,2},{4,5},{5,4},{6,7},{7,6},{8,9},{9,8},{10,11... | collective-permute-start | bytes 1572872 | tf_op jit(solution)/shard_map/ppermute | solution.py:318
  93.0 8.4 %collective-permute-start.17 = (bf16[1,32,4096]{2,1,0:T(8,128)(2,1)S(1)}, bf16[1,32,4096]{2,1,0:T(8,128)(2,1)S(1)}, u32[]{:S(2)}, u32[]{:S(2)}) collective-permute-start(bf16[1,32,4096]{2,1,0:T(8,128)(2,1)S(1)} %fusion.35), channel_id=1, source_target_pairs={{0,2},{1,3},{2,0},{3,1},{4,6},{5,7},{6,4},{7,5},{8,10},{9,11},{10,... | collective-permute-start | bytes 786440 | tf_op jit(solution)/shard_map/ppermute | solution.py:318

commit v15 on v14

--- a/solution.py
+++ b/solution.py
@@ -177,7 +177,7 @@
     )
 
 
-def ring_gather(block, own_index, owners):
+def ring_gather(block, own_index, owners, rider):
     if owners % 2:
         ring = list(range(owners))
     else:
@@ -203,7 +203,12 @@
             break
         moving_right = jax.tree.map(lambda x: lax.ppermute(x, "seq", right), moving_right)
         moving_left = jax.tree.map(lambda x: lax.ppermute(x, "seq", left), moving_left)
-        moving_right, moving_left = lax.optimization_barrier((moving_right, moving_left))
+        if step == owners // 2 - 1 or owners < 4:
+            moving_right, moving_left, rider = lax.optimization_barrier(
+                (moving_right, moving_left, rider)
+            )
+        else:
+            moving_right, moving_left = lax.optimization_barrier((moving_right, moving_left))
         pieces[-step] = moving_right
         pieces[step] = moving_left
     offsets = sorted(pieces)
@@ -212,7 +217,7 @@
     )
     where = jnp.asarray(place, jnp.int32)[own_index]
     order = jnp.asarray(ring, jnp.int32)[(where + jnp.asarray(offsets, jnp.int32)) % owners]
-    return stacked, order
+    return stacked, order, rider
 
 
 def gathered_plan(projected, destination, doc_lengths, random_blocks, global_owner, out_weight):
@@ -225,13 +230,6 @@
     blocks_all = tokens // BLK
     score_scale = 1.0 / math.sqrt(HD)
     capacity = 2 * (tok_dev // owners)
-    (keyval, key_dest), key_order = ring_gather(
-        (projected[:, 1:, :], destination), own_index, owners
-    )
-    arrival_dest = key_dest
-    target_all = arrival_dest.reshape(owners, tok_dev) // tok_dev
-    onehot = (target_all[:, :, None] == jnp.arange(owners, dtype=jnp.int32)).astype(jnp.int32)
-    slot_all = jnp.sum((jnp.cumsum(onehot, axis=1) - onehot) * onehot, axis=2)
     target = destination // tok_dev
     mine = (target[:, None] == jnp.arange(owners, dtype=jnp.int32)[None, :]).astype(jnp.int32)
     slot = jnp.sum((jnp.cumsum(mine, axis=0) - mine) * mine, axis=1)
@@ -241,6 +239,13 @@
     ).astype(projected.dtype)
     outgoing = jnp.dot(send_pick, projected[:, 0, :], preferred_element_type=jnp.float32)
     outgoing = outgoing.astype(projected.dtype).reshape(owners, capacity, columns)
+    (keyval, key_dest), key_order, outgoing = ring_gather(
+        (projected[:, 1:, :], destination), own_index, owners, outgoing
+    )
+    arrival_dest = key_dest
+    target_all = arrival_dest.reshape(owners, tok_dev) // tok_dev
+    onehot = (target_all[:, :, None] == jnp.arange(owners, dtype=jnp.int32)).astype(jnp.int32)
+    slot_all = jnp.sum((jnp.cumsum(onehot, axis=1) - onehot) * onehot, axis=2)
     incoming = lax.all_to_all(outgoing, "seq", split_axis=0, concat_axis=0, tiled=True)
     my_pos = own_index * tok_dev + jnp.arange(tok_dev, dtype=jnp.int32)
     source = jnp.repeat(key_order, tok_dev)

time: 103 us -> 97.5 us (0.947)
  starting transfers between devices: 28.3 us -> 22.7 us
  waiting for transfers between devices: 39.4 us -> 36.9 us
  other arithmetic: 10 us -> 11.3 us
  local copies, waits for them, and re-layouts: 17.8 us -> 19.1 us
    ppermute x6, starting transfers between devices: 17.2 us -> 11.5 us  [ring_gather(): lax.ppermute(x, 'seq', right)]
    ppermute x6, waiting for transfers between devices: 19.6 us -> 16.6 us  [ring_gather(): lax.ppermute(x, 'seq', right)]
    ppermute x2, starting transfers between devices: 2.52 us -> 1.01 us  [ring_gather(): lax.ppermute(x[cut:], 'seq', left)]
    ppermute x2, starting transfers between devices: 1.59 us -> 3.09 us  [ring_gather(): lax.ppermute(x[:cut], 'seq', right)]
    ppermute x2, waiting for transfers between devices: 2.03 us -> 3.44 us  [ring_gather(): lax.ppermute(x[cut:], 'seq', left)]
    ppermute x6, starting transfers between devices: 0.54 us -> 1.81 us  [ring_gather(): lax.ppermute(x, 'seq', left)]
    all_to_all x1, starting transfers between devices: 4.82 us -> 3.67 us  [gathered_plan(): lax.all_to_all(outgoing, 'seq', split_axis=0, concat_axis=0, tiled=True)]
    unnamed x22 -> x16, local copies, waits for them, and re-layouts: 2.07 us -> 2.74 us
  transfers between devices with their start and end apart: 19 -> 19, of which waited for: 9 -> 10; matrix products, arithmetic and copies ran while one was open for 23% -> 27% of each run, Pallas kernels for 0% -> 0%
where the time goes in v15:
time: 97.5 us; the launch traced here: 96.5 us
  waiting for transfers between devices  36.9 us (38%)
  starting transfers between devices  22.7 us (23%)
  local copies, waits for them, and re-layouts  19.1 us (20%)
  other arithmetic  11.3 us (12%)
  matrix products  6.29 us (6%)
    ppermute x6, waiting for transfers between devices, ring_gather(): lax.ppermute(x, 'seq', right)  16.6 us
    ppermute x6, starting transfers between devices, ring_gather(): lax.ppermute(x, 'seq', right)  11.5 us
    ppermute x2, waiting for transfers between devices, head_sum(): got = lax.ppermute(send, 'head', [(i, i ^ bit) for i in range(members)])  8.75 us
    concatenate x2, local copies, waits for them, and re-layouts, ring_gather(): jnp.concatenate(parts, axis=0)  7.29 us
    ppermute x6, waiting for transfers between devices, ring_gather(): lax.ppermute(x, 'seq', left)  4.33 us
    slice x1, local copies, waits for them, and re-layouts, gathered_plan(): keys = keyval[:, 0, :].reshape(tokens, heads_here, HD)  3.99 us
    ppermute x2, waiting for transfers between devices, ring_gather(): lax.ppermute(x[:cut], 'seq', right)  3.75 us
    all_to_all x1, starting transfers between devices, gathered_plan(): lax.all_to_all(outgoing, 'seq', split_axis=0, concat_axis=0, tiled=True)  3.67 us
  transfers between devices with their start and end apart: 19, of which 10 were waited for; matrix products, arithmetic and copies ran while one was open for 27% of the time, Pallas kernels for 0%

profile of v15, /device:TPU:0, one launch (start us, length us, event | category | flops | bytes accessed | tf_op | source)
XLA Modules:
  0.0 96.5 jit_solution(15271090227341720451)
XLA Ops:
  0.0 1.1 %slice.53 = bf16[128,2,1024]{2,0,1:T(8,128)(2,1)S(1)} slice(bf16[128,3,1024]{2,0,1:T(8,128)(2,1)} %param.9), slice={[0:128], [1:3], [0:1024]} | slice | bytes 1048576 | tf_op jit(solution)/shard_map/slice | solution.py:243
  1.4 3.1 %collective-permute-start = (bf16[128,2,1024]{0,2,1:T(8,128)(2,1)S(1)}, bf16[128,2,1024]{0,2,1:T(8,128)(2,1)S(1)}, u32[]{:S(2)}, u32[]{:S(2)}) collective-permute-start(bf16[128,2,1024]{0,2,1:T(8,128)(2,1)S(1)} %copy.54), channel_id=1, source_target_pairs={{0,8},{8,16},{16,24},{24,28},{28,20},{20,12},{12,4},{4,0},{1,9},{9... | collective-permute-start | bytes 1572872 | tf_op jit(solution)/shard_map/ppermute | solution.py:204
  4.5 2.0 %collective-permute-start.1 = (s32[128]{0:T(128)}, s32[128]{0:T(128)S(1)}, u32[]{:S(2)}, u32[]{:S(2)}) collective-permute-start(s32[128]{0:T(128)} %param.10), channel_id=1, source_target_pairs={{0,8},{8,16},{16,24},{24,28},{28,20},{20,12},{12,4},{4,0},{1,9},{9... | collective-permute-start | bytes 1544 | tf_op jit(solution)/shard_map/ppermute | solution.py:204
  8.6 1.2 %dynamic_slice.3 = s32[1]{0:T(128)} dynamic-slice(s32[8]{0:T(128)} %constant.121.clone, s32[]{:T(128)S(6)} %select_n.197), dynamic_slice_sizes={1} | dynamic-slice | bytes 12 | tf_op jit(solution)/shard_map/dynamic_slice | solution.py:218
  9.9 6.6 %collective-permute-done.1 = s32[128]{0:T(128)S(1)} collective-permute-done((s32[128]{0:T(128)}, s32[128]{0:T(128)S(1)}, u32[]{:S(2)}, u32[]{:S(2)}) %collective-permute-start.1) | collective-permute-done | bytes 544 | tf_op jit(solution)/shard_map/ppermute | solution.py:204
  16.4 1.5 %collective-permute-done.3 = s32[128]{0:T(128)S(1)} collective-permute-done((s32[128]{0:T(128)}, s32[128]{0:T(128)S(1)}, u32[]{:S(2)}, u32[]{:S(2)}) %collective-permute-start.3) | collective-permute-done | bytes 544 | tf_op jit(solution)/shard_map/ppermute | solution.py:205
  17.9 1.6 %collective-permute-start.4 = (bf16[128,2,1024]{0,2,1:T(8,128)(2,1)S(1)}, bf16[128,2,1024]{0,2,1:T(8,128)(2,1)S(1)}, u32[]{:S(2)}, u32[]{:S(2)}) collective-permute-start(bf16[128,2,1024]{0,2,1:T(8,128)(2,1)S(1)} %collective-permute-done), channel_id=1, source_target_pairs={{0,8},{8,16},{16,24},{24,28},{28,20},{20,12},{12,4},{4,0},{1,9},{9... | collective-permute-start | bytes 1572872 | tf_op jit(solution)/shard_map/ppermute | solution.py:204
  20.0 1.3 %compare_select_fusion = s32[8]{0:T(128)S(1)} fusion(s32[8]{0:T(128)} %constant.123.clone, s32[]{:T(128)} %bitcast.7), kind=kLoop, calls=%fused_computation.83 | loop fusion | flops 120 | bytes 68 | tf_op jit(solution)/shard_map/select_n | solution.py:219
  21.9 1.6 %collective-permute-start.5 = (s32[128]{0:T(128)S(1)}, s32[128]{0:T(128)S(1)}, u32[]{:S(2)}, u32[]{:S(2)}) collective-permute-start(s32[128]{0:T(128)S(1)} %collective-permute-done.1), channel_id=1, source_target_pairs={{0,8},{8,16},{16,24},{24,28},{28,20},{20,12},{12,4},{4,0},{1,9},{9... | collective-permute-start | bytes 1544 | tf_op jit(solution)/shard_map/ppermute | solution.py:204
  24.0 6.4 %collective-permute-done.5 = s32[128]{0:T(128)S(1)} collective-permute-done((s32[128]{0:T(128)S(1)}, s32[128]{0:T(128)S(1)}, u32[]{:S(2)}, u32[]{:S(2)}) %collective-permute-start.5) | collective-permute-done | bytes 544 | tf_op jit(solution)/shard_map/ppermute | solution.py:204
  30.4 1.3 %collective-permute-done.7 = s32[128]{0:T(128)S(1)} collective-permute-done((s32[128]{0:T(128)S(1)}, s32[128]{0:T(128)S(1)}, u32[]{:S(2)}, u32[]{:S(2)}) %collective-permute-start.7) | collective-permute-done | bytes 544 | tf_op jit(solution)/shard_map/ppermute | solution.py:205
  31.8 1.6 %collective-permute-start.8 = (bf16[128,2,1024]{0,2,1:T(8,128)(2,1)S(1)}, bf16[128,2,1024]{0,2,1:T(8,128)(2,1)}, u32[]{:S(2)}, u32[]{:S(2)}) collective-permute-start(bf16[128,2,1024]{0,2,1:T(8,128)(2,1)S(1)} %collective-permute-done.4), channel_id=1, source_target_pairs={{0,8},{8,16},{16,24},{24,28},{28,20},{20,12},{12,4},{4,0},{1,9},{9... | collective-permute-start | bytes 1572872 | tf_op jit(solution)/shard_map/ppermute | solution.py:204
  35.5 2.1 %convolution_convert_fusion = bf16[256,1024]{1,0:T(8,128)(2,1)} fusion(bf16[128,3,1024]{2,0,1:T(8,128)(2,1)} %param.9, s32[128]{0:T(128)S(1)} %multiply_add_fusion), kind=kOutput, calls=%fused_computation.19 | convolution fusion | flops 67403776 | bytes 786944 | tf_op jit(solution)/shard_map/dot_general | solution.py:240
  37.5 1.6 %collective-permute-start.9 = (s32[128]{0:T(128)S(1)}, s32[128]{0:T(128)S(1)}, u32[]{:S(2)}, u32[]{:S(2)}) collective-permute-start(s32[128]{0:T(128)S(1)} %collective-permute-done.5), channel_id=1, source_target_pairs={{0,8},{8,16},{16,24},{24,28},{28,20},{20,12},{12,4},{4,0},{1,9},{9... | collective-permute-start | bytes 1544 | tf_op jit(solution)/shard_map/ppermute | solution.py:204
  39.5 3.6 %collective-permute-done.9 = s32[128]{0:T(128)S(1)} collective-permute-done((s32[128]{0:T(128)S(1)}, s32[128]{0:T(128)S(1)}, u32[]{:S(2)}, u32[]{:S(2)}) %collective-permute-start.9) | collective-permute-done | bytes 544 | tf_op jit(solution)/shard_map/ppermute | solution.py:204
  43.1 1.5 %collective-permute-done.11 = s32[128]{0:T(128)S(1)} collective-permute-done((s32[128]{0:T(128)S(1)}, s32[128]{0:T(128)S(1)}, u32[]{:S(2)}, u32[]{:S(2)}) %collective-permute-start.11) | collective-permute-done | bytes 544 | tf_op jit(solution)/shard_map/ppermute | solution.py:205
  44.6 1.5 %collective-permute-start.12 = (bf16[64,2,1024]{0,2,1:T(8,128)(2,1)}, bf16[64,2,1024]{0,2,1:T(8,128)(2,1)}, u32[]{:S(2)}, u32[]{:S(2)}) collective-permute-start(bf16[64,2,1024]{0,2,1:T(8,128)(2,1)} %bitcast.85), channel_id=1, source_target_pairs={{0,8},{8,16},{16,24},{24,28},{28,20},{20,12},{12,4},{4,0},{1,9},{9... | collective-permute-start | bytes 786440 | tf_op jit(solution)/shard_map/ppermute | solution.py:197
  46.1 1.0 %slice.57 = bf16[64,2,1024]{0,2,1:T(8,128)(2,1)} slice(bf16[128,2,1024]{0,2,1:T(8,128)(2,1)S(1)} %collective-permute-done.10), slice={[64:128], [0:2], [0:1024]} | slice | bytes 524288 | tf_op jit(solution)/shard_map/slice | solution.py:198
  48.4 1.6 %collective-permute-start.13 = (s32[64]{0:T(128)S(1)}, s32[64]{0:T(128)S(1)}, u32[]{:S(2)}, u32[]{:S(2)}) collective-permute-start(s32[64]{0:T(128)S(1)} %bitcast.99), channel_id=1, source_target_pairs={{0,8},{8,16},{16,24},{24,28},{28,20},{20,12},{12,4},{4,0},{1,9},{9... | collective-permute-start | bytes 776 | tf_op jit(solution)/shard_map/ppermute | solution.py:197
  50.5 3.7 %all-to-all-start = ((bf16[8,32,1024]{2,1,0:T(8,128)(2,1)}), bf16[8,32,1024]{2,1,0:T(8,128)(2,1)S(1)}, u32[]{:S(2)}, u32[]{:S(2)}) async-start(bf16[8,32,1024]{2,1,0:T(8,128)(2,1)} %bitcast.1), calls=%async_computation | async-start | bytes 1048576 | tf_op jit(solution)/shard_map/all_to_all | solution.py:249
  54.2 3.7 %collective-permute-done.13 = s32[64]{0:T(128)S(1)} collective-permute-done((s32[64]{0:T(128)S(1)}, s32[64]{0:T(128)S(1)}, u32[]{:S(2)}, u32[]{:S(2)}) %collective-permute-start.13) | collective-permute-done | bytes 288 | tf_op jit(solution)/shard_map/ppermute | solution.py:197
  58.0 3.4 %collective-permute-done.15 = s32[64]{0:T(128)S(1)} collective-permute-done((s32[64]{0:T(128)S(1)}, s32[64]{0:T(128)S(1)}, u32[]{:S(2)}, u32[]{:S(2)}) %collective-permute-start.15) | collective-permute-done | bytes 288 | tf_op jit(solution)/shard_map/ppermute | solution.py:198
  61.6 2.5 %select_reduce_fusion.1 = s32[8,128]{0,1:T(8,128)S(1)} fusion(s32[8,128]{0,1:T(8,128)S(1)} %copy.47), kind=kOutput, calls=%fused_computation.39 | output fusion | flops 1096704 | bytes 8192 | tf_op jit(solution)/shard_map/jit(cumsum)/reduce_window_sum | solution.py:248
  64.5 7.2 %concatenate.26 = bf16[1024,2,1024]{0,2,1:T(8,128)(2,1)} concatenate(bf16[64,2,1024]{0,2,1:T(8,128)(2,1)} %collective-permute-done.12, bf16[64,2,1024]{0,2,1:T(8,128)(2,1)} %collective-permute-done.14, bf16[128,2,1024]{0,2,1:T(8,128)(2,1)} %collective-permute-done.8, bf16[128,2,1024]{0,2,1:T(8,128)(2,1)} %copy-done.2, bf16[128,2,1024]{0,2,1:T(8,128)(2,1)S(1)} %collective-permute-done, ...), dimensions={0} | concatenate | bytes 8388608 | tf_op jit(solution)/shard_map/concatenate | solution.py:216
  72.9 4.0 %fusion.58 = (bf16[1024,1,1024]{0,2,1:T(8,128)(2,1)S(1)}, bf16[1024,1,1024]{0,2,1:T(8,128)(2,1)}) fusion(bf16[1024,2,1024]{0,2,1:T(8,128)(2,1)} %concatenate.26), kind=kLoop, calls=%fused_computation.120 | loop fusion | bytes 8388608 | tf_op jit(solution)/shard_map/slice | solution.py:262
  77.9 2.2 %multiply_reduce_fusion = (f32[8,128]{1,0:T(8,128)S(1)}, f32[8,128,1024]{2,1,0:T(8,128)S(1)}) fusion(f32[128,1024]{1,0:T(8,128)S(1)} %fusion.33, f32[8,128,1024]{2,1,0:T(8,128)S(1)} %fusion.37, pred[128,1024]{1,0:T(8,128)(4,1)S(1)} %fusion.34), kind=kOutput, calls=%fused_computation.3 | output fusion | flops 7341055 | bytes 9048064 | tf_op jit(solution)/shard_map/sub | solution.py:291
  80.9 1.1 %fusion.24 = bf16[128,8,128]{0,2,1:T(8,128)(2,1)S(1)} fusion(f32[8,128,128]{2,1,0:T(8,128)S(1)} %fusion.5, bf16[1024,8,128]{0,2,1:T(8,128)(2,1)S(1)} %bitcast.94, f32[8,128,1024]{2,1,0:T(8,128)S(1)} %get-tuple-element.45, f32[128,1024]{1,0:T(8,128)S(1)} %fusion.33, pred[]{:T(512)S(6)} %eq.216, f32[128,8]{0,1:T(8,128)S(1)} %bitcast.103), kind=kOutput, calls=%fused_computation.30 | convolution fusion | flops 274071552 | bytes 7606273 | tf_op jit(solution)/shard_map/hqk,khd->qhd/dot_general | solution.py:298
  82.3 1.5 %slice-done.1 = s8[4194304]{0:T(1024)(128)(4,1)S(1)} async-done(((s8[8388608]{0:T(1024)(128)(4,1)}), s8[4194304]{0:T(1024)(128)(4,1)S(1)}, s32[]{:S(2)}) %slice-start.1) | async-done | bytes 4194328
  83.7 1.3 %fusion.59 = f32[128,4096]{1,0:T(8,128)S(1)} fusion(bf16[128,1024]{0,1:T(8,128)(2,1)S(1)} %bitcast.96, bf16[1024,4096]{1,0:T(8,128)(2,1)S(1)} %bitcast.89), kind=kOutput, calls=%fused_computation.121 | convolution fusion | flops 1073741824 | bytes 10747904 | tf_op jit(solution)/shard_map/dot_general | solution.py:304
  85.2 1.9 %collective-permute-done.16 = bf16[2,32,4096]{2,1,0:T(8,128)(2,1)S(1)} collective-permute-done((bf16[2,32,4096]{2,1,0:T(8,128)(2,1)S(1)}, bf16[2,32,4096]{2,1,0:T(8,128)(2,1)S(1)}, u32[]{:S(2)}, u32[]{:S(2)}) %collective-permute-start.16) | collective-permute-done | bytes 524320 | tf_op jit(solution)/shard_map/ppermute | solution.py:323
  87.3 1.6 %collective-permute-start.17 = (bf16[1,32,4096]{2,1,0:T(8,128)(2,1)S(1)}, bf16[1,32,4096]{2,1,0:T(8,128)(2,1)S(1)}, u32[]{:S(2)}, u32[]{:S(2)}) collective-permute-start(bf16[1,32,4096]{2,1,0:T(8,128)(2,1)S(1)} %fusion.35), channel_id=1, source_target_pairs={{0,2},{1,3},{2,0},{3,1},{4,6},{5,7},{6,4},{7,5},{8,10},{9,11},{10,... | collective-permute-start | bytes 786440 | tf_op jit(solution)/shard_map/ppermute | solution.py:323
  88.9 6.9 %collective-permute-done.17 = bf16[1,32,4096]{2,1,0:T(8,128)(2,1)S(1)} collective-permute-done((bf16[1,32,4096]{2,1,0:T(8,128)(2,1)S(1)}, bf16[1,32,4096]{2,1,0:T(8,128)(2,1)S(1)}, u32[]{:S(2)}, u32[]{:S(2)}) %collective-permute-start.17) | collective-permute-done | bytes 262176 | tf_op jit(solution)/shard_map/ppermute | solution.py:323
  (69 shorter events, 13.1 us)
Async XLA Ops:
  0.0 47.7 %copy-start = (s32[8]{0:T(128)S(1)}, s32[8]{0:T(128)}, u32[]{:S(2)}) copy-start(s32[8]{0:T(128)} %constant.122.clone) | copy-start | bytes 100
  0.0 61.4 %copy-start.3 = (s32[128]{0:T(128)S(1)}, s32[128]{0:T(128)}, u32[]{:S(2)}) copy-start(s32[128]{0:T(128)} %param.10) | copy-start | bytes 1540
  0.0 47.6 %copy-start.4 = (s32[8]{0:T(128)S(1)}, s32[8]{0:T(128)}, u32[]{:S(2)}) copy-start(s32[8]{0:T(128)} %param.13) | copy-start | bytes 100
  1.4 16.5 %collective-permute-start = (bf16[128,2,1024]{0,2,1:T(8,128)(2,1)S(1)}, bf16[128,2,1024]{0,2,1:T(8,128)(2,1)S(1)}, u32[]{:S(2)}, u32[]{:S(2)}) collective-permute-start(bf16[128,2,1024]{0,2,1:T(8,128)(2,1)S(1)} %copy.54), channel_id=1, source_target_pairs={{0,8},{8,16},{16,24},{24,28},{28,20},{20,12},{12,4},{4,0},{1,9},{9... | collective-permute-start | bytes 1572872 | tf_op jit(solution)/shard_map/ppermute | solution.py:204
  4.5 13.5 %collective-permute-start.2 = (bf16[128,2,1024]{0,2,1:T(8,128)(2,1)S(1)}, bf16[128,2,1024]{0,2,1:T(8,128)(2,1)S(1)}, u32[]{:S(2)}, u32[]{:S(2)}) collective-permute-start(bf16[128,2,1024]{0,2,1:T(8,128)(2,1)S(1)} %copy.54), channel_id=1, source_target_pairs={{0,4},{8,0},{16,8},{24,16},{28,24},{20,28},{12,20},{4,12},{1,5},{9... | collective-permute-start | bytes 1572872 | tf_op jit(solution)/shard_map/ppermute | solution.py:205
  4.5 11.9 %collective-permute-start.1 = (s32[128]{0:T(128)}, s32[128]{0:T(128)S(1)}, u32[]{:S(2)}, u32[]{:S(2)}) collective-permute-start(s32[128]{0:T(128)} %param.10), channel_id=1, source_target_pairs={{0,8},{8,16},{16,24},{24,28},{28,20},{20,12},{12,4},{4,0},{1,9},{9... | collective-permute-start | bytes 1544 | tf_op jit(solution)/shard_map/ppermute | solution.py:204
  6.5 11.4 %collective-permute-start.3 = (s32[128]{0:T(128)}, s32[128]{0:T(128)S(1)}, u32[]{:S(2)}, u32[]{:S(2)}) collective-permute-start(s32[128]{0:T(128)} %param.10), channel_id=1, source_target_pairs={{0,4},{8,0},{16,8},{24,16},{28,24},{20,28},{12,20},{4,12},{1,5},{9... | collective-permute-start | bytes 1544 | tf_op jit(solution)/shard_map/ppermute | solution.py:205
  17.9 13.8 %collective-permute-start.4 = (bf16[128,2,1024]{0,2,1:T(8,128)(2,1)S(1)}, bf16[128,2,1024]{0,2,1:T(8,128)(2,1)S(1)}, u32[]{:S(2)}, u32[]{:S(2)}) collective-permute-start(bf16[128,2,1024]{0,2,1:T(8,128)(2,1)S(1)} %collective-permute-done), channel_id=1, source_target_pairs={{0,8},{8,16},{16,24},{24,28},{28,20},{20,12},{12,4},{4,0},{1,9},{9... | collective-permute-start | bytes 1572872 | tf_op jit(solution)/shard_map/ppermute | solution.py:204
  19.5 12.2 %collective-permute-start.6 = (bf16[128,2,1024]{0,2,1:T(8,128)(2,1)S(1)}, bf16[128,2,1024]{0,2,1:T(8,128)(2,1)}, u32[]{:S(2)}, u32[]{:S(2)}) collective-permute-start(bf16[128,2,1024]{0,2,1:T(8,128)(2,1)S(1)} %collective-permute-done.2), channel_id=1, source_target_pairs={{0,4},{8,0},{16,8},{24,16},{28,24},{20,28},{12,20},{4,12},{1,5},{9... | collective-permute-start | bytes 1572872 | tf_op jit(solution)/shard_map/ppermute | solution.py:205
  21.9 8.5 %collective-permute-start.5 = (s32[128]{0:T(128)S(1)}, s32[128]{0:T(128)S(1)}, u32[]{:S(2)}, u32[]{:S(2)}) collective-permute-start(s32[128]{0:T(128)S(1)} %collective-permute-done.1), channel_id=1, source_target_pairs={{0,8},{8,16},{16,24},{24,28},{28,20},{20,12},{12,4},{4,0},{1,9},{9... | collective-permute-start | bytes 1544 | tf_op jit(solution)/shard_map/ppermute | solution.py:204
  23.5 8.2 %collective-permute-start.7 = (s32[128]{0:T(128)S(1)}, s32[128]{0:T(128)S(1)}, u32[]{:S(2)}, u32[]{:S(2)}) collective-permute-start(s32[128]{0:T(128)S(1)} %collective-permute-done.3), channel_id=1, source_target_pairs={{0,4},{8,0},{16,8},{24,16},{28,24},{20,28},{12,20},{4,12},{1,5},{9... | collective-permute-start | bytes 1544 | tf_op jit(solution)/shard_map/ppermute | solution.py:205
  31.8 18.8 %copy-start.2 = (bf16[128,2,1024]{0,2,1:T(8,128)(2,1)}, bf16[128,2,1024]{0,2,1:T(8,128)(2,1)S(1)}, u32[]{:S(2)}) copy-start(bf16[128,2,1024]{0,2,1:T(8,128)(2,1)S(1)} %collective-permute-done.4) | copy-start | bytes 1572868
  31.8 12.8 %collective-permute-start.8 = (bf16[128,2,1024]{0,2,1:T(8,128)(2,1)S(1)}, bf16[128,2,1024]{0,2,1:T(8,128)(2,1)}, u32[]{:S(2)}, u32[]{:S(2)}) collective-permute-start(bf16[128,2,1024]{0,2,1:T(8,128)(2,1)S(1)} %collective-permute-done.4), channel_id=1, source_target_pairs={{0,8},{8,16},{16,24},{24,28},{28,20},{20,12},{12,4},{4,0},{1,9},{9... | collective-permute-start | bytes 1572872 | tf_op jit(solution)/shard_map/ppermute | solution.py:204
  33.4 11.2 %collective-permute-start.10 = (bf16[128,2,1024]{0,2,1:T(8,128)(2,1)}, bf16[128,2,1024]{0,2,1:T(8,128)(2,1)S(1)}, u32[]{:S(2)}, u32[]{:S(2)}) collective-permute-start(bf16[128,2,1024]{0,2,1:T(8,128)(2,1)} %collective-permute-done.6), channel_id=1, source_target_pairs={{0,4},{8,0},{16,8},{24,16},{28,24},{20,28},{12,20},{4,12},{1,5},{9... | collective-permute-start | bytes 1572872 | tf_op jit(solution)/shard_map/ppermute | solution.py:205
  37.5 5.6 %collective-permute-start.9 = (s32[128]{0:T(128)S(1)}, s32[128]{0:T(128)S(1)}, u32[]{:S(2)}, u32[]{:S(2)}) collective-permute-start(s32[128]{0:T(128)S(1)} %collective-permute-done.5), channel_id=1, source_target_pairs={{0,8},{8,16},{16,24},{24,28},{28,20},{20,12},{12,4},{4,0},{1,9},{9... | collective-permute-start | bytes 1544 | tf_op jit(solution)/shard_map/ppermute | solution.py:204
  39.1 5.5 %collective-permute-start.11 = (s32[128]{0:T(128)S(1)}, s32[128]{0:T(128)S(1)}, u32[]{:S(2)}, u32[]{:S(2)}) collective-permute-start(s32[128]{0:T(128)S(1)} %collective-permute-done.7), channel_id=1, source_target_pairs={{0,4},{8,0},{16,8},{24,16},{28,24},{20,28},{12,20},{4,12},{1,5},{9... | collective-permute-start | bytes 1544 | tf_op jit(solution)/shard_map/ppermute | solution.py:205
  44.6 16.8 %collective-permute-start.12 = (bf16[64,2,1024]{0,2,1:T(8,128)(2,1)}, bf16[64,2,1024]{0,2,1:T(8,128)(2,1)}, u32[]{:S(2)}, u32[]{:S(2)}) collective-permute-start(bf16[64,2,1024]{0,2,1:T(8,128)(2,1)} %bitcast.85), channel_id=1, source_target_pairs={{0,8},{8,16},{16,24},{24,28},{28,20},{20,12},{12,4},{4,0},{1,9},{9... | collective-permute-start | bytes 786440 | tf_op jit(solution)/shard_map/ppermute | solution.py:197
  47.1 14.3 %collective-permute-start.14 = (bf16[64,2,1024]{0,2,1:T(8,128)(2,1)}, bf16[64,2,1024]{0,2,1:T(8,128)(2,1)}, u32[]{:S(2)}, u32[]{:S(2)}) collective-permute-start(bf16[64,2,1024]{0,2,1:T(8,128)(2,1)} %slice.57), channel_id=1, source_target_pairs={{0,4},{8,0},{16,8},{24,16},{28,24},{20,28},{12,20},{4,12},{1,5},{9... | collective-permute-start | bytes 786440 | tf_op jit(solution)/shard_map/ppermute | solution.py:198
  48.4 9.6 %collective-permute-start.13 = (s32[64]{0:T(128)S(1)}, s32[64]{0:T(128)S(1)}, u32[]{:S(2)}, u32[]{:S(2)}) collective-permute-start(s32[64]{0:T(128)S(1)} %bitcast.99), channel_id=1, source_target_pairs={{0,8},{8,16},{16,24},{24,28},{28,20},{20,12},{12,4},{4,0},{1,9},{9... | collective-permute-start | bytes 776 | tf_op jit(solution)/shard_map/ppermute | solution.py:197
  50.0 11.4 %collective-permute-start.15 = (s32[64]{0:T(128)S(1)}, s32[64]{0:T(128)S(1)}, u32[]{:S(2)}, u32[]{:S(2)}) collective-permute-start(s32[64]{0:T(128)S(1)} %slice.58), channel_id=1, source_target_pairs={{0,4},{8,0},{16,8},{24,16},{28,24},{20,28},{12,20},{4,12},{1,5},{9... | collective-permute-start | bytes 776 | tf_op jit(solution)/shard_map/ppermute | solution.py:198
  50.5 26.4 %all-to-all-start = ((bf16[8,32,1024]{2,1,0:T(8,128)(2,1)}), bf16[8,32,1024]{2,1,0:T(8,128)(2,1)S(1)}, u32[]{:S(2)}, u32[]{:S(2)}) async-start(bf16[8,32,1024]{2,1,0:T(8,128)(2,1)} %bitcast.1), calls=%async_computation | async-start | bytes 1048576 | tf_op jit(solution)/shard_map/all_to_all | solution.py:249
  77.9 2.2 %copy-start.1 = (bf16[1024,1,1024]{0,2,1:T(8,128)(2,1)S(1)}, bf16[1024,1,1024]{0,2,1:T(8,128)(2,1)}, u32[]{:S(2)}) copy-start(bf16[1024,1,1024]{0,2,1:T(8,128)(2,1)} %get-tuple-element.43) | copy-start | bytes 6291460
  80.1 2.2 %slice-start = ((s8[8388608]{0:T(1024)(128)(4,1)}), s8[4194304]{0:T(1024)(128)(4,1)S(1)}, s32[]{:S(2)}) async-start(s8[8388608]{0:T(1024)(128)(4,1)} %bitcast.88), calls=%async_computation.1 | async-start | bytes 8388608
  80.9 2.8 %slice-start.1 = ((s8[8388608]{0:T(1024)(128)(4,1)}), s8[4194304]{0:T(1024)(128)(4,1)S(1)}, s32[]{:S(2)}) async-start(s8[8388608]{0:T(1024)(128)(4,1)} %bitcast.88), calls=%async_computation.2 | async-start | bytes 8388608
  85.1 2.0 %collective-permute-start.16 = (bf16[2,32,4096]{2,1,0:T(8,128)(2,1)S(1)}, bf16[2,32,4096]{2,1,0:T(8,128)(2,1)S(1)}, u32[]{:S(2)}, u32[]{:S(2)}) collective-permute-start(bf16[2,32,4096]{2,1,0:T(8,128)(2,1)S(1)} %fusion.31), channel_id=1, source_target_pairs={{0,1},{1,0},{2,3},{3,2},{4,5},{5,4},{6,7},{7,6},{8,9},{9,8},{10,11... | collective-permute-start | bytes 1572872 | tf_op jit(solution)/shard_map/ppermute | solution.py:323
  87.3 8.4 %collective-permute-start.17 = (bf16[1,32,4096]{2,1,0:T(8,128)(2,1)S(1)}, bf16[1,32,4096]{2,1,0:T(8,128)(2,1)S(1)}, u32[]{:S(2)}, u32[]{:S(2)}) collective-permute-start(bf16[1,32,4096]{2,1,0:T(8,128)(2,1)S(1)} %fusion.35), channel_id=1, source_target_pairs={{0,2},{1,3},{2,0},{3,1},{4,6},{5,7},{6,4},{7,5},{8,10},{9,11},{10,... | collective-permute-start | bytes 786440 | tf_op jit(solution)/shard_map/ppermute | solution.py:323

commit v16 on v13

--- a/solution.py
+++ b/solution.py
@@ -205,7 +205,7 @@
     )
     where = jnp.asarray(place, jnp.int32)[own_index]
     order = jnp.asarray(ring, jnp.int32)[(where + jnp.asarray(offsets, jnp.int32)) % owners]
-    return stacked, order
+    return stacked, order, [pieces[k] for k in offsets]
 
 
 def gathered_plan(projected, destination, doc_lengths, random_blocks, global_owner, out_weight):
@@ -218,9 +218,10 @@
     blocks_all = tokens // BLK
     score_scale = 1.0 / math.sqrt(HD)
     capacity = 2 * (tok_dev // owners)
-    (keyval, key_dest), key_order = ring_gather(
+    (_, key_dest), key_order, arrived = ring_gather(
         (projected[:, 1:, :], destination), own_index, owners
     )
+    arrived = [piece for piece, _ in arrived]
     arrival_dest = key_dest
     target_all = arrival_dest.reshape(owners, tok_dev) // tok_dev
     onehot = (target_all[:, :, None] == jnp.arange(owners, dtype=jnp.int32)).astype(jnp.int32)
@@ -247,12 +248,19 @@
         land_pick, incoming.reshape(owners * capacity, columns), preferred_element_type=jnp.float32
     )
     queries = queries.astype(projected.dtype).reshape(tok_dev, heads_here, HD)
-    keys = keyval[:, 0, :].reshape(tokens, heads_here, HD)
-    values = keyval[:, 1, :].reshape(tokens, heads_here, HD)
-    scores = (
-        jnp.einsum("qhd,khd->hqk", queries, keys, preferred_element_type=jnp.float32)
-        * score_scale
-    )
+    values = [piece[:, 1, :].reshape(tok_dev, heads_here, HD) for piece in arrived]
+    scores = jnp.concatenate(
+        [
+            jnp.einsum(
+                "qhd,khd->hqk",
+                queries,
+                piece[:, 0, :].reshape(tok_dev, heads_here, HD),
+                preferred_element_type=jnp.float32,
+            )
+            for piece in arrived
+        ],
+        axis=2,
+    ) * score_scale
     bounds = jnp.cumsum(doc_lengths)
     key_block = key_dest // BLK
     key_doc = segment_of(key_dest, bounds)
@@ -283,10 +291,13 @@
     weighted = rounded * count_f
     weight_hi = weighted.astype(jnp.bfloat16)
     weight_lo = (weighted - weight_hi.astype(jnp.float32)).astype(jnp.bfloat16)
-    mixed_sum = jnp.einsum("hqk,khd->qhd", weight_hi, values, preferred_element_type=jnp.float32)
-    mixed_sum = mixed_sum + jnp.einsum(
-        "hqk,khd->qhd", weight_lo, values, preferred_element_type=jnp.float32
-    )
+    mixed_sum = 0.0
+    for index, piece_values in enumerate(values):
+        span = slice(index * tok_dev, (index + 1) * tok_dev)
+        for weight in (weight_hi, weight_lo):
+            mixed_sum = mixed_sum + jnp.einsum(
+                "hqk,khd->qhd", weight[:, :, span], piece_values, preferred_element_type=jnp.float32
+            )
     attn_rows = (mixed_sum / jnp.transpose(denominator)[..., None]).reshape(tok_dev, columns)
     attn_rows = attn_rows.astype(jnp.bfloat16)
     projected_rows = jnp.dot(attn_rows, out_weight, preferred_element_type=jnp.float32)

time: 86.5 us -> 96 us (1.11)
  matrix products: 6.25 us -> 12.8 us
  other arithmetic: 10.6 us -> 12.8 us
    ppermute x8, waiting for transfers between devices: 19.1 us -> 9.11 us  [ring_gather(): lax.ppermute(x, 'seq', right)]
    dot_general x3 -> x24, matrix products: 2.66 us -> 9.17 us  [the longest x8 5.52 us: gathered_plan(): jnp.einsum('qhd,khd->hqk', queries, piece[:, 0, :].reshape(tok_dev, heads...]
    all_to_all x1, waiting for transfers between devices: 0.01 us -> 6.5 us  [gathered_plan(): lax.all_to_all(outgoing, 'seq', split_axis=0, concat_axis=0, tiled=True)]
    slice x1 -> x6, local copies, waits for them, and re-layouts: 1.8 us -> 6.89 us  [gathered_plan(): piece[:, 1, :].reshape(tok_dev, heads_here, HD)]
    unnamed x32 -> x20, local copies, waits for them, and re-layouts: 7.14 us -> 2.74 us
    ppermute x6, waiting for transfers between devices: 4.07 us -> 7.58 us  [ring_gather(): lax.ppermute(x, 'seq', left)]
    reshape x1, other arithmetic: 0.13 us -> 1.17 us  [head_sum(): pairs = partial.reshape(partial.shape[0] // 2, 2, rows, partial.shape[2])]
    convert_element_type x1, other arithmetic: 0.53 us -> 1.51 us  [gathered_plan(): count_f = count.astype(jnp.float32)[None]]
  transfers between devices with their start and end apart: 17 -> 17, of which waited for: 10 -> 8; matrix products, arithmetic and copies ran while one was open for 24% -> 23% of each run, Pallas kernels for 0% -> 0%
where the time goes in v16:
time: 96 us; the launch traced here: 95.4 us
  waiting for transfers between devices  32.1 us (33%)
  starting transfers between devices  21.9 us (23%)
  local copies, waits for them, and re-layouts  14.3 us (15%)
  other arithmetic  12.8 us (13%)
  matrix products  12.8 us (13%)
  between operations  1.67 us (2%)
    ppermute x8, starting transfers between devices, ring_gather(): lax.ppermute(x, 'seq', right)  14.6 us
    ppermute x8, waiting for transfers between devices, ring_gather(): lax.ppermute(x, 'seq', right)  9.11 us
    ppermute x2, waiting for transfers between devices, head_sum(): got = lax.ppermute(send, 'head', [(i, i ^ bit) for i in range(members)])  8.88 us
    ppermute x6, waiting for transfers between devices, ring_gather(): lax.ppermute(x, 'seq', left)  7.58 us
    slice x6, local copies, waits for them, and re-layouts, gathered_plan(): piece[:, 1, :].reshape(tok_dev, heads_here, HD)  6.89 us
    all_to_all x1, waiting for transfers between devices, gathered_plan(): lax.all_to_all(outgoing, 'seq', split_axis=0, concat_axis=0, tiled=True)  6.5 us
    dot_general x8, matrix products, gathered_plan(): jnp.einsum('qhd,khd->hqk', queries, piece[:, 0, :].reshape(tok_dev, heads...  5.52 us
    all_to_all x1, starting transfers between devices, gathered_plan(): lax.all_to_all(outgoing, 'seq', split_axis=0, concat_axis=0, tiled=True)  3.81 us
  transfers between devices with their start and end apart: 17, of which 8 were waited for; matrix products, arithmetic and copies ran while one was open for 23% of the time, Pallas kernels for 0%

profile of v16, /device:TPU:0, one launch (start us, length us, event | category | flops | bytes accessed | tf_op | source)
XLA Modules:
  0.0 95.4 jit_solution(10108757980554642660)
XLA Ops:
  1.4 3.1 %collective-permute-start = (bf16[128,2,1024]{0,2,1:T(8,128)(2,1)S(1)}, bf16[128,2,1024]{0,2,1:T(8,128)(2,1)S(1)}, u32[]{:S(2)}, u32[]{:S(2)}) collective-permute-start(bf16[128,2,1024]{0,2,1:T(8,128)(2,1)S(1)} %copy.268), channel_id=1, source_target_pairs={{0,8},{8,16},{16,24},{24,28},{28,20},{20,12},{12,4},{4,0},{1,9},{9... | collective-permute-start | bytes 1572872 | tf_op jit(solution)/shard_map/ppermute | solution.py:195
  4.4 2.0 %collective-permute-start.1 = (s32[128]{0:T(128)}, s32[128]{0:T(128)S(1)}, u32[]{:S(2)}, u32[]{:S(2)}) collective-permute-start(s32[128]{0:T(128)} %param.10), channel_id=1, source_target_pairs={{0,8},{8,16},{16,24},{24,28},{28,20},{20,12},{12,4},{4,0},{1,9},{9... | collective-permute-start | bytes 1544 | tf_op jit(solution)/shard_map/ppermute | solution.py:195
  9.0 1.2 %dynamic_slice.3 = s32[1]{0:T(128)} dynamic-slice(s32[8]{0:T(128)} %constant.121.clone, s32[]{:T(128)S(6)} %select_n.196), dynamic_slice_sizes={1} | dynamic-slice | bytes 12 | tf_op jit(solution)/shard_map/dynamic_slice | solution.py:206
  10.3 1.3 %compare_select_fusion = s32[8]{0:T(128)S(1)} fusion(s32[8]{0:T(128)} %constant.123.clone, s32[]{:T(128)} %bitcast.5), kind=kLoop, calls=%fused_computation.144 | loop fusion | flops 120 | bytes 68 | tf_op jit(solution)/shard_map/select_n | solution.py:207
  13.2 1.3 %gather_fusion.1 = s32[8]{0:T(128)S(1)} fusion(s32[8]{0:T(128)} %constant.122.clone, s32[1024]{0:T(1024)S(1)} %get-tuple-element.65), kind=kCustom, calls=%fused_computation.1 | custom fusion | bytes 96 | tf_op jit(solution)/shard_map/gather | solution.py:207
  15.2 1.2 %collective-permute-done.1 = s32[128]{0:T(128)S(1)} collective-permute-done((s32[128]{0:T(128)}, s32[128]{0:T(128)S(1)}, u32[]{:S(2)}, u32[]{:S(2)}) %collective-permute-start.1) | collective-permute-done | bytes 544 | tf_op jit(solution)/shard_map/ppermute | solution.py:195
  16.4 1.5 %collective-permute-done.3 = s32[128]{0:T(128)S(1)} collective-permute-done((s32[128]{0:T(128)}, s32[128]{0:T(128)S(1)}, u32[]{:S(2)}, u32[]{:S(2)}) %collective-permute-start.3) | collective-permute-done | bytes 544 | tf_op jit(solution)/shard_map/ppermute | solution.py:198
  17.9 1.6 %collective-permute-start.4 = (bf16[128,2,1024]{0,2,1:T(8,128)(2,1)S(1)}, bf16[128,2,1024]{0,2,1:T(8,128)(2,1)S(1)}, u32[]{:S(2)}, u32[]{:S(2)}) collective-permute-start(bf16[128,2,1024]{0,2,1:T(8,128)(2,1)S(1)} %collective-permute-done), channel_id=1, source_target_pairs={{0,8},{8,16},{16,24},{24,28},{28,20},{20,12},{12,4},{4,0},{1,9},{9... | collective-permute-start | bytes 1572872 | tf_op jit(solution)/shard_map/ppermute | solution.py:195
  20.2 1.6 %collective-permute-start.5 = (s32[128]{0:T(128)S(1)}, s32[128]{0:T(128)S(1)}, u32[]{:S(2)}, u32[]{:S(2)}) collective-permute-start(s32[128]{0:T(128)S(1)} %collective-permute-done.1), channel_id=1, source_target_pairs={{0,8},{8,16},{16,24},{24,28},{28,20},{20,12},{12,4},{4,0},{1,9},{9... | collective-permute-start | bytes 1544 | tf_op jit(solution)/shard_map/ppermute | solution.py:195
  22.5 7.9 %collective-permute-done.5 = s32[128]{0:T(128)S(1)} collective-permute-done((s32[128]{0:T(128)S(1)}, s32[128]{0:T(128)S(1)}, u32[]{:S(2)}, u32[]{:S(2)}) %collective-permute-start.5) | collective-permute-done | bytes 544 | tf_op jit(solution)/shard_map/ppermute | solution.py:195
  30.4 1.3 %collective-permute-done.7 = s32[128]{0:T(128)S(1)} collective-permute-done((s32[128]{0:T(128)S(1)}, s32[128]{0:T(128)S(1)}, u32[]{:S(2)}, u32[]{:S(2)}) %collective-permute-start.7) | collective-permute-done | bytes 544 | tf_op jit(solution)/shard_map/ppermute | solution.py:198
  32.2 1.6 %collective-permute-start.8 = (bf16[128,2,1024]{0,2,1:T(8,128)(2,1)S(1)}, bf16[128,2,1024]{0,2,1:T(8,128)(2,1)}, u32[]{:S(2)}, u32[]{:S(2)}) collective-permute-start(bf16[128,2,1024]{0,2,1:T(8,128)(2,1)S(1)} %collective-permute-done.4), channel_id=1, source_target_pairs={{0,8},{8,16},{16,24},{24,28},{28,20},{20,12},{12,4},{4,0},{1,9},{9... | collective-permute-start | bytes 1572872 | tf_op jit(solution)/shard_map/ppermute | solution.py:195
  35.0 1.6 %collective-permute-start.9 = (s32[128]{0:T(128)S(1)}, s32[128]{0:T(128)S(1)}, u32[]{:S(2)}, u32[]{:S(2)}) collective-permute-start(s32[128]{0:T(128)S(1)} %collective-permute-done.5), channel_id=1, source_target_pairs={{0,8},{8,16},{16,24},{24,28},{28,20},{20,12},{12,4},{4,0},{1,9},{9... | collective-permute-start | bytes 1544 | tf_op jit(solution)/shard_map/ppermute | solution.py:195
  36.6 1.9 %fusion.83 = (bf16[128,1,1024]{0,2,1:T(8,128)(2,1)S(1)}, bf16[128,1,1024]{0,2,1:T(8,128)(2,1)}, bf16[128,1,1024]{0,2,1:T(8,128)(2,1)}, bf16[128,1,1024]{0,2,1:T(8,128)(2,1)S(1)}) fusion(bf16[128,2,1024]{0,2,1:T(8,128)(2,1)S(1)} %collective-permute-done.4, bf16[128,2,1024]{0,2,1:T(8,128)(2,1)} %collective-permute-done.6), kind=kLoop, calls=%fused_computation.183 | loop fusion | bytes 2097152 | tf_op jit(solution)/shard_map/slice | solution.py:251
  38.5 4.7 %collective-permute-done.11 = s32[128]{0:T(128)S(1)} collective-permute-done((s32[128]{0:T(128)S(1)}, s32[128]{0:T(128)S(1)}, u32[]{:S(2)}, u32[]{:S(2)}) %collective-permute-start.11) | collective-permute-done | bytes 544 | tf_op jit(solution)/shard_map/ppermute | solution.py:198
  43.2 1.6 %collective-permute-start.13 = (s32[128]{0:T(128)S(1)}, s32[128]{0:T(128)S(1)}, u32[]{:S(2)}, u32[]{:S(2)}) collective-permute-start(s32[128]{0:T(128)S(1)} %collective-permute-done.9), channel_id=1, source_target_pairs={{0,8},{8,16},{16,24},{24,28},{28,20},{20,12},{12,4},{4,0},{1,9},{9... | collective-permute-start | bytes 1544 | tf_op jit(solution)/shard_map/ppermute | solution.py:195
  44.8 1.5 %collective-permute-start.12 = (bf16[128,2,1024]{0,2,1:T(8,128)(2,1)}, bf16[128,2,1024]{0,2,1:T(8,128)(2,1)}, u32[]{:S(2)}, u32[]{:S(2)}) collective-permute-start(bf16[128,2,1024]{0,2,1:T(8,128)(2,1)} %collective-permute-done.8), channel_id=1, source_target_pairs={{0,8},{8,16},{16,24},{24,28},{28,20},{20,12},{12,4},{4,0},{1,9},{9... | collective-permute-start | bytes 1572872 | tf_op jit(solution)/shard_map/ppermute | solution.py:195
  46.4 1.9 %fusion.85 = (bf16[128,1,1024]{0,2,1:T(8,128)(2,1)S(1)}, bf16[128,1,1024]{0,2,1:T(8,128)(2,1)}, bf16[128,1,1024]{0,2,1:T(8,128)(2,1)S(1)}, bf16[128,1,1024]{0,2,1:T(8,128)(2,1)}) fusion(bf16[128,2,1024]{0,2,1:T(8,128)(2,1)} %collective-permute-done.8, bf16[128,2,1024]{0,2,1:T(8,128)(2,1)S(1)} %collective-permute-done.10), kind=kLoop, calls=%fused_computation.185 | loop fusion | bytes 2097152 | tf_op jit(solution)/shard_map/slice | solution.py:251
  48.4 2.5 %select_reduce_fusion.1 = s32[8,128]{0,1:T(8,128)S(1)} fusion(s32[8,128]{0,1:T(8,128)S(1)} %copy.206), kind=kOutput, calls=%fused_computation.63 | output fusion | flops 1096704 | bytes 8192 | tf_op jit(solution)/shard_map/jit(cumsum)/reduce_window_sum | solution.py:228
  51.6 2.1 %convolution_convert_fusion = bf16[256,1024]{1,0:T(8,128)(2,1)} fusion(bf16[128,3,1024]{2,0,1:T(8,128)(2,1)} %param.9, s32[128]{0:T(128)S(1)} %get-tuple-element.60), kind=kOutput, calls=%fused_computation.21 | convolution fusion | flops 67403776 | bytes 786944 | tf_op jit(solution)/shard_map/dot_general | solution.py:236
  53.6 3.8 %all-to-all-start = ((bf16[8,32,1024]{2,1,0:T(8,128)(2,1)}), bf16[8,32,1024]{2,1,0:T(8,128)(2,1)S(1)}, u32[]{:S(2)}, u32[]{:S(2)}) async-start(bf16[8,32,1024]{2,1,0:T(8,128)(2,1)} %bitcast.16), calls=%async_computation | async-start | bytes 1048576 | tf_op jit(solution)/shard_map/all_to_all | solution.py:238
  58.8 1.5 %fusion.26 = f32[128,1024]{0,1:T(8,128)} fusion(s32[1024]{0:T(1024)S(1)} %and_convert_fusion, s32[128]{0:T(128)S(1)} %get-tuple-element.31, s32[128]{0:T(128)S(1)} %get-tuple-element.30, s32[128]{0:T(128)S(1)} %get-tuple-element.29, s32[128]{0:T(128)S(1)} %get-tuple-element.61, s32[128]{0:T(128)S(1)} %get-tuple-element.62, s32[128]{0:T(128)S(1)} %get-tuple-element.63, ...), kind=kLoop, calls=%fused_computation.66 | loop fusion | flops 2883584 | bytes 540161 | tf_op jit(solution)/shard_map/convert_element_type | solution.py:288
  61.4 6.5 %all-to-all-done = bf16[8,32,1024]{2,1,0:T(8,128)(2,1)S(1)} async-done(((bf16[8,32,1024]{2,1,0:T(8,128)(2,1)}), bf16[8,32,1024]{2,1,0:T(8,128)(2,1)S(1)}, u32[]{:S(2)}, u32[]{:S(2)}) %all-to-all-start) | async-done | bytes 524320 | tf_op jit(solution)/shard_map/all_to_all | solution.py:238
  68.5 1.3 %convolution_dynamic-update-slice_fusion.6 = f32[8,128,1024]{1,2,0:T(8,128)S(1)} fusion(f32[8,128,1024]{1,2,0:T(8,128)S(1)} %convolution_dynamic-update-slice_fusion.7, bf16[128,8,128]{0,2,1:T(8,128)(2,1)} %bitcast.188, bf16[16,8,8,128]{3,2,1,0:T(8,128)(2,1)S(1)} %fusion.18), kind=kOutput, calls=%fused_computation.19 | convolution fusion | flops 33554432 | bytes 1048576 | tf_op jit(solution)/shard_map/qhd,khd->hqk/dot_general | solution.py:254
  69.8 1.3 %convolution_dynamic-update-slice_fusion.5 = f32[8,128,1024]{1,2,0:T(8,128)S(1)} fusion(f32[8,128,1024]{1,2,0:T(8,128)S(1)} %convolution_dynamic-update-slice_fusion.6, bf16[128,8,128]{0,2,1:T(8,128)(2,1)} %bitcast.186, bf16[16,8,8,128]{3,2,1,0:T(8,128)(2,1)S(1)} %fusion.18), kind=kOutput, calls=%fused_computation.18 | convolution fusion | flops 33554432 | bytes 1048576 | tf_op jit(solution)/shard_map/qhd,khd->hqk/dot_general | solution.py:254
  71.0 1.3 %convolution_dynamic-update-slice_fusion.4 = f32[8,128,1024]{1,2,0:T(8,128)S(1)} fusion(f32[8,128,1024]{1,2,0:T(8,128)S(1)} %convolution_dynamic-update-slice_fusion.5, bf16[128,8,128]{0,2,1:T(8,128)(2,1)} %bitcast.184, bf16[16,8,8,128]{3,2,1,0:T(8,128)(2,1)S(1)} %fusion.18), kind=kOutput, calls=%fused_computation.17 | convolution fusion | flops 33554432 | bytes 1048576 | tf_op jit(solution)/shard_map/qhd,khd->hqk/dot_general | solution.py:254
  73.7 2.6 %multiply_reduce_fusion = (f32[8,128]{1,0:T(8,128)S(1)}, bf16[8,128,1024]{1,2,0:T(8,128)(2,1)S(1)}, bf16[8,128,1024]{1,2,0:T(8,128)(2,1)S(1)}) fusion(f32[128,1024]{0,1:T(8,128)S(1)} %copy-done.2, pred[]{:T(512)S(6)} %eq.210, f32[8,128,1024]{1,2,0:T(8,128)S(1)} %convolution_dynamic-update-slice_fusion, pred[128,1024]{0,1:T(8,128)(4,1)S(1)} %fusion.27), kind=kOutput, calls=%fused_computation.3 | output fusion | flops 15729663 | bytes 9048065 | tf_op jit(solution)/shard_map/sub | solution.py:287
  80.0 1.5 %slice-done.1 = s8[4194304]{0:T(1024)(128)(4,1)S(1)} async-done(((s8[8388608]{0:T(1024)(128)(4,1)}), s8[4194304]{0:T(1024)(128)(4,1)S(1)}, s32[]{:S(2)}) %slice-start.1) | async-done | bytes 4194328
  81.5 1.3 %fusion.89 = f32[128,4096]{1,0:T(8,128)S(1)} fusion(bf16[128,1024]{0,1:T(8,128)(2,1)S(1)} %bitcast.180, bf16[1024,4096]{1,0:T(8,128)(2,1)S(1)} %bitcast.160), kind=kOutput, calls=%fused_computation.189 | convolution fusion | flops 1073741824 | bytes 10747904 | tf_op jit(solution)/shard_map/dot_general | solution.py:303
  83.0 2.0 %collective-permute-done.14 = bf16[2,32,4096]{2,1,0:T(8,128)(2,1)} collective-permute-done((bf16[2,32,4096]{2,1,0:T(8,128)(2,1)S(1)}, bf16[2,32,4096]{2,1,0:T(8,128)(2,1)}, u32[]{:S(2)}, u32[]{:S(2)}) %collective-permute-start.14) | collective-permute-done | bytes 524320 | tf_op jit(solution)/shard_map/ppermute | solution.py:322
  86.2 1.6 %collective-permute-start.15 = (bf16[1,32,4096]{2,1,0:T(8,128)(2,1)S(1)}, bf16[1,32,4096]{2,1,0:T(8,128)(2,1)S(1)}, u32[]{:S(2)}, u32[]{:S(2)}) collective-permute-start(bf16[1,32,4096]{2,1,0:T(8,128)(2,1)S(1)} %fusion.28), channel_id=1, source_target_pairs={{0,2},{1,3},{2,0},{3,1},{4,6},{5,7},{6,4},{7,5},{8,10},{9,11},{10,... | collective-permute-start | bytes 786440 | tf_op jit(solution)/shard_map/ppermute | solution.py:322
  87.8 6.9 %collective-permute-done.15 = bf16[1,32,4096]{2,1,0:T(8,128)(2,1)S(1)} collective-permute-done((bf16[1,32,4096]{2,1,0:T(8,128)(2,1)S(1)}, bf16[1,32,4096]{2,1,0:T(8,128)(2,1)S(1)}, u32[]{:S(2)}, u32[]{:S(2)}) %collective-permute-start.15) | collective-permute-done | bytes 262176 | tf_op jit(solution)/shard_map/ppermute | solution.py:322
  (93 shorter events, 18.8 us)
Async XLA Ops:
  1.4 16.5 %collective-permute-start = (bf16[128,2,1024]{0,2,1:T(8,128)(2,1)S(1)}, bf16[128,2,1024]{0,2,1:T(8,128)(2,1)S(1)}, u32[]{:S(2)}, u32[]{:S(2)}) collective-permute-start(bf16[128,2,1024]{0,2,1:T(8,128)(2,1)S(1)} %copy.268), channel_id=1, source_target_pairs={{0,8},{8,16},{16,24},{24,28},{28,20},{20,12},{12,4},{4,0},{1,9},{9... | collective-permute-start | bytes 1572872 | tf_op jit(solution)/shard_map/ppermute | solution.py:195
  4.4 13.5 %collective-permute-start.2 = (bf16[128,2,1024]{0,2,1:T(8,128)(2,1)S(1)}, bf16[128,2,1024]{0,2,1:T(8,128)(2,1)S(1)}, u32[]{:S(2)}, u32[]{:S(2)}) collective-permute-start(bf16[128,2,1024]{0,2,1:T(8,128)(2,1)S(1)} %copy.268), channel_id=1, source_target_pairs={{0,4},{8,0},{16,8},{24,16},{28,24},{20,28},{12,20},{4,12},{1,5},{9... | collective-permute-start | bytes 1572872 | tf_op jit(solution)/shard_map/ppermute | solution.py:198
  4.4 11.9 %collective-permute-start.1 = (s32[128]{0:T(128)}, s32[128]{0:T(128)S(1)}, u32[]{:S(2)}, u32[]{:S(2)}) collective-permute-start(s32[128]{0:T(128)} %param.10), channel_id=1, source_target_pairs={{0,8},{8,16},{16,24},{24,28},{28,20},{20,12},{12,4},{4,0},{1,9},{9... | collective-permute-start | bytes 1544 | tf_op jit(solution)/shard_map/ppermute | solution.py:195
  6.5 11.4 %collective-permute-start.3 = (s32[128]{0:T(128)}, s32[128]{0:T(128)S(1)}, u32[]{:S(2)}, u32[]{:S(2)}) collective-permute-start(s32[128]{0:T(128)} %param.10), channel_id=1, source_target_pairs={{0,4},{8,0},{16,8},{24,16},{28,24},{20,28},{12,20},{4,12},{1,5},{9... | collective-permute-start | bytes 1544 | tf_op jit(solution)/shard_map/ppermute | solution.py:198
  9.0 39.3 %copy-start.3 = (s32[128]{0:T(128)S(1)}, s32[128]{0:T(128)}, u32[]{:S(2)}) copy-start(s32[128]{0:T(128)} %param.10) | copy-start | bytes 1540
  17.9 13.8 %collective-permute-start.4 = (bf16[128,2,1024]{0,2,1:T(8,128)(2,1)S(1)}, bf16[128,2,1024]{0,2,1:T(8,128)(2,1)S(1)}, u32[]{:S(2)}, u32[]{:S(2)}) collective-permute-start(bf16[128,2,1024]{0,2,1:T(8,128)(2,1)S(1)} %collective-permute-done), channel_id=1, source_target_pairs={{0,8},{8,16},{16,24},{24,28},{28,20},{20,12},{12,4},{4,0},{1,9},{9... | collective-permute-start | bytes 1572872 | tf_op jit(solution)/shard_map/ppermute | solution.py:195
  19.5 12.2 %collective-permute-start.6 = (bf16[128,2,1024]{0,2,1:T(8,128)(2,1)S(1)}, bf16[128,2,1024]{0,2,1:T(8,128)(2,1)}, u32[]{:S(2)}, u32[]{:S(2)}) collective-permute-start(bf16[128,2,1024]{0,2,1:T(8,128)(2,1)S(1)} %collective-permute-done.2), channel_id=1, source_target_pairs={{0,4},{8,0},{16,8},{24,16},{28,24},{20,28},{12,20},{4,12},{1,5},{9... | collective-permute-start | bytes 1572872 | tf_op jit(solution)/shard_map/ppermute | solution.py:198
  20.2 10.1 %collective-permute-start.5 = (s32[128]{0:T(128)S(1)}, s32[128]{0:T(128)S(1)}, u32[]{:S(2)}, u32[]{:S(2)}) collective-permute-start(s32[128]{0:T(128)S(1)} %collective-permute-done.1), channel_id=1, source_target_pairs={{0,8},{8,16},{16,24},{24,28},{28,20},{20,12},{12,4},{4,0},{1,9},{9... | collective-permute-start | bytes 1544 | tf_op jit(solution)/shard_map/ppermute | solution.py:195
  21.9 9.9 %collective-permute-start.7 = (s32[128]{0:T(128)S(1)}, s32[128]{0:T(128)S(1)}, u32[]{:S(2)}, u32[]{:S(2)}) collective-permute-start(s32[128]{0:T(128)S(1)} %collective-permute-done.3), channel_id=1, source_target_pairs={{0,4},{8,0},{16,8},{24,16},{28,24},{20,28},{12,20},{4,12},{1,5},{9... | collective-permute-start | bytes 1544 | tf_op jit(solution)/shard_map/ppermute | solution.py:198
  31.7 11.5 %collective-permute-start.10 = (bf16[128,2,1024]{0,2,1:T(8,128)(2,1)}, bf16[128,2,1024]{0,2,1:T(8,128)(2,1)S(1)}, u32[]{:S(2)}, u32[]{:S(2)}) collective-permute-start(bf16[128,2,1024]{0,2,1:T(8,128)(2,1)} %collective-permute-done.6), channel_id=1, source_target_pairs={{0,4},{8,0},{16,8},{24,16},{28,24},{20,28},{12,20},{4,12},{1,5},{9... | collective-permute-start | bytes 1572872 | tf_op jit(solution)/shard_map/ppermute | solution.py:198
  32.2 11.0 %collective-permute-start.8 = (bf16[128,2,1024]{0,2,1:T(8,128)(2,1)S(1)}, bf16[128,2,1024]{0,2,1:T(8,128)(2,1)}, u32[]{:S(2)}, u32[]{:S(2)}) collective-permute-start(bf16[128,2,1024]{0,2,1:T(8,128)(2,1)S(1)} %collective-permute-done.4), channel_id=1, source_target_pairs={{0,8},{8,16},{16,24},{24,28},{28,20},{20,12},{12,4},{4,0},{1,9},{9... | collective-permute-start | bytes 1572872 | tf_op jit(solution)/shard_map/ppermute | solution.py:195
  34.5 8.7 %collective-permute-start.11 = (s32[128]{0:T(128)S(1)}, s32[128]{0:T(128)S(1)}, u32[]{:S(2)}, u32[]{:S(2)}) collective-permute-start(s32[128]{0:T(128)S(1)} %collective-permute-done.7), channel_id=1, source_target_pairs={{0,4},{8,0},{16,8},{24,16},{28,24},{20,28},{12,20},{4,12},{1,5},{9... | collective-permute-start | bytes 1544 | tf_op jit(solution)/shard_map/ppermute | solution.py:198
  35.0 8.2 %collective-permute-start.9 = (s32[128]{0:T(128)S(1)}, s32[128]{0:T(128)S(1)}, u32[]{:S(2)}, u32[]{:S(2)}) collective-permute-start(s32[128]{0:T(128)S(1)} %collective-permute-done.5), channel_id=1, source_target_pairs={{0,8},{8,16},{16,24},{24,28},{28,20},{20,12},{12,4},{4,0},{1,9},{9... | collective-permute-start | bytes 1544 | tf_op jit(solution)/shard_map/ppermute | solution.py:195
  43.2 5.1 %collective-permute-start.13 = (s32[128]{0:T(128)S(1)}, s32[128]{0:T(128)S(1)}, u32[]{:S(2)}, u32[]{:S(2)}) collective-permute-start(s32[128]{0:T(128)S(1)} %collective-permute-done.9), channel_id=1, source_target_pairs={{0,8},{8,16},{16,24},{24,28},{28,20},{20,12},{12,4},{4,0},{1,9},{9... | collective-permute-start | bytes 1544 | tf_op jit(solution)/shard_map/ppermute | solution.py:195
  44.8 15.5 %collective-permute-start.12 = (bf16[128,2,1024]{0,2,1:T(8,128)(2,1)}, bf16[128,2,1024]{0,2,1:T(8,128)(2,1)}, u32[]{:S(2)}, u32[]{:S(2)}) collective-permute-start(bf16[128,2,1024]{0,2,1:T(8,128)(2,1)} %collective-permute-done.8), channel_id=1, source_target_pairs={{0,8},{8,16},{16,24},{24,28},{28,20},{20,12},{12,4},{4,0},{1,9},{9... | collective-permute-start | bytes 1572872 | tf_op jit(solution)/shard_map/ppermute | solution.py:195
  53.6 14.2 %all-to-all-start = ((bf16[8,32,1024]{2,1,0:T(8,128)(2,1)}), bf16[8,32,1024]{2,1,0:T(8,128)(2,1)S(1)}, u32[]{:S(2)}, u32[]{:S(2)}) async-start(bf16[8,32,1024]{2,1,0:T(8,128)(2,1)} %bitcast.16), calls=%async_computation | async-start | bytes 1048576 | tf_op jit(solution)/shard_map/all_to_all | solution.py:238
  67.9 5.1 %copy-start = (bf16[128,1,1024]{0,2,1:T(8,128)(2,1)S(1)}, bf16[128,1,1024]{0,2,1:T(8,128)(2,1)}, u32[]{:S(2)}) copy-start(bf16[128,1,1024]{0,2,1:T(8,128)(2,1)} %get-tuple-element.55) | copy-start | bytes 786436
  67.9 5.5 %copy-start.1 = (bf16[128,1,1024]{0,2,1:T(8,128)(2,1)S(1)}, bf16[128,1,1024]{0,2,1:T(8,128)(2,1)}, u32[]{:S(2)}) copy-start(bf16[128,1,1024]{0,2,1:T(8,128)(2,1)} %get-tuple-element.58) | copy-start | bytes 786436
  68.1 5.5 %copy-start.2 = (f32[128,1024]{0,1:T(8,128)S(1)}, f32[128,1024]{0,1:T(8,128)}, u32[]{:S(2)}) copy-start(f32[128,1024]{0,1:T(8,128)} %fusion.26) | copy-start | bytes 1572868
  77.8 2.2 %slice-start = ((s8[8388608]{0:T(1024)(128)(4,1)}), s8[4194304]{0:T(1024)(128)(4,1)S(1)}, s32[]{:S(2)}) async-start(s8[8388608]{0:T(1024)(128)(4,1)} %bitcast.159), calls=%async_computation.1 | async-start | bytes 8388608
  79.0 2.5 %slice-start.1 = ((s8[8388608]{0:T(1024)(128)(4,1)}), s8[4194304]{0:T(1024)(128)(4,1)S(1)}, s32[]{:S(2)}) async-start(s8[8388608]{0:T(1024)(128)(4,1)} %bitcast.159), calls=%async_computation.2 | async-start | bytes 8388608
  82.9 2.1 %collective-permute-start.14 = (bf16[2,32,4096]{2,1,0:T(8,128)(2,1)S(1)}, bf16[2,32,4096]{2,1,0:T(8,128)(2,1)}, u32[]{:S(2)}, u32[]{:S(2)}) collective-permute-start(bf16[2,32,4096]{2,1,0:T(8,128)(2,1)S(1)} %fusion.24), channel_id=1, source_target_pairs={{0,1},{1,0},{2,3},{3,2},{4,5},{5,4},{6,7},{7,6},{8,9},{9,8},{10,11... | collective-permute-start | bytes 1572872 | tf_op jit(solution)/shard_map/ppermute | solution.py:322
  86.2 8.4 %collective-permute-start.15 = (bf16[1,32,4096]{2,1,0:T(8,128)(2,1)S(1)}, bf16[1,32,4096]{2,1,0:T(8,128)(2,1)S(1)}, u32[]{:S(2)}, u32[]{:S(2)}) collective-permute-start(bf16[1,32,4096]{2,1,0:T(8,128)(2,1)S(1)} %fusion.28), channel_id=1, source_target_pairs={{0,2},{1,3},{2,0},{3,1},{4,6},{5,7},{6,4},{7,5},{8,10},{9,11},{10,... | collective-permute-start | bytes 786440 | tf_op jit(solution)/shard_map/ppermute | solution.py:322

commit v17 on v13

--- a/solution.py
+++ b/solution.py
@@ -177,7 +177,7 @@
     )
 
 
-def ring_gather(block, own_index, owners):
+def ring_gather(block, own_index, owners, rider):
     if owners % 2:
         ring = list(range(owners))
     else:
@@ -196,7 +196,12 @@
         pieces[-step] = moving_right
         if step <= (owners - 1) // 2:
             moving_left = jax.tree.map(lambda x: lax.ppermute(x, "seq", left), moving_left)
-            moving_right, moving_left = lax.optimization_barrier((moving_right, moving_left))
+            if step == 1:
+                moving_right, moving_left, rider = lax.optimization_barrier(
+                    (moving_right, moving_left, rider)
+                )
+            else:
+                moving_right, moving_left = lax.optimization_barrier((moving_right, moving_left))
             pieces[step] = moving_left
         pieces[-step] = moving_right
     offsets = sorted(pieces)
@@ -205,7 +210,7 @@
     )
     where = jnp.asarray(place, jnp.int32)[own_index]
     order = jnp.asarray(ring, jnp.int32)[(where + jnp.asarray(offsets, jnp.int32)) % owners]
-    return stacked, order
+    return stacked, order, rider
 
 
 def gathered_plan(projected, destination, doc_lengths, random_blocks, global_owner, out_weight):
@@ -218,9 +223,9 @@
     blocks_all = tokens // BLK
     score_scale = 1.0 / math.sqrt(HD)
     capacity = 2 * (tok_dev // owners)
-    (keyval, key_dest), key_order = ring_gather(
-        (projected[:, 1:, :], destination), own_index, owners
-    )
+    keyval, key_order, arrival = ring_gather(projected[:, 1:, :], own_index, owners, destination)
+    key_dest = lax.all_gather(arrival, "seq", tiled=True).reshape(owners, tok_dev)[key_order]
+    key_dest = key_dest.reshape(-1)
     arrival_dest = key_dest
     target_all = arrival_dest.reshape(owners, tok_dev) // tok_dev
     onehot = (target_all[:, :, None] == jnp.arange(owners, dtype=jnp.int32)).astype(jnp.int32)

time: 86.5 us -> 99.6 us (1.15)
  blocking collectives: 0 us -> 28.3 us
  starting transfers between devices: 21.2 us -> 15.6 us
  waiting for transfers between devices: 31.9 us -> 27.2 us
  local copies, waits for them, and re-layouts: 13.8 us -> 11.4 us
  between operations: 1.68 us -> 0.44 us
    all_gather x0 -> x1, blocking collectives: none -> 28.3 us  [gathered_plan(): lax.all_gather(arrival, 'seq', tiled=True).reshape(owners, tok_dev)]
    ppermute x8 -> x4, starting transfers between devices: 14 us -> 6.71 us  [ring_gather(): lax.ppermute(x, 'seq', right)]
    ppermute x6 -> x3, waiting for transfers between devices: 4.07 us -> 1.36 us  [ring_gather(): lax.ppermute(x, 'seq', left)]
    all_to_all x1, starting transfers between devices: 3.67 us -> 6.27 us  [gathered_plan(): lax.all_to_all(outgoing, 'seq', split_axis=0, concat_axis=0, tiled=True)]
    ppermute x8 -> x4, waiting for transfers between devices: 19.1 us -> 17.1 us  [ring_gather(): lax.ppermute(x, 'seq', right)]
    slice x1, local copies, waits for them, and re-layouts: 1.8 us -> 0.44 us  [gathered_plan(): keys = keyval[:, 0, :].reshape(tokens, heads_here, HD)]
    unnamed x32 -> x31, local copies, waits for them, and re-layouts: 7.14 us -> 6.83 us
  transfers between devices with their start and end apart: 17 -> 10, of which waited for: 10 -> 5; matrix products, arithmetic and copies ran while one was open for 24% -> 12% of each run, Pallas kernels for 0% -> 0%
where the time goes in v17:
time: 99.6 us; the launch traced here: 99.1 us
  blocking collectives  28.3 us (28%)
  waiting for transfers between devices  27.2 us (27%)
  starting transfers between devices  15.6 us (16%)
  local copies, waits for them, and re-layouts  11.4 us (11%)
  other arithmetic  9.97 us (10%)
  matrix products  6.22 us (6%)
    all_gather x1, blocking collectives, gathered_plan(): lax.all_gather(arrival, 'seq', tiled=True).reshape(owners, tok_dev)  28.3 us
    ppermute x4, waiting for transfers between devices, ring_gather(): lax.ppermute(x, 'seq', right)  17.1 us
    ppermute x2, waiting for transfers between devices, head_sum(): got = lax.ppermute(send, 'head', [(i, i ^ bit) for i in range(members)])  8.74 us
    unnamed x31, local copies, waits for them, and re-layouts  6.83 us
    ppermute x4, starting transfers between devices, ring_gather(): lax.ppermute(x, 'seq', right)  6.71 us
    all_to_all x1, starting transfers between devices, gathered_plan(): lax.all_to_all(outgoing, 'seq', split_axis=0, concat_axis=0, tiled=True)  6.27 us
    another operation x1, other arithmetic, gathered_plan(): slot_all = jnp.sum((jnp.cumsum(onehot, axis=1) - onehot) * onehot, axis=2)  2.52 us
    sub x1, other arithmetic, gathered_plan(): near_exp = jnp.exp(near_scores - row_peak[..., None])  2.18 us
  transfers between devices with their start and end apart: 10, of which 5 were waited for; matrix products, arithmetic and copies ran while one was open for 12% of the time, Pallas kernels for 0%

profile of v17, /device:TPU:0, one launch (start us, length us, event | category | flops | bytes accessed | tf_op | source)
XLA Modules:
  0.0 99.1 jit_solution(6807169001840220198)
XLA Ops:
  0.0 1.2 %slice.41 = bf16[128,2,1024]{2,0,1:T(8,128)(2,1)S(1)} slice(bf16[128,3,1024]{2,0,1:T(8,128)(2,1)} %param.9), slice={[0:128], [1:3], [0:1024]} | slice | bytes 1048576 | tf_op jit(solution)/shard_map/slice | solution.py:226
  1.5 3.1 %collective-permute-start = (bf16[128,2,1024]{0,2,1:T(8,128)(2,1)S(1)}, bf16[128,2,1024]{0,2,1:T(8,128)(2,1)S(1)}, u32[]{:S(2)}, u32[]{:S(2)}) collective-permute-start(bf16[128,2,1024]{0,2,1:T(8,128)(2,1)S(1)} %copy.57), channel_id=1, source_target_pairs={{0,8},{8,16},{16,24},{24,28},{28,20},{20,12},{12,4},{4,0},{1,9},{9... | collective-permute-start | bytes 1572872 | tf_op jit(solution)/shard_map/ppermute | solution.py:195
  4.6 0.7 and_select_fusion
  5.7 0.7 multiply_add_fusion
  6.3 2.1 %convolution_convert_fusion = bf16[256,1024]{1,0:T(8,128)(2,1)} fusion(bf16[128,3,1024]{2,0,1:T(8,128)(2,1)} %param.9, s32[128]{0:T(128)S(1)} %multiply_add_fusion), kind=kOutput, calls=%fused_computation.20 | convolution fusion | flops 67403776 | bytes 786944 | tf_op jit(solution)/shard_map/dot_general | solution.py:240
  8.4 6.3 %all-to-all-start = ((bf16[8,32,1024]{2,1,0:T(8,128)(2,1)}), bf16[8,32,1024]{2,1,0:T(8,128)(2,1)S(1)}, u32[]{:S(2)}, u32[]{:S(2)}) async-start(bf16[8,32,1024]{2,1,0:T(8,128)(2,1)} %bitcast.13), calls=%async_computation | async-start | bytes 1048576 | tf_op jit(solution)/shard_map/all_to_all | solution.py:242
  14.8 0.6 dynamic_slice.3
  15.4 0.7 compare_select_fusion.2
  16.1 0.6 gather_fusion
  17.0 0.6 gather_fusion.2
  18.0 1.4 %collective-permute-done.1 = bf16[128,2,1024]{0,2,1:T(8,128)(2,1)S(1)} collective-permute-done((bf16[128,2,1024]{0,2,1:T(8,128)(2,1)S(1)}, bf16[128,2,1024]{0,2,1:T(8,128)(2,1)S(1)}, u32[]{:S(2)}, u32[]{:S(2)}) %collective-permute-start.1) | collective-permute-done | bytes 524320 | tf_op jit(solution)/shard_map/ppermute | solution.py:198
  19.3 2.1 %collective-permute-start.2 = (bf16[128,2,1024]{0,2,1:T(8,128)(2,1)S(1)}, bf16[128,2,1024]{0,2,1:T(8,128)(2,1)}, u32[]{:S(2)}, u32[]{:S(2)}) collective-permute-start(bf16[128,2,1024]{0,2,1:T(8,128)(2,1)S(1)} %collective-permute-done), channel_id=1, source_target_pairs={{0,8},{8,16},{16,24},{24,28},{28,20},{20,12},{12,4},{4,0},{1,9},{9... | collective-permute-start | bytes 1572872 | tf_op jit(solution)/shard_map/ppermute | solution.py:195
  21.5 28.3 %all-gather = s32[8,1,128]{2,1,0:T(1,128)S(1)} all-gather(s32[1,1,128]{2,1,0:T(1,128)S(1)} %bitcast.91), channel_id=1, replica_groups=mesh['seq'=8,'head'=4] {'seq'}, dimensions={0}, use_global_device_ids=true | all-gather | bytes 4608 | tf_op jit(solution)/shard_map/all_gather | solution.py:227
  49.8 0.6 gather_fusion.1
  50.5 2.5 %select_reduce_fusion.1 = s32[8,128]{0,1:T(8,128)S(1)} fusion(s32[8,128]{0,1:T(8,128)S(1)} %copy.50), kind=kOutput, calls=%fused_computation.40 | output fusion | flops 1096704 | bytes 8192 | tf_op jit(solution)/shard_map/jit(cumsum)/reduce_window_sum | solution.py:232
  53.1 1.1 %collective-permute-start.4 = (bf16[128,2,1024]{0,2,1:T(8,128)(2,1)}, bf16[128,2,1024]{0,2,1:T(8,128)(2,1)}, u32[]{:S(2)}, u32[]{:S(2)}) collective-permute-start(bf16[128,2,1024]{0,2,1:T(8,128)(2,1)} %collective-permute-done.2), channel_id=1, source_target_pairs={{0,8},{8,16},{16,24},{24,28},{28,20},{20,12},{12,4},{4,0},{1,9},{9... | collective-permute-start | bytes 1572872 | tf_op jit(solution)/shard_map/ppermute | solution.py:195
  54.3 1.0 collective-permute-start.5
  55.9 9.4 %collective-permute-done.4 = bf16[128,2,1024]{0,2,1:T(8,128)(2,1)} collective-permute-done((bf16[128,2,1024]{0,2,1:T(8,128)(2,1)}, bf16[128,2,1024]{0,2,1:T(8,128)(2,1)}, u32[]{:S(2)}, u32[]{:S(2)}) %collective-permute-start.4) | collective-permute-done | bytes 524320 | tf_op jit(solution)/shard_map/ppermute | solution.py:195
  67.1 7.7 %collective-permute-done.6 = bf16[128,2,1024]{0,2,1:T(8,128)(2,1)} collective-permute-done((bf16[128,2,1024]{0,2,1:T(8,128)(2,1)}, bf16[128,2,1024]{0,2,1:T(8,128)(2,1)}, u32[]{:S(2)}, u32[]{:S(2)}) %collective-permute-start.6) | collective-permute-done | bytes 524320 | tf_op jit(solution)/shard_map/ppermute | solution.py:195
  74.8 1.2 %constant_dynamic-update-slice_fusion.7 = bf16[1024,2,1024]{0,2,1:T(8,128)(2,1)S(1)} fusion(bf16[128,2,1024]{0,2,1:T(8,128)(2,1)} %collective-permute-done.6), kind=kLoop, calls=%fused_computation.70 | loop fusion | bytes 1048576
  76.0 1.2 %constant_dynamic-update-slice_fusion.6 = bf16[1024,2,1024]{0,2,1:T(8,128)(2,1)S(1)} fusion(bf16[1024,2,1024]{0,2,1:T(8,128)(2,1)S(1)} %constant_dynamic-update-slice_fusion.7, bf16[128,2,1024]{0,2,1:T(8,128)(2,1)} %collective-permute-done.4), kind=kLoop, calls=%fused_computation.69 | loop fusion | bytes 1048576
  77.2 1.2 %constant_dynamic-update-slice_fusion.5 = bf16[1024,2,1024]{0,2,1:T(8,128)(2,1)S(1)} fusion(bf16[1024,2,1024]{0,2,1:T(8,128)(2,1)S(1)} %constant_dynamic-update-slice_fusion.6, bf16[128,2,1024]{0,2,1:T(8,128)(2,1)} %collective-permute-done.2), kind=kLoop, calls=%fused_computation.68 | loop fusion | bytes 1048576
  79.8 0.7 fusion.37
  80.5 2.2 %multiply_reduce_fusion = (f32[8,128]{1,0:T(8,128)S(1)}, f32[8,128,1024]{2,1,0:T(8,128)S(1)}) fusion(f32[128,1024]{1,0:T(8,128)S(1)} %fusion.33, f32[8,128,1024]{2,1,0:T(8,128)S(1)} %fusion.37, pred[128,1024]{1,0:T(8,128)(4,1)S(1)} %fusion.34), kind=kOutput, calls=%fused_computation.4 | output fusion | flops 7341055 | bytes 9048064 | tf_op jit(solution)/shard_map/sub | solution.py:284
  82.7 0.8 fusion.5
  83.5 1.1 %fusion.24 = bf16[128,8,128]{0,2,1:T(8,128)(2,1)S(1)} fusion(f32[8,128,128]{2,1,0:T(8,128)S(1)} %fusion.5, bf16[1024,8,128]{0,2,1:T(8,128)(2,1)S(1)} %bitcast.85, f32[8,128,1024]{2,1,0:T(8,128)S(1)} %get-tuple-element.25, f32[128,1024]{1,0:T(8,128)S(1)} %fusion.33, pred[]{:T(512)S(6)} %eq.210, f32[128,8]{0,1:T(8,128)S(1)} %bitcast.97), kind=kOutput, calls=%fused_computation.31 | convolution fusion | flops 274071552 | bytes 7606273 | tf_op jit(solution)/shard_map/hqk,khd->qhd/dot_general | solution.py:291
  84.9 1.5 %slice-done.1 = s8[4194304]{0:T(1024)(128)(4,1)S(1)} async-done(((s8[8388608]{0:T(1024)(128)(4,1)}), s8[4194304]{0:T(1024)(128)(4,1)S(1)}, s32[]{:S(2)}) %slice-start.1) | async-done | bytes 4194328
  86.4 1.3 %fusion.59 = f32[128,4096]{1,0:T(8,128)S(1)} fusion(bf16[128,1024]{0,1:T(8,128)(2,1)S(1)} %bitcast.87, bf16[1024,4096]{1,0:T(8,128)(2,1)S(1)} %bitcast.80), kind=kOutput, calls=%fused_computation.131 | convolution fusion | flops 1073741824 | bytes 10747904 | tf_op jit(solution)/shard_map/dot_general | solution.py:297
  87.8 1.9 %collective-permute-done.7 = bf16[2,32,4096]{2,1,0:T(8,128)(2,1)S(1)} collective-permute-done((bf16[2,32,4096]{2,1,0:T(8,128)(2,1)S(1)}, bf16[2,32,4096]{2,1,0:T(8,128)(2,1)S(1)}, u32[]{:S(2)}, u32[]{:S(2)}) %collective-permute-start.7) | collective-permute-done | bytes 524320 | tf_op jit(solution)/shard_map/ppermute | solution.py:316
  89.9 1.6 %collective-permute-start.8 = (bf16[1,32,4096]{2,1,0:T(8,128)(2,1)S(1)}, bf16[1,32,4096]{2,1,0:T(8,128)(2,1)S(1)}, u32[]{:S(2)}, u32[]{:S(2)}) collective-permute-start(bf16[1,32,4096]{2,1,0:T(8,128)(2,1)S(1)} %fusion.35), channel_id=1, source_target_pairs={{0,2},{1,3},{2,0},{3,1},{4,6},{5,7},{6,4},{7,5},{8,10},{9,11},{10,... | collective-permute-start | bytes 786440 | tf_op jit(solution)/shard_map/ppermute | solution.py:316
  91.5 6.9 %collective-permute-done.8 = bf16[1,32,4096]{2,1,0:T(8,128)(2,1)S(1)} collective-permute-done((bf16[1,32,4096]{2,1,0:T(8,128)(2,1)S(1)}, bf16[1,32,4096]{2,1,0:T(8,128)(2,1)S(1)}, u32[]{:S(2)}, u32[]{:S(2)}) %collective-permute-start.8) | collective-permute-done | bytes 262176 | tf_op jit(solution)/shard_map/ppermute | solution.py:316
  98.3 0.8 fusion.36
  (67 shorter events, 5.9 us)
Async XLA Ops:
  0.0 14.8 %copy-start.8 = (s32[8]{0:T(128)S(1)}, s32[8]{0:T(128)}, u32[]{:S(2)}) copy-start(s32[8]{0:T(128)} %constant.121.clone) | copy-start | bytes 100
  0.0 15.4 %copy-start.7 = (s32[8]{0:T(128)S(1)}, s32[8]{0:T(128)}, u32[]{:S(2)}) copy-start(s32[8]{0:T(128)} %constant.123.clone) | copy-start | bytes 100
  0.0 16.1 %copy-start = (s32[8]{0:T(128)S(1)}, s32[8]{0:T(128)}, u32[]{:S(2)}) copy-start(s32[8]{0:T(128)} %constant.122.clone) | copy-start | bytes 100
  0.0 21.5 %copy-start.4 = (s32[128]{0:T(128)S(1)}, s32[128]{0:T(128)}, u32[]{:S(2)}) copy-start(s32[128]{0:T(128)} %param.10) | copy-start | bytes 1540
  0.0 14.7 %copy-start.5 = (s32[8]{0:T(128)S(1)}, s32[8]{0:T(128)}, u32[]{:S(2)}) copy-start(s32[8]{0:T(128)} %param.13) | copy-start | bytes 100
  0.0 16.7 %copy-start.6 = (s32[4]{0:T(128)S(1)}, s32[4]{0:T(128)}, u32[]{:S(2)}) copy-start(s32[4]{0:T(128)} %param.11) | copy-start | bytes 52
  0.0 16.9 %copy-start.3 = (s32[8,3]{0,1:T(4,128)S(1)}, s32[8,3]{0,1:T(4,128)}, u32[]{:S(2)}) copy-start(s32[8,3]{0,1:T(4,128)} %param.12) | copy-start | bytes 292
  1.5 16.5 %collective-permute-start = (bf16[128,2,1024]{0,2,1:T(8,128)(2,1)S(1)}, bf16[128,2,1024]{0,2,1:T(8,128)(2,1)S(1)}, u32[]{:S(2)}, u32[]{:S(2)}) collective-permute-start(bf16[128,2,1024]{0,2,1:T(8,128)(2,1)S(1)} %copy.57), channel_id=1, source_target_pairs={{0,8},{8,16},{16,24},{24,28},{28,20},{20,12},{12,4},{4,0},{1,9},{9... | collective-permute-start | bytes 1572872 | tf_op jit(solution)/shard_map/ppermute | solution.py:195
  4.6 14.8 %collective-permute-start.1 = (bf16[128,2,1024]{0,2,1:T(8,128)(2,1)S(1)}, bf16[128,2,1024]{0,2,1:T(8,128)(2,1)S(1)}, u32[]{:S(2)}, u32[]{:S(2)}) collective-permute-start(bf16[128,2,1024]{0,2,1:T(8,128)(2,1)S(1)} %copy.57), channel_id=1, source_target_pairs={{0,4},{8,0},{16,8},{24,16},{28,24},{20,28},{12,20},{4,12},{1,5},{9... | collective-permute-start | bytes 1572872 | tf_op jit(solution)/shard_map/ppermute | solution.py:198
  8.4 58.4 %all-to-all-start = ((bf16[8,32,1024]{2,1,0:T(8,128)(2,1)}), bf16[8,32,1024]{2,1,0:T(8,128)(2,1)S(1)}, u32[]{:S(2)}, u32[]{:S(2)}) async-start(bf16[8,32,1024]{2,1,0:T(8,128)(2,1)} %bitcast.13), calls=%async_computation | async-start | bytes 1048576 | tf_op jit(solution)/shard_map/all_to_all | solution.py:242
  19.3 33.8 %collective-permute-start.2 = (bf16[128,2,1024]{0,2,1:T(8,128)(2,1)S(1)}, bf16[128,2,1024]{0,2,1:T(8,128)(2,1)}, u32[]{:S(2)}, u32[]{:S(2)}) collective-permute-start(bf16[128,2,1024]{0,2,1:T(8,128)(2,1)S(1)} %collective-permute-done), channel_id=1, source_target_pairs={{0,8},{8,16},{16,24},{24,28},{28,20},{20,12},{12,4},{4,0},{1,9},{9... | collective-permute-start | bytes 1572872 | tf_op jit(solution)/shard_map/ppermute | solution.py:195
  21.5 31.6 %collective-permute-start.3 = (bf16[128,2,1024]{0,2,1:T(8,128)(2,1)S(1)}, bf16[128,2,1024]{0,2,1:T(8,128)(2,1)S(1)}, u32[]{:S(2)}, u32[]{:S(2)}) collective-permute-start(bf16[128,2,1024]{0,2,1:T(8,128)(2,1)S(1)} %collective-permute-done.1), channel_id=1, source_target_pairs={{0,4},{8,0},{16,8},{24,16},{28,24},{20,28},{12,20},{4,12},{1,5},{9... | collective-permute-start | bytes 1572872 | tf_op jit(solution)/shard_map/ppermute | solution.py:198
  53.1 12.1 %collective-permute-start.4 = (bf16[128,2,1024]{0,2,1:T(8,128)(2,1)}, bf16[128,2,1024]{0,2,1:T(8,128)(2,1)}, u32[]{:S(2)}, u32[]{:S(2)}) collective-permute-start(bf16[128,2,1024]{0,2,1:T(8,128)(2,1)} %collective-permute-done.2), channel_id=1, source_target_pairs={{0,8},{8,16},{16,24},{24,28},{28,20},{20,12},{12,4},{4,0},{1,9},{9... | collective-permute-start | bytes 1572872 | tf_op jit(solution)/shard_map/ppermute | solution.py:195
  54.3 11.0 %collective-permute-start.5 = (bf16[128,2,1024]{0,2,1:T(8,128)(2,1)S(1)}, bf16[128,2,1024]{0,2,1:T(8,128)(2,1)S(1)}, u32[]{:S(2)}, u32[]{:S(2)}) collective-permute-start(bf16[128,2,1024]{0,2,1:T(8,128)(2,1)S(1)} %collective-permute-done.3), channel_id=1, source_target_pairs={{0,4},{8,0},{16,8},{24,16},{28,24},{20,28},{12,20},{4,12},{1,5},{9... | collective-permute-start | bytes 1572872 | tf_op jit(solution)/shard_map/ppermute | solution.py:198
  65.3 0.8 copy-start.1
  65.3 9.5 %collective-permute-start.6 = (bf16[128,2,1024]{0,2,1:T(8,128)(2,1)}, bf16[128,2,1024]{0,2,1:T(8,128)(2,1)}, u32[]{:S(2)}, u32[]{:S(2)}) collective-permute-start(bf16[128,2,1024]{0,2,1:T(8,128)(2,1)} %collective-permute-done.4), channel_id=1, source_target_pairs={{0,8},{8,16},{16,24},{24,28},{28,20},{20,12},{12,4},{4,0},{1,9},{9... | collective-permute-start | bytes 1572872 | tf_op jit(solution)/shard_map/ppermute | solution.py:195
  66.8 12.3 %copy-start.2 = (bf16[128,2,1024]{0,2,1:T(8,128)(2,1)S(1)}, bf16[128,2,1024]{0,2,1:T(8,128)(2,1)}, u32[]{:S(2)}) copy-start(bf16[128,2,1024]{0,2,1:T(8,128)(2,1)} %copy-done.1) | copy-start | bytes 1572868
  82.7 2.2 %slice-start = ((s8[8388608]{0:T(1024)(128)(4,1)}), s8[4194304]{0:T(1024)(128)(4,1)S(1)}, s32[]{:S(2)}) async-start(s8[8388608]{0:T(1024)(128)(4,1)} %bitcast.79), calls=%async_computation.1 | async-start | bytes 8388608
  83.5 2.9 %slice-start.1 = ((s8[8388608]{0:T(1024)(128)(4,1)}), s8[4194304]{0:T(1024)(128)(4,1)S(1)}, s32[]{:S(2)}) async-start(s8[8388608]{0:T(1024)(128)(4,1)} %bitcast.79), calls=%async_computation.2 | async-start | bytes 8388608
  87.8 2.0 %collective-permute-start.7 = (bf16[2,32,4096]{2,1,0:T(8,128)(2,1)S(1)}, bf16[2,32,4096]{2,1,0:T(8,128)(2,1)S(1)}, u32[]{:S(2)}, u32[]{:S(2)}) collective-permute-start(bf16[2,32,4096]{2,1,0:T(8,128)(2,1)S(1)} %fusion.31), channel_id=1, source_target_pairs={{0,1},{1,0},{2,3},{3,2},{4,5},{5,4},{6,7},{7,6},{8,9},{9,8},{10,11... | collective-permute-start | bytes 1572872 | tf_op jit(solution)/shard_map/ppermute | solution.py:316
  89.9 8.4 %collective-permute-start.8 = (bf16[1,32,4096]{2,1,0:T(8,128)(2,1)S(1)}, bf16[1,32,4096]{2,1,0:T(8,128)(2,1)S(1)}, u32[]{:S(2)}, u32[]{:S(2)}) collective-permute-start(bf16[1,32,4096]{2,1,0:T(8,128)(2,1)S(1)} %fusion.35), channel_id=1, source_target_pairs={{0,2},{1,3},{2,0},{3,1},{4,6},{5,7},{6,4},{7,5},{8,10},{9,11},{10,... | collective-permute-start | bytes 786440 | tf_op jit(solution)/shard_map/ppermute | solution.py:316

commit v18 on v17

--- a/solution.py
+++ b/solution.py
@@ -197,9 +197,15 @@
         if step <= (owners - 1) // 2:
             moving_left = jax.tree.map(lambda x: lax.ppermute(x, "seq", left), moving_left)
             if step == 1:
-                moving_right, moving_left, rider = lax.optimization_barrier(
-                    (moving_right, moving_left, rider)
+                moving_right, moving_left, first = lax.optimization_barrier(
+                    (moving_right, moving_left, rider[0])
                 )
+                rider = (first, rider[1])
+            elif step == owners // 2 - 1:
+                moving_right, moving_left, second = lax.optimization_barrier(
+                    (moving_right, moving_left, rider[1])
+                )
+                rider = (rider[0], second)
             else:
                 moving_right, moving_left = lax.optimization_barrier((moving_right, moving_left))
             pieces[step] = moving_left
@@ -223,13 +229,6 @@
     blocks_all = tokens // BLK
     score_scale = 1.0 / math.sqrt(HD)
     capacity = 2 * (tok_dev // owners)
-    keyval, key_order, arrival = ring_gather(projected[:, 1:, :], own_index, owners, destination)
-    key_dest = lax.all_gather(arrival, "seq", tiled=True).reshape(owners, tok_dev)[key_order]
-    key_dest = key_dest.reshape(-1)
-    arrival_dest = key_dest
-    target_all = arrival_dest.reshape(owners, tok_dev) // tok_dev
-    onehot = (target_all[:, :, None] == jnp.arange(owners, dtype=jnp.int32)).astype(jnp.int32)
-    slot_all = jnp.sum((jnp.cumsum(onehot, axis=1) - onehot) * onehot, axis=2)
     target = destination // tok_dev
     mine = (target[:, None] == jnp.arange(owners, dtype=jnp.int32)[None, :]).astype(jnp.int32)
     slot = jnp.sum((jnp.cumsum(mine, axis=0) - mine) * mine, axis=1)
@@ -239,6 +238,15 @@
     ).astype(projected.dtype)
     outgoing = jnp.dot(send_pick, projected[:, 0, :], preferred_element_type=jnp.float32)
     outgoing = outgoing.astype(projected.dtype).reshape(owners, capacity, columns)
+    keyval, key_order, (arrival, outgoing) = ring_gather(
+        projected[:, 1:, :], own_index, owners, (destination, outgoing)
+    )
+    key_dest = lax.all_gather(arrival, "seq", tiled=True).reshape(owners, tok_dev)[key_order]
+    key_dest = key_dest.reshape(-1)
+    arrival_dest = key_dest
+    target_all = arrival_dest.reshape(owners, tok_dev) // tok_dev
+    onehot = (target_all[:, :, None] == jnp.arange(owners, dtype=jnp.int32)).astype(jnp.int32)
+    slot_all = jnp.sum((jnp.cumsum(onehot, axis=1) - onehot) * onehot, axis=2)
     incoming = lax.all_to_all(outgoing, "seq", split_axis=0, concat_axis=0, tiled=True)
     my_pos = own_index * tok_dev + jnp.arange(tok_dev, dtype=jnp.int32)
     source = jnp.repeat(key_order, tok_dev)

time: 99.6 us -> 97.3 us (0.977)
  blocking collectives: 28.3 us -> 24 us
  local copies, waits for them, and re-layouts: 11.4 us -> 15 us
  starting transfers between devices: 15.6 us -> 12.5 us
  other arithmetic: 9.97 us -> 11.2 us
  between operations: 0.44 us -> 1.65 us
  waiting for transfers between devices: 27.2 us -> 26.2 us
    all_gather x1, blocking collectives: 28.3 us -> 24 us  [gathered_plan(): lax.all_gather(arrival, 'seq', tiled=True).reshape(owners, tok_dev)]
    all_to_all x1, starting transfers between devices: 6.27 us -> 3.68 us  [gathered_plan(): lax.all_to_all(outgoing, 'seq', split_axis=0, concat_axis=0, tiled=True)]
    ppermute x4, starting transfers between devices: 6.71 us -> 4.71 us  [ring_gather(): lax.ppermute(x, 'seq', right)]
    ppermute x3, starting transfers between devices: 0.97 us -> 2.47 us  [ring_gather(): lax.ppermute(x, 'seq', left)]
    slice x1, local copies, waits for them, and re-layouts: 0.44 us -> 1.8 us  [gathered_plan(): keys = keyval[:, 0, :].reshape(tokens, heads_here, HD)]
    ppermute x4, waiting for transfers between devices: 17.1 us -> 15.9 us  [ring_gather(): lax.ppermute(x, 'seq', right)]
    unnamed x31 -> x25, local copies, waits for them, and re-layouts: 6.83 us -> 7.84 us
  transfers between devices with their start and end apart: 10 -> 10, of which waited for: 5 -> 6; matrix products, arithmetic and copies ran while one was open for 12% -> 22% of each run, Pallas kernels for 0% -> 0%
where the time goes in v18:
time: 97.3 us; the launch traced here: 96.8 us
  waiting for transfers between devices  26.2 us (27%)
  blocking collectives  24 us (25%)
  local copies, waits for them, and re-layouts  15 us (15%)
  starting transfers between devices  12.5 us (13%)
  other arithmetic  11.2 us (12%)
  matrix products  6.24 us (6%)
  between operations  1.65 us (2%)
    all_gather x1, blocking collectives, gathered_plan(): lax.all_gather(arrival, 'seq', tiled=True).reshape(owners, tok_dev)  24 us
    ppermute x4, waiting for transfers between devices, ring_gather(): lax.ppermute(x, 'seq', right)  15.9 us
    ppermute x2, waiting for transfers between devices, head_sum(): got = lax.ppermute(send, 'head', [(i, i ^ bit) for i in range(members)])  8.74 us
    unnamed x25, local copies, waits for them, and re-layouts  7.84 us
    ppermute x4, starting transfers between devices, ring_gather(): lax.ppermute(x, 'seq', right)  4.71 us
    all_to_all x1, starting transfers between devices, gathered_plan(): lax.all_to_all(outgoing, 'seq', split_axis=0, concat_axis=0, tiled=True)  3.68 us
    another operation x1, other arithmetic, gathered_plan(): slot_all = jnp.sum((jnp.cumsum(onehot, axis=1) - onehot) * onehot, axis=2)  2.52 us
    ppermute x3, starting transfers between devices, ring_gather(): lax.ppermute(x, 'seq', left)  2.47 us
  transfers between devices with their start and end apart: 10, of which 6 were waited for; matrix products, arithmetic and copies ran while one was open for 22% of the time, Pallas kernels for 0%

profile of v18, /device:TPU:0, one launch (start us, length us, event | category | flops | bytes accessed | tf_op | source)
XLA Modules:
  0.0 96.8 jit_solution(12418053486139931585)
XLA Ops:
  0.0 1.1 %slice.41 = bf16[128,2,1024]{2,0,1:T(8,128)(2,1)S(1)} slice(bf16[128,3,1024]{2,0,1:T(8,128)(2,1)} %param.9), slice={[0:128], [1:3], [0:1024]} | slice | bytes 1048576 | tf_op jit(solution)/shard_map/slice | solution.py:242
  1.4 3.1 %collective-permute-start = (bf16[128,2,1024]{0,2,1:T(8,128)(2,1)S(1)}, bf16[128,2,1024]{0,2,1:T(8,128)(2,1)S(1)}, u32[]{:S(2)}, u32[]{:S(2)}) collective-permute-start(bf16[128,2,1024]{0,2,1:T(8,128)(2,1)S(1)} %copy.57), channel_id=1, source_target_pairs={{0,8},{8,16},{16,24},{24,28},{28,20},{20,12},{12,4},{4,0},{1,9},{9... | collective-permute-start | bytes 1572872 | tf_op jit(solution)/shard_map/ppermute | solution.py:195
  4.5 1.2 %dynamic_slice.3 = s32[1]{0:T(128)} dynamic-slice(s32[8]{0:T(128)} %constant.121.clone, s32[]{:T(128)S(6)} %select_n.198), dynamic_slice_sizes={1} | dynamic-slice | bytes 12 | tf_op jit(solution)/shard_map/dynamic_slice | solution.py:217
  5.7 1.3 %compare_select_fusion.2 = s32[8]{0:T(128)S(1)} fusion(s32[8]{0:T(128)} %constant.123.clone, s32[]{:T(128)} %bitcast.8), kind=kLoop, calls=%fused_computation.93 | loop fusion | flops 120 | bytes 68 | tf_op jit(solution)/shard_map/select_n | solution.py:218
  7.1 1.3 %gather_fusion = s32[8]{0:T(128)S(1)} fusion(s32[8]{0:T(128)} %constant.122.clone, s32[1024]{0:T(1024)S(1)} %get-tuple-element.29), kind=kCustom, calls=%fused_computation | custom fusion | bytes 96 | tf_op jit(solution)/shard_map/gather | solution.py:218
  10.8 0.8 reduce-window.8
  11.7 0.8 copy.49
  13.4 0.7 multiply_add_fusion
  14.0 2.0 %convolution_convert_fusion = bf16[256,1024]{1,0:T(8,128)(2,1)} fusion(bf16[128,3,1024]{2,0,1:T(8,128)(2,1)} %param.9, s32[128]{0:T(128)S(1)} %multiply_add_fusion), kind=kOutput, calls=%fused_computation.20 | convolution fusion | flops 67403776 | bytes 786944 | tf_op jit(solution)/shard_map/dot_general | solution.py:239
  16.3 1.5 %collective-permute-done.1 = bf16[128,2,1024]{0,2,1:T(8,128)(2,1)S(1)} collective-permute-done((bf16[128,2,1024]{0,2,1:T(8,128)(2,1)S(1)}, bf16[128,2,1024]{0,2,1:T(8,128)(2,1)S(1)}, u32[]{:S(2)}, u32[]{:S(2)}) %collective-permute-start.1) | collective-permute-done | bytes 524320 | tf_op jit(solution)/shard_map/ppermute | solution.py:198
  17.9 1.6 %collective-permute-start.2 = (bf16[128,2,1024]{0,2,1:T(8,128)(2,1)S(1)}, bf16[128,2,1024]{0,2,1:T(8,128)(2,1)}, u32[]{:S(2)}, u32[]{:S(2)}) collective-permute-start(bf16[128,2,1024]{0,2,1:T(8,128)(2,1)S(1)} %collective-permute-done), channel_id=1, source_target_pairs={{0,8},{8,16},{16,24},{24,28},{28,20},{20,12},{12,4},{4,0},{1,9},{9... | collective-permute-start | bytes 1572872 | tf_op jit(solution)/shard_map/ppermute | solution.py:195
  19.9 24.0 %all-gather = s32[8,1,128]{2,1,0:T(1,128)S(1)} all-gather(s32[1,1,128]{2,1,0:T(1,128)S(1)} %bitcast.91), channel_id=1, replica_groups=mesh['seq'=8,'head'=4] {'seq'}, dimensions={0}, use_global_device_ids=true | all-gather | bytes 4608 | tf_op jit(solution)/shard_map/all_gather | solution.py:244
  44.5 2.5 %select_reduce_fusion.1 = s32[8,128]{0,1:T(8,128)S(1)} fusion(s32[8,128]{0,1:T(8,128)S(1)} %copy.50), kind=kOutput, calls=%fused_computation.40 | output fusion | flops 1096704 | bytes 8192 | tf_op jit(solution)/shard_map/jit(cumsum)/reduce_window_sum | solution.py:249
  47.3 2.0 %collective-permute-start.5 = (bf16[128,2,1024]{0,2,1:T(8,128)(2,1)S(1)}, bf16[128,2,1024]{0,2,1:T(8,128)(2,1)S(1)}, u32[]{:S(2)}, u32[]{:S(2)}) collective-permute-start(bf16[128,2,1024]{0,2,1:T(8,128)(2,1)S(1)} %collective-permute-done.3), channel_id=1, source_target_pairs={{0,4},{8,0},{16,8},{24,16},{28,24},{20,28},{12,20},{4,12},{1,5},{9... | collective-permute-start | bytes 1572872 | tf_op jit(solution)/shard_map/ppermute | solution.py:198
  49.5 10.0 %collective-permute-done.4 = bf16[128,2,1024]{0,2,1:T(8,128)(2,1)} collective-permute-done((bf16[128,2,1024]{0,2,1:T(8,128)(2,1)}, bf16[128,2,1024]{0,2,1:T(8,128)(2,1)}, u32[]{:S(2)}, u32[]{:S(2)}) %collective-permute-start.4) | collective-permute-done | bytes 524320 | tf_op jit(solution)/shard_map/ppermute | solution.py:195
  59.6 0.7 copy-done.3
  61.4 3.7 %all-to-all-start = ((bf16[8,32,1024]{2,1,0:T(8,128)(2,1)}), bf16[8,32,1024]{2,1,0:T(8,128)(2,1)S(1)}, u32[]{:S(2)}, u32[]{:S(2)}) async-start(bf16[8,32,1024]{2,1,0:T(8,128)(2,1)} %bitcast.1), calls=%async_computation | async-start | bytes 1048576 | tf_op jit(solution)/shard_map/all_to_all | solution.py:250
  65.2 5.7 %collective-permute-done.6 = bf16[128,2,1024]{0,2,1:T(8,128)(2,1)} collective-permute-done((bf16[128,2,1024]{0,2,1:T(8,128)(2,1)}, bf16[128,2,1024]{0,2,1:T(8,128)(2,1)}, u32[]{:S(2)}, u32[]{:S(2)}) %collective-permute-start.6) | collective-permute-done | bytes 524320 | tf_op jit(solution)/shard_map/ppermute | solution.py:195
  70.8 1.2 %constant_dynamic-update-slice_fusion.7 = bf16[1024,2,1024]{0,2,1:T(8,128)(2,1)S(1)} fusion(bf16[128,2,1024]{0,2,1:T(8,128)(2,1)} %collective-permute-done.6), kind=kLoop, calls=%fused_computation.70 | loop fusion | bytes 1048576
  72.0 1.2 %constant_dynamic-update-slice_fusion.6 = bf16[1024,2,1024]{0,2,1:T(8,128)(2,1)S(1)} fusion(bf16[1024,2,1024]{0,2,1:T(8,128)(2,1)S(1)} %constant_dynamic-update-slice_fusion.7, bf16[128,2,1024]{0,2,1:T(8,128)(2,1)} %collective-permute-done.4), kind=kLoop, calls=%fused_computation.69 | loop fusion | bytes 1048576
  73.2 1.2 %constant_dynamic-update-slice_fusion.5 = bf16[1024,2,1024]{0,2,1:T(8,128)(2,1)S(1)} fusion(bf16[1024,2,1024]{0,2,1:T(8,128)(2,1)S(1)} %constant_dynamic-update-slice_fusion.6, bf16[128,2,1024]{0,2,1:T(8,128)(2,1)} %collective-permute-done.2), kind=kLoop, calls=%fused_computation.68 | loop fusion | bytes 1048576
  75.4 1.8 %fusion.58 = (bf16[1024,1,1024]{0,2,1:T(8,128)(2,1)S(1)}, bf16[1024,1,1024]{0,2,1:T(8,128)(2,1)}) fusion(bf16[1024,2,1024]{0,2,1:T(8,128)(2,1)S(1)} %constant_dynamic-update-slice_fusion), kind=kLoop, calls=%fused_computation.130 | loop fusion | bytes 8388608 | tf_op jit(solution)/shard_map/slice | solution.py:263
  77.5 0.7 fusion.37
  78.2 2.2 %multiply_reduce_fusion = (f32[8,128]{1,0:T(8,128)S(1)}, f32[8,128,1024]{2,1,0:T(8,128)S(1)}) fusion(f32[128,1024]{1,0:T(8,128)S(1)} %fusion.33, f32[8,128,1024]{2,1,0:T(8,128)S(1)} %fusion.37, pred[128,1024]{1,0:T(8,128)(4,1)S(1)} %fusion.34), kind=kOutput, calls=%fused_computation.4 | output fusion | flops 7341055 | bytes 9048064 | tf_op jit(solution)/shard_map/sub | solution.py:292
  80.4 0.8 fusion.5
  81.2 1.1 %fusion.24 = bf16[128,8,128]{0,2,1:T(8,128)(2,1)S(1)} fusion(f32[8,128,128]{2,1,0:T(8,128)S(1)} %fusion.5, bf16[1024,8,128]{0,2,1:T(8,128)(2,1)S(1)} %bitcast.85, f32[8,128,1024]{2,1,0:T(8,128)S(1)} %get-tuple-element.27, f32[128,1024]{1,0:T(8,128)S(1)} %fusion.33, pred[]{:T(512)S(6)} %eq.216, f32[128,8]{0,1:T(8,128)S(1)} %bitcast.97), kind=kOutput, calls=%fused_computation.31 | convolution fusion | flops 274071552 | bytes 7606273 | tf_op jit(solution)/shard_map/hqk,khd->qhd/dot_general | solution.py:299
  82.5 1.5 %slice-done.1 = s8[4194304]{0:T(1024)(128)(4,1)S(1)} async-done(((s8[8388608]{0:T(1024)(128)(4,1)}), s8[4194304]{0:T(1024)(128)(4,1)S(1)}, s32[]{:S(2)}) %slice-start.1) | async-done | bytes 4194328
  84.0 1.3 %fusion.59 = f32[128,4096]{1,0:T(8,128)S(1)} fusion(bf16[128,1024]{0,1:T(8,128)(2,1)S(1)} %bitcast.87, bf16[1024,4096]{1,0:T(8,128)(2,1)S(1)} %bitcast.80), kind=kOutput, calls=%fused_computation.131 | convolution fusion | flops 1073741824 | bytes 10747904 | tf_op jit(solution)/shard_map/dot_general | solution.py:305
  85.5 1.9 %collective-permute-done.7 = bf16[2,32,4096]{2,1,0:T(8,128)(2,1)S(1)} collective-permute-done((bf16[2,32,4096]{2,1,0:T(8,128)(2,1)S(1)}, bf16[2,32,4096]{2,1,0:T(8,128)(2,1)S(1)}, u32[]{:S(2)}, u32[]{:S(2)}) %collective-permute-start.7) | collective-permute-done | bytes 524320 | tf_op jit(solution)/shard_map/ppermute | solution.py:324
  87.6 1.6 %collective-permute-start.8 = (bf16[1,32,4096]{2,1,0:T(8,128)(2,1)S(1)}, bf16[1,32,4096]{2,1,0:T(8,128)(2,1)S(1)}, u32[]{:S(2)}, u32[]{:S(2)}) collective-permute-start(bf16[1,32,4096]{2,1,0:T(8,128)(2,1)S(1)} %fusion.35), channel_id=1, source_target_pairs={{0,2},{1,3},{2,0},{3,1},{4,6},{5,7},{6,4},{7,5},{8,10},{9,11},{10,... | collective-permute-start | bytes 786440 | tf_op jit(solution)/shard_map/ppermute | solution.py:324
  89.2 6.9 %collective-permute-done.8 = bf16[1,32,4096]{2,1,0:T(8,128)(2,1)S(1)} collective-permute-done((bf16[1,32,4096]{2,1,0:T(8,128)(2,1)S(1)}, bf16[1,32,4096]{2,1,0:T(8,128)(2,1)S(1)}, u32[]{:S(2)}, u32[]{:S(2)}) %collective-permute-start.8) | collective-permute-done | bytes 262176 | tf_op jit(solution)/shard_map/ppermute | solution.py:324
  96.0 0.8 fusion.36
  (61 shorter events, 7.1 us)
Async XLA Ops:
  0.0 19.9 %copy-start.5 = (s32[128]{0:T(128)S(1)}, s32[128]{0:T(128)}, u32[]{:S(2)}) copy-start(s32[128]{0:T(128)} %param.10) | copy-start | bytes 1540
  1.4 14.9 %collective-permute-start = (bf16[128,2,1024]{0,2,1:T(8,128)(2,1)S(1)}, bf16[128,2,1024]{0,2,1:T(8,128)(2,1)S(1)}, u32[]{:S(2)}, u32[]{:S(2)}) collective-permute-start(bf16[128,2,1024]{0,2,1:T(8,128)(2,1)S(1)} %copy.57), channel_id=1, source_target_pairs={{0,8},{8,16},{16,24},{24,28},{28,20},{20,12},{12,4},{4,0},{1,9},{9... | collective-permute-start | bytes 1572872 | tf_op jit(solution)/shard_map/ppermute | solution.py:195
  4.5 13.4 %collective-permute-start.1 = (bf16[128,2,1024]{0,2,1:T(8,128)(2,1)S(1)}, bf16[128,2,1024]{0,2,1:T(8,128)(2,1)S(1)}, u32[]{:S(2)}, u32[]{:S(2)}) collective-permute-start(bf16[128,2,1024]{0,2,1:T(8,128)(2,1)S(1)} %copy.57), channel_id=1, source_target_pairs={{0,4},{8,0},{16,8},{24,16},{28,24},{20,28},{12,20},{4,12},{1,5},{9... | collective-permute-start | bytes 1572872 | tf_op jit(solution)/shard_map/ppermute | solution.py:198
  17.9 29.3 %collective-permute-start.2 = (bf16[128,2,1024]{0,2,1:T(8,128)(2,1)S(1)}, bf16[128,2,1024]{0,2,1:T(8,128)(2,1)}, u32[]{:S(2)}, u32[]{:S(2)}) collective-permute-start(bf16[128,2,1024]{0,2,1:T(8,128)(2,1)S(1)} %collective-permute-done), channel_id=1, source_target_pairs={{0,8},{8,16},{16,24},{24,28},{28,20},{20,12},{12,4},{4,0},{1,9},{9... | collective-permute-start | bytes 1572872 | tf_op jit(solution)/shard_map/ppermute | solution.py:195
  19.4 27.8 %collective-permute-start.3 = (bf16[128,2,1024]{0,2,1:T(8,128)(2,1)S(1)}, bf16[128,2,1024]{0,2,1:T(8,128)(2,1)S(1)}, u32[]{:S(2)}, u32[]{:S(2)}) collective-permute-start(bf16[128,2,1024]{0,2,1:T(8,128)(2,1)S(1)} %collective-permute-done.1), channel_id=1, source_target_pairs={{0,4},{8,0},{16,8},{24,16},{28,24},{20,28},{12,20},{4,12},{1,5},{9... | collective-permute-start | bytes 1572872 | tf_op jit(solution)/shard_map/ppermute | solution.py:198
  47.2 14.2 %copy-start.1 = (bf16[128,2,1024]{0,2,1:T(8,128)(2,1)}, bf16[128,2,1024]{0,2,1:T(8,128)(2,1)S(1)}, u32[]{:S(2)}) copy-start(bf16[128,2,1024]{0,2,1:T(8,128)(2,1)S(1)} %collective-permute-done.3) | copy-start | bytes 1572868
  47.2 12.3 %collective-permute-start.4 = (bf16[128,2,1024]{0,2,1:T(8,128)(2,1)}, bf16[128,2,1024]{0,2,1:T(8,128)(2,1)}, u32[]{:S(2)}, u32[]{:S(2)}) collective-permute-start(bf16[128,2,1024]{0,2,1:T(8,128)(2,1)} %collective-permute-done.2), channel_id=1, source_target_pairs={{0,8},{8,16},{16,24},{24,28},{28,20},{20,12},{12,4},{4,0},{1,9},{9... | collective-permute-start | bytes 1572872 | tf_op jit(solution)/shard_map/ppermute | solution.py:195
  47.3 12.2 %collective-permute-start.5 = (bf16[128,2,1024]{0,2,1:T(8,128)(2,1)S(1)}, bf16[128,2,1024]{0,2,1:T(8,128)(2,1)S(1)}, u32[]{:S(2)}, u32[]{:S(2)}) collective-permute-start(bf16[128,2,1024]{0,2,1:T(8,128)(2,1)S(1)} %collective-permute-done.3), channel_id=1, source_target_pairs={{0,4},{8,0},{16,8},{24,16},{28,24},{20,28},{12,20},{4,12},{1,5},{9... | collective-permute-start | bytes 1572872 | tf_op jit(solution)/shard_map/ppermute | solution.py:198
  59.5 0.8 copy-start.3
  59.5 11.3 %collective-permute-start.6 = (bf16[128,2,1024]{0,2,1:T(8,128)(2,1)}, bf16[128,2,1024]{0,2,1:T(8,128)(2,1)}, u32[]{:S(2)}, u32[]{:S(2)}) collective-permute-start(bf16[128,2,1024]{0,2,1:T(8,128)(2,1)} %collective-permute-done.4), channel_id=1, source_target_pairs={{0,8},{8,16},{16,24},{24,28},{28,20},{20,12},{12,4},{4,0},{1,9},{9... | collective-permute-start | bytes 1572872 | tf_op jit(solution)/shard_map/ppermute | solution.py:195
  61.4 15.8 %all-to-all-start = ((bf16[8,32,1024]{2,1,0:T(8,128)(2,1)}), bf16[8,32,1024]{2,1,0:T(8,128)(2,1)S(1)}, u32[]{:S(2)}, u32[]{:S(2)}) async-start(bf16[8,32,1024]{2,1,0:T(8,128)(2,1)} %bitcast.1), calls=%async_computation | async-start | bytes 1048576 | tf_op jit(solution)/shard_map/all_to_all | solution.py:250
  65.1 9.9 %copy-start.2 = (bf16[128,2,1024]{0,2,1:T(8,128)(2,1)S(1)}, bf16[128,2,1024]{0,2,1:T(8,128)(2,1)}, u32[]{:S(2)}) copy-start(bf16[128,2,1024]{0,2,1:T(8,128)(2,1)} %copy-done.1) | copy-start | bytes 1572868
  65.1 10.1 %copy-start.4 = (bf16[128,2,1024]{0,2,1:T(8,128)(2,1)S(1)}, bf16[128,2,1024]{0,2,1:T(8,128)(2,1)}, u32[]{:S(2)}) copy-start(bf16[128,2,1024]{0,2,1:T(8,128)(2,1)} %copy-done.3) | copy-start | bytes 1572868
  78.2 2.2 %copy-start = (bf16[1024,1,1024]{0,2,1:T(8,128)(2,1)S(1)}, bf16[1024,1,1024]{0,2,1:T(8,128)(2,1)}, u32[]{:S(2)}) copy-start(bf16[1024,1,1024]{0,2,1:T(8,128)(2,1)} %get-tuple-element.25) | copy-start | bytes 6291460
  80.4 2.2 %slice-start = ((s8[8388608]{0:T(1024)(128)(4,1)}), s8[4194304]{0:T(1024)(128)(4,1)S(1)}, s32[]{:S(2)}) async-start(s8[8388608]{0:T(1024)(128)(4,1)} %bitcast.79), calls=%async_computation.1 | async-start | bytes 8388608
  81.2 2.8 %slice-start.1 = ((s8[8388608]{0:T(1024)(128)(4,1)}), s8[4194304]{0:T(1024)(128)(4,1)S(1)}, s32[]{:S(2)}) async-start(s8[8388608]{0:T(1024)(128)(4,1)} %bitcast.79), calls=%async_computation.2 | async-start | bytes 8388608
  85.4 2.0 %collective-permute-start.7 = (bf16[2,32,4096]{2,1,0:T(8,128)(2,1)S(1)}, bf16[2,32,4096]{2,1,0:T(8,128)(2,1)S(1)}, u32[]{:S(2)}, u32[]{:S(2)}) collective-permute-start(bf16[2,32,4096]{2,1,0:T(8,128)(2,1)S(1)} %fusion.31), channel_id=1, source_target_pairs={{0,1},{1,0},{2,3},{3,2},{4,5},{5,4},{6,7},{7,6},{8,9},{9,8},{10,11... | collective-permute-start | bytes 1572872 | tf_op jit(solution)/shard_map/ppermute | solution.py:324
  87.6 8.4 %collective-permute-start.8 = (bf16[1,32,4096]{2,1,0:T(8,128)(2,1)S(1)}, bf16[1,32,4096]{2,1,0:T(8,128)(2,1)S(1)}, u32[]{:S(2)}, u32[]{:S(2)}) collective-permute-start(bf16[1,32,4096]{2,1,0:T(8,128)(2,1)S(1)} %fusion.35), channel_id=1, source_target_pairs={{0,2},{1,3},{2,0},{3,1},{4,6},{5,7},{6,4},{7,5},{8,10},{9,11},{10,... | collective-permute-start | bytes 786440 | tf_op jit(solution)/shard_map/ppermute | solution.py:324

commit v19 on v17

--- a/solution.py
+++ b/solution.py
@@ -196,7 +196,7 @@
         pieces[-step] = moving_right
         if step <= (owners - 1) // 2:
             moving_left = jax.tree.map(lambda x: lax.ppermute(x, "seq", left), moving_left)
-            if step == 1:
+            if step == owners // 2 - 1:
                 moving_right, moving_left, rider = lax.optimization_barrier(
                     (moving_right, moving_left, rider)
                 )
@@ -223,13 +223,11 @@
     blocks_all = tokens // BLK
     score_scale = 1.0 / math.sqrt(HD)
     capacity = 2 * (tok_dev // owners)
-    keyval, key_order, arrival = ring_gather(projected[:, 1:, :], own_index, owners, destination)
-    key_dest = lax.all_gather(arrival, "seq", tiled=True).reshape(owners, tok_dev)[key_order]
-    key_dest = key_dest.reshape(-1)
-    arrival_dest = key_dest
-    target_all = arrival_dest.reshape(owners, tok_dev) // tok_dev
-    onehot = (target_all[:, :, None] == jnp.arange(owners, dtype=jnp.int32)).astype(jnp.int32)
-    slot_all = jnp.sum((jnp.cumsum(onehot, axis=1) - onehot) * onehot, axis=2)
+    lanes = jnp.arange(128, dtype=jnp.int32)[None, :]
+    dest_hi = jnp.where(lanes == 0, (destination // 32)[:, None], 0)
+    dest_lo = jnp.where(lanes == 0, (destination % 32)[:, None], 0)
+    tag = jnp.stack([dest_hi, dest_lo], axis=1).astype(projected.dtype)
+    message = jnp.concatenate([projected[:, 1:, :], tag], axis=2)
     target = destination // tok_dev
     mine = (target[:, None] == jnp.arange(owners, dtype=jnp.int32)[None, :]).astype(jnp.int32)
     slot = jnp.sum((jnp.cumsum(mine, axis=0) - mine) * mine, axis=1)
@@ -239,6 +237,15 @@
     ).astype(projected.dtype)
     outgoing = jnp.dot(send_pick, projected[:, 0, :], preferred_element_type=jnp.float32)
     outgoing = outgoing.astype(projected.dtype).reshape(owners, capacity, columns)
+    stacked, key_order, outgoing = ring_gather(message, own_index, owners, outgoing)
+    key_dest = stacked[:, 0, columns].astype(jnp.int32) * 32 + stacked[:, 1, columns].astype(
+        jnp.int32
+    )
+    keyval = stacked[:, :, :columns]
+    arrival_dest = key_dest
+    target_all = arrival_dest.reshape(owners, tok_dev) // tok_dev
+    onehot = (target_all[:, :, None] == jnp.arange(owners, dtype=jnp.int32)).astype(jnp.int32)
+    slot_all = jnp.sum((jnp.cumsum(onehot, axis=1) - onehot) * onehot, axis=2)
     incoming = lax.all_to_all(outgoing, "seq", split_axis=0, concat_axis=0, tiled=True)
     my_pos = own_index * tok_dev + jnp.arange(tok_dev, dtype=jnp.int32)
     source = jnp.repeat(key_order, tok_dev)

time: 99.6 us -> 103 us (1.034)
  the two profiles are of different devices: /device:TPU:0 before, /device:TPU:16 now
where the time goes in v19:
time: 103 us; the launch traced here: 102 us
  waiting for transfers between devices  53.4 us (52%)
  local copies, waits for them, and re-layouts  17.8 us (17%)
  starting transfers between devices  13.9 us (13%)
  other arithmetic  10.3 us (10%)
  matrix products  6.29 us (6%)
    ppermute x4, waiting for transfers between devices, ring_gather(): lax.ppermute(x, 'seq', right)  41.8 us
    ppermute x2, waiting for transfers between devices, head_sum(): got = lax.ppermute(send, 'head', [(i, i ^ bit) for i in range(members)])  8.75 us
    unnamed x26, local copies, waits for them, and re-layouts  8.55 us
    all_to_all x1, starting transfers between devices, gathered_plan(): lax.all_to_all(outgoing, 'seq', split_axis=0, concat_axis=0, tiled=True)  5.6 us
    ppermute x4, starting transfers between devices, ring_gather(): lax.ppermute(x, 'seq', right)  4.32 us
    slice x1, local copies, waits for them, and re-layouts, gathered_plan(): keys = keyval[:, 0, :].reshape(tokens, heads_here, HD)  4.04 us
    ppermute x3, waiting for transfers between devices, ring_gather(): lax.ppermute(x, 'seq', left)  2.84 us
    another operation x1, other arithmetic, gathered_plan(): slot_all = jnp.sum((jnp.cumsum(onehot, axis=1) - onehot) * onehot, axis=2)  2.52 us
  transfers between devices with their start and end apart: 10, of which 9 were waited for; matrix products, arithmetic and copies ran while one was open for 21% of the time, Pallas kernels for 0%

profile of v19, /device:TPU:16, one launch (start us, length us, event | category | flops | bytes accessed | tf_op | source)
XLA Modules:
  0.0 102.1 jit_solution(11939647030628174506)
XLA Ops:
  0.0 0.7 and_select_fusion.6
  0.7 1.1 %slice.50 = bf16[128,2,1024]{2,0,1:T(8,128)(2,1)S(1)} slice(bf16[128,3,1024]{2,0,1:T(8,128)(2,1)} %param.9), slice={[0:128], [1:3], [0:1024]} | slice | bytes 1048576 | tf_op jit(solution)/shard_map/slice | solution.py:230
  2.2 1.6 %collective-permute-start = (bf16[128,2,1152]{0,2,1:T(8,128)(2,1)S(1)}, bf16[128,2,1152]{0,2,1:T(8,128)(2,1)S(1)}, u32[]{:S(2)}, u32[]{:S(2)}) collective-permute-start(bf16[128,2,1152]{0,2,1:T(8,128)(2,1)S(1)} %maximum_maximum_fusion), channel_id=1, source_target_pairs={{0,8},{8,16},{16,24},{24,28},{28,20},{20,12},{12,4},{4,0},{1,9},{9... | collective-permute-start | bytes 1769480 | tf_op jit(solution)/shard_map/ppermute | solution.py:195
  4.3 13.0 %collective-permute-done = bf16[128,2,1152]{0,2,1:T(8,128)(2,1)S(1)} collective-permute-done((bf16[128,2,1152]{0,2,1:T(8,128)(2,1)S(1)}, bf16[128,2,1152]{0,2,1:T(8,128)(2,1)S(1)}, u32[]{:S(2)}, u32[]{:S(2)}) %collective-permute-start) | collective-permute-done | bytes 589856 | tf_op jit(solution)/shard_map/ppermute | solution.py:195
  17.4 1.3 %collective-permute-done.1 = bf16[128,2,1152]{0,2,1:T(8,128)(2,1)S(1)} collective-permute-done((bf16[128,2,1152]{0,2,1:T(8,128)(2,1)S(1)}, bf16[128,2,1152]{0,2,1:T(8,128)(2,1)S(1)}, u32[]{:S(2)}, u32[]{:S(2)}) %collective-permute-start.1) | collective-permute-done | bytes 589856 | tf_op jit(solution)/shard_map/ppermute | solution.py:198
  18.7 1.5 %collective-permute-start.2 = (bf16[128,2,1152]{0,2,1:T(8,128)(2,1)S(1)}, bf16[128,2,1152]{0,2,1:T(8,128)(2,1)S(1)}, u32[]{:S(2)}, u32[]{:S(2)}) collective-permute-start(bf16[128,2,1152]{0,2,1:T(8,128)(2,1)S(1)} %collective-permute-done), channel_id=1, source_target_pairs={{0,8},{8,16},{16,24},{24,28},{28,20},{20,12},{12,4},{4,0},{1,9},{9... | collective-permute-start | bytes 1769480 | tf_op jit(solution)/shard_map/ppermute | solution.py:195
  20.7 1.2 %dynamic_slice.3 = s32[1]{0:T(128)} dynamic-slice(s32[8]{0:T(128)} %constant.141.clone, s32[]{:T(128)S(6)} %select_n.229), dynamic_slice_sizes={1} | dynamic-slice | bytes 12 | tf_op jit(solution)/shard_map/dynamic_slice | solution.py:211
  21.9 1.3 %compare_select_fusion = s32[8]{0:T(128)S(1)} fusion(s32[8]{0:T(128)} %constant.143.clone, s32[]{:T(128)} %bitcast.8), kind=kLoop, calls=%fused_computation.96 | loop fusion | flops 120 | bytes 68 | tf_op jit(solution)/shard_map/select_n | solution.py:212
  23.3 9.2 %collective-permute-done.2 = bf16[128,2,1152]{0,2,1:T(8,128)(2,1)S(1)} collective-permute-done((bf16[128,2,1152]{0,2,1:T(8,128)(2,1)S(1)}, bf16[128,2,1152]{0,2,1:T(8,128)(2,1)S(1)}, u32[]{:S(2)}, u32[]{:S(2)}) %collective-permute-start.2) | collective-permute-done | bytes 589856 | tf_op jit(solution)/shard_map/ppermute | solution.py:195
  32.5 1.2 %collective-permute-done.3 = bf16[128,2,1152]{0,2,1:T(8,128)(2,1)S(1)} collective-permute-done((bf16[128,2,1152]{0,2,1:T(8,128)(2,1)S(1)}, bf16[128,2,1152]{0,2,1:T(8,128)(2,1)S(1)}, u32[]{:S(2)}, u32[]{:S(2)}) %collective-permute-start.3) | collective-permute-done | bytes 589856 | tf_op jit(solution)/shard_map/ppermute | solution.py:198
  34.4 1.4 %collective-permute-start.5 = (bf16[128,2,1152]{0,2,1:T(8,128)(2,1)S(1)}, bf16[128,2,1152]{0,2,1:T(8,128)(2,1)}, u32[]{:S(2)}, u32[]{:S(2)}) collective-permute-start(bf16[128,2,1152]{0,2,1:T(8,128)(2,1)S(1)} %collective-permute-done.3), channel_id=1, source_target_pairs={{0,4},{8,0},{16,8},{24,16},{28,24},{20,28},{12,20},{4,12},{1,5},{9... | collective-permute-start | bytes 1769480 | tf_op jit(solution)/shard_map/ppermute | solution.py:198
  36.2 2.1 %convolution_convert_fusion = bf16[256,1024]{1,0:T(8,128)(2,1)} fusion(bf16[128,3,1024]{2,0,1:T(8,128)(2,1)} %param.9, s32[128]{0:T(128)S(1)} %multiply_add_fusion), kind=kOutput, calls=%fused_computation.19 | convolution fusion | flops 67403776 | bytes 786944 | tf_op jit(solution)/shard_map/dot_general | solution.py:238
  38.2 8.5 %collective-permute-done.4 = bf16[128,2,1152]{0,2,1:T(8,128)(2,1)} collective-permute-done((bf16[128,2,1152]{0,2,1:T(8,128)(2,1)S(1)}, bf16[128,2,1152]{0,2,1:T(8,128)(2,1)}, u32[]{:S(2)}, u32[]{:S(2)}) %collective-permute-start.4) | collective-permute-done | bytes 589856 | tf_op jit(solution)/shard_map/ppermute | solution.py:195
  49.6 5.6 %all-to-all-start = ((bf16[8,32,1024]{2,1,0:T(8,128)(2,1)}), bf16[8,32,1024]{2,1,0:T(8,128)(2,1)S(1)}, u32[]{:S(2)}, u32[]{:S(2)}) async-start(bf16[8,32,1024]{2,1,0:T(8,128)(2,1)} %bitcast.1), calls=%async_computation | async-start | bytes 1048576 | tf_op jit(solution)/shard_map/all_to_all | solution.py:249
  55.2 11.0 %collective-permute-done.6 = bf16[128,2,1152]{0,2,1:T(8,128)(2,1)} collective-permute-done((bf16[128,2,1152]{0,2,1:T(8,128)(2,1)}, bf16[128,2,1152]{0,2,1:T(8,128)(2,1)}, u32[]{:S(2)}, u32[]{:S(2)}) %collective-permute-start.6) | collective-permute-done | bytes 589856 | tf_op jit(solution)/shard_map/ppermute | solution.py:195
  66.2 1.2 %constant_dynamic-update-slice_fusion.7 = bf16[1024,2,1152]{0,2,1:T(8,128)(2,1)S(1)} fusion(bf16[128,2,1152]{0,2,1:T(8,128)(2,1)} %collective-permute-done.6), kind=kLoop, calls=%fused_computation.72 | loop fusion | bytes 1179648
  67.5 1.3 %constant_dynamic-update-slice_fusion.6 = bf16[1024,2,1152]{0,2,1:T(8,128)(2,1)S(1)} fusion(bf16[1024,2,1152]{0,2,1:T(8,128)(2,1)S(1)} %constant_dynamic-update-slice_fusion.7, bf16[128,2,1152]{0,2,1:T(8,128)(2,1)} %collective-permute-done.4), kind=kLoop, calls=%fused_computation.71 | loop fusion | bytes 1179648
  68.7 1.3 %constant_dynamic-update-slice_fusion.5 = bf16[1024,2,1152]{0,2,1:T(8,128)(2,1)S(1)} fusion(bf16[1024,2,1152]{0,2,1:T(8,128)(2,1)S(1)} %constant_dynamic-update-slice_fusion.6, bf16[128,2,1152]{0,2,1:T(8,128)(2,1)} %copy-done.3), kind=kLoop, calls=%fused_computation.70 | loop fusion | bytes 1179648
  70.8 1.3 %constant_dynamic-update-slice_fusion = bf16[1024,2,1152]{0,2,1:T(8,128)(2,1)S(1)} fusion(bf16[1024,2,1152]{0,2,1:T(8,128)(2,1)S(1)} %constant_dynamic-update-slice_fusion.1, bf16[128,2,1152]{0,2,1:T(8,128)(2,1)} %collective-permute-done.5), kind=kLoop, calls=%fused_computation.65 | loop fusion | bytes 1179648 | tf_op jit(solution)/shard_map/concatenate | solution.py:209
  72.1 2.1 %copy-done.2 = bf16[1024,2,1152]{0,2,1:T(8,128)(2,1)} copy-done((bf16[1024,2,1152]{0,2,1:T(8,128)(2,1)}, bf16[1024,2,1152]{0,2,1:T(8,128)(2,1)S(1)}, u32[]{:S(2)}) %copy-start.2) | copy-done | bytes 4718616
  74.4 2.5 %select_reduce_fusion.1 = s32[8,128]{0,1:T(8,128)S(1)} fusion(s32[8,128]{0,1:T(8,128)S(1)} %copy.51), kind=kOutput, calls=%fused_computation.40 | output fusion | flops 1096704 | bytes 8192 | tf_op jit(solution)/shard_map/jit(cumsum)/reduce_window_sum | solution.py:248
  78.4 4.0 %fusion.59 = (bf16[1024,1,1024]{0,2,1:T(8,128)(2,1)S(1)}, bf16[1024,1,1024]{0,2,1:T(8,128)(2,1)}) fusion(bf16[1024,2,1152]{0,2,1:T(8,128)(2,1)} %copy-done.2), kind=kLoop, calls=%fused_computation.139 | loop fusion | bytes 8388608 | tf_op jit(solution)/shard_map/slice | solution.py:262
  82.8 0.7 fusion.37
  83.5 2.2 %multiply_reduce_fusion = (f32[8,128]{1,0:T(8,128)S(1)}, f32[8,128,1024]{2,1,0:T(8,128)S(1)}) fusion(f32[128,1024]{1,0:T(8,128)S(1)} %fusion.33, f32[8,128,1024]{2,1,0:T(8,128)S(1)} %fusion.37, pred[128,1024]{1,0:T(8,128)(4,1)S(1)} %fusion.34), kind=kOutput, calls=%fused_computation.3 | output fusion | flops 7341055 | bytes 9048064 | tf_op jit(solution)/shard_map/sub | solution.py:291
  85.7 0.8 fusion.5
  86.5 1.1 %fusion.24 = bf16[128,8,128]{0,2,1:T(8,128)(2,1)S(1)} fusion(f32[8,128,128]{2,1,0:T(8,128)S(1)} %fusion.5, bf16[1024,8,128]{0,2,1:T(8,128)(2,1)S(1)} %bitcast.78, f32[8,128,1024]{2,1,0:T(8,128)S(1)} %get-tuple-element.30, f32[128,1024]{1,0:T(8,128)S(1)} %fusion.33, pred[]{:T(512)S(6)} %eq.229, f32[128,8]{0,1:T(8,128)S(1)} %bitcast.91), kind=kOutput, calls=%fused_computation.30 | convolution fusion | flops 274071552 | bytes 7606273 | tf_op jit(solution)/shard_map/hqk,khd->qhd/dot_general | solution.py:298
  87.8 1.5 %slice-done.1 = s8[4194304]{0:T(1024)(128)(4,1)S(1)} async-done(((s8[8388608]{0:T(1024)(128)(4,1)}), s8[4194304]{0:T(1024)(128)(4,1)S(1)}, s32[]{:S(2)}) %slice-start.1) | async-done | bytes 4194328
  89.3 1.3 %fusion.60 = f32[128,4096]{1,0:T(8,128)S(1)} fusion(bf16[128,1024]{0,1:T(8,128)(2,1)S(1)} %bitcast.80, bf16[1024,4096]{1,0:T(8,128)(2,1)S(1)} %bitcast.73), kind=kOutput, calls=%fused_computation.140 | convolution fusion | flops 1073741824 | bytes 10747904 | tf_op jit(solution)/shard_map/dot_general | solution.py:304
  90.8 1.9 %collective-permute-done.7 = bf16[2,32,4096]{2,1,0:T(8,128)(2,1)S(1)} collective-permute-done((bf16[2,32,4096]{2,1,0:T(8,128)(2,1)S(1)}, bf16[2,32,4096]{2,1,0:T(8,128)(2,1)S(1)}, u32[]{:S(2)}, u32[]{:S(2)}) %collective-permute-start.7) | collective-permute-done | bytes 524320 | tf_op jit(solution)/shard_map/ppermute | solution.py:323
  92.9 1.6 %collective-permute-start.8 = (bf16[1,32,4096]{2,1,0:T(8,128)(2,1)S(1)}, bf16[1,32,4096]{2,1,0:T(8,128)(2,1)S(1)}, u32[]{:S(2)}, u32[]{:S(2)}) collective-permute-start(bf16[1,32,4096]{2,1,0:T(8,128)(2,1)S(1)} %fusion.35), channel_id=1, source_target_pairs={{0,2},{1,3},{2,0},{3,1},{4,6},{5,7},{6,4},{7,5},{8,10},{9,11},{10,... | collective-permute-start | bytes 786440 | tf_op jit(solution)/shard_map/ppermute | solution.py:323
  94.5 6.9 %collective-permute-done.8 = bf16[1,32,4096]{2,1,0:T(8,128)(2,1)S(1)} collective-permute-done((bf16[1,32,4096]{2,1,0:T(8,128)(2,1)S(1)}, bf16[1,32,4096]{2,1,0:T(8,128)(2,1)S(1)}, u32[]{:S(2)}, u32[]{:S(2)}) %collective-permute-start.8) | collective-permute-done | bytes 262176 | tf_op jit(solution)/shard_map/ppermute | solution.py:323
  101.3 0.8 fusion.36
  (62 shorter events, 8.4 us)
Async XLA Ops:
  0.0 48.6 %copy-start = (s32[8]{0:T(128)S(1)}, s32[8]{0:T(128)}, u32[]{:S(2)}) copy-start(s32[8]{0:T(128)} %constant.142.clone) | copy-start | bytes 100
  0.0 47.6 %copy-start.5 = (s32[8]{0:T(128)S(1)}, s32[8]{0:T(128)}, u32[]{:S(2)}) copy-start(s32[8]{0:T(128)} %param.13) | copy-start | bytes 100
  0.0 47.7 %copy-start.6 = (s32[4]{0:T(128)S(1)}, s32[4]{0:T(128)}, u32[]{:S(2)}) copy-start(s32[4]{0:T(128)} %param.11) | copy-start | bytes 52
  0.0 47.9 %copy-start.4 = (s32[8,3]{0,1:T(4,128)S(1)}, s32[8,3]{0,1:T(4,128)}, u32[]{:S(2)}) copy-start(s32[8,3]{0,1:T(4,128)} %param.12) | copy-start | bytes 292
  2.2 15.1 %collective-permute-start = (bf16[128,2,1152]{0,2,1:T(8,128)(2,1)S(1)}, bf16[128,2,1152]{0,2,1:T(8,128)(2,1)S(1)}, u32[]{:S(2)}, u32[]{:S(2)}) collective-permute-start(bf16[128,2,1152]{0,2,1:T(8,128)(2,1)S(1)} %maximum_maximum_fusion), channel_id=1, source_target_pairs={{0,8},{8,16},{16,24},{24,28},{28,20},{20,12},{12,4},{4,0},{1,9},{9... | collective-permute-start | bytes 1769480 | tf_op jit(solution)/shard_map/ppermute | solution.py:195
  3.9 14.8 %collective-permute-start.1 = (bf16[128,2,1152]{0,2,1:T(8,128)(2,1)S(1)}, bf16[128,2,1152]{0,2,1:T(8,128)(2,1)S(1)}, u32[]{:S(2)}, u32[]{:S(2)}) collective-permute-start(bf16[128,2,1152]{0,2,1:T(8,128)(2,1)S(1)} %maximum_maximum_fusion), channel_id=1, source_target_pairs={{0,4},{8,0},{16,8},{24,16},{28,24},{20,28},{12,20},{4,12},{1,5},{9... | collective-permute-start | bytes 1769480 | tf_op jit(solution)/shard_map/ppermute | solution.py:198
  18.7 13.9 %collective-permute-start.2 = (bf16[128,2,1152]{0,2,1:T(8,128)(2,1)S(1)}, bf16[128,2,1152]{0,2,1:T(8,128)(2,1)S(1)}, u32[]{:S(2)}, u32[]{:S(2)}) collective-permute-start(bf16[128,2,1152]{0,2,1:T(8,128)(2,1)S(1)} %collective-permute-done), channel_id=1, source_target_pairs={{0,8},{8,16},{16,24},{24,28},{28,20},{20,12},{12,4},{4,0},{1,9},{9... | collective-permute-start | bytes 1769480 | tf_op jit(solution)/shard_map/ppermute | solution.py:195
  20.2 13.6 %collective-permute-start.3 = (bf16[128,2,1152]{0,2,1:T(8,128)(2,1)S(1)}, bf16[128,2,1152]{0,2,1:T(8,128)(2,1)S(1)}, u32[]{:S(2)}, u32[]{:S(2)}) collective-permute-start(bf16[128,2,1152]{0,2,1:T(8,128)(2,1)S(1)} %collective-permute-done.1), channel_id=1, source_target_pairs={{0,4},{8,0},{16,8},{24,16},{28,24},{20,28},{12,20},{4,12},{1,5},{9... | collective-permute-start | bytes 1769480 | tf_op jit(solution)/shard_map/ppermute | solution.py:198
  32.5 17.0 %copy-start.3 = (bf16[128,2,1152]{0,2,1:T(8,128)(2,1)}, bf16[128,2,1152]{0,2,1:T(8,128)(2,1)S(1)}, u32[]{:S(2)}) copy-start(bf16[128,2,1152]{0,2,1:T(8,128)(2,1)S(1)} %collective-permute-done.2) | copy-start | bytes 1769476
  33.8 12.9 %collective-permute-start.4 = (bf16[128,2,1152]{0,2,1:T(8,128)(2,1)S(1)}, bf16[128,2,1152]{0,2,1:T(8,128)(2,1)}, u32[]{:S(2)}, u32[]{:S(2)}) collective-permute-start(bf16[128,2,1152]{0,2,1:T(8,128)(2,1)S(1)} %collective-permute-done.2), channel_id=1, source_target_pairs={{0,8},{8,16},{16,24},{24,28},{28,20},{20,12},{12,4},{4,0},{1,9},{9... | collective-permute-start | bytes 1769480 | tf_op jit(solution)/shard_map/ppermute | solution.py:195
  34.4 12.7 %collective-permute-start.5 = (bf16[128,2,1152]{0,2,1:T(8,128)(2,1)S(1)}, bf16[128,2,1152]{0,2,1:T(8,128)(2,1)}, u32[]{:S(2)}, u32[]{:S(2)}) collective-permute-start(bf16[128,2,1152]{0,2,1:T(8,128)(2,1)S(1)} %collective-permute-done.3), channel_id=1, source_target_pairs={{0,4},{8,0},{16,8},{24,16},{28,24},{20,28},{12,20},{4,12},{1,5},{9... | collective-permute-start | bytes 1769480 | tf_op jit(solution)/shard_map/ppermute | solution.py:198
  47.0 19.2 %collective-permute-start.6 = (bf16[128,2,1152]{0,2,1:T(8,128)(2,1)}, bf16[128,2,1152]{0,2,1:T(8,128)(2,1)}, u32[]{:S(2)}, u32[]{:S(2)}) collective-permute-start(bf16[128,2,1152]{0,2,1:T(8,128)(2,1)} %collective-permute-done.4), channel_id=1, source_target_pairs={{0,8},{8,16},{16,24},{24,28},{28,20},{20,12},{12,4},{4,0},{1,9},{9... | collective-permute-start | bytes 1769480 | tf_op jit(solution)/shard_map/ppermute | solution.py:195
  49.6 32.9 %all-to-all-start = ((bf16[8,32,1024]{2,1,0:T(8,128)(2,1)}), bf16[8,32,1024]{2,1,0:T(8,128)(2,1)S(1)}, u32[]{:S(2)}, u32[]{:S(2)}) async-start(bf16[8,32,1024]{2,1,0:T(8,128)(2,1)} %bitcast.1), calls=%async_computation | async-start | bytes 1048576 | tf_op jit(solution)/shard_map/all_to_all | solution.py:249
  72.1 2.1 %copy-start.2 = (bf16[1024,2,1152]{0,2,1:T(8,128)(2,1)}, bf16[1024,2,1152]{0,2,1:T(8,128)(2,1)S(1)}, u32[]{:S(2)}) copy-start(bf16[1024,2,1152]{0,2,1:T(8,128)(2,1)S(1)} %constant_dynamic-update-slice_fusion) | copy-start | bytes 14155780
  83.5 2.2 %copy-start.1 = (bf16[1024,1,1024]{0,2,1:T(8,128)(2,1)S(1)}, bf16[1024,1,1024]{0,2,1:T(8,128)(2,1)}, u32[]{:S(2)}) copy-start(bf16[1024,1,1024]{0,2,1:T(8,128)(2,1)} %get-tuple-element.23) | copy-start | bytes 6291460
  85.6 2.2 %slice-start = ((s8[8388608]{0:T(1024)(128)(4,1)}), s8[4194304]{0:T(1024)(128)(4,1)S(1)}, s32[]{:S(2)}) async-start(s8[8388608]{0:T(1024)(128)(4,1)} %bitcast.72), calls=%async_computation.1 | async-start | bytes 8388608
  86.5 2.8 %slice-start.1 = ((s8[8388608]{0:T(1024)(128)(4,1)}), s8[4194304]{0:T(1024)(128)(4,1)S(1)}, s32[]{:S(2)}) async-start(s8[8388608]{0:T(1024)(128)(4,1)} %bitcast.72), calls=%async_computation.2 | async-start | bytes 8388608
  90.7 2.0 %collective-permute-start.7 = (bf16[2,32,4096]{2,1,0:T(8,128)(2,1)S(1)}, bf16[2,32,4096]{2,1,0:T(8,128)(2,1)S(1)}, u32[]{:S(2)}, u32[]{:S(2)}) collective-permute-start(bf16[2,32,4096]{2,1,0:T(8,128)(2,1)S(1)} %fusion.31), channel_id=1, source_target_pairs={{0,1},{1,0},{2,3},{3,2},{4,5},{5,4},{6,7},{7,6},{8,9},{9,8},{10,11... | collective-permute-start | bytes 1572872 | tf_op jit(solution)/shard_map/ppermute | solution.py:323
  92.9 8.4 %collective-permute-start.8 = (bf16[1,32,4096]{2,1,0:T(8,128)(2,1)S(1)}, bf16[1,32,4096]{2,1,0:T(8,128)(2,1)S(1)}, u32[]{:S(2)}, u32[]{:S(2)}) collective-permute-start(bf16[1,32,4096]{2,1,0:T(8,128)(2,1)S(1)} %fusion.35), channel_id=1, source_target_pairs={{0,2},{1,3},{2,0},{3,1},{4,6},{5,7},{6,4},{7,5},{8,10},{9,11},{10,... | collective-permute-start | bytes 786440 | tf_op jit(solution)/shard_map/ppermute | solution.py:323

commit v20 on v17

--- a/solution.py
+++ b/solution.py
@@ -177,7 +177,7 @@
     )
 
 
-def ring_gather(block, own_index, owners, rider):
+def ring_gather(block, own_index, owners, rider=None):
     if owners % 2:
         ring = list(range(owners))
     else:
@@ -196,7 +196,7 @@
         pieces[-step] = moving_right
         if step <= (owners - 1) // 2:
             moving_left = jax.tree.map(lambda x: lax.ppermute(x, "seq", left), moving_left)
-            if step == 1:
+            if step == 1 and rider is not None:
                 moving_right, moving_left, rider = lax.optimization_barrier(
                     (moving_right, moving_left, rider)
                 )
@@ -223,9 +223,8 @@
     blocks_all = tokens // BLK
     score_scale = 1.0 / math.sqrt(HD)
     capacity = 2 * (tok_dev // owners)
-    keyval, key_order, arrival = ring_gather(projected[:, 1:, :], own_index, owners, destination)
-    key_dest = lax.all_gather(arrival, "seq", tiled=True).reshape(owners, tok_dev)[key_order]
-    key_dest = key_dest.reshape(-1)
+    dest_ring, key_order, _ = ring_gather(destination, own_index, owners)
+    keyval, _, key_dest = ring_gather(projected[:, 1:, :], own_index, owners, dest_ring)
     arrival_dest = key_dest
     target_all = arrival_dest.reshape(owners, tok_dev) // tok_dev
     onehot = (target_all[:, :, None] == jnp.arange(owners, dtype=jnp.int32)).astype(jnp.int32)

time: 99.6 us -> 103 us (1.034)
  blocking collectives: 28.3 us -> 0 us
  waiting for transfers between devices: 27.2 us -> 47.5 us
  starting transfers between devices: 15.6 us -> 24.1 us
  between operations: 0.44 us -> 1.61 us
    all_gather x1 -> x0, blocking collectives: 28.3 us -> none  [gathered_plan(): lax.all_gather(arrival, 'seq', tiled=True).reshape(owners, tok_dev)]
    ppermute x3 -> x6, waiting for transfers between devices: 1.36 us -> 17 us  [ring_gather(): lax.ppermute(x, 'seq', left)]
    ppermute x4 -> x8, starting transfers between devices: 6.71 us -> 16.1 us  [ring_gather(): lax.ppermute(x, 'seq', right)]
    ppermute x4 -> x8, waiting for transfers between devices: 17.1 us -> 21.7 us  [ring_gather(): lax.ppermute(x, 'seq', right)]
    all_to_all x1, starting transfers between devices: 6.27 us -> 3.81 us  [gathered_plan(): lax.all_to_all(outgoing, 'seq', split_axis=0, concat_axis=0, tiled=True)]
    ppermute x3 -> x6, starting transfers between devices: 0.97 us -> 2.54 us  [ring_gather(): lax.ppermute(x, 'seq', left)]
    unnamed x31 -> x22, local copies, waits for them, and re-layouts: 6.83 us -> 7.16 us
  transfers between devices with their start and end apart: 10 -> 17, of which waited for: 5 -> 11; matrix products, arithmetic and copies ran while one was open for 12% -> 15% of each run, Pallas kernels for 0% -> 0%
where the time goes in v20:
time: 103 us; the launch traced here: 102 us
  waiting for transfers between devices  47.5 us (46%)
  starting transfers between devices  24.1 us (23%)
  local copies, waits for them, and re-layouts  12.4 us (12%)
  other arithmetic  10.6 us (10%)
  matrix products  6.23 us (6%)
  between operations  1.61 us (2%)
    ppermute x8, waiting for transfers between devices, ring_gather(): lax.ppermute(x, 'seq', right)  21.7 us
    ppermute x6, waiting for transfers between devices, ring_gather(): lax.ppermute(x, 'seq', left)  17 us
    ppermute x8, starting transfers between devices, ring_gather(): lax.ppermute(x, 'seq', right)  16.1 us
    ppermute x2, waiting for transfers between devices, head_sum(): got = lax.ppermute(send, 'head', [(i, i ^ bit) for i in range(members)])  8.75 us
    unnamed x22, local copies, waits for them, and re-layouts  7.16 us
    all_to_all x1, starting transfers between devices, gathered_plan(): lax.all_to_all(outgoing, 'seq', split_axis=0, concat_axis=0, tiled=True)  3.81 us
    ppermute x6, starting transfers between devices, ring_gather(): lax.ppermute(x, 'seq', left)  2.54 us
    another operation x1, other arithmetic, gathered_plan(): slot_all = jnp.sum((jnp.cumsum(onehot, axis=1) - onehot) * onehot, axis=2)  2.52 us
  transfers between devices with their start and end apart: 17, of which 11 were waited for; matrix products, arithmetic and copies ran while one was open for 15% of the time, Pallas kernels for 0%

profile of v20, /device:TPU:0, one launch (start us, length us, event | category | flops | bytes accessed | tf_op | source)
XLA Modules:
  0.0 102.3 jit_solution(2079214265194838090)
XLA Ops:
  0.0 3.0 %collective-permute-start.2 = (s32[128]{0:T(128)}, s32[128]{0:T(128)S(1)}, u32[]{:S(2)}, u32[]{:S(2)}) collective-permute-start(s32[128]{0:T(128)} %param.10), channel_id=1, source_target_pairs={{0,8},{8,16},{16,24},{24,28},{28,20},{20,12},{12,4},{4,0},{1,9},{9... | collective-permute-start | bytes 1544 | tf_op jit(solution)/shard_map/ppermute | solution.py:195
  4.4 2.1 %collective-permute-start = (bf16[128,2,1024]{0,2,1:T(8,128)(2,1)S(1)}, bf16[128,2,1024]{0,2,1:T(8,128)(2,1)S(1)}, u32[]{:S(2)}, u32[]{:S(2)}) collective-permute-start(bf16[128,2,1024]{0,2,1:T(8,128)(2,1)S(1)} %copy.54), channel_id=1, source_target_pairs={{0,8},{8,16},{16,24},{24,28},{28,20},{20,12},{12,4},{4,0},{1,9},{9... | collective-permute-start | bytes 1572872 | tf_op jit(solution)/shard_map/ppermute | solution.py:195
  6.5 1.2 %dynamic_slice.3 = s32[1]{0:T(128)} dynamic-slice(s32[8]{0:T(128)} %constant.121.clone, s32[]{:T(128)S(6)} %select_n.192), dynamic_slice_sizes={1} | dynamic-slice | bytes 12 | tf_op jit(solution)/shard_map/dynamic_slice | solution.py:211
  7.7 1.3 %compare_select_fusion = s32[8]{0:T(128)S(1)} fusion(s32[8]{0:T(128)} %constant.123.clone, s32[]{:T(128)} %bitcast.5), kind=kLoop, calls=%fused_computation.99 | loop fusion | flops 120 | bytes 68 | tf_op jit(solution)/shard_map/select_n | solution.py:212
  9.1 1.3 %gather_fusion.1 = s32[8]{0:T(128)S(1)} fusion(s32[8]{0:T(128)} %constant.122.clone, s32[1024]{0:T(1024)S(1)} %get-tuple-element.46), kind=kCustom, calls=%fused_computation.1 | custom fusion | bytes 96 | tf_op jit(solution)/shard_map/gather | solution.py:212
  12.8 2.1 %collective-permute-start.4 = (s32[128]{0:T(128)S(1)}, s32[128]{0:T(128)S(1)}, u32[]{:S(2)}, u32[]{:S(2)}) collective-permute-start(s32[128]{0:T(128)S(1)} %collective-permute-done.2), channel_id=1, source_target_pairs={{0,8},{8,16},{16,24},{24,28},{28,20},{20,12},{12,4},{4,0},{1,9},{9... | collective-permute-start | bytes 1544 | tf_op jit(solution)/shard_map/ppermute | solution.py:195
  15.0 2.9 %collective-permute-done.4 = s32[128]{0:T(128)S(1)} collective-permute-done((s32[128]{0:T(128)S(1)}, s32[128]{0:T(128)S(1)}, u32[]{:S(2)}, u32[]{:S(2)}) %collective-permute-start.4) | collective-permute-done | bytes 544 | tf_op jit(solution)/shard_map/ppermute | solution.py:195
  17.9 1.5 %collective-permute-done.5 = s32[128]{0:T(128)S(1)} collective-permute-done((s32[128]{0:T(128)S(1)}, s32[128]{0:T(128)S(1)}, u32[]{:S(2)}, u32[]{:S(2)}) %collective-permute-start.5) | collective-permute-done | bytes 544 | tf_op jit(solution)/shard_map/ppermute | solution.py:198
  19.4 1.6 %collective-permute-start.6 = (s32[128]{0:T(128)S(1)}, s32[128]{0:T(128)S(1)}, u32[]{:S(2)}, u32[]{:S(2)}) collective-permute-start(s32[128]{0:T(128)S(1)} %collective-permute-done.4), channel_id=1, source_target_pairs={{0,8},{8,16},{16,24},{24,28},{28,20},{20,12},{12,4},{4,0},{1,9},{9... | collective-permute-start | bytes 1544 | tf_op jit(solution)/shard_map/ppermute | solution.py:195
  21.4 1.5 %collective-permute-done.6 = s32[128]{0:T(128)S(1)} collective-permute-done((s32[128]{0:T(128)S(1)}, s32[128]{0:T(128)S(1)}, u32[]{:S(2)}, u32[]{:S(2)}) %collective-permute-start.6) | collective-permute-done | bytes 544 | tf_op jit(solution)/shard_map/ppermute | solution.py:195
  22.9 1.6 %collective-permute-done.7 = s32[128]{0:T(128)S(1)} collective-permute-done((s32[128]{0:T(128)S(1)}, s32[128]{0:T(128)S(1)}, u32[]{:S(2)}, u32[]{:S(2)}) %collective-permute-start.7) | collective-permute-done | bytes 544 | tf_op jit(solution)/shard_map/ppermute | solution.py:198
  24.5 1.6 %collective-permute-start.8 = (s32[128]{0:T(128)S(1)}, s32[128]{0:T(128)S(1)}, u32[]{:S(2)}, u32[]{:S(2)}) collective-permute-start(s32[128]{0:T(128)S(1)} %collective-permute-done.6), channel_id=1, source_target_pairs={{0,8},{8,16},{16,24},{24,28},{28,20},{20,12},{12,4},{4,0},{1,9},{9... | collective-permute-start | bytes 1544 | tf_op jit(solution)/shard_map/ppermute | solution.py:195
  29.2 2.1 %convolution_convert_fusion = bf16[256,1024]{1,0:T(8,128)(2,1)} fusion(bf16[128,3,1024]{2,0,1:T(8,128)(2,1)} %param.9, s32[128]{0:T(128)S(1)} %get-tuple-element.41), kind=kOutput, calls=%fused_computation.19 | convolution fusion | flops 67403776 | bytes 786944 | tf_op jit(solution)/shard_map/dot_general | solution.py:239
  31.2 3.8 %all-to-all-start = ((bf16[8,32,1024]{2,1,0:T(8,128)(2,1)}), bf16[8,32,1024]{2,1,0:T(8,128)(2,1)S(1)}, u32[]{:S(2)}, u32[]{:S(2)}) async-start(bf16[8,32,1024]{2,1,0:T(8,128)(2,1)} %bitcast.9), calls=%async_computation | async-start | bytes 1048576 | tf_op jit(solution)/shard_map/all_to_all | solution.py:241
  35.1 2.1 %collective-permute-start.10 = (bf16[128,2,1024]{0,2,1:T(8,128)(2,1)S(1)}, bf16[128,2,1024]{0,2,1:T(8,128)(2,1)S(1)}, u32[]{:S(2)}, u32[]{:S(2)}) collective-permute-start(bf16[128,2,1024]{0,2,1:T(8,128)(2,1)S(1)} %collective-permute-done.1), channel_id=1, source_target_pairs={{0,4},{8,0},{16,8},{24,16},{28,24},{20,28},{12,20},{4,12},{1,5},{9... | collective-permute-start | bytes 1572872 | tf_op jit(solution)/shard_map/ppermute | solution.py:198
  37.3 2.5 %select_reduce_fusion.1 = s32[8,128]{0,1:T(8,128)S(1)} fusion(s32[8,128]{0,1:T(8,128)S(1)} %copy.47), kind=kOutput, calls=%fused_computation.39 | output fusion | flops 1096704 | bytes 8192 | tf_op jit(solution)/shard_map/jit(cumsum)/reduce_window_sum | solution.py:231
  39.9 12.8 %collective-permute-done.10 = bf16[128,2,1024]{0,2,1:T(8,128)(2,1)S(1)} collective-permute-done((bf16[128,2,1024]{0,2,1:T(8,128)(2,1)S(1)}, bf16[128,2,1024]{0,2,1:T(8,128)(2,1)S(1)}, u32[]{:S(2)}, u32[]{:S(2)}) %collective-permute-start.10) | collective-permute-done | bytes 524320 | tf_op jit(solution)/shard_map/ppermute | solution.py:198
  52.8 4.3 %collective-permute-start.11 = (bf16[128,2,1024]{0,2,1:T(8,128)(2,1)}, bf16[128,2,1024]{0,2,1:T(8,128)(2,1)}, u32[]{:S(2)}, u32[]{:S(2)}) collective-permute-start(bf16[128,2,1024]{0,2,1:T(8,128)(2,1)} %collective-permute-done.9), channel_id=1, source_target_pairs={{0,8},{8,16},{16,24},{24,28},{28,20},{20,12},{12,4},{4,0},{1,9},{9... | collective-permute-start | bytes 1572872 | tf_op jit(solution)/shard_map/ppermute | solution.py:195
  57.8 9.0 %collective-permute-done.11 = bf16[128,2,1024]{0,2,1:T(8,128)(2,1)} collective-permute-done((bf16[128,2,1024]{0,2,1:T(8,128)(2,1)}, bf16[128,2,1024]{0,2,1:T(8,128)(2,1)}, u32[]{:S(2)}, u32[]{:S(2)}) %collective-permute-start.11) | collective-permute-done | bytes 524320 | tf_op jit(solution)/shard_map/ppermute | solution.py:195
  66.7 1.1 %collective-permute-done.12 = bf16[128,2,1024]{0,2,1:T(8,128)(2,1)S(1)} collective-permute-done((bf16[128,2,1024]{0,2,1:T(8,128)(2,1)S(1)}, bf16[128,2,1024]{0,2,1:T(8,128)(2,1)S(1)}, u32[]{:S(2)}, u32[]{:S(2)}) %collective-permute-start.12) | collective-permute-done | bytes 524320 | tf_op jit(solution)/shard_map/ppermute | solution.py:198
  67.8 1.4 %collective-permute-start.13 = (bf16[128,2,1024]{0,2,1:T(8,128)(2,1)}, bf16[128,2,1024]{0,2,1:T(8,128)(2,1)}, u32[]{:S(2)}, u32[]{:S(2)}) collective-permute-start(bf16[128,2,1024]{0,2,1:T(8,128)(2,1)} %collective-permute-done.11), channel_id=1, source_target_pairs={{0,8},{8,16},{16,24},{24,28},{28,20},{20,12},{12,4},{4,0},{1,9},{9... | collective-permute-start | bytes 1572872 | tf_op jit(solution)/shard_map/ppermute | solution.py:195
  70.3 7.7 %collective-permute-done.13 = bf16[128,2,1024]{0,2,1:T(8,128)(2,1)} collective-permute-done((bf16[128,2,1024]{0,2,1:T(8,128)(2,1)}, bf16[128,2,1024]{0,2,1:T(8,128)(2,1)}, u32[]{:S(2)}, u32[]{:S(2)}) %collective-permute-start.13) | collective-permute-done | bytes 524320 | tf_op jit(solution)/shard_map/ppermute | solution.py:195
  78.0 1.2 %constant_dynamic-update-slice_fusion.8 = bf16[1024,2,1024]{0,2,1:T(8,128)(2,1)S(1)} fusion(bf16[128,2,1024]{0,2,1:T(8,128)(2,1)} %collective-permute-done.13), kind=kLoop, calls=%fused_computation.70 | loop fusion | bytes 1048576
  79.2 1.2 %constant_dynamic-update-slice_fusion.7 = bf16[1024,2,1024]{0,2,1:T(8,128)(2,1)S(1)} fusion(bf16[1024,2,1024]{0,2,1:T(8,128)(2,1)S(1)} %constant_dynamic-update-slice_fusion.8, bf16[128,2,1024]{0,2,1:T(8,128)(2,1)} %collective-permute-done.11), kind=kLoop, calls=%fused_computation.69 | loop fusion | bytes 1048576
  80.4 1.2 %constant_dynamic-update-slice_fusion.6 = bf16[1024,2,1024]{0,2,1:T(8,128)(2,1)S(1)} fusion(bf16[1024,2,1024]{0,2,1:T(8,128)(2,1)S(1)} %constant_dynamic-update-slice_fusion.7, bf16[128,2,1024]{0,2,1:T(8,128)(2,1)} %collective-permute-done.9), kind=kLoop, calls=%fused_computation.68 | loop fusion | bytes 1048576
  83.7 2.2 %multiply_reduce_fusion = (f32[8,128]{1,0:T(8,128)S(1)}, f32[8,128,1024]{2,1,0:T(8,128)S(1)}) fusion(f32[128,1024]{1,0:T(8,128)S(1)} %fusion.33, f32[8,128,1024]{2,1,0:T(8,128)S(1)} %fusion.37, pred[128,1024]{1,0:T(8,128)(4,1)S(1)} %fusion.34), kind=kOutput, calls=%fused_computation.3 | output fusion | flops 7341055 | bytes 9048064 | tf_op jit(solution)/shard_map/sub | solution.py:283
  86.7 1.1 %fusion.24 = bf16[128,8,128]{0,2,1:T(8,128)(2,1)S(1)} fusion(f32[8,128,128]{2,1,0:T(8,128)S(1)} %fusion.5, bf16[1024,8,128]{0,2,1:T(8,128)(2,1)S(1)} %bitcast.92, f32[8,128,1024]{2,1,0:T(8,128)S(1)} %get-tuple-element.39, f32[128,1024]{1,0:T(8,128)S(1)} %fusion.33, pred[]{:T(512)S(6)} %eq.210, f32[128,8]{0,1:T(8,128)S(1)} %bitcast.100), kind=kOutput, calls=%fused_computation.30 | convolution fusion | flops 274071552 | bytes 7606273 | tf_op jit(solution)/shard_map/hqk,khd->qhd/dot_general | solution.py:290
  88.1 1.5 %slice-done.1 = s8[4194304]{0:T(1024)(128)(4,1)S(1)} async-done(((s8[8388608]{0:T(1024)(128)(4,1)}), s8[4194304]{0:T(1024)(128)(4,1)S(1)}, s32[]{:S(2)}) %slice-start.1) | async-done | bytes 4194328
  89.6 1.3 %fusion.59 = f32[128,4096]{1,0:T(8,128)S(1)} fusion(bf16[128,1024]{0,1:T(8,128)(2,1)S(1)} %bitcast.94, bf16[1024,4096]{1,0:T(8,128)(2,1)S(1)} %bitcast.87), kind=kOutput, calls=%fused_computation.137 | convolution fusion | flops 1073741824 | bytes 10747904 | tf_op jit(solution)/shard_map/dot_general | solution.py:296
  91.1 1.9 %collective-permute-done.14 = bf16[2,32,4096]{2,1,0:T(8,128)(2,1)S(1)} collective-permute-done((bf16[2,32,4096]{2,1,0:T(8,128)(2,1)S(1)}, bf16[2,32,4096]{2,1,0:T(8,128)(2,1)S(1)}, u32[]{:S(2)}, u32[]{:S(2)}) %collective-permute-start.14) | collective-permute-done | bytes 524320 | tf_op jit(solution)/shard_map/ppermute | solution.py:315
  93.1 1.6 %collective-permute-start.15 = (bf16[1,32,4096]{2,1,0:T(8,128)(2,1)S(1)}, bf16[1,32,4096]{2,1,0:T(8,128)(2,1)S(1)}, u32[]{:S(2)}, u32[]{:S(2)}) collective-permute-start(bf16[1,32,4096]{2,1,0:T(8,128)(2,1)S(1)} %fusion.35), channel_id=1, source_target_pairs={{0,2},{1,3},{2,0},{3,1},{4,6},{5,7},{6,4},{7,5},{8,10},{9,11},{10,... | collective-permute-start | bytes 786440 | tf_op jit(solution)/shard_map/ppermute | solution.py:315
  94.7 6.9 %collective-permute-done.15 = bf16[1,32,4096]{2,1,0:T(8,128)(2,1)S(1)} collective-permute-done((bf16[1,32,4096]{2,1,0:T(8,128)(2,1)S(1)}, bf16[1,32,4096]{2,1,0:T(8,128)(2,1)S(1)}, u32[]{:S(2)}, u32[]{:S(2)}) %collective-permute-start.15) | collective-permute-done | bytes 262176 | tf_op jit(solution)/shard_map/ppermute | solution.py:315
  (69 shorter events, 12.4 us)
Async XLA Ops:
  0.0 12.8 %collective-permute-start.2 = (s32[128]{0:T(128)}, s32[128]{0:T(128)S(1)}, u32[]{:S(2)}, u32[]{:S(2)}) collective-permute-start(s32[128]{0:T(128)} %param.10), channel_id=1, source_target_pairs={{0,8},{8,16},{16,24},{24,28},{28,20},{20,12},{12,4},{4,0},{1,9},{9... | collective-permute-start | bytes 1544 | tf_op jit(solution)/shard_map/ppermute | solution.py:195
  3.0 9.8 %collective-permute-start.3 = (s32[128]{0:T(128)}, s32[128]{0:T(128)S(1)}, u32[]{:S(2)}, u32[]{:S(2)}) collective-permute-start(s32[128]{0:T(128)} %param.10), channel_id=1, source_target_pairs={{0,4},{8,0},{16,8},{24,16},{28,24},{20,28},{12,20},{4,12},{1,5},{9... | collective-permute-start | bytes 1544 | tf_op jit(solution)/shard_map/ppermute | solution.py:198
  4.4 30.7 %collective-permute-start = (bf16[128,2,1024]{0,2,1:T(8,128)(2,1)S(1)}, bf16[128,2,1024]{0,2,1:T(8,128)(2,1)S(1)}, u32[]{:S(2)}, u32[]{:S(2)}) collective-permute-start(bf16[128,2,1024]{0,2,1:T(8,128)(2,1)S(1)} %copy.54), channel_id=1, source_target_pairs={{0,8},{8,16},{16,24},{24,28},{28,20},{20,12},{12,4},{4,0},{1,9},{9... | collective-permute-start | bytes 1572872 | tf_op jit(solution)/shard_map/ppermute | solution.py:195
  6.5 28.6 %collective-permute-start.1 = (bf16[128,2,1024]{0,2,1:T(8,128)(2,1)S(1)}, bf16[128,2,1024]{0,2,1:T(8,128)(2,1)S(1)}, u32[]{:S(2)}, u32[]{:S(2)}) collective-permute-start(bf16[128,2,1024]{0,2,1:T(8,128)(2,1)S(1)} %copy.54), channel_id=1, source_target_pairs={{0,4},{8,0},{16,8},{24,16},{28,24},{20,28},{12,20},{4,12},{1,5},{9... | collective-permute-start | bytes 1572872 | tf_op jit(solution)/shard_map/ppermute | solution.py:198
  12.8 5.1 %collective-permute-start.4 = (s32[128]{0:T(128)S(1)}, s32[128]{0:T(128)S(1)}, u32[]{:S(2)}, u32[]{:S(2)}) collective-permute-start(s32[128]{0:T(128)S(1)} %collective-permute-done.2), channel_id=1, source_target_pairs={{0,8},{8,16},{16,24},{24,28},{28,20},{20,12},{12,4},{4,0},{1,9},{9... | collective-permute-start | bytes 1544 | tf_op jit(solution)/shard_map/ppermute | solution.py:195
  14.9 4.5 %collective-permute-start.5 = (s32[128]{0:T(128)S(1)}, s32[128]{0:T(128)S(1)}, u32[]{:S(2)}, u32[]{:S(2)}) collective-permute-start(s32[128]{0:T(128)S(1)} %collective-permute-done.3), channel_id=1, source_target_pairs={{0,4},{8,0},{16,8},{24,16},{28,24},{20,28},{12,20},{4,12},{1,5},{9... | collective-permute-start | bytes 1544 | tf_op jit(solution)/shard_map/ppermute | solution.py:198
  19.4 3.5 %collective-permute-start.6 = (s32[128]{0:T(128)S(1)}, s32[128]{0:T(128)S(1)}, u32[]{:S(2)}, u32[]{:S(2)}) collective-permute-start(s32[128]{0:T(128)S(1)} %collective-permute-done.4), channel_id=1, source_target_pairs={{0,8},{8,16},{16,24},{24,28},{28,20},{20,12},{12,4},{4,0},{1,9},{9... | collective-permute-start | bytes 1544 | tf_op jit(solution)/shard_map/ppermute | solution.py:195
  20.9 3.5 %collective-permute-start.7 = (s32[128]{0:T(128)S(1)}, s32[128]{0:T(128)S(1)}, u32[]{:S(2)}, u32[]{:S(2)}) collective-permute-start(s32[128]{0:T(128)S(1)} %collective-permute-done.5), channel_id=1, source_target_pairs={{0,4},{8,0},{16,8},{24,16},{28,24},{20,28},{12,20},{4,12},{1,5},{9... | collective-permute-start | bytes 1544 | tf_op jit(solution)/shard_map/ppermute | solution.py:198
  24.5 3.5 %collective-permute-start.8 = (s32[128]{0:T(128)S(1)}, s32[128]{0:T(128)S(1)}, u32[]{:S(2)}, u32[]{:S(2)}) collective-permute-start(s32[128]{0:T(128)S(1)} %collective-permute-done.6), channel_id=1, source_target_pairs={{0,8},{8,16},{16,24},{24,28},{28,20},{20,12},{12,4},{4,0},{1,9},{9... | collective-permute-start | bytes 1544 | tf_op jit(solution)/shard_map/ppermute | solution.py:195
  31.2 38.8 %all-to-all-start = ((bf16[8,32,1024]{2,1,0:T(8,128)(2,1)}), bf16[8,32,1024]{2,1,0:T(8,128)(2,1)S(1)}, u32[]{:S(2)}, u32[]{:S(2)}) async-start(bf16[8,32,1024]{2,1,0:T(8,128)(2,1)} %bitcast.9), calls=%async_computation | async-start | bytes 1048576 | tf_op jit(solution)/shard_map/all_to_all | solution.py:241
  35.1 17.7 %collective-permute-start.10 = (bf16[128,2,1024]{0,2,1:T(8,128)(2,1)S(1)}, bf16[128,2,1024]{0,2,1:T(8,128)(2,1)S(1)}, u32[]{:S(2)}, u32[]{:S(2)}) collective-permute-start(bf16[128,2,1024]{0,2,1:T(8,128)(2,1)S(1)} %collective-permute-done.1), channel_id=1, source_target_pairs={{0,4},{8,0},{16,8},{24,16},{28,24},{20,28},{12,20},{4,12},{1,5},{9... | collective-permute-start | bytes 1572872 | tf_op jit(solution)/shard_map/ppermute | solution.py:198
  37.2 15.6 %collective-permute-start.9 = (bf16[128,2,1024]{0,2,1:T(8,128)(2,1)S(1)}, bf16[128,2,1024]{0,2,1:T(8,128)(2,1)}, u32[]{:S(2)}, u32[]{:S(2)}) collective-permute-start(bf16[128,2,1024]{0,2,1:T(8,128)(2,1)S(1)} %collective-permute-done), channel_id=1, source_target_pairs={{0,8},{8,16},{16,24},{24,28},{28,20},{20,12},{12,4},{4,0},{1,9},{9... | collective-permute-start | bytes 1572872 | tf_op jit(solution)/shard_map/ppermute | solution.py:195
  52.8 13.9 %collective-permute-start.11 = (bf16[128,2,1024]{0,2,1:T(8,128)(2,1)}, bf16[128,2,1024]{0,2,1:T(8,128)(2,1)}, u32[]{:S(2)}, u32[]{:S(2)}) collective-permute-start(bf16[128,2,1024]{0,2,1:T(8,128)(2,1)} %collective-permute-done.9), channel_id=1, source_target_pairs={{0,8},{8,16},{16,24},{24,28},{28,20},{20,12},{12,4},{4,0},{1,9},{9... | collective-permute-start | bytes 1572872 | tf_op jit(solution)/shard_map/ppermute | solution.py:195
  57.1 10.7 %collective-permute-start.12 = (bf16[128,2,1024]{0,2,1:T(8,128)(2,1)S(1)}, bf16[128,2,1024]{0,2,1:T(8,128)(2,1)S(1)}, u32[]{:S(2)}, u32[]{:S(2)}) collective-permute-start(bf16[128,2,1024]{0,2,1:T(8,128)(2,1)S(1)} %collective-permute-done.10), channel_id=1, source_target_pairs={{0,4},{8,0},{16,8},{24,16},{28,24},{20,28},{12,20},{4,12},{1,5},{9... | collective-permute-start | bytes 1572872 | tf_op jit(solution)/shard_map/ppermute | solution.py:198
  67.8 1.4 %copy-start = (bf16[128,2,1024]{0,2,1:T(8,128)(2,1)}, bf16[128,2,1024]{0,2,1:T(8,128)(2,1)S(1)}, u32[]{:S(2)}) copy-start(bf16[128,2,1024]{0,2,1:T(8,128)(2,1)S(1)} %collective-permute-done.12) | copy-start | bytes 1572868
  67.8 10.1 %collective-permute-start.13 = (bf16[128,2,1024]{0,2,1:T(8,128)(2,1)}, bf16[128,2,1024]{0,2,1:T(8,128)(2,1)}, u32[]{:S(2)}, u32[]{:S(2)}) collective-permute-start(bf16[128,2,1024]{0,2,1:T(8,128)(2,1)} %collective-permute-done.11), channel_id=1, source_target_pairs={{0,8},{8,16},{16,24},{24,28},{28,20},{20,12},{12,4},{4,0},{1,9},{9... | collective-permute-start | bytes 1572872 | tf_op jit(solution)/shard_map/ppermute | solution.py:195
  70.0 12.4 %copy-start.1 = (bf16[128,2,1024]{0,2,1:T(8,128)(2,1)S(1)}, bf16[128,2,1024]{0,2,1:T(8,128)(2,1)}, u32[]{:S(2)}) copy-start(bf16[128,2,1024]{0,2,1:T(8,128)(2,1)} %copy-done) | copy-start | bytes 1572868
  85.9 2.2 %slice-start = ((s8[8388608]{0:T(1024)(128)(4,1)}), s8[4194304]{0:T(1024)(128)(4,1)S(1)}, s32[]{:S(2)}) async-start(s8[8388608]{0:T(1024)(128)(4,1)} %bitcast.86), calls=%async_computation.1 | async-start | bytes 8388608
  86.7 2.9 %slice-start.1 = ((s8[8388608]{0:T(1024)(128)(4,1)}), s8[4194304]{0:T(1024)(128)(4,1)S(1)}, s32[]{:S(2)}) async-start(s8[8388608]{0:T(1024)(128)(4,1)} %bitcast.86), calls=%async_computation.2 | async-start | bytes 8388608
  91.0 2.0 %collective-permute-start.14 = (bf16[2,32,4096]{2,1,0:T(8,128)(2,1)S(1)}, bf16[2,32,4096]{2,1,0:T(8,128)(2,1)S(1)}, u32[]{:S(2)}, u32[]{:S(2)}) collective-permute-start(bf16[2,32,4096]{2,1,0:T(8,128)(2,1)S(1)} %fusion.31), channel_id=1, source_target_pairs={{0,1},{1,0},{2,3},{3,2},{4,5},{5,4},{6,7},{7,6},{8,9},{9,8},{10,11... | collective-permute-start | bytes 1572872 | tf_op jit(solution)/shard_map/ppermute | solution.py:315
  93.1 8.4 %collective-permute-start.15 = (bf16[1,32,4096]{2,1,0:T(8,128)(2,1)S(1)}, bf16[1,32,4096]{2,1,0:T(8,128)(2,1)S(1)}, u32[]{:S(2)}, u32[]{:S(2)}) collective-permute-start(bf16[1,32,4096]{2,1,0:T(8,128)(2,1)S(1)} %fusion.35), channel_id=1, source_target_pairs={{0,2},{1,3},{2,0},{3,1},{4,6},{5,7},{6,4},{7,5},{8,10},{9,11},{10,... | collective-permute-start | bytes 786440 | tf_op jit(solution)/shard_map/ppermute | solution.py:315

commit v21 on v13

--- a/solution.py
+++ b/solution.py
@@ -283,10 +283,9 @@
     weighted = rounded * count_f
     weight_hi = weighted.astype(jnp.bfloat16)
     weight_lo = (weighted - weight_hi.astype(jnp.float32)).astype(jnp.bfloat16)
-    mixed_sum = jnp.einsum("hqk,khd->qhd", weight_hi, values, preferred_element_type=jnp.float32)
-    mixed_sum = mixed_sum + jnp.einsum(
-        "hqk,khd->qhd", weight_lo, values, preferred_element_type=jnp.float32
-    )
+    both = jnp.concatenate([weight_hi, weight_lo], axis=1)
+    both_sum = jnp.einsum("hqk,khd->qhd", both, values, preferred_element_type=jnp.float32)
+    mixed_sum = both_sum[:tok_dev] + both_sum[tok_dev:]
     attn_rows = (mixed_sum / jnp.transpose(denominator)[..., None]).reshape(tok_dev, columns)
     attn_rows = attn_rows.astype(jnp.bfloat16)
     projected_rows = jnp.dot(attn_rows, out_weight, preferred_element_type=jnp.float32)

time: 86.5 us -> 84 us (0.971)
  local copies, waits for them, and re-layouts: 13.8 us -> 11 us
  other arithmetic: 10.6 us -> 11.8 us
    unnamed x32 -> x28, local copies, waits for them, and re-layouts: 7.14 us -> 4.43 us
    dot_general x2 -> x1, matrix products: 1.96 us -> 1.71 us  [gathered_plan(): jnp.einsum('hqk,khd->qhd', both, values, preferred_element_type=jnp.float32)]
  transfers between devices with their start and end apart: 17 -> 17, of which waited for: 10 -> 9; matrix products, arithmetic and copies ran while one was open for 24% -> 24% of each run, Pallas kernels for 0% -> 0%
where the time goes in v21:
time: 84 us; the launch traced here: 83.3 us
  waiting for transfers between devices  31.7 us (38%)
  starting transfers between devices  21.1 us (25%)
  other arithmetic  11.8 us (14%)
  local copies, waits for them, and re-layouts  11 us (13%)
  matrix products  6.02 us (7%)
  between operations  1.65 us (2%)
    ppermute x8, waiting for transfers between devices, ring_gather(): lax.ppermute(x, 'seq', right)  18.9 us
    ppermute x8, starting transfers between devices, ring_gather(): lax.ppermute(x, 'seq', right)  14 us
    ppermute x2, waiting for transfers between devices, head_sum(): got = lax.ppermute(send, 'head', [(i, i ^ bit) for i in range(members)])  8.75 us
    unnamed x28, local copies, waits for them, and re-layouts  4.43 us
    ppermute x6, waiting for transfers between devices, ring_gather(): lax.ppermute(x, 'seq', left)  4.07 us
    all_to_all x1, starting transfers between devices, gathered_plan(): lax.all_to_all(outgoing, 'seq', split_axis=0, concat_axis=0, tiled=True)  3.67 us
    another operation x1, other arithmetic, gathered_plan(): slot_all = jnp.sum((jnp.cumsum(onehot, axis=1) - onehot) * onehot, axis=2)  2.52 us
    sub x1, other arithmetic, gathered_plan(): near_exp = jnp.exp(near_scores - row_peak[..., None])  2.48 us
  transfers between devices with their start and end apart: 17, of which 9 were waited for; matrix products, arithmetic and copies ran while one was open for 24% of the time, Pallas kernels for 0%

profile of v21, /device:TPU:0, one launch (start us, length us, event | category | flops | bytes accessed | tf_op | source)
XLA Modules:
  0.0 83.3 jit_solution(2117435716712030889)
XLA Ops:
  0.0 1.1 %slice.47 = bf16[128,2,1024]{2,0,1:T(8,128)(2,1)S(1)} slice(bf16[128,3,1024]{2,0,1:T(8,128)(2,1)} %param.9), slice={[0:128], [1:3], [0:1024]} | slice | bytes 1048576 | tf_op jit(solution)/shard_map/slice | solution.py:222
  1.4 3.1 %collective-permute-start = (bf16[128,2,1024]{0,2,1:T(8,128)(2,1)S(1)}, bf16[128,2,1024]{0,2,1:T(8,128)(2,1)S(1)}, u32[]{:S(2)}, u32[]{:S(2)}) collective-permute-start(bf16[128,2,1024]{0,2,1:T(8,128)(2,1)S(1)} %copy.55), channel_id=1, source_target_pairs={{0,8},{8,16},{16,24},{24,28},{28,20},{20,12},{12,4},{4,0},{1,9},{9... | collective-permute-start | bytes 1572872 | tf_op jit(solution)/shard_map/ppermute | solution.py:195
  4.5 2.0 %collective-permute-start.1 = (s32[128]{0:T(128)}, s32[128]{0:T(128)S(1)}, u32[]{:S(2)}, u32[]{:S(2)}) collective-permute-start(s32[128]{0:T(128)} %param.10), channel_id=1, source_target_pairs={{0,8},{8,16},{16,24},{24,28},{28,20},{20,12},{12,4},{4,0},{1,9},{9... | collective-permute-start | bytes 1544 | tf_op jit(solution)/shard_map/ppermute | solution.py:195
  6.5 1.2 %dynamic_slice.3 = s32[1]{0:T(128)} dynamic-slice(s32[8]{0:T(128)} %constant.121.clone, s32[]{:T(128)S(6)} %select_n.196), dynamic_slice_sizes={1} | dynamic-slice | bytes 12 | tf_op jit(solution)/shard_map/dynamic_slice | solution.py:206
  7.7 8.7 %collective-permute-done.1 = s32[128]{0:T(128)S(1)} collective-permute-done((s32[128]{0:T(128)}, s32[128]{0:T(128)S(1)}, u32[]{:S(2)}, u32[]{:S(2)}) %collective-permute-start.1) | collective-permute-done | bytes 544 | tf_op jit(solution)/shard_map/ppermute | solution.py:195
  16.4 1.5 %collective-permute-done.3 = s32[128]{0:T(128)S(1)} collective-permute-done((s32[128]{0:T(128)}, s32[128]{0:T(128)S(1)}, u32[]{:S(2)}, u32[]{:S(2)}) %collective-permute-start.3) | collective-permute-done | bytes 544 | tf_op jit(solution)/shard_map/ppermute | solution.py:198
  17.9 1.6 %collective-permute-start.4 = (bf16[128,2,1024]{0,2,1:T(8,128)(2,1)S(1)}, bf16[128,2,1024]{0,2,1:T(8,128)(2,1)S(1)}, u32[]{:S(2)}, u32[]{:S(2)}) collective-permute-start(bf16[128,2,1024]{0,2,1:T(8,128)(2,1)S(1)} %collective-permute-done), channel_id=1, source_target_pairs={{0,8},{8,16},{16,24},{24,28},{28,20},{20,12},{12,4},{4,0},{1,9},{9... | collective-permute-start | bytes 1572872 | tf_op jit(solution)/shard_map/ppermute | solution.py:195
  20.0 1.3 %compare_select_fusion = s32[8]{0:T(128)S(1)} fusion(s32[8]{0:T(128)} %constant.123.clone, s32[]{:T(128)} %bitcast.5), kind=kLoop, calls=%fused_computation.95 | loop fusion | flops 120 | bytes 68 | tf_op jit(solution)/shard_map/select_n | solution.py:207
  21.3 1.6 %collective-permute-start.5 = (s32[128]{0:T(128)S(1)}, s32[128]{0:T(128)S(1)}, u32[]{:S(2)}, u32[]{:S(2)}) collective-permute-start(s32[128]{0:T(128)S(1)} %collective-permute-done.1), channel_id=1, source_target_pairs={{0,8},{8,16},{16,24},{24,28},{28,20},{20,12},{12,4},{4,0},{1,9},{9... | collective-permute-start | bytes 1544 | tf_op jit(solution)/shard_map/ppermute | solution.py:195
  23.4 0.8 reduce-window.8
  25.6 1.3 %gather_fusion.1 = s32[8]{0:T(128)S(1)} fusion(s32[8]{0:T(128)} %constant.122.clone, s32[1024]{0:T(1024)S(1)} %get-tuple-element.45), kind=kCustom, calls=%fused_computation.1 | custom fusion | bytes 96 | tf_op jit(solution)/shard_map/gather | solution.py:207
  26.9 3.5 %collective-permute-done.5 = s32[128]{0:T(128)S(1)} collective-permute-done((s32[128]{0:T(128)S(1)}, s32[128]{0:T(128)S(1)}, u32[]{:S(2)}, u32[]{:S(2)}) %collective-permute-start.5) | collective-permute-done | bytes 544 | tf_op jit(solution)/shard_map/ppermute | solution.py:195
  30.4 1.3 %collective-permute-done.7 = s32[128]{0:T(128)S(1)} collective-permute-done((s32[128]{0:T(128)S(1)}, s32[128]{0:T(128)S(1)}, u32[]{:S(2)}, u32[]{:S(2)}) %collective-permute-start.7) | collective-permute-done | bytes 544 | tf_op jit(solution)/shard_map/ppermute | solution.py:198
  31.7 1.6 %collective-permute-start.8 = (bf16[128,2,1024]{0,2,1:T(8,128)(2,1)S(1)}, bf16[128,2,1024]{0,2,1:T(8,128)(2,1)}, u32[]{:S(2)}, u32[]{:S(2)}) collective-permute-start(bf16[128,2,1024]{0,2,1:T(8,128)(2,1)S(1)} %collective-permute-done.4), channel_id=1, source_target_pairs={{0,8},{8,16},{16,24},{24,28},{28,20},{20,12},{12,4},{4,0},{1,9},{9... | collective-permute-start | bytes 1572872 | tf_op jit(solution)/shard_map/ppermute | solution.py:195
  34.0 1.6 %collective-permute-start.9 = (s32[128]{0:T(128)S(1)}, s32[128]{0:T(128)S(1)}, u32[]{:S(2)}, u32[]{:S(2)}) collective-permute-start(s32[128]{0:T(128)S(1)} %collective-permute-done.5), channel_id=1, source_target_pairs={{0,8},{8,16},{16,24},{24,28},{28,20},{20,12},{12,4},{4,0},{1,9},{9... | collective-permute-start | bytes 1544 | tf_op jit(solution)/shard_map/ppermute | solution.py:195
  36.8 6.2 %collective-permute-done.9 = s32[128]{0:T(128)S(1)} collective-permute-done((s32[128]{0:T(128)S(1)}, s32[128]{0:T(128)S(1)}, u32[]{:S(2)}, u32[]{:S(2)}) %collective-permute-start.9) | collective-permute-done | bytes 544 | tf_op jit(solution)/shard_map/ppermute | solution.py:195
  42.9 1.3 %collective-permute-done.11 = s32[128]{0:T(128)S(1)} collective-permute-done((s32[128]{0:T(128)S(1)}, s32[128]{0:T(128)S(1)}, u32[]{:S(2)}, u32[]{:S(2)}) %collective-permute-start.11) | collective-permute-done | bytes 544 | tf_op jit(solution)/shard_map/ppermute | solution.py:198
  44.2 1.6 %collective-permute-start.13 = (s32[128]{0:T(128)S(1)}, s32[128]{0:T(128)S(1)}, u32[]{:S(2)}, u32[]{:S(2)}) collective-permute-start(s32[128]{0:T(128)S(1)} %collective-permute-done.9), channel_id=1, source_target_pairs={{0,8},{8,16},{16,24},{24,28},{28,20},{20,12},{12,4},{4,0},{1,9},{9... | collective-permute-start | bytes 1544 | tf_op jit(solution)/shard_map/ppermute | solution.py:195
  46.4 0.9 %collective-permute-start.12 = (bf16[128,2,1024]{0,2,1:T(8,128)(2,1)}, bf16[128,2,1024]{0,2,1:T(8,128)(2,1)}, u32[]{:S(2)}, u32[]{:S(2)}) collective-permute-start(bf16[128,2,1024]{0,2,1:T(8,128)(2,1)} %collective-permute-done.8), channel_id=1, source_target_pairs={{0,8},{8,16},{16,24},{24,28},{28,20},{20,12},{12,4},{4,0},{1,9},{9... | collective-permute-start | bytes 1572872 | tf_op jit(solution)/shard_map/ppermute | solution.py:195
  49.1 2.1 %convolution_convert_fusion = bf16[256,1024]{1,0:T(8,128)(2,1)} fusion(bf16[128,3,1024]{2,0,1:T(8,128)(2,1)} %param.9, s32[128]{0:T(128)S(1)} %get-tuple-element.40), kind=kOutput, calls=%fused_computation.18 | convolution fusion | flops 67403776 | bytes 786944 | tf_op jit(solution)/shard_map/dot_general | solution.py:235
  51.1 3.7 %all-to-all-start = ((bf16[8,32,1024]{2,1,0:T(8,128)(2,1)}), bf16[8,32,1024]{2,1,0:T(8,128)(2,1)S(1)}, u32[]{:S(2)}, u32[]{:S(2)}) async-start(bf16[8,32,1024]{2,1,0:T(8,128)(2,1)} %bitcast.16), calls=%async_computation | async-start | bytes 1048576 | tf_op jit(solution)/shard_map/all_to_all | solution.py:237
  55.0 2.5 %select_reduce_fusion.1 = s32[8,128]{0,1:T(8,128)S(1)} fusion(s32[8,128]{0,1:T(8,128)S(1)} %copy.48), kind=kOutput, calls=%fused_computation.37 | output fusion | flops 1096704 | bytes 8192 | tf_op jit(solution)/shard_map/jit(cumsum)/reduce_window_sum | solution.py:227
  58.5 1.3 %fusion.23 = f32[128,1024]{1,0:T(8,128)} fusion(s32[1024]{0:T(1024)S(1)} %and_convert_fusion, s32[1024]{0:T(1024)S(1)} %add_select_fusion.2, s32[1024]{0:T(1024)S(1)} %convert_reduce_fusion, s32[128]{0:T(128)S(1)} %get-tuple-element.31, s32[128]{0:T(128)S(1)} %get-tuple-element.30, s32[128]{0:T(128)S(1)} %get-tuple-element.29, s32[128]{0:T(128)S(1)} %get-tuple-element.41, ...), kind=kLoop, calls=%fused_computation.40 | loop fusion | flops 2883584 | bytes 540161 | tf_op jit(solution)/shard_map/convert_element_type | solution.py:280
  59.8 1.2 %constant_dynamic-update-slice_fusion.7 = bf16[1024,2,1024]{0,2,1:T(8,128)(2,1)S(1)} fusion(bf16[128,2,1024]{0,2,1:T(8,128)(2,1)} %collective-permute-done.12), kind=kLoop, calls=%fused_computation.67 | loop fusion | bytes 1048576
  61.0 1.2 %constant_dynamic-update-slice_fusion.6 = bf16[1024,2,1024]{0,2,1:T(8,128)(2,1)S(1)} fusion(bf16[1024,2,1024]{0,2,1:T(8,128)(2,1)S(1)} %constant_dynamic-update-slice_fusion.7, bf16[128,2,1024]{0,2,1:T(8,128)(2,1)} %collective-permute-done.8), kind=kLoop, calls=%fused_computation.66 | loop fusion | bytes 1048576
  63.4 1.8 %fusion.48 = (bf16[1024,1,1024]{0,2,1:T(8,128)(2,1)S(1)}, bf16[1024,1,1024]{0,2,1:T(8,128)(2,1)}) fusion(bf16[1024,2,1024]{0,2,1:T(8,128)(2,1)S(1)} %constant_dynamic-update-slice_fusion), kind=kLoop, calls=%fused_computation.133 | loop fusion | bytes 8388608 | tf_op jit(solution)/shard_map/slice | solution.py:250
  66.2 2.5 %multiply_reduce_fusion = (f32[8,128]{1,0:T(8,128)S(1)}, bf16[8,128,1024]{2,1,0:T(8,128)(2,1)S(1)}, bf16[8,128,1024]{2,1,0:T(8,128)(2,1)S(1)}) fusion(f32[128,1024]{1,0:T(8,128)S(1)} %copy-done.3, pred[]{:T(512)S(6)} %eq.210, f32[8,128,1024]{2,1,0:T(8,128)S(1)} %fusion.27, pred[128,1024]{1,0:T(8,128)(4,1)S(1)} %fusion.24), kind=kOutput, calls=%fused_computation.7 | output fusion | flops 15729663 | bytes 9048065 | tf_op jit(solution)/shard_map/sub | solution.py:279
  68.7 1.7 %fusion.10 = f32[256,8,128]{0,2,1:T(8,128)S(1)} fusion(bf16[1024,8,128]{0,2,1:T(8,128)(2,1)S(1)} %bitcast.79, bf16[8,128,1024]{2,1,0:T(8,128)(2,1)S(1)} %get-tuple-element.34, bf16[8,128,1024]{2,1,0:T(8,128)(2,1)S(1)} %get-tuple-element.33), kind=kOutput, calls=%fused_computation.17 | convolution fusion | flops 545259520 | bytes 7340032 | tf_op jit(solution)/shard_map/hqk,khd->qhd/dot_general | solution.py:287
  70.5 1.3 %fusion.49 = f32[128,4096]{1,0:T(8,128)S(1)} fusion(bf16[128,1024]{0,1:T(8,128)(2,1)S(1)} %bitcast.80, bf16[1024,4096]{1,0:T(8,128)(2,1)S(1)} %bitcast.74), kind=kOutput, calls=%fused_computation.134 | convolution fusion | flops 1073741824 | bytes 10747904 | tf_op jit(solution)/shard_map/dot_general | solution.py:291
  72.0 1.9 %collective-permute-done.14 = bf16[2,32,4096]{2,1,0:T(8,128)(2,1)S(1)} collective-permute-done((bf16[2,32,4096]{2,1,0:T(8,128)(2,1)S(1)}, bf16[2,32,4096]{2,1,0:T(8,128)(2,1)S(1)}, u32[]{:S(2)}, u32[]{:S(2)}) %collective-permute-start.14) | collective-permute-done | bytes 524320 | tf_op jit(solution)/shard_map/ppermute | solution.py:310
  74.1 1.6 %collective-permute-start.15 = (bf16[1,32,4096]{2,1,0:T(8,128)(2,1)S(1)}, bf16[1,32,4096]{2,1,0:T(8,128)(2,1)S(1)}, u32[]{:S(2)}, u32[]{:S(2)}) collective-permute-start(bf16[1,32,4096]{2,1,0:T(8,128)(2,1)S(1)} %fusion.25), channel_id=1, source_target_pairs={{0,2},{1,3},{2,0},{3,1},{4,6},{5,7},{6,4},{7,5},{8,10},{9,11},{10,... | collective-permute-start | bytes 786440 | tf_op jit(solution)/shard_map/ppermute | solution.py:310
  75.6 6.9 %collective-permute-done.15 = bf16[1,32,4096]{2,1,0:T(8,128)(2,1)S(1)} collective-permute-done((bf16[1,32,4096]{2,1,0:T(8,128)(2,1)S(1)}, bf16[1,32,4096]{2,1,0:T(8,128)(2,1)S(1)}, u32[]{:S(2)}, u32[]{:S(2)}) %collective-permute-start.15) | collective-permute-done | bytes 262176 | tf_op jit(solution)/shard_map/ppermute | solution.py:310
  (76 shorter events, 9.9 us)
Async XLA Ops:
  0.0 54.8 %copy-start.4 = (s32[128]{0:T(128)S(1)}, s32[128]{0:T(128)}, u32[]{:S(2)}) copy-start(s32[128]{0:T(128)} %param.10) | copy-start | bytes 1540
  1.4 16.5 %collective-permute-start = (bf16[128,2,1024]{0,2,1:T(8,128)(2,1)S(1)}, bf16[128,2,1024]{0,2,1:T(8,128)(2,1)S(1)}, u32[]{:S(2)}, u32[]{:S(2)}) collective-permute-start(bf16[128,2,1024]{0,2,1:T(8,128)(2,1)S(1)} %copy.55), channel_id=1, source_target_pairs={{0,8},{8,16},{16,24},{24,28},{28,20},{20,12},{12,4},{4,0},{1,9},{9... | collective-permute-start | bytes 1572872 | tf_op jit(solution)/shard_map/ppermute | solution.py:195
  4.4 13.5 %collective-permute-start.2 = (bf16[128,2,1024]{0,2,1:T(8,128)(2,1)S(1)}, bf16[128,2,1024]{0,2,1:T(8,128)(2,1)S(1)}, u32[]{:S(2)}, u32[]{:S(2)}) collective-permute-start(bf16[128,2,1024]{0,2,1:T(8,128)(2,1)S(1)} %copy.55), channel_id=1, source_target_pairs={{0,4},{8,0},{16,8},{24,16},{28,24},{20,28},{12,20},{4,12},{1,5},{9... | collective-permute-start | bytes 1572872 | tf_op jit(solution)/shard_map/ppermute | solution.py:198
  4.5 11.9 %collective-permute-start.1 = (s32[128]{0:T(128)}, s32[128]{0:T(128)S(1)}, u32[]{:S(2)}, u32[]{:S(2)}) collective-permute-start(s32[128]{0:T(128)} %param.10), channel_id=1, source_target_pairs={{0,8},{8,16},{16,24},{24,28},{28,20},{20,12},{12,4},{4,0},{1,9},{9... | collective-permute-start | bytes 1544 | tf_op jit(solution)/shard_map/ppermute | solution.py:195
  6.5 11.4 %collective-permute-start.3 = (s32[128]{0:T(128)}, s32[128]{0:T(128)S(1)}, u32[]{:S(2)}, u32[]{:S(2)}) collective-permute-start(s32[128]{0:T(128)} %param.10), channel_id=1, source_target_pairs={{0,4},{8,0},{16,8},{24,16},{28,24},{20,28},{12,20},{4,12},{1,5},{9... | collective-permute-start | bytes 1544 | tf_op jit(solution)/shard_map/ppermute | solution.py:198
  17.9 13.8 %collective-permute-start.4 = (bf16[128,2,1024]{0,2,1:T(8,128)(2,1)S(1)}, bf16[128,2,1024]{0,2,1:T(8,128)(2,1)S(1)}, u32[]{:S(2)}, u32[]{:S(2)}) collective-permute-start(bf16[128,2,1024]{0,2,1:T(8,128)(2,1)S(1)} %collective-permute-done), channel_id=1, source_target_pairs={{0,8},{8,16},{16,24},{24,28},{28,20},{20,12},{12,4},{4,0},{1,9},{9... | collective-permute-start | bytes 1572872 | tf_op jit(solution)/shard_map/ppermute | solution.py:195
  19.5 12.2 %collective-permute-start.6 = (bf16[128,2,1024]{0,2,1:T(8,128)(2,1)S(1)}, bf16[128,2,1024]{0,2,1:T(8,128)(2,1)S(1)}, u32[]{:S(2)}, u32[]{:S(2)}) collective-permute-start(bf16[128,2,1024]{0,2,1:T(8,128)(2,1)S(1)} %collective-permute-done.2), channel_id=1, source_target_pairs={{0,4},{8,0},{16,8},{24,16},{28,24},{20,28},{12,20},{4,12},{1,5},{9... | collective-permute-start | bytes 1572872 | tf_op jit(solution)/shard_map/ppermute | solution.py:198
  21.3 9.1 %collective-permute-start.5 = (s32[128]{0:T(128)S(1)}, s32[128]{0:T(128)S(1)}, u32[]{:S(2)}, u32[]{:S(2)}) collective-permute-start(s32[128]{0:T(128)S(1)} %collective-permute-done.1), channel_id=1, source_target_pairs={{0,8},{8,16},{16,24},{24,28},{28,20},{20,12},{12,4},{4,0},{1,9},{9... | collective-permute-start | bytes 1544 | tf_op jit(solution)/shard_map/ppermute | solution.py:195
  22.9 8.8 %collective-permute-start.7 = (s32[128]{0:T(128)S(1)}, s32[128]{0:T(128)S(1)}, u32[]{:S(2)}, u32[]{:S(2)}) collective-permute-start(s32[128]{0:T(128)S(1)} %collective-permute-done.3), channel_id=1, source_target_pairs={{0,4},{8,0},{16,8},{24,16},{28,24},{20,28},{12,20},{4,12},{1,5},{9... | collective-permute-start | bytes 1544 | tf_op jit(solution)/shard_map/ppermute | solution.py:198
  31.7 12.5 %collective-permute-start.8 = (bf16[128,2,1024]{0,2,1:T(8,128)(2,1)S(1)}, bf16[128,2,1024]{0,2,1:T(8,128)(2,1)}, u32[]{:S(2)}, u32[]{:S(2)}) collective-permute-start(bf16[128,2,1024]{0,2,1:T(8,128)(2,1)S(1)} %collective-permute-done.4), channel_id=1, source_target_pairs={{0,8},{8,16},{16,24},{24,28},{28,20},{20,12},{12,4},{4,0},{1,9},{9... | collective-permute-start | bytes 1572872 | tf_op jit(solution)/shard_map/ppermute | solution.py:195
  33.3 10.9 %collective-permute-start.10 = (bf16[128,2,1024]{0,2,1:T(8,128)(2,1)S(1)}, bf16[128,2,1024]{0,2,1:T(8,128)(2,1)S(1)}, u32[]{:S(2)}, u32[]{:S(2)}) collective-permute-start(bf16[128,2,1024]{0,2,1:T(8,128)(2,1)S(1)} %collective-permute-done.6), channel_id=1, source_target_pairs={{0,4},{8,0},{16,8},{24,16},{28,24},{20,28},{12,20},{4,12},{1,5},{9... | collective-permute-start | bytes 1572872 | tf_op jit(solution)/shard_map/ppermute | solution.py:198
  34.0 8.9 %collective-permute-start.9 = (s32[128]{0:T(128)S(1)}, s32[128]{0:T(128)S(1)}, u32[]{:S(2)}, u32[]{:S(2)}) collective-permute-start(s32[128]{0:T(128)S(1)} %collective-permute-done.5), channel_id=1, source_target_pairs={{0,8},{8,16},{16,24},{24,28},{28,20},{20,12},{12,4},{4,0},{1,9},{9... | collective-permute-start | bytes 1544 | tf_op jit(solution)/shard_map/ppermute | solution.py:195
  35.6 8.6 %collective-permute-start.11 = (s32[128]{0:T(128)S(1)}, s32[128]{0:T(128)S(1)}, u32[]{:S(2)}, u32[]{:S(2)}) collective-permute-start(s32[128]{0:T(128)S(1)} %collective-permute-done.7), channel_id=1, source_target_pairs={{0,4},{8,0},{16,8},{24,16},{28,24},{20,28},{12,20},{4,12},{1,5},{9... | collective-permute-start | bytes 1544 | tf_op jit(solution)/shard_map/ppermute | solution.py:198
  44.2 6.9 %copy-start.1 = (bf16[128,2,1024]{0,2,1:T(8,128)(2,1)}, bf16[128,2,1024]{0,2,1:T(8,128)(2,1)S(1)}, u32[]{:S(2)}) copy-start(bf16[128,2,1024]{0,2,1:T(8,128)(2,1)S(1)} %collective-permute-done.10) | copy-start | bytes 1572868
  44.2 3.7 %collective-permute-start.13 = (s32[128]{0:T(128)S(1)}, s32[128]{0:T(128)S(1)}, u32[]{:S(2)}, u32[]{:S(2)}) collective-permute-start(s32[128]{0:T(128)S(1)} %collective-permute-done.9), channel_id=1, source_target_pairs={{0,8},{8,16},{16,24},{24,28},{28,20},{20,12},{12,4},{4,0},{1,9},{9... | collective-permute-start | bytes 1544 | tf_op jit(solution)/shard_map/ppermute | solution.py:195
  46.4 13.4 %collective-permute-start.12 = (bf16[128,2,1024]{0,2,1:T(8,128)(2,1)}, bf16[128,2,1024]{0,2,1:T(8,128)(2,1)}, u32[]{:S(2)}, u32[]{:S(2)}) collective-permute-start(bf16[128,2,1024]{0,2,1:T(8,128)(2,1)} %collective-permute-done.8), channel_id=1, source_target_pairs={{0,8},{8,16},{16,24},{24,28},{28,20},{20,12},{12,4},{4,0},{1,9},{9... | collective-permute-start | bytes 1572872 | tf_op jit(solution)/shard_map/ppermute | solution.py:195
  51.1 14.0 %all-to-all-start = ((bf16[8,32,1024]{2,1,0:T(8,128)(2,1)}), bf16[8,32,1024]{2,1,0:T(8,128)(2,1)S(1)}, u32[]{:S(2)}, u32[]{:S(2)}) async-start(bf16[8,32,1024]{2,1,0:T(8,128)(2,1)} %bitcast.16), calls=%async_computation | async-start | bytes 1048576 | tf_op jit(solution)/shard_map/all_to_all | solution.py:237
  57.5 5.6 %copy-start.2 = (bf16[128,2,1024]{0,2,1:T(8,128)(2,1)S(1)}, bf16[128,2,1024]{0,2,1:T(8,128)(2,1)}, u32[]{:S(2)}) copy-start(bf16[128,2,1024]{0,2,1:T(8,128)(2,1)} %copy-done.1) | copy-start | bytes 1572868
  65.2 1.0 %copy-start.3 = (f32[128,1024]{1,0:T(8,128)S(1)}, f32[128,1024]{1,0:T(8,128)}, u32[]{:S(2)}) copy-start(f32[128,1024]{1,0:T(8,128)} %fusion.23) | copy-start | bytes 1572868
  65.4 5.1 %slice-start = ((s8[8388608]{0:T(1024)(128)(4,1)}), s8[4194304]{0:T(1024)(128)(4,1)S(1)}, s32[]{:S(2)}) async-start(s8[8388608]{0:T(1024)(128)(4,1)} %bitcast.73), calls=%async_computation.1 | async-start | bytes 8388608
  66.2 2.5 %copy-start = (bf16[1024,1,1024]{0,2,1:T(8,128)(2,1)S(1)}, bf16[1024,1,1024]{0,2,1:T(8,128)(2,1)}, u32[]{:S(2)}) copy-start(bf16[1024,1,1024]{0,2,1:T(8,128)(2,1)} %get-tuple-element.36) | copy-start | bytes 6291460
  66.2 4.3 %slice-start.1 = ((s8[8388608]{0:T(1024)(128)(4,1)}), s8[4194304]{0:T(1024)(128)(4,1)S(1)}, s32[]{:S(2)}) async-start(s8[8388608]{0:T(1024)(128)(4,1)} %bitcast.73), calls=%async_computation.2 | async-start | bytes 8388608
  71.9 2.0 %collective-permute-start.14 = (bf16[2,32,4096]{2,1,0:T(8,128)(2,1)S(1)}, bf16[2,32,4096]{2,1,0:T(8,128)(2,1)S(1)}, u32[]{:S(2)}, u32[]{:S(2)}) collective-permute-start(bf16[2,32,4096]{2,1,0:T(8,128)(2,1)S(1)} %fusion.19), channel_id=1, source_target_pairs={{0,1},{1,0},{2,3},{3,2},{4,5},{5,4},{6,7},{7,6},{8,9},{9,8},{10,11... | collective-permute-start | bytes 1572872 | tf_op jit(solution)/shard_map/ppermute | solution.py:310
  74.1 8.4 %collective-permute-start.15 = (bf16[1,32,4096]{2,1,0:T(8,128)(2,1)S(1)}, bf16[1,32,4096]{2,1,0:T(8,128)(2,1)S(1)}, u32[]{:S(2)}, u32[]{:S(2)}) collective-permute-start(bf16[1,32,4096]{2,1,0:T(8,128)(2,1)S(1)} %fusion.25), channel_id=1, source_target_pairs={{0,2},{1,3},{2,0},{3,1},{4,6},{5,7},{6,4},{7,5},{8,10},{9,11},{10,... | collective-permute-start | bytes 786440 | tf_op jit(solution)/shard_map/ppermute | solution.py:310

commit v22 on v21

--- a/solution.py
+++ b/solution.py
@@ -247,6 +247,7 @@
         land_pick, incoming.reshape(owners * capacity, columns), preferred_element_type=jnp.float32
     )
     queries = queries.astype(projected.dtype).reshape(tok_dev, heads_here, HD)
+    queries, out_weight = lax.optimization_barrier((queries, out_weight))
     keys = keyval[:, 0, :].reshape(tokens, heads_here, HD)
     values = keyval[:, 1, :].reshape(tokens, heads_here, HD)
     scores = (

time: 84 us -> 84 us (level)
    unnamed x28 -> x29, local copies, waits for them, and re-layouts: 4.43 us -> 4.43 us
where the time goes in v22:
time: 84 us; the launch traced here: 83.3 us
  waiting for transfers between devices  31.7 us (38%)
  starting transfers between devices  21.1 us (25%)
  other arithmetic  11.8 us (14%)
  local copies, waits for them, and re-layouts  11 us (13%)
  matrix products  6.02 us (7%)
  between operations  1.68 us (2%)
    ppermute x8, waiting for transfers between devices, ring_gather(): lax.ppermute(x, 'seq', right)  18.9 us
    ppermute x8, starting transfers between devices, ring_gather(): lax.ppermute(x, 'seq', right)  13.9 us
    ppermute x2, waiting for transfers between devices, head_sum(): got = lax.ppermute(send, 'head', [(i, i ^ bit) for i in range(members)])  8.75 us
    unnamed x29, local copies, waits for them, and re-layouts  4.43 us
    ppermute x6, waiting for transfers between devices, ring_gather(): lax.ppermute(x, 'seq', left)  4.07 us
    all_to_all x1, starting transfers between devices, gathered_plan(): lax.all_to_all(outgoing, 'seq', split_axis=0, concat_axis=0, tiled=True)  3.67 us
    another operation x1, other arithmetic, gathered_plan(): slot_all = jnp.sum((jnp.cumsum(onehot, axis=1) - onehot) * onehot, axis=2)  2.52 us
    sub x1, other arithmetic, gathered_plan(): near_exp = jnp.exp(near_scores - row_peak[..., None])  2.49 us
  transfers between devices with their start and end apart: 17, of which 9 were waited for; matrix products, arithmetic and copies ran while one was open for 24% of the time, Pallas kernels for 0%

profile of v22, /device:TPU:0, one launch (start us, length us, event | category | flops | bytes accessed | tf_op | source)
XLA Modules:
  0.0 83.3 jit_solution(11989921403116456740)
XLA Ops:
  0.0 1.1 %slice.47 = bf16[128,2,1024]{2,0,1:T(8,128)(2,1)S(1)} slice(bf16[128,3,1024]{2,0,1:T(8,128)(2,1)} %param.9), slice={[0:128], [1:3], [0:1024]} | slice | bytes 1048576 | tf_op jit(solution)/shard_map/slice | solution.py:222
  1.4 3.1 %collective-permute-start = (bf16[128,2,1024]{0,2,1:T(8,128)(2,1)S(1)}, bf16[128,2,1024]{0,2,1:T(8,128)(2,1)S(1)}, u32[]{:S(2)}, u32[]{:S(2)}) collective-permute-start(bf16[128,2,1024]{0,2,1:T(8,128)(2,1)S(1)} %copy.55), channel_id=1, source_target_pairs={{0,8},{8,16},{16,24},{24,28},{28,20},{20,12},{12,4},{4,0},{1,9},{9... | collective-permute-start | bytes 1572872 | tf_op jit(solution)/shard_map/ppermute | solution.py:195
  4.5 2.0 %collective-permute-start.1 = (s32[128]{0:T(128)}, s32[128]{0:T(128)S(1)}, u32[]{:S(2)}, u32[]{:S(2)}) collective-permute-start(s32[128]{0:T(128)} %param.10), channel_id=1, source_target_pairs={{0,8},{8,16},{16,24},{24,28},{28,20},{20,12},{12,4},{4,0},{1,9},{9... | collective-permute-start | bytes 1544 | tf_op jit(solution)/shard_map/ppermute | solution.py:195
  6.5 0.8 reduce-window.8
  7.3 1.2 %dynamic_slice.3 = s32[1]{0:T(128)} dynamic-slice(s32[8]{0:T(128)} %constant.121.clone, s32[]{:T(128)S(6)} %select_n.196), dynamic_slice_sizes={1} | dynamic-slice | bytes 12 | tf_op jit(solution)/shard_map/dynamic_slice | solution.py:206
  8.6 7.8 %collective-permute-done.1 = s32[128]{0:T(128)S(1)} collective-permute-done((s32[128]{0:T(128)}, s32[128]{0:T(128)S(1)}, u32[]{:S(2)}, u32[]{:S(2)}) %collective-permute-start.1) | collective-permute-done | bytes 544 | tf_op jit(solution)/shard_map/ppermute | solution.py:195
  16.4 1.5 %collective-permute-done.3 = s32[128]{0:T(128)S(1)} collective-permute-done((s32[128]{0:T(128)}, s32[128]{0:T(128)S(1)}, u32[]{:S(2)}, u32[]{:S(2)}) %collective-permute-start.3) | collective-permute-done | bytes 544 | tf_op jit(solution)/shard_map/ppermute | solution.py:198
  17.9 1.6 %collective-permute-start.4 = (bf16[128,2,1024]{0,2,1:T(8,128)(2,1)S(1)}, bf16[128,2,1024]{0,2,1:T(8,128)(2,1)S(1)}, u32[]{:S(2)}, u32[]{:S(2)}) collective-permute-start(bf16[128,2,1024]{0,2,1:T(8,128)(2,1)S(1)} %collective-permute-done), channel_id=1, source_target_pairs={{0,8},{8,16},{16,24},{24,28},{28,20},{20,12},{12,4},{4,0},{1,9},{9... | collective-permute-start | bytes 1572872 | tf_op jit(solution)/shard_map/ppermute | solution.py:195
  20.0 1.3 %compare_select_fusion = s32[8]{0:T(128)S(1)} fusion(s32[8]{0:T(128)} %constant.123.clone, s32[]{:T(128)} %bitcast.5), kind=kLoop, calls=%fused_computation.94 | loop fusion | flops 120 | bytes 68 | tf_op jit(solution)/shard_map/select_n | solution.py:207
  21.3 1.6 %collective-permute-start.5 = (s32[128]{0:T(128)S(1)}, s32[128]{0:T(128)S(1)}, u32[]{:S(2)}, u32[]{:S(2)}) collective-permute-start(s32[128]{0:T(128)S(1)} %collective-permute-done.1), channel_id=1, source_target_pairs={{0,8},{8,16},{16,24},{24,28},{28,20},{20,12},{12,4},{4,0},{1,9},{9... | collective-permute-start | bytes 1544 | tf_op jit(solution)/shard_map/ppermute | solution.py:195
  24.8 1.3 %gather_fusion.1 = s32[8]{0:T(128)S(1)} fusion(s32[8]{0:T(128)} %constant.122.clone, s32[1024]{0:T(1024)S(1)} %get-tuple-element.47), kind=kCustom, calls=%fused_computation.1 | custom fusion | bytes 96 | tf_op jit(solution)/shard_map/gather | solution.py:207
  26.1 4.3 %collective-permute-done.5 = s32[128]{0:T(128)S(1)} collective-permute-done((s32[128]{0:T(128)S(1)}, s32[128]{0:T(128)S(1)}, u32[]{:S(2)}, u32[]{:S(2)}) %collective-permute-start.5) | collective-permute-done | bytes 544 | tf_op jit(solution)/shard_map/ppermute | solution.py:195
  30.4 1.3 %collective-permute-done.7 = s32[128]{0:T(128)S(1)} collective-permute-done((s32[128]{0:T(128)S(1)}, s32[128]{0:T(128)S(1)}, u32[]{:S(2)}, u32[]{:S(2)}) %collective-permute-start.7) | collective-permute-done | bytes 544 | tf_op jit(solution)/shard_map/ppermute | solution.py:198
  31.7 1.6 %collective-permute-start.8 = (bf16[128,2,1024]{0,2,1:T(8,128)(2,1)S(1)}, bf16[128,2,1024]{0,2,1:T(8,128)(2,1)}, u32[]{:S(2)}, u32[]{:S(2)}) collective-permute-start(bf16[128,2,1024]{0,2,1:T(8,128)(2,1)S(1)} %collective-permute-done.4), channel_id=1, source_target_pairs={{0,8},{8,16},{16,24},{24,28},{28,20},{20,12},{12,4},{4,0},{1,9},{9... | collective-permute-start | bytes 1572872 | tf_op jit(solution)/shard_map/ppermute | solution.py:195
  33.9 1.6 %collective-permute-start.9 = (s32[128]{0:T(128)S(1)}, s32[128]{0:T(128)S(1)}, u32[]{:S(2)}, u32[]{:S(2)}) collective-permute-start(s32[128]{0:T(128)S(1)} %collective-permute-done.5), channel_id=1, source_target_pairs={{0,8},{8,16},{16,24},{24,28},{28,20},{20,12},{12,4},{4,0},{1,9},{9... | collective-permute-start | bytes 1544 | tf_op jit(solution)/shard_map/ppermute | solution.py:195
  36.7 6.2 %collective-permute-done.9 = s32[128]{0:T(128)S(1)} collective-permute-done((s32[128]{0:T(128)S(1)}, s32[128]{0:T(128)S(1)}, u32[]{:S(2)}, u32[]{:S(2)}) %collective-permute-start.9) | collective-permute-done | bytes 544 | tf_op jit(solution)/shard_map/ppermute | solution.py:195
  42.9 1.3 %collective-permute-done.11 = s32[128]{0:T(128)S(1)} collective-permute-done((s32[128]{0:T(128)S(1)}, s32[128]{0:T(128)S(1)}, u32[]{:S(2)}, u32[]{:S(2)}) %collective-permute-start.11) | collective-permute-done | bytes 544 | tf_op jit(solution)/shard_map/ppermute | solution.py:198
  44.2 1.6 %collective-permute-start.13 = (s32[128]{0:T(128)S(1)}, s32[128]{0:T(128)S(1)}, u32[]{:S(2)}, u32[]{:S(2)}) collective-permute-start(s32[128]{0:T(128)S(1)} %collective-permute-done.9), channel_id=1, source_target_pairs={{0,8},{8,16},{16,24},{24,28},{28,20},{20,12},{12,4},{4,0},{1,9},{9... | collective-permute-start | bytes 1544 | tf_op jit(solution)/shard_map/ppermute | solution.py:195
  46.4 0.9 %collective-permute-start.12 = (bf16[128,2,1024]{0,2,1:T(8,128)(2,1)}, bf16[128,2,1024]{0,2,1:T(8,128)(2,1)}, u32[]{:S(2)}, u32[]{:S(2)}) collective-permute-start(bf16[128,2,1024]{0,2,1:T(8,128)(2,1)} %collective-permute-done.8), channel_id=1, source_target_pairs={{0,8},{8,16},{16,24},{24,28},{28,20},{20,12},{12,4},{4,0},{1,9},{9... | collective-permute-start | bytes 1572872 | tf_op jit(solution)/shard_map/ppermute | solution.py:195
  49.1 2.1 %convolution_convert_fusion = bf16[256,1024]{1,0:T(8,128)(2,1)} fusion(bf16[128,3,1024]{2,0,1:T(8,128)(2,1)} %param.9, s32[128]{0:T(128)S(1)} %get-tuple-element.44), kind=kOutput, calls=%fused_computation.18 | convolution fusion | flops 67403776 | bytes 786944 | tf_op jit(solution)/shard_map/dot_general | solution.py:235
  51.1 3.7 %all-to-all-start = ((bf16[8,32,1024]{2,1,0:T(8,128)(2,1)}), bf16[8,32,1024]{2,1,0:T(8,128)(2,1)S(1)}, u32[]{:S(2)}, u32[]{:S(2)}) async-start(bf16[8,32,1024]{2,1,0:T(8,128)(2,1)} %bitcast.16), calls=%async_computation | async-start | bytes 1048576 | tf_op jit(solution)/shard_map/all_to_all | solution.py:237
  55.0 2.5 %select_reduce_fusion.1 = s32[8,128]{0,1:T(8,128)S(1)} fusion(s32[8,128]{0,1:T(8,128)S(1)} %copy.48), kind=kOutput, calls=%fused_computation.37 | output fusion | flops 1096704 | bytes 8192 | tf_op jit(solution)/shard_map/jit(cumsum)/reduce_window_sum | solution.py:227
  58.5 1.3 %fusion.23 = f32[128,1024]{1,0:T(8,128)} fusion(s32[1024]{0:T(1024)S(1)} %and_convert_fusion, s32[1024]{0:T(1024)S(1)} %add_select_fusion.2, s32[1024]{0:T(1024)S(1)} %convert_reduce_fusion, s32[128]{0:T(128)S(1)} %get-tuple-element.35, s32[128]{0:T(128)S(1)} %get-tuple-element.34, s32[128]{0:T(128)S(1)} %get-tuple-element.33, s32[128]{0:T(128)S(1)} %get-tuple-element.45, ...), kind=kLoop, calls=%fused_computation.40 | loop fusion | flops 2883584 | bytes 540161 | tf_op jit(solution)/shard_map/convert_element_type | solution.py:281
  59.8 1.2 %constant_dynamic-update-slice_fusion.7 = bf16[1024,2,1024]{0,2,1:T(8,128)(2,1)S(1)} fusion(bf16[128,2,1024]{0,2,1:T(8,128)(2,1)} %collective-permute-done.12), kind=kLoop, calls=%fused_computation.66 | loop fusion | bytes 1048576
  61.0 1.2 %constant_dynamic-update-slice_fusion.6 = bf16[1024,2,1024]{0,2,1:T(8,128)(2,1)S(1)} fusion(bf16[1024,2,1024]{0,2,1:T(8,128)(2,1)S(1)} %constant_dynamic-update-slice_fusion.7, bf16[128,2,1024]{0,2,1:T(8,128)(2,1)} %collective-permute-done.8), kind=kLoop, calls=%fused_computation.65 | loop fusion | bytes 1048576
  63.4 1.8 %fusion.47 = (bf16[1024,1,1024]{0,2,1:T(8,128)(2,1)S(1)}, bf16[1024,1,1024]{0,2,1:T(8,128)(2,1)}) fusion(bf16[1024,2,1024]{0,2,1:T(8,128)(2,1)S(1)} %constant_dynamic-update-slice_fusion), kind=kLoop, calls=%fused_computation.132 | loop fusion | bytes 8388608 | tf_op jit(solution)/shard_map/slice | solution.py:251
  66.2 2.5 %multiply_reduce_fusion = (f32[8,128]{1,0:T(8,128)S(1)}, bf16[8,128,1024]{2,1,0:T(8,128)(2,1)S(1)}, bf16[8,128,1024]{2,1,0:T(8,128)(2,1)S(1)}) fusion(f32[128,1024]{1,0:T(8,128)S(1)} %copy-done.3, pred[]{:T(512)S(6)} %eq.210, f32[8,128,1024]{2,1,0:T(8,128)S(1)} %fusion.28, pred[128,1024]{1,0:T(8,128)(4,1)S(1)} %fusion.24), kind=kOutput, calls=%fused_computation.7 | output fusion | flops 15729663 | bytes 9048065 | tf_op jit(solution)/shard_map/sub | solution.py:280
  68.7 1.7 %fusion.10 = f32[256,8,128]{0,2,1:T(8,128)S(1)} fusion(bf16[1024,8,128]{0,2,1:T(8,128)(2,1)S(1)} %bitcast.77, bf16[8,128,1024]{2,1,0:T(8,128)(2,1)S(1)} %get-tuple-element.38, bf16[8,128,1024]{2,1,0:T(8,128)(2,1)S(1)} %get-tuple-element.37), kind=kOutput, calls=%fused_computation.17 | convolution fusion | flops 545259520 | bytes 7340032 | tf_op jit(solution)/shard_map/hqk,khd->qhd/dot_general | solution.py:288
  70.6 1.3 %fusion.48 = f32[128,4096]{1,0:T(8,128)S(1)} fusion(bf16[128,1024]{0,1:T(8,128)(2,1)S(1)} %bitcast.78, bf16[1024,4096]{1,0:T(8,128)(2,1)S(1)} %bitcast.72), kind=kOutput, calls=%fused_computation.133 | convolution fusion | flops 1073741824 | bytes 10747904 | tf_op jit(solution)/shard_map/dot_general | solution.py:292
  72.0 1.9 %collective-permute-done.14 = bf16[2,32,4096]{2,1,0:T(8,128)(2,1)S(1)} collective-permute-done((bf16[2,32,4096]{2,1,0:T(8,128)(2,1)S(1)}, bf16[2,32,4096]{2,1,0:T(8,128)(2,1)S(1)}, u32[]{:S(2)}, u32[]{:S(2)}) %collective-permute-start.14) | collective-permute-done | bytes 524320 | tf_op jit(solution)/shard_map/ppermute | solution.py:311
  74.1 1.6 %collective-permute-start.15 = (bf16[1,32,4096]{2,1,0:T(8,128)(2,1)S(1)}, bf16[1,32,4096]{2,1,0:T(8,128)(2,1)S(1)}, u32[]{:S(2)}, u32[]{:S(2)}) collective-permute-start(bf16[1,32,4096]{2,1,0:T(8,128)(2,1)S(1)} %fusion.25), channel_id=1, source_target_pairs={{0,2},{1,3},{2,0},{3,1},{4,6},{5,7},{6,4},{7,5},{8,10},{9,11},{10,... | collective-permute-start | bytes 786440 | tf_op jit(solution)/shard_map/ppermute | solution.py:311
  75.7 6.9 %collective-permute-done.15 = bf16[1,32,4096]{2,1,0:T(8,128)(2,1)S(1)} collective-permute-done((bf16[1,32,4096]{2,1,0:T(8,128)(2,1)S(1)}, bf16[1,32,4096]{2,1,0:T(8,128)(2,1)S(1)}, u32[]{:S(2)}, u32[]{:S(2)}) %collective-permute-start.15) | collective-permute-done | bytes 262176 | tf_op jit(solution)/shard_map/ppermute | solution.py:311
  (78 shorter events, 9.9 us)
Async XLA Ops:
  0.0 54.8 %copy-start.4 = (s32[128]{0:T(128)S(1)}, s32[128]{0:T(128)}, u32[]{:S(2)}) copy-start(s32[128]{0:T(128)} %param.10) | copy-start | bytes 1540
  1.4 16.5 %collective-permute-start = (bf16[128,2,1024]{0,2,1:T(8,128)(2,1)S(1)}, bf16[128,2,1024]{0,2,1:T(8,128)(2,1)S(1)}, u32[]{:S(2)}, u32[]{:S(2)}) collective-permute-start(bf16[128,2,1024]{0,2,1:T(8,128)(2,1)S(1)} %copy.55), channel_id=1, source_target_pairs={{0,8},{8,16},{16,24},{24,28},{28,20},{20,12},{12,4},{4,0},{1,9},{9... | collective-permute-start | bytes 1572872 | tf_op jit(solution)/shard_map/ppermute | solution.py:195
  4.4 13.5 %collective-permute-start.2 = (bf16[128,2,1024]{0,2,1:T(8,128)(2,1)S(1)}, bf16[128,2,1024]{0,2,1:T(8,128)(2,1)S(1)}, u32[]{:S(2)}, u32[]{:S(2)}) collective-permute-start(bf16[128,2,1024]{0,2,1:T(8,128)(2,1)S(1)} %copy.55), channel_id=1, source_target_pairs={{0,4},{8,0},{16,8},{24,16},{28,24},{20,28},{12,20},{4,12},{1,5},{9... | collective-permute-start | bytes 1572872 | tf_op jit(solution)/shard_map/ppermute | solution.py:198
  4.5 11.9 %collective-permute-start.1 = (s32[128]{0:T(128)}, s32[128]{0:T(128)S(1)}, u32[]{:S(2)}, u32[]{:S(2)}) collective-permute-start(s32[128]{0:T(128)} %param.10), channel_id=1, source_target_pairs={{0,8},{8,16},{16,24},{24,28},{28,20},{20,12},{12,4},{4,0},{1,9},{9... | collective-permute-start | bytes 1544 | tf_op jit(solution)/shard_map/ppermute | solution.py:195
  6.5 11.4 %collective-permute-start.3 = (s32[128]{0:T(128)}, s32[128]{0:T(128)S(1)}, u32[]{:S(2)}, u32[]{:S(2)}) collective-permute-start(s32[128]{0:T(128)} %param.10), channel_id=1, source_target_pairs={{0,4},{8,0},{16,8},{24,16},{28,24},{20,28},{12,20},{4,12},{1,5},{9... | collective-permute-start | bytes 1544 | tf_op jit(solution)/shard_map/ppermute | solution.py:198
  17.9 13.8 %collective-permute-start.4 = (bf16[128,2,1024]{0,2,1:T(8,128)(2,1)S(1)}, bf16[128,2,1024]{0,2,1:T(8,128)(2,1)S(1)}, u32[]{:S(2)}, u32[]{:S(2)}) collective-permute-start(bf16[128,2,1024]{0,2,1:T(8,128)(2,1)S(1)} %collective-permute-done), channel_id=1, source_target_pairs={{0,8},{8,16},{16,24},{24,28},{28,20},{20,12},{12,4},{4,0},{1,9},{9... | collective-permute-start | bytes 1572872 | tf_op jit(solution)/shard_map/ppermute | solution.py:195
  19.5 12.2 %collective-permute-start.6 = (bf16[128,2,1024]{0,2,1:T(8,128)(2,1)S(1)}, bf16[128,2,1024]{0,2,1:T(8,128)(2,1)S(1)}, u32[]{:S(2)}, u32[]{:S(2)}) collective-permute-start(bf16[128,2,1024]{0,2,1:T(8,128)(2,1)S(1)} %collective-permute-done.2), channel_id=1, source_target_pairs={{0,4},{8,0},{16,8},{24,16},{28,24},{20,28},{12,20},{4,12},{1,5},{9... | collective-permute-start | bytes 1572872 | tf_op jit(solution)/shard_map/ppermute | solution.py:198
  21.3 9.0 %collective-permute-start.5 = (s32[128]{0:T(128)S(1)}, s32[128]{0:T(128)S(1)}, u32[]{:S(2)}, u32[]{:S(2)}) collective-permute-start(s32[128]{0:T(128)S(1)} %collective-permute-done.1), channel_id=1, source_target_pairs={{0,8},{8,16},{16,24},{24,28},{28,20},{20,12},{12,4},{4,0},{1,9},{9... | collective-permute-start | bytes 1544 | tf_op jit(solution)/shard_map/ppermute | solution.py:195
  22.9 8.8 %collective-permute-start.7 = (s32[128]{0:T(128)S(1)}, s32[128]{0:T(128)S(1)}, u32[]{:S(2)}, u32[]{:S(2)}) collective-permute-start(s32[128]{0:T(128)S(1)} %collective-permute-done.3), channel_id=1, source_target_pairs={{0,4},{8,0},{16,8},{24,16},{28,24},{20,28},{12,20},{4,12},{1,5},{9... | collective-permute-start | bytes 1544 | tf_op jit(solution)/shard_map/ppermute | solution.py:198
  31.7 12.5 %collective-permute-start.8 = (bf16[128,2,1024]{0,2,1:T(8,128)(2,1)S(1)}, bf16[128,2,1024]{0,2,1:T(8,128)(2,1)}, u32[]{:S(2)}, u32[]{:S(2)}) collective-permute-start(bf16[128,2,1024]{0,2,1:T(8,128)(2,1)S(1)} %collective-permute-done.4), channel_id=1, source_target_pairs={{0,8},{8,16},{16,24},{24,28},{28,20},{20,12},{12,4},{4,0},{1,9},{9... | collective-permute-start | bytes 1572872 | tf_op jit(solution)/shard_map/ppermute | solution.py:195
  33.3 10.9 %collective-permute-start.10 = (bf16[128,2,1024]{0,2,1:T(8,128)(2,1)S(1)}, bf16[128,2,1024]{0,2,1:T(8,128)(2,1)S(1)}, u32[]{:S(2)}, u32[]{:S(2)}) collective-permute-start(bf16[128,2,1024]{0,2,1:T(8,128)(2,1)S(1)} %collective-permute-done.6), channel_id=1, source_target_pairs={{0,4},{8,0},{16,8},{24,16},{28,24},{20,28},{12,20},{4,12},{1,5},{9... | collective-permute-start | bytes 1572872 | tf_op jit(solution)/shard_map/ppermute | solution.py:198
  33.9 9.0 %collective-permute-start.9 = (s32[128]{0:T(128)S(1)}, s32[128]{0:T(128)S(1)}, u32[]{:S(2)}, u32[]{:S(2)}) collective-permute-start(s32[128]{0:T(128)S(1)} %collective-permute-done.5), channel_id=1, source_target_pairs={{0,8},{8,16},{16,24},{24,28},{28,20},{20,12},{12,4},{4,0},{1,9},{9... | collective-permute-start | bytes 1544 | tf_op jit(solution)/shard_map/ppermute | solution.py:195
  35.6 8.6 %collective-permute-start.11 = (s32[128]{0:T(128)S(1)}, s32[128]{0:T(128)S(1)}, u32[]{:S(2)}, u32[]{:S(2)}) collective-permute-start(s32[128]{0:T(128)S(1)} %collective-permute-done.7), channel_id=1, source_target_pairs={{0,4},{8,0},{16,8},{24,16},{28,24},{20,28},{12,20},{4,12},{1,5},{9... | collective-permute-start | bytes 1544 | tf_op jit(solution)/shard_map/ppermute | solution.py:198
  44.2 6.9 %copy-start.1 = (bf16[128,2,1024]{0,2,1:T(8,128)(2,1)}, bf16[128,2,1024]{0,2,1:T(8,128)(2,1)S(1)}, u32[]{:S(2)}) copy-start(bf16[128,2,1024]{0,2,1:T(8,128)(2,1)S(1)} %collective-permute-done.10) | copy-start | bytes 1572868
  44.2 3.7 %collective-permute-start.13 = (s32[128]{0:T(128)S(1)}, s32[128]{0:T(128)S(1)}, u32[]{:S(2)}, u32[]{:S(2)}) collective-permute-start(s32[128]{0:T(128)S(1)} %collective-permute-done.9), channel_id=1, source_target_pairs={{0,8},{8,16},{16,24},{24,28},{28,20},{20,12},{12,4},{4,0},{1,9},{9... | collective-permute-start | bytes 1544 | tf_op jit(solution)/shard_map/ppermute | solution.py:195
  46.4 13.4 %collective-permute-start.12 = (bf16[128,2,1024]{0,2,1:T(8,128)(2,1)}, bf16[128,2,1024]{0,2,1:T(8,128)(2,1)}, u32[]{:S(2)}, u32[]{:S(2)}) collective-permute-start(bf16[128,2,1024]{0,2,1:T(8,128)(2,1)} %collective-permute-done.8), channel_id=1, source_target_pairs={{0,8},{8,16},{16,24},{24,28},{28,20},{20,12},{12,4},{4,0},{1,9},{9... | collective-permute-start | bytes 1572872 | tf_op jit(solution)/shard_map/ppermute | solution.py:195
  51.1 14.0 %all-to-all-start = ((bf16[8,32,1024]{2,1,0:T(8,128)(2,1)}), bf16[8,32,1024]{2,1,0:T(8,128)(2,1)S(1)}, u32[]{:S(2)}, u32[]{:S(2)}) async-start(bf16[8,32,1024]{2,1,0:T(8,128)(2,1)} %bitcast.16), calls=%async_computation | async-start | bytes 1048576 | tf_op jit(solution)/shard_map/all_to_all | solution.py:237
  57.5 5.6 %copy-start.2 = (bf16[128,2,1024]{0,2,1:T(8,128)(2,1)S(1)}, bf16[128,2,1024]{0,2,1:T(8,128)(2,1)}, u32[]{:S(2)}) copy-start(bf16[128,2,1024]{0,2,1:T(8,128)(2,1)} %copy-done.1) | copy-start | bytes 1572868
  65.2 1.0 %copy-start.3 = (f32[128,1024]{1,0:T(8,128)S(1)}, f32[128,1024]{1,0:T(8,128)}, u32[]{:S(2)}) copy-start(f32[128,1024]{1,0:T(8,128)} %fusion.23) | copy-start | bytes 1572868
  65.5 5.0 %slice-start = ((s8[8388608]{0:T(1024)(128)(4,1)}), s8[4194304]{0:T(1024)(128)(4,1)S(1)}, s32[]{:S(2)}) async-start(s8[8388608]{0:T(1024)(128)(4,1)} %bitcast.71), calls=%async_computation.1 | async-start | bytes 8388608
  66.2 2.5 %copy-start = (bf16[1024,1,1024]{0,2,1:T(8,128)(2,1)S(1)}, bf16[1024,1,1024]{0,2,1:T(8,128)(2,1)}, u32[]{:S(2)}) copy-start(bf16[1024,1,1024]{0,2,1:T(8,128)(2,1)} %get-tuple-element.40) | copy-start | bytes 6291460
  66.2 4.3 %slice-start.1 = ((s8[8388608]{0:T(1024)(128)(4,1)}), s8[4194304]{0:T(1024)(128)(4,1)S(1)}, s32[]{:S(2)}) async-start(s8[8388608]{0:T(1024)(128)(4,1)} %bitcast.71), calls=%async_computation.2 | async-start | bytes 8388608
  72.0 2.0 %collective-permute-start.14 = (bf16[2,32,4096]{2,1,0:T(8,128)(2,1)S(1)}, bf16[2,32,4096]{2,1,0:T(8,128)(2,1)S(1)}, u32[]{:S(2)}, u32[]{:S(2)}) collective-permute-start(bf16[2,32,4096]{2,1,0:T(8,128)(2,1)S(1)} %fusion.19), channel_id=1, source_target_pairs={{0,1},{1,0},{2,3},{3,2},{4,5},{5,4},{6,7},{7,6},{8,9},{9,8},{10,11... | collective-permute-start | bytes 1572872 | tf_op jit(solution)/shard_map/ppermute | solution.py:311
  74.1 8.4 %collective-permute-start.15 = (bf16[1,32,4096]{2,1,0:T(8,128)(2,1)S(1)}, bf16[1,32,4096]{2,1,0:T(8,128)(2,1)S(1)}, u32[]{:S(2)}, u32[]{:S(2)}) collective-permute-start(bf16[1,32,4096]{2,1,0:T(8,128)(2,1)S(1)} %fusion.25), channel_id=1, source_target_pairs={{0,2},{1,3},{2,0},{3,1},{4,6},{5,7},{6,4},{7,5},{8,10},{9,11},{10,... | collective-permute-start | bytes 786440 | tf_op jit(solution)/shard_map/ppermute | solution.py:311

commit v23 on v21

--- a/solution.py
+++ b/solution.py
@@ -254,24 +254,28 @@
         * score_scale
     )
     bounds = jnp.cumsum(doc_lengths)
-    key_block = key_dest // BLK
-    key_doc = segment_of(key_dest, bounds)
     query_block = my_pos // BLK
     query_doc = segment_of(my_pos, bounds)
-    same_doc = query_doc[:, None] == key_doc[None, :]
-    window = jnp.zeros((tok_dev, tokens), jnp.int32)
-    for step in (-1, 0, 1):
-        near = (query_block + step) % blocks_all
-        window = window + (key_block[None, :] == near[:, None]).astype(jnp.int32)
-    window = jnp.where(same_doc, window, 0)
     chosen = random_blocks[query_block]
-    drawn = jnp.zeros((tok_dev, tokens), jnp.int32)
-    for r in range(chosen.shape[1]):
-        drawn = drawn + (key_block[None, :] == chosen[:, r][:, None]).astype(jnp.int32)
     glob_start = global_owner[0] * tok_dev
-    in_glob = (key_dest >= glob_start) & (key_dest < glob_start + tok_dev)
     holds_glob = own_index == global_owner[0]
-    count = window + drawn + in_glob[None, :].astype(jnp.int32)
+
+    def key_count(piece_dest):
+        key_block = piece_dest // BLK
+        same_doc = query_doc[:, None] == segment_of(piece_dest, bounds)[None, :]
+        window = jnp.zeros((tok_dev, piece_dest.shape[0]), jnp.int32)
+        for step in (-1, 0, 1):
+            near = (query_block + step) % blocks_all
+            window = window + (key_block[None, :] == near[:, None]).astype(jnp.int32)
+        window = jnp.where(same_doc, window, 0)
+        for r in range(chosen.shape[1]):
+            window = window + (key_block[None, :] == chosen[:, r][:, None]).astype(jnp.int32)
+        in_glob = (piece_dest >= glob_start) & (piece_dest < glob_start + tok_dev)
+        return window + in_glob[None, :].astype(jnp.int32)
+
+    count = jnp.concatenate(
+        [key_count(key_dest[i * tok_dev : (i + 1) * tok_dev]) for i in range(owners)], axis=1
+    )
     count = jnp.where(holds_glob, 1, count)
     live = count > 0
     near_scores = jnp.where(live[None], scores, big_negative)

time: 84 us -> 91.9 us (1.094)
  waiting for transfers between devices: 31.7 us -> 37.9 us
  other arithmetic: 11.8 us -> 13 us
    ppermute x8, waiting for transfers between devices: 18.9 us -> 25 us  [ring_gather(): lax.ppermute(x, 'seq', right)]
    unnamed x4 -> x10, other arithmetic: 0.67 us -> 1.99 us
    unnamed x28 -> x27, local copies, waits for them, and re-layouts: 4.43 us -> 5.23 us
  transfers between devices with their start and end apart: 17 -> 17, of which waited for: 9 -> 9; matrix products, arithmetic and copies ran while one was open for 24% -> 23% of each run, Pallas kernels for 0% -> 0%
where the time goes in v23:
time: 91.9 us; the launch traced here: 91.5 us
  waiting for transfers between devices  37.9 us (41%)
  starting transfers between devices  21 us (23%)
  other arithmetic  13 us (14%)
  local copies, waits for them, and re-layouts  11.8 us (13%)
  matrix products  6.02 us (7%)
  between operations  1.72 us (2%)
    ppermute x8, waiting for transfers between devices, ring_gather(): lax.ppermute(x, 'seq', right)  25 us
    ppermute x8, starting transfers between devices, ring_gather(): lax.ppermute(x, 'seq', right)  13.9 us
    ppermute x2, waiting for transfers between devices, head_sum(): got = lax.ppermute(send, 'head', [(i, i ^ bit) for i in range(members)])  8.75 us
    unnamed x27, local copies, waits for them, and re-layouts  5.23 us
    ppermute x6, waiting for transfers between devices, ring_gather(): lax.ppermute(x, 'seq', left)  4.07 us
    all_to_all x1, starting transfers between devices, gathered_plan(): lax.all_to_all(outgoing, 'seq', split_axis=0, concat_axis=0, tiled=True)  3.67 us
    another operation x1, other arithmetic, gathered_plan(): slot_all = jnp.sum((jnp.cumsum(onehot, axis=1) - onehot) * onehot, axis=2)  2.52 us
    sub x1, other arithmetic, gathered_plan(): near_exp = jnp.exp(near_scores - row_peak[..., None])  2.48 us
  transfers between devices with their start and end apart: 17, of which 9 were waited for; matrix products, arithmetic and copies ran while one was open for 23% of the time, Pallas kernels for 0%

profile of v23, /device:TPU:0, one launch (start us, length us, event | category | flops | bytes accessed | tf_op | source)
XLA Modules:
  0.0 91.5 jit_solution(8544702280785059674)
XLA Ops:
  0.0 1.1 %slice.28 = bf16[128,2,1024]{2,0,1:T(8,128)(2,1)S(1)} slice(bf16[128,3,1024]{2,0,1:T(8,128)(2,1)} %param.9), slice={[0:128], [1:3], [0:1024]} | slice | bytes 1048576 | tf_op jit(solution)/shard_map/slice | solution.py:222
  1.4 3.1 %collective-permute-start = (bf16[128,2,1024]{0,2,1:T(8,128)(2,1)S(1)}, bf16[128,2,1024]{0,2,1:T(8,128)(2,1)S(1)}, u32[]{:S(2)}, u32[]{:S(2)}) collective-permute-start(bf16[128,2,1024]{0,2,1:T(8,128)(2,1)S(1)} %copy.55), channel_id=1, source_target_pairs={{0,8},{8,16},{16,24},{24,28},{28,20},{20,12},{12,4},{4,0},{1,9},{9... | collective-permute-start | bytes 1572872 | tf_op jit(solution)/shard_map/ppermute | solution.py:195
  4.5 2.0 %collective-permute-start.1 = (s32[128]{0:T(128)}, s32[128]{0:T(128)S(1)}, u32[]{:S(2)}, u32[]{:S(2)}) collective-permute-start(s32[128]{0:T(128)} %param.10), channel_id=1, source_target_pairs={{0,8},{8,16},{16,24},{24,28},{28,20},{20,12},{12,4},{4,0},{1,9},{9... | collective-permute-start | bytes 1544 | tf_op jit(solution)/shard_map/ppermute | solution.py:195
  7.3 1.2 %dynamic_slice.3 = s32[1]{0:T(128)} dynamic-slice(s32[8]{0:T(128)} %constant.226.clone, s32[]{:T(128)S(6)} %select_n.295), dynamic_slice_sizes={1} | dynamic-slice | bytes 12 | tf_op jit(solution)/shard_map/dynamic_slice | solution.py:206
  8.5 1.3 %compare_select_fusion = s32[8]{0:T(128)S(1)} fusion(s32[8]{0:T(128)} %constant.228.clone, s32[]{:T(128)} %bitcast.5), kind=kLoop, calls=%fused_computation.93 | loop fusion | flops 120 | bytes 68 | tf_op jit(solution)/shard_map/select_n | solution.py:207
  12.0 1.3 %gather_fusion.1 = s32[8]{0:T(128)S(1)} fusion(s32[8]{0:T(128)} %constant.227.clone, s32[1024]{0:T(1024)S(1)} %get-tuple-element.70), kind=kCustom, calls=%fused_computation.1 | custom fusion | bytes 96 | tf_op jit(solution)/shard_map/gather | solution.py:207
  13.3 3.1 %collective-permute-done.1 = s32[128]{0:T(128)S(1)} collective-permute-done((s32[128]{0:T(128)}, s32[128]{0:T(128)S(1)}, u32[]{:S(2)}, u32[]{:S(2)}) %collective-permute-start.1) | collective-permute-done | bytes 544 | tf_op jit(solution)/shard_map/ppermute | solution.py:195
  16.4 1.5 %collective-permute-done.3 = s32[128]{0:T(128)S(1)} collective-permute-done((s32[128]{0:T(128)}, s32[128]{0:T(128)S(1)}, u32[]{:S(2)}, u32[]{:S(2)}) %collective-permute-start.3) | collective-permute-done | bytes 544 | tf_op jit(solution)/shard_map/ppermute | solution.py:198
  17.9 1.6 %collective-permute-start.4 = (bf16[128,2,1024]{0,2,1:T(8,128)(2,1)S(1)}, bf16[128,2,1024]{0,2,1:T(8,128)(2,1)S(1)}, u32[]{:S(2)}, u32[]{:S(2)}) collective-permute-start(bf16[128,2,1024]{0,2,1:T(8,128)(2,1)S(1)} %collective-permute-done), channel_id=1, source_target_pairs={{0,8},{8,16},{16,24},{24,28},{28,20},{20,12},{12,4},{4,0},{1,9},{9... | collective-permute-start | bytes 1572872 | tf_op jit(solution)/shard_map/ppermute | solution.py:195
  20.6 1.6 %collective-permute-start.5 = (s32[128]{0:T(128)S(1)}, s32[128]{0:T(128)S(1)}, u32[]{:S(2)}, u32[]{:S(2)}) collective-permute-start(s32[128]{0:T(128)S(1)} %collective-permute-done.1), channel_id=1, source_target_pairs={{0,8},{8,16},{16,24},{24,28},{28,20},{20,12},{12,4},{4,0},{1,9},{9... | collective-permute-start | bytes 1544 | tf_op jit(solution)/shard_map/ppermute | solution.py:195
  23.5 6.9 %collective-permute-done.5 = s32[128]{0:T(128)S(1)} collective-permute-done((s32[128]{0:T(128)S(1)}, s32[128]{0:T(128)S(1)}, u32[]{:S(2)}, u32[]{:S(2)}) %collective-permute-start.5) | collective-permute-done | bytes 544 | tf_op jit(solution)/shard_map/ppermute | solution.py:195
  30.4 1.3 %collective-permute-done.7 = s32[128]{0:T(128)S(1)} collective-permute-done((s32[128]{0:T(128)S(1)}, s32[128]{0:T(128)S(1)}, u32[]{:S(2)}, u32[]{:S(2)}) %collective-permute-start.7) | collective-permute-done | bytes 544 | tf_op jit(solution)/shard_map/ppermute | solution.py:198
  31.7 1.6 %collective-permute-start.8 = (bf16[128,2,1024]{0,2,1:T(8,128)(2,1)S(1)}, bf16[128,2,1024]{0,2,1:T(8,128)(2,1)}, u32[]{:S(2)}, u32[]{:S(2)}) collective-permute-start(bf16[128,2,1024]{0,2,1:T(8,128)(2,1)S(1)} %collective-permute-done.4), channel_id=1, source_target_pairs={{0,8},{8,16},{16,24},{24,28},{28,20},{20,12},{12,4},{4,0},{1,9},{9... | collective-permute-start | bytes 1572872 | tf_op jit(solution)/shard_map/ppermute | solution.py:195
  33.8 1.6 %collective-permute-start.9 = (s32[128]{0:T(128)S(1)}, s32[128]{0:T(128)S(1)}, u32[]{:S(2)}, u32[]{:S(2)}) collective-permute-start(s32[128]{0:T(128)S(1)} %collective-permute-done.5), channel_id=1, source_target_pairs={{0,8},{8,16},{16,24},{24,28},{28,20},{20,12},{12,4},{4,0},{1,9},{9... | collective-permute-start | bytes 1544 | tf_op jit(solution)/shard_map/ppermute | solution.py:195
  35.9 7.1 %collective-permute-done.9 = s32[128]{0:T(128)S(1)} collective-permute-done((s32[128]{0:T(128)S(1)}, s32[128]{0:T(128)S(1)}, u32[]{:S(2)}, u32[]{:S(2)}) %collective-permute-start.9) | collective-permute-done | bytes 544 | tf_op jit(solution)/shard_map/ppermute | solution.py:195
  43.0 1.3 %collective-permute-done.11 = s32[128]{0:T(128)S(1)} collective-permute-done((s32[128]{0:T(128)S(1)}, s32[128]{0:T(128)S(1)}, u32[]{:S(2)}, u32[]{:S(2)}) %collective-permute-start.11) | collective-permute-done | bytes 544 | tf_op jit(solution)/shard_map/ppermute | solution.py:198
  45.1 1.5 %collective-permute-start.12 = (bf16[128,2,1024]{0,2,1:T(8,128)(2,1)}, bf16[128,2,1024]{0,2,1:T(8,128)(2,1)}, u32[]{:S(2)}, u32[]{:S(2)}) collective-permute-start(bf16[128,2,1024]{0,2,1:T(8,128)(2,1)} %collective-permute-done.8), channel_id=1, source_target_pairs={{0,8},{8,16},{16,24},{24,28},{28,20},{20,12},{12,4},{4,0},{1,9},{9... | collective-permute-start | bytes 1572872 | tf_op jit(solution)/shard_map/ppermute | solution.py:195
  46.6 0.9 collective-permute-start.13
  47.5 7.9 %collective-permute-done.13 = s32[128]{0:T(128)S(1)} collective-permute-done((s32[128]{0:T(128)S(1)}, s32[128]{0:T(128)S(1)}, u32[]{:S(2)}, u32[]{:S(2)}) %collective-permute-start.13) | collective-permute-done | bytes 544 | tf_op jit(solution)/shard_map/ppermute | solution.py:195
  56.6 2.1 %convolution_convert_fusion = bf16[256,1024]{1,0:T(8,128)(2,1)} fusion(bf16[128,3,1024]{2,0,1:T(8,128)(2,1)} %param.9, s32[128]{0:T(128)S(1)} %get-tuple-element.72), kind=kOutput, calls=%fused_computation.18 | convolution fusion | flops 67403776 | bytes 786944 | tf_op jit(solution)/shard_map/dot_general | solution.py:235
  58.6 3.7 %all-to-all-start = ((bf16[8,32,1024]{2,1,0:T(8,128)(2,1)}), bf16[8,32,1024]{2,1,0:T(8,128)(2,1)S(1)}, u32[]{:S(2)}, u32[]{:S(2)}) async-start(bf16[8,32,1024]{2,1,0:T(8,128)(2,1)} %bitcast.16), calls=%async_computation | async-start | bytes 1048576 | tf_op jit(solution)/shard_map/all_to_all | solution.py:237
  62.5 2.5 %select_reduce_fusion.1 = s32[8,128]{0,1:T(8,128)S(1)} fusion(s32[8,128]{0,1:T(8,128)S(1)} %copy.48), kind=kOutput, calls=%fused_computation.37 | output fusion | flops 1096704 | bytes 8192 | tf_op jit(solution)/shard_map/jit(cumsum)/reduce_window_sum | solution.py:227
  67.1 0.8 select_convert_fusion.2
  68.0 1.2 %constant_dynamic-update-slice_fusion.7 = bf16[1024,2,1024]{0,2,1:T(8,128)(2,1)S(1)} fusion(bf16[128,2,1024]{0,2,1:T(8,128)(2,1)} %collective-permute-done.12), kind=kLoop, calls=%fused_computation.74 | loop fusion | bytes 1048576
  69.2 1.2 %constant_dynamic-update-slice_fusion.6 = bf16[1024,2,1024]{0,2,1:T(8,128)(2,1)S(1)} fusion(bf16[1024,2,1024]{0,2,1:T(8,128)(2,1)S(1)} %constant_dynamic-update-slice_fusion.7, bf16[128,2,1024]{0,2,1:T(8,128)(2,1)} %collective-permute-done.8), kind=kLoop, calls=%fused_computation.73 | loop fusion | bytes 1048576
  71.6 1.8 %fusion.44 = (bf16[1024,1,1024]{0,2,1:T(8,128)(2,1)S(1)}, bf16[1024,1,1024]{0,2,1:T(8,128)(2,1)}) fusion(bf16[1024,2,1024]{0,2,1:T(8,128)(2,1)S(1)} %constant_dynamic-update-slice_fusion), kind=kLoop, calls=%fused_computation.175 | loop fusion | bytes 8388608 | tf_op jit(solution)/shard_map/slice | solution.py:250
  74.4 2.5 %multiply_reduce_fusion = (f32[8,128]{1,0:T(8,128)S(1)}, bf16[8,128,1024]{2,1,0:T(8,128)(2,1)S(1)}, bf16[8,128,1024]{2,1,0:T(8,128)(2,1)S(1)}) fusion(f32[128,1024]{1,0:T(8,128)S(1)} %copy-done.5, pred[]{:T(512)S(6)} %eq.335, f32[8,128,1024]{2,1,0:T(8,128)S(1)} %fusion.25, pred[128,1024]{1,0:T(8,128)(4,1)S(1)} %select_compare_fusion), kind=kOutput, calls=%fused_computation.7 | output fusion | flops 15729663 | bytes 9048065 | tf_op jit(solution)/shard_map/sub | solution.py:283
  76.9 1.7 %fusion.10 = f32[256,8,128]{0,2,1:T(8,128)S(1)} fusion(bf16[1024,8,128]{0,2,1:T(8,128)(2,1)S(1)} %bitcast.79, bf16[8,128,1024]{2,1,0:T(8,128)(2,1)S(1)} %get-tuple-element.43, bf16[8,128,1024]{2,1,0:T(8,128)(2,1)S(1)} %get-tuple-element.42), kind=kOutput, calls=%fused_computation.17 | convolution fusion | flops 545259520 | bytes 7340032 | tf_op jit(solution)/shard_map/hqk,khd->qhd/dot_general | solution.py:291
  78.7 1.3 %fusion.45 = f32[128,4096]{1,0:T(8,128)S(1)} fusion(bf16[128,1024]{0,1:T(8,128)(2,1)S(1)} %bitcast.80, bf16[1024,4096]{1,0:T(8,128)(2,1)S(1)} %bitcast.74), kind=kOutput, calls=%fused_computation.176 | convolution fusion | flops 1073741824 | bytes 10747904 | tf_op jit(solution)/shard_map/dot_general | solution.py:295
  80.2 1.9 %collective-permute-done.14 = bf16[2,32,4096]{2,1,0:T(8,128)(2,1)S(1)} collective-permute-done((bf16[2,32,4096]{2,1,0:T(8,128)(2,1)S(1)}, bf16[2,32,4096]{2,1,0:T(8,128)(2,1)S(1)}, u32[]{:S(2)}, u32[]{:S(2)}) %collective-permute-start.14) | collective-permute-done | bytes 524320 | tf_op jit(solution)/shard_map/ppermute | solution.py:314
  82.3 1.6 %collective-permute-start.15 = (bf16[1,32,4096]{2,1,0:T(8,128)(2,1)S(1)}, bf16[1,32,4096]{2,1,0:T(8,128)(2,1)S(1)}, u32[]{:S(2)}, u32[]{:S(2)}) collective-permute-start(bf16[1,32,4096]{2,1,0:T(8,128)(2,1)S(1)} %fusion.23), channel_id=1, source_target_pairs={{0,2},{1,3},{2,0},{3,1},{4,6},{5,7},{6,4},{7,5},{8,10},{9,11},{10,... | collective-permute-start | bytes 786440 | tf_op jit(solution)/shard_map/ppermute | solution.py:314
  83.8 6.9 %collective-permute-done.15 = bf16[1,32,4096]{2,1,0:T(8,128)(2,1)S(1)} collective-permute-done((bf16[1,32,4096]{2,1,0:T(8,128)(2,1)S(1)}, bf16[1,32,4096]{2,1,0:T(8,128)(2,1)S(1)}, u32[]{:S(2)}, u32[]{:S(2)}) %collective-permute-start.15) | collective-permute-done | bytes 262176 | tf_op jit(solution)/shard_map/ppermute | solution.py:314
  (91 shorter events, 12.8 us)
Async XLA Ops:
  0.0 62.3 %copy-start.6 = (s32[128]{0:T(128)S(1)}, s32[128]{0:T(128)}, u32[]{:S(2)}) copy-start(s32[128]{0:T(128)} %param.10) | copy-start | bytes 1540
  1.4 16.5 %collective-permute-start = (bf16[128,2,1024]{0,2,1:T(8,128)(2,1)S(1)}, bf16[128,2,1024]{0,2,1:T(8,128)(2,1)S(1)}, u32[]{:S(2)}, u32[]{:S(2)}) collective-permute-start(bf16[128,2,1024]{0,2,1:T(8,128)(2,1)S(1)} %copy.55), channel_id=1, source_target_pairs={{0,8},{8,16},{16,24},{24,28},{28,20},{20,12},{12,4},{4,0},{1,9},{9... | collective-permute-start | bytes 1572872 | tf_op jit(solution)/shard_map/ppermute | solution.py:195
  4.5 13.5 %collective-permute-start.2 = (bf16[128,2,1024]{0,2,1:T(8,128)(2,1)S(1)}, bf16[128,2,1024]{0,2,1:T(8,128)(2,1)S(1)}, u32[]{:S(2)}, u32[]{:S(2)}) collective-permute-start(bf16[128,2,1024]{0,2,1:T(8,128)(2,1)S(1)} %copy.55), channel_id=1, source_target_pairs={{0,4},{8,0},{16,8},{24,16},{28,24},{20,28},{12,20},{4,12},{1,5},{9... | collective-permute-start | bytes 1572872 | tf_op jit(solution)/shard_map/ppermute | solution.py:198
  4.5 11.9 %collective-permute-start.1 = (s32[128]{0:T(128)}, s32[128]{0:T(128)S(1)}, u32[]{:S(2)}, u32[]{:S(2)}) collective-permute-start(s32[128]{0:T(128)} %param.10), channel_id=1, source_target_pairs={{0,8},{8,16},{16,24},{24,28},{28,20},{20,12},{12,4},{4,0},{1,9},{9... | collective-permute-start | bytes 1544 | tf_op jit(solution)/shard_map/ppermute | solution.py:195
  6.5 11.4 %collective-permute-start.3 = (s32[128]{0:T(128)}, s32[128]{0:T(128)S(1)}, u32[]{:S(2)}, u32[]{:S(2)}) collective-permute-start(s32[128]{0:T(128)} %param.10), channel_id=1, source_target_pairs={{0,4},{8,0},{16,8},{24,16},{28,24},{20,28},{12,20},{4,12},{1,5},{9... | collective-permute-start | bytes 1544 | tf_op jit(solution)/shard_map/ppermute | solution.py:198
  17.9 13.8 %collective-permute-start.4 = (bf16[128,2,1024]{0,2,1:T(8,128)(2,1)S(1)}, bf16[128,2,1024]{0,2,1:T(8,128)(2,1)S(1)}, u32[]{:S(2)}, u32[]{:S(2)}) collective-permute-start(bf16[128,2,1024]{0,2,1:T(8,128)(2,1)S(1)} %collective-permute-done), channel_id=1, source_target_pairs={{0,8},{8,16},{16,24},{24,28},{28,20},{20,12},{12,4},{4,0},{1,9},{9... | collective-permute-start | bytes 1572872 | tf_op jit(solution)/shard_map/ppermute | solution.py:195
  19.5 12.2 %collective-permute-start.6 = (bf16[128,2,1024]{0,2,1:T(8,128)(2,1)S(1)}, bf16[128,2,1024]{0,2,1:T(8,128)(2,1)S(1)}, u32[]{:S(2)}, u32[]{:S(2)}) collective-permute-start(bf16[128,2,1024]{0,2,1:T(8,128)(2,1)S(1)} %collective-permute-done.2), channel_id=1, source_target_pairs={{0,4},{8,0},{16,8},{24,16},{28,24},{20,28},{12,20},{4,12},{1,5},{9... | collective-permute-start | bytes 1572872 | tf_op jit(solution)/shard_map/ppermute | solution.py:198
  20.6 9.8 %collective-permute-start.5 = (s32[128]{0:T(128)S(1)}, s32[128]{0:T(128)S(1)}, u32[]{:S(2)}, u32[]{:S(2)}) collective-permute-start(s32[128]{0:T(128)S(1)} %collective-permute-done.1), channel_id=1, source_target_pairs={{0,8},{8,16},{16,24},{24,28},{28,20},{20,12},{12,4},{4,0},{1,9},{9... | collective-permute-start | bytes 1544 | tf_op jit(solution)/shard_map/ppermute | solution.py:195
  22.2 9.5 %collective-permute-start.7 = (s32[128]{0:T(128)S(1)}, s32[128]{0:T(128)S(1)}, u32[]{:S(2)}, u32[]{:S(2)}) collective-permute-start(s32[128]{0:T(128)S(1)} %collective-permute-done.3), channel_id=1, source_target_pairs={{0,4},{8,0},{16,8},{24,16},{28,24},{20,28},{12,20},{4,12},{1,5},{9... | collective-permute-start | bytes 1544 | tf_op jit(solution)/shard_map/ppermute | solution.py:198
  31.7 26.9 %copy-start.1 = (bf16[128,2,1024]{0,2,1:T(8,128)(2,1)}, bf16[128,2,1024]{0,2,1:T(8,128)(2,1)S(1)}, u32[]{:S(2)}) copy-start(bf16[128,2,1024]{0,2,1:T(8,128)(2,1)S(1)} %collective-permute-done.4) | copy-start | bytes 1572868
  31.7 12.6 %collective-permute-start.8 = (bf16[128,2,1024]{0,2,1:T(8,128)(2,1)S(1)}, bf16[128,2,1024]{0,2,1:T(8,128)(2,1)}, u32[]{:S(2)}, u32[]{:S(2)}) collective-permute-start(bf16[128,2,1024]{0,2,1:T(8,128)(2,1)S(1)} %collective-permute-done.4), channel_id=1, source_target_pairs={{0,8},{8,16},{16,24},{24,28},{28,20},{20,12},{12,4},{4,0},{1,9},{9... | collective-permute-start | bytes 1572872 | tf_op jit(solution)/shard_map/ppermute | solution.py:195
  33.3 10.9 %collective-permute-start.10 = (bf16[128,2,1024]{0,2,1:T(8,128)(2,1)S(1)}, bf16[128,2,1024]{0,2,1:T(8,128)(2,1)S(1)}, u32[]{:S(2)}, u32[]{:S(2)}) collective-permute-start(bf16[128,2,1024]{0,2,1:T(8,128)(2,1)S(1)} %collective-permute-done.6), channel_id=1, source_target_pairs={{0,4},{8,0},{16,8},{24,16},{28,24},{20,28},{12,20},{4,12},{1,5},{9... | collective-permute-start | bytes 1572872 | tf_op jit(solution)/shard_map/ppermute | solution.py:198
  33.8 9.2 %collective-permute-start.9 = (s32[128]{0:T(128)S(1)}, s32[128]{0:T(128)S(1)}, u32[]{:S(2)}, u32[]{:S(2)}) collective-permute-start(s32[128]{0:T(128)S(1)} %collective-permute-done.5), channel_id=1, source_target_pairs={{0,8},{8,16},{16,24},{24,28},{28,20},{20,12},{12,4},{4,0},{1,9},{9... | collective-permute-start | bytes 1544 | tf_op jit(solution)/shard_map/ppermute | solution.py:195
  35.4 8.8 %collective-permute-start.11 = (s32[128]{0:T(128)S(1)}, s32[128]{0:T(128)S(1)}, u32[]{:S(2)}, u32[]{:S(2)}) collective-permute-start(s32[128]{0:T(128)S(1)} %collective-permute-done.7), channel_id=1, source_target_pairs={{0,4},{8,0},{16,8},{24,16},{28,24},{20,28},{12,20},{4,12},{1,5},{9... | collective-permute-start | bytes 1544 | tf_op jit(solution)/shard_map/ppermute | solution.py:198
  44.3 0.8 copy-start.3
  45.1 22.9 %collective-permute-start.12 = (bf16[128,2,1024]{0,2,1:T(8,128)(2,1)}, bf16[128,2,1024]{0,2,1:T(8,128)(2,1)}, u32[]{:S(2)}, u32[]{:S(2)}) collective-permute-start(bf16[128,2,1024]{0,2,1:T(8,128)(2,1)} %collective-permute-done.8), channel_id=1, source_target_pairs={{0,8},{8,16},{16,24},{24,28},{28,20},{20,12},{12,4},{4,0},{1,9},{9... | collective-permute-start | bytes 1572872 | tf_op jit(solution)/shard_map/ppermute | solution.py:195
  46.6 8.8 %collective-permute-start.13 = (s32[128]{0:T(128)S(1)}, s32[128]{0:T(128)S(1)}, u32[]{:S(2)}, u32[]{:S(2)}) collective-permute-start(s32[128]{0:T(128)S(1)} %collective-permute-done.9), channel_id=1, source_target_pairs={{0,8},{8,16},{16,24},{24,28},{28,20},{20,12},{12,4},{4,0},{1,9},{9... | collective-permute-start | bytes 1544 | tf_op jit(solution)/shard_map/ppermute | solution.py:195
  58.6 14.7 %all-to-all-start = ((bf16[8,32,1024]{2,1,0:T(8,128)(2,1)}), bf16[8,32,1024]{2,1,0:T(8,128)(2,1)S(1)}, u32[]{:S(2)}, u32[]{:S(2)}) async-start(bf16[8,32,1024]{2,1,0:T(8,128)(2,1)} %bitcast.16), calls=%async_computation | async-start | bytes 1048576 | tf_op jit(solution)/shard_map/all_to_all | solution.py:237
  65.1 5.4 %copy-start.2 = (bf16[128,2,1024]{0,2,1:T(8,128)(2,1)S(1)}, bf16[128,2,1024]{0,2,1:T(8,128)(2,1)}, u32[]{:S(2)}) copy-start(bf16[128,2,1024]{0,2,1:T(8,128)(2,1)} %copy-done.1) | copy-start | bytes 1572868
  67.1 4.2 %copy-start.4 = (bf16[128,2,1024]{0,2,1:T(8,128)(2,1)S(1)}, bf16[128,2,1024]{0,2,1:T(8,128)(2,1)}, u32[]{:S(2)}) copy-start(bf16[128,2,1024]{0,2,1:T(8,128)(2,1)} %copy-done.3) | copy-start | bytes 1572868
  73.3 1.0 %copy-start.5 = (f32[128,1024]{1,0:T(8,128)S(1)}, f32[128,1024]{1,0:T(8,128)}, u32[]{:S(2)}) copy-start(f32[128,1024]{1,0:T(8,128)} %select_convert_fusion.2) | copy-start | bytes 1572868
  73.6 5.1 %slice-start = ((s8[8388608]{0:T(1024)(128)(4,1)}), s8[4194304]{0:T(1024)(128)(4,1)S(1)}, s32[]{:S(2)}) async-start(s8[8388608]{0:T(1024)(128)(4,1)} %bitcast.73), calls=%async_computation.1 | async-start | bytes 8388608
  74.4 2.5 %copy-start = (bf16[1024,1,1024]{0,2,1:T(8,128)(2,1)S(1)}, bf16[1024,1,1024]{0,2,1:T(8,128)(2,1)}, u32[]{:S(2)}) copy-start(bf16[1024,1,1024]{0,2,1:T(8,128)(2,1)} %get-tuple-element.45) | copy-start | bytes 6291460
  74.4 4.3 %slice-start.1 = ((s8[8388608]{0:T(1024)(128)(4,1)}), s8[4194304]{0:T(1024)(128)(4,1)S(1)}, s32[]{:S(2)}) async-start(s8[8388608]{0:T(1024)(128)(4,1)} %bitcast.73), calls=%async_computation.2 | async-start | bytes 8388608
  80.1 2.0 %collective-permute-start.14 = (bf16[2,32,4096]{2,1,0:T(8,128)(2,1)S(1)}, bf16[2,32,4096]{2,1,0:T(8,128)(2,1)S(1)}, u32[]{:S(2)}, u32[]{:S(2)}) collective-permute-start(bf16[2,32,4096]{2,1,0:T(8,128)(2,1)S(1)} %fusion.19), channel_id=1, source_target_pairs={{0,1},{1,0},{2,3},{3,2},{4,5},{5,4},{6,7},{7,6},{8,9},{9,8},{10,11... | collective-permute-start | bytes 1572872 | tf_op jit(solution)/shard_map/ppermute | solution.py:314
  82.3 8.4 %collective-permute-start.15 = (bf16[1,32,4096]{2,1,0:T(8,128)(2,1)S(1)}, bf16[1,32,4096]{2,1,0:T(8,128)(2,1)S(1)}, u32[]{:S(2)}, u32[]{:S(2)}) collective-permute-start(bf16[1,32,4096]{2,1,0:T(8,128)(2,1)S(1)} %fusion.23), channel_id=1, source_target_pairs={{0,2},{1,3},{2,0},{3,1},{4,6},{5,7},{6,4},{7,5},{8,10},{9,11},{10,... | collective-permute-start | bytes 786440 | tf_op jit(solution)/shard_map/ppermute | solution.py:314
